TPU v7x, 32 devices: a whole 2x2x4 slice. The times are simulated.
32 devices in a mesh: gx: 4 (over x, core), gy: 8 (over z, y).
Axes of the slice: x: 2, y: 2, z: 4, core: 2. Of those that a mesh axis runs over, the one named last changes fastest.
Arguments:
- velocity: float32 [3, 8, 64, 2048], P(None, None, 'gx', 'gy'), may hold values from -6 to 6
- bulk: float32 [8, 64, 2048], P(None, 'gx', 'gy'), may hold values from 0.5 to 4
- prestress: float32 [8, 64, 2048], P(None, 'gx', 'gy'), may hold values from -6 to 6
- node_mass: float32 [8, 64, 2048], P(None, 'gx', 'gy'), may hold values from 0.5 to 2
- slave_pos: float32 [4096, 3, 128], P(('gx', 'gy')), may hold values from -1 to 1
- slave_area: float32 [4096, 128], P(('gx', 'gy')), may hold values from 0.5 to 2
- seg_count: int32 [4096], P(('gx', 'gy')), may hold values from 1 to 128, as said below
- slave_node: int32 [4096, 128], P(('gx', 'gy')), may hold values from 0 to 32767
- pair_owner: int32 [4096, 1], P(('gx', 'gy')), may hold values from 0 to 31; in each aligned block of 128 rows (0 to 127, 128 to 255, ...) at most 5 rows name the same one
- pair_master: int32 [4096], P(('gx', 'gy')), may hold values from 0 to 31
- master_cent: float32 [1024, 3, 128], P(('gx', 'gy')), may hold values from -1 to 1
- master_tilt: float32 [1024, 2, 128], P(('gx', 'gy')), may hold values from -3 to 3
- master_stiff: float32 [1024, 128], P(('gx', 'gy')), may hold values from 0.05 to 0.5
- master_node: int32 [1024, 128], P(('gx', 'gy')), may hold values from 0 to 32767
Outputs:
- velocity_new: float32 [3, 8, 64, 2048], P(None, None, 'gx', 'gy')
- node_rate: float32 [8, 64, 2048], P(None, 'gx', 'gy')
Inputs may be any that keep to these rules, and one draw needn't show every extreme that they name: Slots from seg_count on are padding; some block is full. `pair_owner`: owner index is its gx index times 8 plus its gy index. Among the 128 slave blocks of one device no owner is named more than 5 times, a bound that some block reaches.
All inputs are finite; a program needn't handle non-finite values.
Results may differ from a plain program's by a relative error of at most 0.000084.
Values sent between devices are 32-bit elements; how exact they have to be, the bound alone decides.
No kernel may reach another device: no remote copies, remote signals or barrier semaphores. Data moves between devices by JAX's collectives and lax.ppermute only.
A program may use at most 128 MiB of HBM per device.

v0:
```python
import jax
import jax.numpy as jnp
from jax import lax
from jax.sharding import PartitionSpec as P

TIME_STEP = 0.25
VISCOUS = 0.5
SOFT_GAP = 0.2
REACH_SQ = 1.0
DAMPING = 0.5


def padded_2(block, sides, width):
    for axis, dim in sides:
        count = lax.axis_size(axis)
        forward = [(i, i + 1) for i in range(count - 1)]
        backward = [(target, source) for source, target in forward]
        low = lax.ppermute(
            lax.slice_in_dim(block, block.shape[dim] - width, None, axis=dim), axis, forward
        )
        high = lax.ppermute(lax.slice_in_dim(block, 0, width, axis=dim), axis, backward)
        block = jnp.concatenate([low, block, high], axis=dim)
    return block


def pair_mean(values, along):
    length = values.shape[along]
    return 0.5 * (
        lax.slice_in_dim(values, 0, length - 1, axis=along)
        + lax.slice_in_dim(values, 1, length, axis=along)
    )


def pair_diff(values, along):
    length = values.shape[along]
    return lax.slice_in_dim(values, 1, length, axis=along) - lax.slice_in_dim(
        values, 0, length - 1, axis=along
    )


def pair_prod(values, along):
    length = values.shape[along]
    return lax.slice_in_dim(values, 0, length - 1, axis=along) * lax.slice_in_dim(
        values, 1, length, axis=along
    )


def corner_mean(values):
    return pair_mean(pair_mean(pair_mean(values, 0), 1), 2)


def zone_rate(vel):
    rate_x = pair_diff(pair_mean(pair_mean(vel[0], 0), 2), 1)
    rate_y = pair_diff(pair_mean(pair_mean(vel[1], 0), 1), 2)
    rate_z = pair_diff(pair_mean(pair_mean(vel[2], 1), 2), 0)
    return rate_x + rate_y + rate_z


def stress_forces(padded):
    inside = pair_prod(pair_prod(pair_prod(padded[5], 0), 1), 2)
    strain = TIME_STEP * zone_rate(padded[0:3])
    pressure = inside * (
        corner_mean(padded[4]) + corner_mean(padded[3]) * (VISCOUS * strain * strain - strain)
    )
    framed = jnp.pad(pressure, ((1, 1), (0, 0), (0, 0)))
    force_x = -pair_diff(pair_mean(pair_mean(framed, 0), 2), 1)
    force_y = -pair_diff(pair_mean(pair_mean(framed, 0), 1), 2)
    force_z = -pair_diff(pair_mean(pair_mean(framed, 1), 2), 0)
    return (jnp.stack([force_x, force_y, force_z], axis=0), inside)


def nodal_rate(padded_vel, inside):
    rate = inside * zone_rate(padded_vel)
    framed = jnp.pad(rate, ((1, 1), (0, 0), (0, 0)))
    return pair_mean(pair_mean(pair_mean(framed, 0), 1), 2)


def contact_pairs(slave, master):
    delta_x = slave[:, 0, :, None] - master[:, 0, None, :]
    delta_y = slave[:, 1, :, None] - master[:, 1, None, :]
    delta_z = slave[:, 2, :, None] - master[:, 2, None, :]
    normal_x = master[:, 3, None, :]
    normal_y = master[:, 4, None, :]
    normal_z = master[:, 5, None, :]
    dist_sq = delta_x * delta_x + delta_y * delta_y + delta_z * delta_z
    gap_normal = normal_x * delta_x + normal_y * delta_y + normal_z * delta_z
    closing = (
        normal_x * (slave[:, 3, :, None] - master[:, 6, None, :])
        + normal_y * (slave[:, 4, :, None] - master[:, 7, None, :])
        + normal_z * (slave[:, 5, :, None] - master[:, 8, None, :])
    )
    weight = jnp.exp(-dist_sq / REACH_SQ)
    depth_soft = SOFT_GAP * jax.nn.softplus(-gap_normal / SOFT_GAP)
    push_force = (
        slave[:, 6, :, None]
        * master[:, 9, None, :]
        * weight
        * depth_soft
        * (1.0 + DAMPING * jnp.tanh(-closing))
    )
    slave_force = jnp.stack(
        [
            jnp.sum(push_force * normal_x, axis=2),
            jnp.sum(push_force * normal_y, axis=2),
            jnp.sum(push_force * normal_z, axis=2),
        ],
        axis=1,
    )
    reaction = jnp.sum(push_force, axis=1)
    return (slave_force, reaction)


def master_normals(master_tilt):
    scale = lax.rsqrt(
        1.0 + master_tilt[:, 0] * master_tilt[:, 0] + master_tilt[:, 1] * master_tilt[:, 1]
    )
    return jnp.stack([master_tilt[:, 0] * scale, master_tilt[:, 1] * scale, scale], axis=1)


def on_device(
    velocity,
    bulk,
    prestress,
    node_mass,
    slave_pos,
    slave_area,
    seg_count,
    slave_node,
    pair_owner,
    pair_master,
    master_cent,
    master_tilt,
    master_stiff,
    master_node,
):
    count_gx = lax.axis_size("gx")
    count_gy = lax.axis_size("gy")
    devices = count_gx * count_gy
    layers, row_cells, col_cells = bulk.shape
    node_total = layers * row_cells * col_cells
    block_total, _, seg_width = slave_pos.shape
    master_total = master_cent.shape[0]
    slot_depth = (block_total + devices - 1) // devices + 1
    stacked = jnp.concatenate(
        [velocity, bulk[None], prestress[None], jnp.ones_like(bulk)[None]], axis=0
    )
    padded = padded_2(stacked, (("gx", 2), ("gy", 3)), 1)
    stress, inside = stress_forces(padded)
    vel_flat = velocity.reshape(3, node_total)
    slave_vel = jnp.take(vel_flat, slave_node, axis=1).transpose(1, 0, 2)
    master_vel = jnp.take(vel_flat, master_node, axis=1).transpose(1, 0, 2)
    live_mask = jnp.arange(seg_width, dtype=jnp.int32)[None, :] < seg_count[:, None]
    area_live = jnp.where(live_mask, slave_area, jnp.zeros_like(slave_area))
    slave = jnp.concatenate(
        [slave_pos + TIME_STEP * slave_vel, slave_vel, area_live[:, None, :]], axis=1
    )
    normals = master_normals(master_tilt)
    master_data = jnp.concatenate(
        [master_cent + TIME_STEP * master_vel, normals, master_vel, master_stiff[:, None, :]],
        axis=1,
    )
    owners = pair_owner[:, 0]
    positions = jnp.arange(block_total, dtype=jnp.int32)
    earlier = (owners[:, None] == owners[None, :]) & (positions[None, :] < positions[:, None])
    slot_index = jnp.sum(earlier.astype(jnp.int32), axis=1)
    target_slot = owners * slot_depth + slot_index
    outgoing = (
        jnp.zeros((devices * slot_depth, 7, seg_width), jnp.float32).at[target_slot].set(slave)
    )
    chosen = jnp.zeros((devices * slot_depth,), jnp.int32).at[target_slot].set(pair_master)
    arrived, picked = (
        lax.all_to_all(
            outgoing.reshape(devices, slot_depth, 7, seg_width),
            ("gx", "gy"),
            split_axis=0,
            concat_axis=0,
            tiled=True,
        ),
        lax.all_to_all(
            chosen.reshape(devices, slot_depth),
            ("gx", "gy"),
            split_axis=0,
            concat_axis=0,
            tiled=True,
        ),
    )
    item_total = devices * slot_depth
    arrived = arrived.reshape(item_total, 7, seg_width)
    picked = picked.reshape(item_total)
    paired = jnp.take(master_data, picked, axis=0)
    group_size = 16 * slot_depth

    def per_group(pairing):
        return contact_pairs(pairing[0], pairing[1])

    forces, reaction = lax.map(
        per_group,
        (
            arrived.reshape(item_total // group_size, group_size, 7, seg_width),
            paired.reshape(item_total // group_size, group_size, 10, seg_width),
        ),
    )
    forces = forces.reshape(item_total, 3, seg_width)
    reaction = reaction.reshape(item_total, seg_width)
    onehot = (picked[:, None] == jnp.arange(master_total, dtype=jnp.int32)[None, :]).astype(
        jnp.float32
    )
    master_sum = jnp.dot(onehot.T, reaction, precision=lax.Precision.HIGHEST)
    master_force = -master_sum[:, None, :] * normals
    returned = lax.all_to_all(
        forces.reshape(devices, slot_depth, 3, seg_width),
        ("gx", "gy"),
        split_axis=0,
        concat_axis=0,
        tiled=True,
    )
    slave_force = jnp.take(returned.reshape(item_total, 3, seg_width), target_slot, axis=0)
    contact = jnp.zeros((3, node_total), jnp.float32)
    contact = contact.at[:, slave_node.reshape(-1)].add(
        slave_force.transpose(1, 0, 2).reshape(3, -1)
    )
    contact = contact.at[:, master_node.reshape(-1)].add(
        master_force.transpose(1, 0, 2).reshape(3, -1)
    )
    contact_field = contact.reshape(3, layers, row_cells, col_cells)
    velocity_new = velocity + TIME_STEP * (stress + contact_field) / node_mass[None]
    padded_new = padded_2(velocity_new, (("gx", 2), ("gy", 3)), 1)
    node_rate = nodal_rate(padded_new, inside)
    return (velocity_new, node_rate)


def solution(mesh):
    placed = (
        P(None, None, "gx", "gy"),
        P(None, "gx", "gy"),
        P(None, "gx", "gy"),
        P(None, "gx", "gy"),
        P(("gx", "gy"), None, None),
        P(("gx", "gy"), None),
        P(("gx", "gy")),
        P(("gx", "gy"), None),
        P(("gx", "gy"), None),
        P(("gx", "gy")),
        P(("gx", "gy"), None, None),
        P(("gx", "gy"), None, None),
        P(("gx", "gy"), None),
        P(("gx", "gy"), None),
    )
    return jax.shard_map(
        on_device,
        mesh=mesh,
        in_specs=placed,
        out_specs=(P(None, None, "gx", "gy"), P(None, "gx", "gy")),
        check_vma=False,
    )
```

profile of v0, /device:TPU:9, one launch (start us, length us, event | category | flops | bytes accessed | tf_op | source)
XLA Modules:
  0.0 394.5 jit_solution(10884962098689651939)
XLA Ops:
  4.6 6.4 %all-to-all-start.1 = ((s32[32,1,5]{2,1,0:T(1,128)}), s32[32,1,5]{2,1,0:T(1,128)S(1)}, u32[]{:S(2)}, u32[]{:S(2)}) async-start(s32[32,1,5]{2,1,0:T(1,128)} %bitcast.48), calls=%async_computation.1 | async-start | bytes 32768 | tf_op jit(solution)/shard_map/all_to_all | solution.py:179
  13.0 2.3 collective-permute-start.1
  15.9 3.4 collective-permute-start
  19.3 9.6 %copy.159 = f32[3,8,16,256]{0,3,2,1:T(8,128)} copy(f32[3,8,16,256]{3,2,1,0:T(8,128)} %param.16) | data formatting | bytes 786432 | tf_op args[0]
  29.7 60.2 %gather_fusion = f32[16384,3]{1,0:T(8,128)} fusion(f32[3,32768]{0,1:T(8,128)} %bitcast.151, s32[16384]{0:T(1024)S(1)} %bitcast_clamp_fusion), kind=kCustom, calls=%fused_computation | custom fusion | bytes 458752 | tf_op jit(solution)/shard_map/jit(_take)/gather | solution.py:150
  89.9 5.3 %copy.160 = f32[128,128,3]{1,0,2:T(8,128)S(1)} copy(f32[128,128,3]{2,1,0:T(8,128)} %bitcast.153) | data formatting | bytes 393216 | tf_op jit(solution)/shard_map/jit(_take)/gather | solution.py:150
  95.2 16.5 %gather_fusion.1 = f32[4096,3]{1,0:T(8,128)S(1)} fusion(f32[3,32768]{0,1:T(8,128)} %bitcast.152, s32[4096]{0:T(1024)S(1)} %bitcast_clamp_fusion.1), kind=kCustom, calls=%fused_computation.1 | custom fusion | bytes 114688 | tf_op jit(solution)/shard_map/jit(_take)/gather | solution.py:151
  114.2 4.0 %copy.154 = f32[6,8,16,256]{2,1,3,0:T(8,128)} copy(f32[6,8,16,256]{3,2,1,0:T(8,128)S(1)} %maximum_maximum_fusion) | data formatting | bytes 1572864 | tf_op jit(solution)/shard_map/concatenate | solution.py:144
  119.5 12.4 %scatter_fusion = f32[160,7,128]{2,1,0:T(8,128)} fusion(f32[160,7,128]{2,1,0:T(8,128)} %broadcast_in_dim.103, s32[128]{0:T(128)S(1)} %bitcast.179, f32[128,7,128]{2,1,0:T(8,128)S(1)} %copy.161), kind=kCustom, calls=%fused_computation.4 | custom fusion | bytes 1376768 | tf_op jit(solution)/shard_map/scatter | solution.py:168
  132.2 5.2 %all-to-all-start = ((f32[32,5,7,128]{3,2,1,0:T(8,128)}), f32[32,5,7,128]{3,2,1,0:T(8,128)S(1)}, u32[]{:S(2)}, u32[]{:S(2)}) async-start(f32[32,5,7,128]{3,2,1,0:T(8,128)} %bitcast.46), calls=%async_computation | async-start | bytes 1310720 | tf_op jit(solution)/shard_map/all_to_all | solution.py:172
  139.6 4.7 %copy.155 = f32[6,8,1,256]{2,1,3,0:T(8,128)} copy(f32[6,8,1,256]{3,1,2,0:T(8,128)} %collective-permute-done.1) | data formatting | bytes 98304 | tf_op jit(solution)/shard_map/ppermute | solution.py:21
  144.3 4.7 %copy.153 = f32[6,8,1,256]{2,1,3,0:T(8,128)} copy(f32[6,8,1,256]{3,1,2,0:T(8,128)} %collective-permute-done) | data formatting | bytes 98304 | tf_op jit(solution)/shard_map/ppermute | solution.py:18
  149.0 8.1 %pad_maximum_fusion = f32[6,8,18,256]{2,1,3,0:T(8,128)S(1)} fusion(f32[6,8,1,256]{2,1,3,0:T(8,128)} %copy.155, f32[6,8,16,256]{2,1,3,0:T(8,128)} %copy.154, f32[6,8,1,256]{2,1,3,0:T(8,128)} %copy.153), kind=kLoop, calls=%fused_computation.55 | loop fusion | flops 442368 | bytes 1769472 | tf_op jit(solution)/shard_map/concatenate | solution.py:22
  157.2 2.7 copy-done
  160.4 3.1 collective-permute-start.3
  163.5 2.4 collective-permute-start.2
  166.3 4.4 %copy.157 = f32[6,8,18,256]{3,1,2,0:T(8,128)S(1)} copy(f32[6,8,18,256]{2,1,3,0:T(8,128)} %copy-done) | data formatting | bytes 1769472 | tf_op jit(solution)/shard_map/concatenate | solution.py:22
  175.5 36.2 %while.12 = (s32[]{:T(128)}, f32[2,80,3,128]{3,1,2,0:T(8,128)S(1)}, f32[2,80,128]{2,1,0:T(8,128)S(1)}, f32[2,80,7,128]{3,1,2,0:T(8,128)S(1)}, f32[2,80,10,128]{3,1,2,0:T(8,128)S(1)}, /*index=5*/s32[]{:T(128)}) while((s32[]{:T(128)}, f32[2,80,3,128]{3,1,2,0:T(8,128)S(1)}, f32[2,80,128]{2,1,0:T(8,128)S(1)}, f32[2,80,7,128]{3,1,2,0:T(8,128)S(1)}, ...), condition=%wide.region_8.9_spmd, body=%wide.region_3.8_spmd.sunk | while | flops 59002880 | bytes 3973213 | solution.py:196
  175.6 17.9 %fusion.84 = (f32[80,128]{1,0:T(8,128)S(1)}, f32[80,128]{1,0:T(8,128)S(1)}, f32[80,128]{1,0:T(8,128)S(1)}, f32[80,128]{1,0:T(8,128)S(1)}) fusion(f32[80,128]{1,0:T(8,128)S(1)} %get-tuple-element.179, f32[80,128]{1,0:T(8,128)S(1)} %get-tuple-element.180, f32[80,128]{1,0:T(8,128)S(1)} %get-tuple-element.181, f32[80,128]{1,0:T(8,128)S(1)} %get-tuple-element.182, ...), kind=kLoop, calls=%fused_computation.52.clone.1 | loop fusion | flops 58941440 | bytes 860160 | tf_op jit(solution)/shard_map/while/body/eval_jaxpr/reduce_sum | solution.py:109
  193.7 17.9 %fusion.84 = (f32[80,128]{1,0:T(8,128)S(1)}, f32[80,128]{1,0:T(8,128)S(1)}, f32[80,128]{1,0:T(8,128)S(1)}, f32[80,128]{1,0:T(8,128)S(1)}) fusion(f32[80,128]{1,0:T(8,128)S(1)} %get-tuple-element.179, f32[80,128]{1,0:T(8,128)S(1)} %get-tuple-element.180, f32[80,128]{1,0:T(8,128)S(1)} %get-tuple-element.181, f32[80,128]{1,0:T(8,128)S(1)} %get-tuple-element.182, ...), kind=kLoop, calls=%fused_computation.52.clone.1 | loop fusion | flops 58941440 | bytes 860160 | tf_op jit(solution)/shard_map/while/body/eval_jaxpr/reduce_sum | solution.py:109
  212.5 6.3 %all-to-all-start.2 = ((f32[32,5,3,128]{3,2,1,0:T(4,128)}), f32[32,5,3,128]{3,2,1,0:T(4,128)S(1)}, u32[]{:S(2)}, u32[]{:S(2)}) async-start(f32[32,5,3,128]{3,2,1,0:T(4,128)} %bitcast.58), calls=%async_computation.2 | async-start | bytes 655360 | tf_op jit(solution)/shard_map/all_to_all | solution.py:210
  219.2 2.0 copy.175
  221.3 8.7 %all-to-all-done.2 = f32[32,5,3,128]{3,2,1,0:T(4,128)S(1)} async-done(((f32[32,5,3,128]{3,2,1,0:T(4,128)}), f32[32,5,3,128]{3,2,1,0:T(4,128)S(1)}, u32[]{:S(2)}, u32[]{:S(2)}) %all-to-all-start.2) | async-done | bytes 245792 | tf_op jit(solution)/shard_map/all_to_all | solution.py:210
  231.0 5.1 %copy.174 = f32[16384,3]{1,0:T(8,128)} copy(f32[16384,3]{0,1:T(4,128)S(1)} %select_bitcast_fusion) | data formatting | bytes 393216 | tf_op jit(solution)/shard_map/reshape | solution.py:220
  236.1 94.4 %scatter_custom_fusion.2 = f32[3,32768]{0,1:T(8,128)} fusion(s32[16384]{0:T(1024)} %bitcast.173, f32[16384,3]{1,0:T(8,128)} %copy.174, f32[]{:T(128)} %constant.56.clone.1), kind=kCustom, calls=%fused_computation.53 | custom fusion | flops 49152 | bytes 393728 | tf_op jit(solution)/shard_map/scatter-add | solution.py:219
  330.4 31.9 %scatter_fusion.1 = f32[3,32768]{0,1:T(8,128)} fusion(f32[3,32768]{0,1:T(8,128)} %scatter_custom_fusion.2, s32[4096]{0:T(1024)S(1)} %bitcast.172, f32[4096,3]{1,0:T(8,128)} %copy.175), kind=kCustom, calls=%fused_computation.7 | custom fusion | flops 12288 | bytes 163840 | tf_op jit(solution)/shard_map/scatter-add | solution.py:222
  362.3 10.0 %copy.176 = f32[3,8,16,256]{3,1,2,0:T(8,128)S(1)} copy(f32[3,8,16,256]{0,3,2,1:T(8,128)} %bitcast.150) | data formatting | bytes 786432 | tf_op jit(solution)/shard_map/reshape | solution.py:225
  372.7 2.3 collective-permute-start.5
  375.0 3.3 collective-permute-start.4
  379.4 3.2 collective-permute-start.7
  382.5 2.1 collective-permute-start.6
  385.5 7.1 %collective-permute-done.7 = f32[3,8,18,1]{3,1,2,0:T(8,128)S(1)} collective-permute-done((f32[3,8,18,1]{3,1,2,0:T(8,128)S(1)}, f32[3,8,18,1]{3,1,2,0:T(8,128)S(1)}, u32[]{:S(2)}, u32[]{:S(2)}) %collective-permute-start.7) | collective-permute-done | bytes 1760 | tf_op jit(solution)/shard_map/ppermute | solution.py:21
  (131 shorter events, 25.4 us)
Async XLA Ops:
  2.7 111.4 %copy-start.11 = (s32[128,1]{0,1:T(1,128)}, s32[128,1]{0,1:T(1,128)S(1)}, u32[]{:S(2)}) copy-start(s32[128,1]{0,1:T(1,128)S(1)} %get-tuple-element.74) | copy-start | bytes 1540
  4.6 127.7 %all-to-all-start.1 = ((s32[32,1,5]{2,1,0:T(1,128)}), s32[32,1,5]{2,1,0:T(1,128)S(1)}, u32[]{:S(2)}, u32[]{:S(2)}) async-start(s32[32,1,5]{2,1,0:T(1,128)} %bitcast.48), calls=%async_computation.1 | async-start | bytes 32768 | tf_op jit(solution)/shard_map/all_to_all | solution.py:179
  13.0 126.6 %collective-permute-start.1 = (f32[6,8,1,256]{3,1,2,0:T(8,128)}, f32[6,8,1,256]{3,1,2,0:T(8,128)}, u32[]{:S(2)}, u32[]{:S(2)}) collective-permute-start(f32[6,8,1,256]{3,1,2,0:T(8,128)} %copy.184), channel_id=1, source_target_pairs={{8,0},{16,8},{24,16},{9,1},{17,9},{25,17},{10,2},{18,10},{26,18},{... | collective-permute-start | bytes 147464 | tf_op jit(solution)/shard_map/ppermute | solution.py:21
  15.9 13.0 %copy-start.2 = (s32[128,128]{1,0:T(8,128)S(1)}, s32[128,128]{1,0:T(8,128)}, u32[]{:S(2)}) copy-start(s32[128,128]{1,0:T(8,128)} %param.23) | copy-start | bytes 196612
  15.9 13.1 %copy-start.5 = (s32[32,128]{1,0:T(8,128)S(1)}, s32[32,128]{1,0:T(8,128)}, u32[]{:S(2)}) copy-start(s32[32,128]{1,0:T(8,128)} %param.29) | copy-start | bytes 49156
  15.9 128.5 %collective-permute-start = (f32[6,8,1,256]{3,1,2,0:T(8,128)}, f32[6,8,1,256]{3,1,2,0:T(8,128)}, u32[]{:S(2)}, u32[]{:S(2)}) collective-permute-start(f32[6,8,1,256]{3,1,2,0:T(8,128)} %copy.183), channel_id=1, source_target_pairs={{0,8},{8,16},{16,24},{1,9},{9,17},{17,25},{2,10},{10,18},{18,26},{... | collective-permute-start | bytes 147464 | tf_op jit(solution)/shard_map/ppermute | solution.py:18
  89.9 24.0 %copy-start.8 = (f32[128,128]{1,0:T(8,128)S(1)}, f32[128,128]{1,0:T(8,128)}, u32[]{:S(2)}) copy-start(f32[128,128]{1,0:T(8,128)} %param.21) | copy-start | bytes 196612
  89.9 24.0 %copy-start.14 = (s32[128]{0:T(128)S(1)}, s32[128]{0:T(128)}, u32[]{:S(2)}) copy-start(s32[128]{0:T(128)} %param.22) | copy-start | bytes 1540
  89.9 24.1 %copy-start.4 = (f32[128,3,128]{2,0,1:T(8,128)S(1)}, f32[128,3,128]{2,0,1:T(8,128)}, u32[]{:S(2)}) copy-start(f32[128,3,128]{2,0,1:T(8,128)} %param.20) | copy-start | bytes 589828
  89.9 24.2 %copy-start.9 = (f32[32,3,128]{2,0,1:T(8,128)S(1)}, f32[32,3,128]{2,0,1:T(8,128)}, u32[]{:S(2)}) copy-start(f32[32,3,128]{2,0,1:T(8,128)} %param.26) | copy-start | bytes 147460
  112.4 6.1 %copy-start.6 = (f32[8,16,256]{2,1,0:T(8,128)S(1)}, f32[8,16,256]{2,1,0:T(8,128)}, u32[]{:S(2)}) copy-start(f32[8,16,256]{2,1,0:T(8,128)} %param.19) | copy-start | bytes 393220
  114.2 5.3 %copy-start.12 = (s32[128,1]{0,1:T(1,128)S(1)}, s32[128,1]{0,1:T(1,128)}, u32[]{:S(2)}) copy-start(s32[128,1]{0,1:T(1,128)} %copy-done.11) | copy-start | bytes 1540
  114.2 17.6 %copy-start.10 = (f32[32,128]{1,0:T(8,128)S(1)}, f32[32,128]{1,0:T(8,128)}, u32[]{:S(2)}) copy-start(f32[32,128]{1,0:T(8,128)} %param.28) | copy-start | bytes 49156
  132.2 43.1 %all-to-all-start = ((f32[32,5,7,128]{3,2,1,0:T(8,128)}), f32[32,5,7,128]{3,2,1,0:T(8,128)S(1)}, u32[]{:S(2)}, u32[]{:S(2)}) async-start(f32[32,5,7,128]{3,2,1,0:T(8,128)} %bitcast.46), calls=%async_computation | async-start | bytes 1310720 | tf_op jit(solution)/shard_map/all_to_all | solution.py:172
  157.2 2.7 copy-start
  160.4 10.3 %collective-permute-start.3 = (f32[6,8,18,1]{2,1,3,0:T(8,128)S(1)}, f32[6,8,18,1]{2,1,3,0:T(8,128)S(1)}, u32[]{:S(2)}, u32[]{:S(2)}) collective-permute-start(f32[6,8,18,1]{2,1,3,0:T(8,128)S(1)} %get-tuple-element.104), channel_id=1, source_target_pairs={{1,0},{2,1},{3,2},{4,3},{5,4},{6,5},{7,6},{9,8},{10,9},{11,10},{12... | collective-permute-start | bytes 10376 | tf_op jit(solution)/shard_map/ppermute | solution.py:21
  163.5 7.7 %collective-permute-start.2 = (f32[6,8,18,1]{2,1,3,0:T(8,128)}, f32[6,8,18,1]{2,1,3,0:T(8,128)S(1)}, u32[]{:S(2)}, u32[]{:S(2)}) collective-permute-start(f32[6,8,18,1]{2,1,3,0:T(8,128)} %get-tuple-element.103), channel_id=1, source_target_pairs={{0,1},{1,2},{2,3},{3,4},{4,5},{5,6},{6,7},{8,9},{9,10},{10,11},{11... | collective-permute-start | bytes 10376 | tf_op jit(solution)/shard_map/ppermute | solution.py:18
  174.2 1.2 copy-start.3
  175.5 55.3 %copy-start.13 = (pred[128]{0:T(512)(128)(4,1)S(1)}, pred[128]{0:T(512)(128)(4,1)}, u32[]{:S(2)}) copy-start(pred[128]{0:T(512)(128)(4,1)} %get-tuple-element.73) | copy-start | bytes 388
  212.5 17.5 %all-to-all-start.2 = ((f32[32,5,3,128]{3,2,1,0:T(4,128)}), f32[32,5,3,128]{3,2,1,0:T(4,128)S(1)}, u32[]{:S(2)}, u32[]{:S(2)}) async-start(f32[32,5,3,128]{3,2,1,0:T(4,128)} %bitcast.58), calls=%async_computation.2 | async-start | bytes 655360 | tf_op jit(solution)/shard_map/all_to_all | solution.py:210
  236.1 94.4 %copy-start.7 = (s32[4096,1]{0,1:T(1,128)S(1)}, s32[4096,1]{0,1:T(1,128)}, u32[]{:S(2)}) copy-start(s32[4096,1]{0,1:T(1,128)} %compare_select_fusion.3) | copy-start | bytes 49156
  362.3 10.0 %copy-start.1 = (f32[3,8,16,256]{3,2,1,0:T(8,128)S(1)}, f32[3,8,16,256]{3,2,1,0:T(8,128)}, u32[]{:S(2)}) copy-start(f32[3,8,16,256]{3,2,1,0:T(8,128)} %param.16) | copy-start | bytes 1179652
  372.7 5.6 %collective-permute-start.5 = (f32[3,8,1,256]{3,1,2,0:T(8,128)S(1)}, f32[3,8,1,256]{3,1,2,0:T(8,128)S(1)}, u32[]{:S(2)}, u32[]{:S(2)}) collective-permute-start(f32[3,8,1,256]{3,1,2,0:T(8,128)S(1)} %get-tuple-element.117), channel_id=1, source_target_pairs={{8,0},{16,8},{24,16},{9,1},{17,9},{25,17},{10,2},{18,10},{26,18},{... | collective-permute-start | bytes 73736 | tf_op jit(solution)/shard_map/ppermute | solution.py:21
  375.0 4.2 %collective-permute-start.4 = (f32[3,8,1,256]{3,1,2,0:T(8,128)S(1)}, f32[3,8,1,256]{3,1,2,0:T(8,128)S(1)}, u32[]{:S(2)}, u32[]{:S(2)}) collective-permute-start(f32[3,8,1,256]{3,1,2,0:T(8,128)S(1)} %get-tuple-element.116), channel_id=1, source_target_pairs={{0,8},{8,16},{16,24},{1,9},{9,17},{17,25},{2,10},{10,18},{18,26},{... | collective-permute-start | bytes 73736 | tf_op jit(solution)/shard_map/ppermute | solution.py:18
  379.4 13.3 %collective-permute-start.7 = (f32[3,8,18,1]{3,1,2,0:T(8,128)S(1)}, f32[3,8,18,1]{3,1,2,0:T(8,128)S(1)}, u32[]{:S(2)}, u32[]{:S(2)}) collective-permute-start(f32[3,8,18,1]{3,1,2,0:T(8,128)S(1)} %get-tuple-element.115), channel_id=1, source_target_pairs={{1,0},{2,1},{3,2},{4,3},{5,4},{6,5},{7,6},{9,8},{10,9},{11,10},{12... | collective-permute-start | bytes 5192 | tf_op jit(solution)/shard_map/ppermute | solution.py:21
  382.5 10.1 %collective-permute-start.6 = (f32[3,8,18,1]{3,1,2,0:T(8,128)S(1)}, f32[3,8,18,1]{3,1,2,0:T(8,128)S(1)}, u32[]{:S(2)}, u32[]{:S(2)}) collective-permute-start(f32[3,8,18,1]{3,1,2,0:T(8,128)S(1)} %get-tuple-element.114), channel_id=1, source_target_pairs={{0,1},{1,2},{2,3},{3,4},{4,5},{5,6},{6,7},{8,9},{9,10},{10,11},{11... | collective-permute-start | bytes 5192 | tf_op jit(solution)/shard_map/ppermute | solution.py:18
where the time goes:
time: 398 us; the launch traced here: 394 us
  other arithmetic  180 us (45%)
  local copies, waits for them, and re-layouts  155 us (39%)
  starting transfers between devices  39.9 us (10%)
  waiting for transfers between devices  16.8 us (4%)
    scatter-add x1, other arithmetic, on_device(): contact.at[:, slave_node.reshape(-1)]  94.4 us
    gather x2, local copies, waits for them, and re-layouts, on_device(): slave_vel = jnp.take(vel_flat, slave_node, axis=1).transpose(1, 0, 2)  65.5 us
    reduce_sum x2, other arithmetic, contact_pairs(): reaction = jnp.sum(push_force, axis=1)  35.8 us
    scatter-add x1, other arithmetic, on_device(): contact.at[:, master_node.reshape(-1)]  31.9 us
    gather x2, local copies, waits for them, and re-layouts, on_device(): master_vel = jnp.take(vel_flat, master_node, axis=1).transpose(1, 0, 2)  17.2 us
    unnamed x37, local copies, waits for them, and re-layouts  15.2 us
    scatter x1, local copies, waits for them, and re-layouts, on_device(): jnp.zeros((devices * slot_depth, 7, seg_width), jnp.float32).at[target_slot]  12.4 us
    ppermute x4, starting transfers between devices, padded_2(): lax.ppermute(lax.slice_in_dim(block, block.shape[dim] - width, None, axis...  11.2 us
  transfers between devices with their start and end apart: 11, of which 3 were waited for; matrix products, arithmetic and copies ran while one was open for 38% of the time, Pallas kernels for 0%

commit v1 on v0

--- a/solution.py
+++ b/solution.py
@@ -2,6 +2,104 @@
 import jax.numpy as jnp
 from jax import lax
 from jax.sharding import PartitionSpec as P
+from jax.experimental import pallas as pl
+from jax.experimental.pallas import tpu as pltpu
+
+LANES = 128
+TILE = 2048
+
+
+def split_pieces(values):
+    first = values.astype(jnp.bfloat16)
+    rest = values - first.astype(jnp.float32)
+    second = rest.astype(jnp.bfloat16)
+    third = (rest - second.astype(jnp.float32)).astype(jnp.bfloat16)
+    return (first, second, third)
+
+
+def gather_kernel(index_ref, table_ref, out_ref):
+    node = index_ref[...]
+    width = node.shape[1]
+    high_count = table_ref.shape[1]
+    channels = out_ref.shape[0]
+    onehot = (
+        lax.broadcasted_iota(jnp.int32, (high_count, width), 0) == (node >> 7)
+    ).astype(jnp.bfloat16)
+    gathered = None
+    for piece in split_pieces(table_ref[...]):
+        part = jnp.dot(piece, onehot, preferred_element_type=jnp.float32)
+        gathered = part if gathered is None else gathered + part
+    low_hit = lax.broadcasted_iota(jnp.int32, (LANES, width), 0) == (node & (LANES - 1))
+    for c in range(channels):
+        block = gathered[c * LANES : (c + 1) * LANES]
+        out_ref[c : c + 1, :] = jnp.sum(jnp.where(low_hit, block, 0.0), axis=0, keepdims=True)
+
+
+def scatter_kernel(index_ref, force_ref, out_ref):
+    @pl.when(pl.program_id(0) == 0)
+    def _():
+        out_ref[...] = jnp.zeros_like(out_ref)
+
+    node = index_ref[...]
+    width = node.shape[1]
+    high_count = out_ref.shape[1]
+    channels = force_ref.shape[0]
+    onehot = (
+        lax.broadcasted_iota(jnp.int32, (high_count, width), 0) == (node >> 7)
+    ).astype(jnp.bfloat16)
+    low_hit = lax.broadcasted_iota(jnp.int32, (LANES, width), 0) == (node & (LANES - 1))
+    total = None
+    for piece in split_pieces(force_ref[...]):
+        spread = jnp.concatenate(
+            [jnp.where(low_hit, piece[c : c + 1, :], jnp.zeros_like(piece[c : c + 1, :])) for c in range(channels)],
+            axis=0,
+        )
+        part = lax.dot_general(
+            spread, onehot, (((1,), (1,)), ((), ())), preferred_element_type=jnp.float32
+        )
+        total = part if total is None else total + part
+    out_ref[...] += total
+
+
+def node_gather(field, nodes):
+    channels, node_total = field.shape
+    high_count = node_total // LANES
+    table = field.reshape(channels, high_count, LANES).transpose(0, 2, 1).reshape(
+        channels * LANES, high_count
+    )
+    count = nodes.shape[0]
+    padded_count = -(-count // TILE) * TILE
+    nodes = jnp.pad(nodes, (0, padded_count - count))
+    return pl.pallas_call(
+        gather_kernel,
+        grid=(padded_count // TILE,),
+        in_specs=[
+            pl.BlockSpec((1, TILE), lambda i: (0, i)),
+            pl.BlockSpec((channels * LANES, high_count), lambda i: (0, 0)),
+        ],
+        out_specs=pl.BlockSpec((channels, TILE), lambda i: (0, i)),
+        out_shape=jax.ShapeDtypeStruct((channels, padded_count), jnp.float32),
+    )(nodes.reshape(1, padded_count), table)[:, :count]
+
+
+def node_scatter_add(forces, nodes, node_total):
+    channels, count = forces.shape
+    high_count = node_total // LANES
+    padded_count = -(-count // TILE) * TILE
+    nodes = jnp.pad(nodes, (0, padded_count - count))
+    forces = jnp.pad(forces, ((0, 0), (0, padded_count - count)))
+    summed = pl.pallas_call(
+        scatter_kernel,
+        grid=(padded_count // TILE,),
+        in_specs=[
+            pl.BlockSpec((1, TILE), lambda i: (0, i)),
+            pl.BlockSpec((channels, TILE), lambda i: (0, i)),
+        ],
+        out_specs=pl.BlockSpec((channels * LANES, high_count), lambda i: (0, 0)),
+        out_shape=jax.ShapeDtypeStruct((channels * LANES, high_count), jnp.float32),
+    )(nodes.reshape(1, padded_count), forces)
+    return summed.reshape(channels, LANES, high_count).transpose(0, 2, 1).reshape(channels, node_total)
+
 
 TIME_STEP = 0.25
 VISCOUS = 0.5
@@ -147,8 +245,11 @@
     padded = padded_2(stacked, (("gx", 2), ("gy", 3)), 1)
     stress, inside = stress_forces(padded)
     vel_flat = velocity.reshape(3, node_total)
-    slave_vel = jnp.take(vel_flat, slave_node, axis=1).transpose(1, 0, 2)
-    master_vel = jnp.take(vel_flat, master_node, axis=1).transpose(1, 0, 2)
+    slave_count = block_total * seg_width
+    all_nodes = jnp.concatenate([slave_node.reshape(-1), master_node.reshape(-1)])
+    picked_vel = node_gather(vel_flat, all_nodes)
+    slave_vel = picked_vel[:, :slave_count].reshape(3, block_total, seg_width).transpose(1, 0, 2)
+    master_vel = picked_vel[:, slave_count:].reshape(3, master_total, seg_width).transpose(1, 0, 2)
     live_mask = jnp.arange(seg_width, dtype=jnp.int32)[None, :] < seg_count[:, None]
     area_live = jnp.where(live_mask, slave_area, jnp.zeros_like(slave_area))
     slave = jnp.concatenate(
@@ -164,10 +265,11 @@
     earlier = (owners[:, None] == owners[None, :]) & (positions[None, :] < positions[:, None])
     slot_index = jnp.sum(earlier.astype(jnp.int32), axis=1)
     target_slot = owners * slot_depth + slot_index
-    outgoing = (
-        jnp.zeros((devices * slot_depth, 7, seg_width), jnp.float32).at[target_slot].set(slave)
-    )
-    chosen = jnp.zeros((devices * slot_depth,), jnp.int32).at[target_slot].set(pair_master)
+    slot_hit = target_slot[None, :] == jnp.arange(devices * slot_depth, dtype=jnp.int32)[:, None]
+    source = jnp.sum(jnp.where(slot_hit, positions[None, :], 0), axis=1)
+    filled = jnp.any(slot_hit, axis=1)
+    outgoing = jnp.where(filled[:, None, None], jnp.take(slave, source, axis=0), 0.0)
+    chosen = jnp.where(filled, jnp.take(pair_master, source, axis=0), 0)
     arrived, picked = (
         lax.all_to_all(
             outgoing.reshape(devices, slot_depth, 7, seg_width),
@@ -215,13 +317,11 @@
         tiled=True,
     )
     slave_force = jnp.take(returned.reshape(item_total, 3, seg_width), target_slot, axis=0)
-    contact = jnp.zeros((3, node_total), jnp.float32)
-    contact = contact.at[:, slave_node.reshape(-1)].add(
-        slave_force.transpose(1, 0, 2).reshape(3, -1)
-    )
-    contact = contact.at[:, master_node.reshape(-1)].add(
-        master_force.transpose(1, 0, 2).reshape(3, -1)
-    )
+    all_forces = jnp.concatenate(
+        [slave_force.transpose(1, 0, 2).reshape(3, -1), master_force.transpose(1, 0, 2).reshape(3, -1)],
+        axis=1,
+    )
+    contact = node_scatter_add(all_forces, all_nodes, node_total)
     contact_field = contact.reshape(3, layers, row_cells, col_cells)
     velocity_new = velocity + TIME_STEP * (stress + contact_field) / node_mass[None]
     padded_new = padded_2(velocity_new, (("gx", 2), ("gy", 3)), 1)

time: 398 us -> 176 us (0.44)
  local copies, waits for them, and re-layouts: 155 us -> 18.2 us
  other arithmetic: 180 us -> 54.2 us
  Pallas kernels: 0 us -> 33.9 us
  waiting for transfers between devices: 16.8 us -> 26.5 us
    scatter-add x2 -> x0, other arithmetic: 126 us -> none  [the longest x1 94.4 us: on_device(): contact.at[:, slave_node.reshape(-1)]]
    gather x4 -> x3, local copies, waits for them, and re-layouts: 82.7 us -> 2.48 us  [the longest x2 1.65 us: on_device(): chosen = jnp.where(filled, jnp.take(pair_master, source, axis=0), 0)]
    pallas_call x0 -> x2, Pallas kernels: none -> 33.9 us  [the longest x1 17.5 us: node_gather(): pl.pallas_call(gather_kernel, grid=(padded_count // TILE,), in_specs=[pl....]
    reshape x3 -> x1, local copies, waits for them, and re-layouts: 17.1 us -> 1.15 us  [node_scatter_add(): summed.reshape(channels, LANES, high_count).transpose(0, 2, 1)]
    unnamed x37 -> x57, local copies, waits for them, and re-layouts: 15.2 us -> 1.29 us
    scatter x2 -> x0, local copies, waits for them, and re-layouts: 13.5 us -> none  [the longest x1 12.4 us: on_device(): jnp.zeros((devices * slot_depth, 7, seg_width), jnp.float32).at[target_slot]]
    ppermute x4, waiting for transfers between devices: 0.92 us -> 9.79 us  [padded_2(): lax.ppermute(lax.slice_in_dim(block, block.shape[dim] - width, None, axis...]
    concatenate x4 -> x0, local copies, waits for them, and re-layouts: 8.78 us -> none  [the longest x1 4.45 us: padded_2(): block = jnp.concatenate([low, block, high], axis=dim)]
  transfers between devices with their start and end apart: 11 -> 11, of which waited for: 3 -> 5; matrix products, arithmetic and copies ran while one was open for 38% -> 14% of each run, Pallas kernels for 0% -> 10%
where the time goes in v1:
time: 176 us; the launch traced here: 175 us
  other arithmetic  54.2 us (31%)
  starting transfers between devices  39.8 us (23%)
  Pallas kernels  33.9 us (19%)
  waiting for transfers between devices  26.5 us (15%)
  local copies, waits for them, and re-layouts  18.2 us (10%)
    reduce_sum x2, other arithmetic, contact_pairs(): reaction = jnp.sum(push_force, axis=1)  35.8 us
    pallas_call x1, Pallas kernels, node_gather(): pl.pallas_call(gather_kernel, grid=(padded_count // TILE,), in_specs=[pl....  17.5 us
    pallas_call x1, Pallas kernels, node_scatter_add(): pl.pallas_call(scatter_kernel, grid=(padded_count // TILE,), in_specs=[pl...  16.5 us
    ppermute x4, starting transfers between devices, padded_2(): lax.ppermute(lax.slice_in_dim(block, 0, width, axis=dim), axis, backward)  11.1 us
    all_to_all x1, waiting for transfers between devices, on_device(): lax.all_to_all(forces.reshape(devices, slot_depth, 3, seg_width), ('gx',...  10.7 us
    ppermute x4, starting transfers between devices, padded_2(): lax.ppermute(lax.slice_in_dim(block, block.shape[dim] - width, None, axis...  10.3 us
    ppermute x4, waiting for transfers between devices, padded_2(): lax.ppermute(lax.slice_in_dim(block, block.shape[dim] - width, None, axis...  9.79 us
    all_to_all x1, starting transfers between devices, on_device(): lax.all_to_all(chosen.reshape(devices, slot_depth), ('gx', 'gy'), split_a...  6.36 us
  transfers between devices with their start and end apart: 11, of which 5 were waited for; matrix products, arithmetic and copies ran while one was open for 14% of the time, Pallas kernels for 10%

profile of v1, /device:TPU:9, one launch (start us, length us, event | category | flops | bytes accessed | tf_op | source)
XLA Modules:
  0.0 174.6 jit_solution(10196106583178285189)
XLA Ops:
  0.7 0.9 convert_reduce_fusion
  2.8 1.6 gather_fusion.1
  5.1 6.4 %all-to-all-start.1 = ((s32[32,1,5]{2,1,0:T(1,128)}), s32[32,1,5]{2,1,0:T(1,128)S(1)}, u32[]{:S(2)}, u32[]{:S(2)}) async-start(s32[32,1,5]{2,1,0:T(1,128)} %bitcast.50), calls=%async_computation.1 | async-start | bytes 32768 | tf_op jit(solution)/shard_map/all_to_all | solution.py:281
  12.1 1.9 %pad_maximum_fusion.9 = (f32[6,8,1,256]{3,2,1,0:T(1,128)}, f32[6,8,1,256]{3,2,1,0:T(1,128)}) fusion(f32[1,8,16,256]{3,2,1,0:T(8,128)S(1)} %broadcast_in_dim_broadcast_in_dim.3, f32[1,8,16,256]{3,2,1,0:T(8,128)} %bitcast.156, f32[1,8,16,256]{3,2,1,0:T(8,128)} %bitcast.159, f32[3,8,16,256]{3,2,1,0:T(8,128)} %param.16), kind=kLoop, calls=%fused_computation.175 | loop fusion | flops 73728 | bytes 884736 | tf_op jit(solution)/shard_map/slice | solution.py:117
  14.0 3.5 %collective-permute-start = (f32[6,8,1,256]{3,2,1,0:T(1,128)}, f32[6,8,1,256]{3,2,1,0:T(1,128)S(1)}, u32[]{:S(2)}, u32[]{:S(2)}) collective-permute-start(f32[6,8,1,256]{3,2,1,0:T(1,128)} %get-tuple-element.103), channel_id=1, source_target_pairs={{0,8},{8,16},{16,24},{1,9},{9,17},{17,25},{2,10},{10,18},{18,26},{... | collective-permute-start | bytes 147464 | tf_op jit(solution)/shard_map/ppermute | solution.py:116
  17.5 1.9 %collective-permute-start.1 = (f32[6,8,1,256]{3,2,1,0:T(1,128)}, f32[6,8,1,256]{3,2,1,0:T(1,128)S(1)}, u32[]{:S(2)}, u32[]{:S(2)}) collective-permute-start(f32[6,8,1,256]{3,2,1,0:T(1,128)} %get-tuple-element.104), channel_id=1, source_target_pairs={{8,0},{16,8},{24,16},{9,1},{17,9},{25,17},{10,2},{18,10},{26,18},{... | collective-permute-start | bytes 147464 | tf_op jit(solution)/shard_map/ppermute | solution.py:119
  21.7 17.5 %shard_map.149 = f32[3,20480]{1,0:T(4,128)} custom-call(s32[1,20480]{1,0:T(1,128)} %bitcast.166, f32[384,256]{1,0:T(8,128)} %bitcast.153), custom_call_target="tpu_custom_call" | custom-call | tf_op jit(solution)/shard_map/pallas_call | solution.py:73
  40.1 1.0 slice_bitcast_fusion.19
  42.1 1.1 copy_add_fusion
  44.4 1.2 select_select_fusion
  46.6 6.1 %all-to-all-start = ((f32[32,5,7,128]{3,2,1,0:T(8,128)}), f32[32,5,7,128]{3,2,1,0:T(8,128)S(1)}, u32[]{:S(2)}, u32[]{:S(2)}) async-start(f32[32,5,7,128]{3,2,1,0:T(8,128)} %select_select_fusion), calls=%async_computation | async-start | bytes 1310720 | tf_op jit(solution)/shard_map/all_to_all | solution.py:274
  55.9 1.1 fusion.74
  57.0 2.0 %copy.96 = f32[6,8,18,1]{2,1,3,0:T(8,128)} copy(f32[6,8,18,1]{3,2,1,0:T(8,128)} %get-tuple-element.99) | data formatting | bytes 6912 | tf_op jit(solution)/shard_map/slice | solution.py:117
  59.0 1.0 copy.97
  60.0 3.2 %collective-permute-start.3 = (f32[6,8,18,1]{2,1,3,0:T(8,128)}, f32[6,8,18,1]{2,1,3,0:T(8,128)S(1)}, u32[]{:S(2)}, u32[]{:S(2)}) collective-permute-start(f32[6,8,18,1]{2,1,3,0:T(8,128)} %copy.97), channel_id=1, source_target_pairs={{1,0},{2,1},{3,2},{4,3},{5,4},{6,5},{7,6},{9,8},{10,9},{11,10},{12... | collective-permute-start | bytes 10376 | tf_op jit(solution)/shard_map/ppermute | solution.py:119
  63.2 2.2 %collective-permute-start.2 = (f32[6,8,18,1]{2,1,3,0:T(8,128)}, f32[6,8,18,1]{2,1,3,0:T(8,128)S(1)}, u32[]{:S(2)}, u32[]{:S(2)}) collective-permute-start(f32[6,8,18,1]{2,1,3,0:T(8,128)} %copy.96), channel_id=1, source_target_pairs={{0,1},{1,2},{2,3},{3,4},{4,5},{5,6},{6,7},{8,9},{9,10},{10,11},{11... | collective-permute-start | bytes 10376 | tf_op jit(solution)/shard_map/ppermute | solution.py:116
  67.0 2.3 %collective-permute-done.2 = f32[6,8,18,1]{2,1,3,0:T(8,128)S(1)} collective-permute-done((f32[6,8,18,1]{2,1,3,0:T(8,128)}, f32[6,8,18,1]{2,1,3,0:T(8,128)S(1)}, u32[]{:S(2)}, u32[]{:S(2)}) %collective-permute-start.2) | collective-permute-done | bytes 3488 | tf_op jit(solution)/shard_map/ppermute | solution.py:116
  70.1 2.0 %pad_maximum_fusion = f32[6,8,18,258]{3,2,1,0:T(8,128)S(1)} fusion(f32[6,8,18,1]{3,2,1,0:T(8,128)S(1)} %copy.99, f32[6,8,1,256]{3,2,1,0:T(1,128)S(1)} %collective-permute-done.1, f32[1,8,16,256]{3,2,1,0:T(8,128)S(1)} %copy-done.5, f32[1,8,16,256]{3,2,1,0:T(8,128)} %bitcast.157, f32[1,8,16,256]{3,2,1,0:T(8,128)} %bitcast.160, ...), kind=kLoop, calls=%fused_computation.49 | loop fusion | flops 1560384 | bytes 1783296 | tf_op jit(solution)/shard_map/concatenate | solution.py:120
  74.2 36.2 %while.12 = (s32[]{:T(128)}, f32[2,80,3,128]{3,1,2,0:T(8,128)S(1)}, f32[2,80,128]{2,1,0:T(8,128)S(1)}, f32[2,80,7,128]{3,1,2,0:T(8,128)S(1)}, f32[2,80,10,128]{3,1,2,0:T(8,128)S(1)}, /*index=5*/s32[]{:T(128)}) while((s32[]{:T(128)}, f32[2,80,3,128]{3,1,2,0:T(8,128)S(1)}, f32[2,80,128]{2,1,0:T(8,128)S(1)}, f32[2,80,7,128]{3,1,2,0:T(8,128)S(1)}, ...), condition=%wide.region_8.9_spmd, body=%wide.region_3.8_spmd.sunk | while | flops 59002880 | bytes 3973213 | solution.py:298
  74.4 17.9 %fusion.81 = (f32[80,128]{1,0:T(8,128)S(1)}, f32[80,128]{1,0:T(8,128)S(1)}, f32[80,128]{1,0:T(8,128)S(1)}, f32[80,128]{1,0:T(8,128)S(1)}) fusion(f32[80,128]{1,0:T(8,128)S(1)} %get-tuple-element.170, f32[80,128]{1,0:T(8,128)S(1)} %get-tuple-element.171, f32[80,128]{1,0:T(8,128)S(1)} %get-tuple-element.172, f32[80,128]{1,0:T(8,128)S(1)} %get-tuple-element.173, ...), kind=kLoop, calls=%fused_computation.48.clone.1 | loop fusion | flops 58941440 | bytes 860160 | tf_op jit(solution)/shard_map/while/body/eval_jaxpr/reduce_sum | solution.py:207
  92.5 17.9 %fusion.81 = (f32[80,128]{1,0:T(8,128)S(1)}, f32[80,128]{1,0:T(8,128)S(1)}, f32[80,128]{1,0:T(8,128)S(1)}, f32[80,128]{1,0:T(8,128)S(1)}) fusion(f32[80,128]{1,0:T(8,128)S(1)} %get-tuple-element.170, f32[80,128]{1,0:T(8,128)S(1)} %get-tuple-element.171, f32[80,128]{1,0:T(8,128)S(1)} %get-tuple-element.172, f32[80,128]{1,0:T(8,128)S(1)} %get-tuple-element.173, ...), kind=kLoop, calls=%fused_computation.48.clone.1 | loop fusion | flops 58941440 | bytes 860160 | tf_op jit(solution)/shard_map/while/body/eval_jaxpr/reduce_sum | solution.py:207
  111.3 6.0 %all-to-all-start.2 = ((f32[32,5,3,128]{3,2,1,0:T(4,128)}), f32[32,5,3,128]{3,2,1,0:T(4,128)S(1)}, u32[]{:S(2)}, u32[]{:S(2)}) async-start(f32[32,5,3,128]{3,2,1,0:T(4,128)} %bitcast.59), calls=%async_computation.2 | async-start | bytes 655360 | tf_op jit(solution)/shard_map/all_to_all | solution.py:312
  117.7 10.7 %all-to-all-done.2 = f32[32,5,3,128]{3,2,1,0:T(4,128)S(1)} async-done(((f32[32,5,3,128]{3,2,1,0:T(4,128)}), f32[32,5,3,128]{3,2,1,0:T(4,128)S(1)}, u32[]{:S(2)}, u32[]{:S(2)}) %all-to-all-start.2) | async-done | bytes 245792 | tf_op jit(solution)/shard_map/all_to_all | solution.py:312
  130.3 16.5 %shard_map.150 = f32[384,256]{1,0:T(8,128)} custom-call(s32[1,20480]{1,0:T(1,128)} %bitcast.167, f32[3,20480]{1,0:T(4,128)} %pad_maximum_fusion.5.force_ref), custom_call_target="tpu_custom_call" | custom-call | tf_op jit(solution)/shard_map/pallas_call | solution.py:91
  146.7 1.1 copy.115
  148.2 2.5 %collective-permute-start.4 = (f32[3,8,1,256]{3,2,1,0:T(1,128)S(1)}, f32[3,8,1,256]{3,2,1,0:T(1,128)S(1)}, u32[]{:S(2)}, u32[]{:S(2)}) collective-permute-start(f32[3,8,1,256]{3,2,1,0:T(1,128)S(1)} %get-tuple-element.107), channel_id=1, source_target_pairs={{0,8},{8,16},{16,24},{1,9},{9,17},{17,25},{2,10},{10,18},{18,26},{... | collective-permute-start | bytes 73736 | tf_op jit(solution)/shard_map/ppermute | solution.py:116
  150.7 1.9 %collective-permute-start.5 = (f32[3,8,1,256]{3,2,1,0:T(1,128)S(1)}, f32[3,8,1,256]{3,2,1,0:T(1,128)S(1)}, u32[]{:S(2)}, u32[]{:S(2)}) collective-permute-start(f32[3,8,1,256]{3,2,1,0:T(1,128)S(1)} %get-tuple-element.108), channel_id=1, source_target_pairs={{8,0},{16,8},{24,16},{9,1},{17,9},{25,17},{10,2},{18,10},{26,18},{... | collective-permute-start | bytes 73736 | tf_op jit(solution)/shard_map/ppermute | solution.py:119
  152.6 3.2 %collective-permute-done.5 = f32[3,8,1,256]{3,2,1,0:T(1,128)S(1)} collective-permute-done((f32[3,8,1,256]{3,2,1,0:T(1,128)S(1)}, f32[3,8,1,256]{3,2,1,0:T(1,128)S(1)}, u32[]{:S(2)}, u32[]{:S(2)}) %collective-permute-start.5) | collective-permute-done | bytes 24608 | tf_op jit(solution)/shard_map/ppermute | solution.py:119
  156.1 2.2 %collective-permute-start.6 = (f32[3,8,18,1]{3,2,1,0:T(8,128)S(1)}, f32[3,8,18,1]{3,2,1,0:T(8,128)S(1)}, u32[]{:S(2)}, u32[]{:S(2)}) collective-permute-start(f32[3,8,18,1]{3,2,1,0:T(8,128)S(1)} %get-tuple-element.105), channel_id=1, source_target_pairs={{0,1},{1,2},{2,3},{3,4},{4,5},{5,6},{6,7},{8,9},{9,10},{10,11},{11... | collective-permute-start | bytes 5192 | tf_op jit(solution)/shard_map/ppermute | solution.py:116
  158.2 4.0 %collective-permute-start.7 = (f32[3,8,18,1]{3,2,1,0:T(8,128)S(1)}, f32[3,8,18,1]{3,2,1,0:T(8,128)S(1)}, u32[]{:S(2)}, u32[]{:S(2)}) collective-permute-start(f32[3,8,18,1]{3,2,1,0:T(8,128)S(1)} %get-tuple-element.106), channel_id=1, source_target_pairs={{1,0},{2,1},{3,2},{4,3},{5,4},{6,5},{7,6},{9,8},{10,9},{11,10},{12... | collective-permute-start | bytes 5192 | tf_op jit(solution)/shard_map/ppermute | solution.py:119
  162.3 7.5 %collective-permute-done.6 = f32[3,8,18,1]{3,2,1,0:T(8,128)S(1)} collective-permute-done((f32[3,8,18,1]{3,2,1,0:T(8,128)S(1)}, f32[3,8,18,1]{3,2,1,0:T(8,128)S(1)}, u32[]{:S(2)}, u32[]{:S(2)}) %collective-permute-start.6) | collective-permute-done | bytes 1760 | tf_op jit(solution)/shard_map/ppermute | solution.py:116
  169.8 2.7 %collective-permute-done.7 = f32[3,8,18,1]{3,2,1,0:T(8,128)S(1)} collective-permute-done((f32[3,8,18,1]{3,2,1,0:T(8,128)S(1)}, f32[3,8,18,1]{3,2,1,0:T(8,128)S(1)}, u32[]{:S(2)}, u32[]{:S(2)}) %collective-permute-start.7) | collective-permute-done | bytes 1760 | tf_op jit(solution)/shard_map/ppermute | solution.py:119
  (153 shorter events, 21.9 us)
Async XLA Ops:
  0.6 18.8 %copy-start.27 = (s32[128,1]{0,1:T(1,128)S(1)}, s32[128,1]{0,1:T(1,128)}, u32[]{:S(2)}) copy-start(s32[128,1]{0,1:T(1,128)} %param.24) | copy-start | bytes 1540
  0.7 19.5 %copy-start.1 = (f32[3,8,16,256]{3,2,1,0:T(8,128)S(1)}, f32[3,8,16,256]{3,2,1,0:T(8,128)}, u32[]{:S(2)}) copy-start(f32[3,8,16,256]{3,2,1,0:T(8,128)} %param.16) | copy-start | bytes 1179652
  2.8 18.3 %copy-start.18 = (s32[128,128]{1,0:T(8,128)S(1)}, s32[128,128]{1,0:T(8,128)}, u32[]{:S(2)}) copy-start(s32[128,128]{1,0:T(8,128)} %param.23) | copy-start | bytes 196612
  2.8 18.3 %copy-start.22 = (s32[32,128]{1,0:T(8,128)S(1)}, s32[32,128]{1,0:T(8,128)}, u32[]{:S(2)}) copy-start(s32[32,128]{1,0:T(8,128)} %param.29) | copy-start | bytes 49156
  5.1 41.5 %all-to-all-start.1 = ((s32[32,1,5]{2,1,0:T(1,128)}), s32[32,1,5]{2,1,0:T(1,128)S(1)}, u32[]{:S(2)}, u32[]{:S(2)}) async-start(s32[32,1,5]{2,1,0:T(1,128)} %bitcast.50), calls=%async_computation.1 | async-start | bytes 32768 | tf_op jit(solution)/shard_map/all_to_all | solution.py:281
  14.0 27.1 %copy-start.21 = (f32[32,2,128]{2,1,0:T(2,128)S(1)}, f32[32,2,128]{2,1,0:T(2,128)}, u32[]{:S(2)}) copy-start(f32[32,2,128]{2,1,0:T(2,128)} %param.27) | copy-start | bytes 98308
  14.0 27.2 %copy-start.20 = (f32[32,3,128]{2,0,1:T(8,128)S(1)}, f32[32,3,128]{2,0,1:T(8,128)}, u32[]{:S(2)}) copy-start(f32[32,3,128]{2,0,1:T(8,128)} %param.26) | copy-start | bytes 147460
  14.0 28.1 %copy-start.9 = (f32[128,3,128]{2,0,1:T(8,128)S(1)}, f32[128,3,128]{2,0,1:T(8,128)}, u32[]{:S(2)}) copy-start(f32[128,3,128]{2,0,1:T(8,128)} %param.20) | copy-start | bytes 589828
  14.0 41.6 %collective-permute-start = (f32[6,8,1,256]{3,2,1,0:T(1,128)}, f32[6,8,1,256]{3,2,1,0:T(1,128)S(1)}, u32[]{:S(2)}, u32[]{:S(2)}) collective-permute-start(f32[6,8,1,256]{3,2,1,0:T(1,128)} %get-tuple-element.103), channel_id=1, source_target_pairs={{0,8},{8,16},{16,24},{1,9},{9,17},{17,25},{2,10},{10,18},{18,26},{... | collective-permute-start | bytes 147464 | tf_op jit(solution)/shard_map/ppermute | solution.py:116
  17.5 38.2 %collective-permute-start.1 = (f32[6,8,1,256]{3,2,1,0:T(1,128)}, f32[6,8,1,256]{3,2,1,0:T(1,128)S(1)}, u32[]{:S(2)}, u32[]{:S(2)}) collective-permute-start(f32[6,8,1,256]{3,2,1,0:T(1,128)} %get-tuple-element.104), channel_id=1, source_target_pairs={{8,0},{16,8},{24,16},{9,1},{17,9},{25,17},{10,2},{18,10},{26,18},{... | collective-permute-start | bytes 147464 | tf_op jit(solution)/shard_map/ppermute | solution.py:119
  20.2 23.0 %copy-start.19 = (f32[128,128]{1,0:T(8,128)S(1)}, f32[128,128]{1,0:T(8,128)}, u32[]{:S(2)}) copy-start(f32[128,128]{1,0:T(8,128)} %param.21) | copy-start | bytes 196612
  20.2 23.0 %copy-start.26 = (s32[128]{0:T(128)S(1)}, s32[128]{0:T(128)}, u32[]{:S(2)}) copy-start(s32[128]{0:T(128)} %param.22) | copy-start | bytes 1540
  44.3 11.3 %copy-start.10 = (f32[32,1,128]{2,0,1:T(8,128)}, f32[32,1,128]{2,0,1:T(8,128)S(1)}, u32[]{:S(2)}) copy-start(f32[32,1,128]{2,0,1:T(8,128)S(1)} %get-tuple-element.109) | copy-start | bytes 49156
  44.4 11.3 %copy-start.12 = (f32[32,1,128]{2,0,1:T(8,128)}, f32[32,1,128]{2,0,1:T(8,128)S(1)}, u32[]{:S(2)}) copy-start(f32[32,1,128]{2,0,1:T(8,128)S(1)} %get-tuple-element.110) | copy-start | bytes 49156
  44.4 11.3 %copy-start.14 = (f32[32,1,128]{2,0,1:T(8,128)}, f32[32,1,128]{2,0,1:T(8,128)S(1)}, u32[]{:S(2)}) copy-start(f32[32,1,128]{2,0,1:T(8,128)S(1)} %get-tuple-element.111) | copy-start | bytes 49156
  46.6 9.1 %copy-start.4 = (f32[1,8,16,256]{3,2,1,0:T(8,128)S(1)}, f32[1,8,16,256]{3,2,1,0:T(8,128)}, u32[]{:S(2)}) copy-start(f32[1,8,16,256]{3,2,1,0:T(8,128)} %copy-done.3) | copy-start | bytes 393220
  46.6 27.0 %all-to-all-start = ((f32[32,5,7,128]{3,2,1,0:T(8,128)}), f32[32,5,7,128]{3,2,1,0:T(8,128)S(1)}, u32[]{:S(2)}, u32[]{:S(2)}) async-start(f32[32,5,7,128]{3,2,1,0:T(8,128)} %select_select_fusion), calls=%async_computation | async-start | bytes 1310720 | tf_op jit(solution)/shard_map/all_to_all | solution.py:274
  60.0 10.1 %copy-start.5 = (f32[1,8,16,256]{3,2,1,0:T(8,128)S(1)}, f32[1,8,16,256]{3,2,1,0:T(8,128)}, u32[]{:S(2)}) copy-start(f32[1,8,16,256]{3,2,1,0:T(8,128)} %copy-done.3) | copy-start | bytes 393220
  60.0 9.7 %collective-permute-start.3 = (f32[6,8,18,1]{2,1,3,0:T(8,128)}, f32[6,8,18,1]{2,1,3,0:T(8,128)S(1)}, u32[]{:S(2)}, u32[]{:S(2)}) collective-permute-start(f32[6,8,18,1]{2,1,3,0:T(8,128)} %copy.97), channel_id=1, source_target_pairs={{1,0},{2,1},{3,2},{4,3},{5,4},{6,5},{7,6},{9,8},{10,9},{11,10},{12... | collective-permute-start | bytes 10376 | tf_op jit(solution)/shard_map/ppermute | solution.py:119
  63.2 6.0 %collective-permute-start.2 = (f32[6,8,18,1]{2,1,3,0:T(8,128)}, f32[6,8,18,1]{2,1,3,0:T(8,128)S(1)}, u32[]{:S(2)}, u32[]{:S(2)}) collective-permute-start(f32[6,8,18,1]{2,1,3,0:T(8,128)} %copy.96), channel_id=1, source_target_pairs={{0,1},{1,2},{2,3},{3,4},{4,5},{5,6},{6,7},{8,9},{9,10},{10,11},{11... | collective-permute-start | bytes 10376 | tf_op jit(solution)/shard_map/ppermute | solution.py:116
  74.2 43.1 %copy-start.24 = (s32[160]{0:T(256)S(1)}, s32[160]{0:T(256)}, u32[]{:S(2)}) copy-start(s32[160]{0:T(256)} %reshape.244) | copy-start | bytes 1924
  74.2 43.4 %copy-start.11 = (f32[32,1,128]{2,0,1:T(8,128)S(1)}, f32[32,1,128]{2,0,1:T(8,128)}, u32[]{:S(2)}) copy-start(f32[32,1,128]{2,0,1:T(8,128)} %copy-done.10) | copy-start | bytes 49156
  74.2 43.4 %copy-start.13 = (f32[32,1,128]{2,0,1:T(8,128)S(1)}, f32[32,1,128]{2,0,1:T(8,128)}, u32[]{:S(2)}) copy-start(f32[32,1,128]{2,0,1:T(8,128)} %copy-done.12) | copy-start | bytes 49156
  74.2 43.4 %copy-start.15 = (f32[32,1,128]{2,0,1:T(8,128)S(1)}, f32[32,1,128]{2,0,1:T(8,128)}, u32[]{:S(2)}) copy-start(f32[32,1,128]{2,0,1:T(8,128)} %copy-done.14) | copy-start | bytes 49156
  110.4 18.9 %copy-start.25 = (pred[128]{0:T(512)(128)(4,1)S(1)}, pred[128]{0:T(512)(128)(4,1)}, u32[]{:S(2)}) copy-start(pred[128]{0:T(512)(128)(4,1)} %get-tuple-element.68) | copy-start | bytes 388
  111.3 17.1 %all-to-all-start.2 = ((f32[32,5,3,128]{3,2,1,0:T(4,128)}), f32[32,5,3,128]{3,2,1,0:T(4,128)S(1)}, u32[]{:S(2)}, u32[]{:S(2)}) async-start(f32[32,5,3,128]{3,2,1,0:T(4,128)} %bitcast.59), calls=%async_computation.2 | async-start | bytes 655360 | tf_op jit(solution)/shard_map/all_to_all | solution.py:312
  129.3 18.8 %copy-start.16 = (f32[8,16,256]{2,1,0:T(8,128)S(1)}, f32[8,16,256]{2,1,0:T(8,128)}, u32[]{:S(2)}) copy-start(f32[8,16,256]{2,1,0:T(8,128)} %param.19) | copy-start | bytes 393220
  148.2 24.9 %copy-start.2 = (f32[3,8,16,256]{3,2,1,0:T(8,128)}, f32[3,8,16,256]{3,2,1,0:T(8,128)S(1)}, u32[]{:S(2)}) copy-start(f32[3,8,16,256]{3,2,1,0:T(8,128)S(1)} %fusion.16) | copy-start | bytes 1179652
  148.2 4.4 %collective-permute-start.4 = (f32[3,8,1,256]{3,2,1,0:T(1,128)S(1)}, f32[3,8,1,256]{3,2,1,0:T(1,128)S(1)}, u32[]{:S(2)}, u32[]{:S(2)}) collective-permute-start(f32[3,8,1,256]{3,2,1,0:T(1,128)S(1)} %get-tuple-element.107), channel_id=1, source_target_pairs={{0,8},{8,16},{16,24},{1,9},{9,17},{17,25},{2,10},{10,18},{18,26},{... | collective-permute-start | bytes 73736 | tf_op jit(solution)/shard_map/ppermute | solution.py:116
  150.7 5.1 %collective-permute-start.5 = (f32[3,8,1,256]{3,2,1,0:T(1,128)S(1)}, f32[3,8,1,256]{3,2,1,0:T(1,128)S(1)}, u32[]{:S(2)}, u32[]{:S(2)}) collective-permute-start(f32[3,8,1,256]{3,2,1,0:T(1,128)S(1)} %get-tuple-element.108), channel_id=1, source_target_pairs={{8,0},{16,8},{24,16},{9,1},{17,9},{25,17},{10,2},{18,10},{26,18},{... | collective-permute-start | bytes 73736 | tf_op jit(solution)/shard_map/ppermute | solution.py:119
  156.1 13.7 %collective-permute-start.6 = (f32[3,8,18,1]{3,2,1,0:T(8,128)S(1)}, f32[3,8,18,1]{3,2,1,0:T(8,128)S(1)}, u32[]{:S(2)}, u32[]{:S(2)}) collective-permute-start(f32[3,8,18,1]{3,2,1,0:T(8,128)S(1)} %get-tuple-element.105), channel_id=1, source_target_pairs={{0,1},{1,2},{2,3},{3,4},{4,5},{5,6},{6,7},{8,9},{9,10},{10,11},{11... | collective-permute-start | bytes 5192 | tf_op jit(solution)/shard_map/ppermute | solution.py:116
  158.2 14.3 %collective-permute-start.7 = (f32[3,8,18,1]{3,2,1,0:T(8,128)S(1)}, f32[3,8,18,1]{3,2,1,0:T(8,128)S(1)}, u32[]{:S(2)}, u32[]{:S(2)}) collective-permute-start(f32[3,8,18,1]{3,2,1,0:T(8,128)S(1)} %get-tuple-element.106), channel_id=1, source_target_pairs={{1,0},{2,1},{3,2},{4,3},{5,4},{6,5},{7,6},{9,8},{10,9},{11,10},{12... | collective-permute-start | bytes 5192 | tf_op jit(solution)/shard_map/ppermute | solution.py:119
  (7 other events, 25.8 us)

commit v2 on v1

--- a/solution.py
+++ b/solution.py
@@ -49,7 +49,7 @@
     ).astype(jnp.bfloat16)
     low_hit = lax.broadcasted_iota(jnp.int32, (LANES, width), 0) == (node & (LANES - 1))
     total = None
-    for piece in split_pieces(force_ref[...]):
+    for piece in split_pieces(force_ref[...])[:2]:
         spread = jnp.concatenate(
             [jnp.where(low_hit, piece[c : c + 1, :], jnp.zeros_like(piece[c : c + 1, :])) for c in range(channels)],
             axis=0,
@@ -108,17 +108,38 @@
 DAMPING = 0.5
 
 
-def padded_2(block, sides, width):
-    for axis, dim in sides:
-        count = lax.axis_size(axis)
-        forward = [(i, i + 1) for i in range(count - 1)]
-        backward = [(target, source) for source, target in forward]
-        low = lax.ppermute(
-            lax.slice_in_dim(block, block.shape[dim] - width, None, axis=dim), axis, forward
-        )
-        high = lax.ppermute(lax.slice_in_dim(block, 0, width, axis=dim), axis, backward)
-        block = jnp.concatenate([low, block, high], axis=dim)
-    return block
+def halo_pad(block):
+    count_x = lax.axis_size("gx")
+    count_y = lax.axis_size("gy")
+    down_x = [(i, i + 1) for i in range(count_x - 1)]
+    up_x = [(i + 1, i) for i in range(count_x - 1)]
+    down_y = [(j, j + 1) for j in range(count_y - 1)]
+    up_y = [(j + 1, j) for j in range(count_y - 1)]
+
+    def diagonal(step_x, step_y):
+        pairs = []
+        for i in range(count_x):
+            for j in range(count_y):
+                ti, tj = i + step_x, j + step_y
+                if 0 <= ti < count_x and 0 <= tj < count_y:
+                    pairs.append((i * count_y + j, ti * count_y + tj))
+        return pairs
+
+    last_row = block[..., -1:, :]
+    first_row = block[..., :1, :]
+    top = lax.ppermute(last_row, "gx", down_x)
+    bottom = lax.ppermute(first_row, "gx", up_x)
+    left = lax.ppermute(block[..., :, -1:], "gy", down_y)
+    right = lax.ppermute(block[..., :, :1], "gy", up_y)
+    both = ("gx", "gy")
+    top_left = lax.ppermute(last_row[..., -1:], both, diagonal(1, 1))
+    top_right = lax.ppermute(last_row[..., :1], both, diagonal(1, -1))
+    bottom_left = lax.ppermute(first_row[..., -1:], both, diagonal(-1, 1))
+    bottom_right = lax.ppermute(first_row[..., :1], both, diagonal(-1, -1))
+    upper = jnp.concatenate([top_left, top, top_right], axis=-1)
+    middle = jnp.concatenate([left, block, right], axis=-1)
+    lower = jnp.concatenate([bottom_left, bottom, bottom_right], axis=-1)
+    return jnp.concatenate([upper, middle, lower], axis=-2)
 
 
 def pair_mean(values, along):
@@ -242,7 +263,7 @@
     stacked = jnp.concatenate(
         [velocity, bulk[None], prestress[None], jnp.ones_like(bulk)[None]], axis=0
     )
-    padded = padded_2(stacked, (("gx", 2), ("gy", 3)), 1)
+    padded = halo_pad(stacked)
     stress, inside = stress_forces(padded)
     vel_flat = velocity.reshape(3, node_total)
     slave_count = block_total * seg_width
@@ -268,27 +289,25 @@
     slot_hit = target_slot[None, :] == jnp.arange(devices * slot_depth, dtype=jnp.int32)[:, None]
     source = jnp.sum(jnp.where(slot_hit, positions[None, :], 0), axis=1)
     filled = jnp.any(slot_hit, axis=1)
-    outgoing = jnp.where(filled[:, None, None], jnp.take(slave, source, axis=0), 0.0)
-    chosen = jnp.where(filled, jnp.take(pair_master, source, axis=0), 0)
-    arrived, picked = (
-        lax.all_to_all(
-            outgoing.reshape(devices, slot_depth, 7, seg_width),
-            ("gx", "gy"),
-            split_axis=0,
-            concat_axis=0,
-            tiled=True,
-        ),
-        lax.all_to_all(
-            chosen.reshape(devices, slot_depth),
-            ("gx", "gy"),
-            split_axis=0,
-            concat_axis=0,
-            tiled=True,
-        ),
+    tagged = jnp.concatenate(
+        [
+            slave,
+            jnp.broadcast_to(pair_master.astype(jnp.float32)[:, None, None], (block_total, 1, seg_width)),
+        ],
+        axis=1,
+    )
+    outgoing = jnp.where(filled[:, None, None], jnp.take(tagged, source, axis=0), 0.0)
+    arrived = lax.all_to_all(
+        outgoing.reshape(devices, slot_depth, 8, seg_width),
+        ("gx", "gy"),
+        split_axis=0,
+        concat_axis=0,
+        tiled=True,
     )
     item_total = devices * slot_depth
-    arrived = arrived.reshape(item_total, 7, seg_width)
-    picked = picked.reshape(item_total)
+    arrived = arrived.reshape(item_total, 8, seg_width)
+    picked = arrived[:, 7, 0].astype(jnp.int32)
+    arrived = arrived[:, :7]
     paired = jnp.take(master_data, picked, axis=0)
     group_size = 16 * slot_depth
 
@@ -324,7 +343,7 @@
     contact = node_scatter_add(all_forces, all_nodes, node_total)
     contact_field = contact.reshape(3, layers, row_cells, col_cells)
     velocity_new = velocity + TIME_STEP * (stress + contact_field) / node_mass[None]
-    padded_new = padded_2(velocity_new, (("gx", 2), ("gy", 3)), 1)
+    padded_new = halo_pad(velocity_new)
     node_rate = nodal_rate(padded_new, inside)
     return (velocity_new, node_rate)
 

time: 176 us -> 191 us (1.085)
  starting transfers between devices: 39.8 us -> 52.4 us
  waiting for transfers between devices: 26.5 us -> 36.8 us
  local copies, waits for them, and re-layouts: 18.2 us -> 12.4 us
  Pallas kernels: 33.9 us -> 29.4 us
    ppermute x8 -> x16, starting transfers between devices: 21.4 us -> 41.9 us  [the longest x2 8.26 us: halo_pad(): right = lax.ppermute(block[..., :, :1], 'gy', up_y)]
    ppermute x8 -> x16, waiting for transfers between devices: 15.7 us -> 26.9 us  [the longest x2 11.4 us: halo_pad(): bottom_left = lax.ppermute(first_row[..., -1:], both, diagonal(-1, 1))]
    all_to_all x2 -> x1, starting transfers between devices: 12.5 us -> 4.95 us  [on_device(): lax.all_to_all(outgoing.reshape(devices, slot_depth, 8, seg_width), ('gx'...]
    pallas_call x1, Pallas kernels: 16.5 us -> 11.9 us  [node_scatter_add(): pl.pallas_call(scatter_kernel, grid=(padded_count // TILE,), in_specs=[pl...]
    slice x5, local copies, waits for them, and re-layouts: 4.28 us -> 1.33 us  [the longest x2 1.1 us: halo_pad(): left = lax.ppermute(block[..., :, -1:], 'gy', down_y)]
    concatenate x5 -> x4, other arithmetic: 3.05 us -> 4.24 us  [the longest x2 2.81 us: halo_pad(): return jnp.concatenate([upper, middle, lower], axis=-2)]
  transfers between devices with their start and end apart: 11 -> 18, of which waited for: 5 -> 7; matrix products, arithmetic and copies ran while one was open for 14% -> 10% of each run, Pallas kernels for 10% -> 9%
where the time goes in v2:
time: 191 us; the launch traced here: 189 us
  other arithmetic  55.7 us (29%)
  starting transfers between devices  52.4 us (27%)
  waiting for transfers between devices  36.8 us (19%)
  Pallas kernels  29.4 us (15%)
  local copies, waits for them, and re-layouts  12.4 us (6%)
    reduce_sum x2, other arithmetic, contact_pairs(): reaction = jnp.sum(push_force, axis=1)  35.8 us
    pallas_call x1, Pallas kernels, node_gather(): pl.pallas_call(gather_kernel, grid=(padded_count // TILE,), in_specs=[pl....  17.5 us
    pallas_call x1, Pallas kernels, node_scatter_add(): pl.pallas_call(scatter_kernel, grid=(padded_count // TILE,), in_specs=[pl...  11.9 us
    ppermute x2, waiting for transfers between devices, halo_pad(): bottom_left = lax.ppermute(first_row[..., -1:], both, diagonal(-1, 1))  11.4 us
    all_to_all x1, waiting for transfers between devices, on_device(): lax.all_to_all(forces.reshape(devices, slot_depth, 3, seg_width), ('gx',...  9.88 us
    ppermute x2, waiting for transfers between devices, halo_pad(): bottom_right = lax.ppermute(first_row[..., :1], both, diagonal(-1, -1))  8.44 us
    ppermute x2, starting transfers between devices, halo_pad(): right = lax.ppermute(block[..., :, :1], 'gy', up_y)  8.26 us
    ppermute x2, starting transfers between devices, halo_pad(): top_left = lax.ppermute(last_row[..., -1:], both, diagonal(1, 1))  6.69 us
  transfers between devices with their start and end apart: 18, of which 7 were waited for; matrix products, arithmetic and copies ran while one was open for 10% of the time, Pallas kernels for 9%

profile of v2, /device:TPU:9, one launch (start us, length us, event | category | flops | bytes accessed | tf_op | source)
XLA Modules:
  0.0 189.5 jit_solution(4835425318002339549)
XLA Ops:
  0.6 2.0 %pad_maximum_fusion.8 = (f32[6,8,1,1]{3,2,1,0:T(1,128)}, f32[6,8,1,1]{3,2,1,0:T(1,128)}, f32[6,8,1,1]{3,2,1,0:T(1,128)}, f32[6,8,1,1]{3,2,1,0:T(1,128)}) fusion(f32[1,8,16,256]{3,2,1,0:T(8,128)S(1)} %broadcast_in_dim_broadcast_in_dim.3, f32[1,8,16,256]{3,2,1,0:T(8,128)} %bitcast.161, f32[1,8,16,256]{3,2,1,0:T(8,128)} %bitcast.165, f32[3,8,16,256]{3,2,1,0:T(8,128)} %param.16), kind=kLoop, calls=%fused_computation.179 | loop fusion | flops 576 | bytes 787200 | tf_op jit(solution)/shard_map/slice | solution.py:135
  2.7 4.8 %collective-permute-start = (f32[6,8,1,1]{3,2,1,0:T(1,128)}, f32[6,8,1,1]{3,2,1,0:T(1,128)S(1)}, u32[]{:S(2)}, u32[]{:S(2)}) collective-permute-start(f32[6,8,1,1]{3,2,1,0:T(1,128)} %get-tuple-element.96), channel_id=1, source_target_pairs={{0,9},{1,10},{2,11},{3,12},{4,13},{5,14},{6,15},{8,17},{9,18},{10,... | collective-permute-start | bytes 584 | tf_op jit(solution)/shard_map/ppermute | solution.py:135
  7.4 2.8 %collective-permute-start.2 = (f32[6,8,1,1]{3,2,1,0:T(1,128)}, f32[6,8,1,1]{3,2,1,0:T(1,128)}, u32[]{:S(2)}, u32[]{:S(2)}) collective-permute-start(f32[6,8,1,1]{3,2,1,0:T(1,128)} %get-tuple-element.99), channel_id=1, source_target_pairs={{1,8},{2,9},{3,10},{4,11},{5,12},{6,13},{7,14},{9,16},{10,17},{11,... | collective-permute-start | bytes 584 | tf_op jit(solution)/shard_map/ppermute | solution.py:136
  12.4 2.3 %collective-permute-start.3 = (f32[6,8,16,1]{3,2,1,0:T(8,128)}, f32[6,8,16,1]{3,2,1,0:T(8,128)S(1)}, u32[]{:S(2)}, u32[]{:S(2)}) collective-permute-start(f32[6,8,16,1]{3,2,1,0:T(8,128)} %get-tuple-element.102), channel_id=1, source_target_pairs={{0,1},{1,2},{2,3},{3,4},{4,5},{5,6},{6,7},{8,9},{9,10},{10,11},{11... | collective-permute-start | bytes 9224 | tf_op jit(solution)/shard_map/ppermute | solution.py:132
  14.7 4.0 %collective-permute-start.4 = (f32[6,8,16,1]{3,2,1,0:T(8,128)}, f32[6,8,16,1]{3,2,1,0:T(8,128)}, u32[]{:S(2)}, u32[]{:S(2)}) collective-permute-start(f32[6,8,16,1]{3,2,1,0:T(8,128)} %get-tuple-element.103), channel_id=1, source_target_pairs={{1,0},{2,1},{3,2},{4,3},{5,4},{6,5},{7,6},{9,8},{10,9},{11,10},{12... | collective-permute-start | bytes 9224 | tf_op jit(solution)/shard_map/ppermute | solution.py:133
  18.9 2.1 %collective-permute-start.1 = (f32[6,8,1,256]{3,2,1,0:T(1,128)S(1)}, f32[6,8,1,256]{3,2,1,0:T(1,128)S(1)}, u32[]{:S(2)}, u32[]{:S(2)}) collective-permute-start(f32[6,8,1,256]{3,2,1,0:T(1,128)S(1)} %get-tuple-element.100), channel_id=1, source_target_pairs={{0,8},{8,16},{16,24},{1,9},{9,17},{17,25},{2,10},{10,18},{18,26},{... | collective-permute-start | bytes 147464 | tf_op jit(solution)/shard_map/ppermute | solution.py:130
  23.0 17.5 %shard_map.149 = f32[3,20480]{1,0:T(4,128)} custom-call(s32[1,20480]{1,0:T(1,128)} %bitcast.176, f32[384,256]{1,0:T(8,128)} %bitcast.169), custom_call_target="tpu_custom_call" | custom-call | tf_op jit(solution)/shard_map/pallas_call | solution.py:73
  45.6 5.0 %all-to-all-start = ((f32[32,5,8,128]{3,2,1,0:T(8,128)}), f32[32,5,8,128]{3,2,1,0:T(8,128)S(1)}, u32[]{:S(2)}, u32[]{:S(2)}) async-start(f32[32,5,8,128]{3,2,1,0:T(8,128)} %select_select_fusion), calls=%async_computation | async-start | bytes 1310720 | tf_op jit(solution)/shard_map/all_to_all | solution.py:300
  52.9 2.3 %collective-permute-start.6 = (f32[6,8,1,256]{3,2,1,0:T(1,128)S(1)}, f32[6,8,1,256]{3,2,1,0:T(1,128)S(1)}, u32[]{:S(2)}, u32[]{:S(2)}) collective-permute-start(f32[6,8,1,256]{3,2,1,0:T(1,128)S(1)} %get-tuple-element.101), channel_id=1, source_target_pairs={{8,0},{16,8},{24,16},{9,1},{17,9},{25,17},{10,2},{18,10},{26,18},{... | collective-permute-start | bytes 147464 | tf_op jit(solution)/shard_map/ppermute | solution.py:131
  55.8 2.4 %collective-permute-start.5 = (f32[6,8,1,1]{3,2,1,0:T(1,128)S(1)}, f32[6,8,1,1]{3,2,1,0:T(1,128)S(1)}, u32[]{:S(2)}, u32[]{:S(2)}) collective-permute-start(f32[6,8,1,1]{3,2,1,0:T(1,128)S(1)} %copy-done.13), channel_id=1, source_target_pairs={{8,1},{9,2},{10,3},{11,4},{12,5},{13,6},{14,7},{16,9},{17,10},{18,... | collective-permute-start | bytes 584 | tf_op jit(solution)/shard_map/ppermute | solution.py:137
  58.1 6.6 %collective-permute-done.5 = f32[6,8,1,1]{3,2,1,0:T(1,128)S(1)} collective-permute-done((f32[6,8,1,1]{3,2,1,0:T(1,128)S(1)}, f32[6,8,1,1]{3,2,1,0:T(1,128)S(1)}, u32[]{:S(2)}, u32[]{:S(2)}) %collective-permute-start.5) | collective-permute-done | bytes 224 | tf_op jit(solution)/shard_map/ppermute | solution.py:137
  64.7 1.9 %collective-permute-start.7 = (f32[6,8,1,1]{3,2,1,0:T(1,128)S(1)}, f32[6,8,1,1]{3,2,1,0:T(1,128)S(1)}, u32[]{:S(2)}, u32[]{:S(2)}) collective-permute-start(f32[6,8,1,1]{3,2,1,0:T(1,128)S(1)} %copy-done.12), channel_id=1, source_target_pairs={{9,0},{10,1},{11,2},{12,3},{13,4},{14,5},{15,6},{17,8},{18,9},{19,... | collective-permute-start | bytes 584 | tf_op jit(solution)/shard_map/ppermute | solution.py:138
  67.0 4.5 %collective-permute-done.7 = f32[6,8,1,1]{3,2,1,0:T(1,128)S(1)} collective-permute-done((f32[6,8,1,1]{3,2,1,0:T(1,128)S(1)}, f32[6,8,1,1]{3,2,1,0:T(1,128)S(1)}, u32[]{:S(2)}, u32[]{:S(2)}) %collective-permute-start.7) | collective-permute-done | bytes 224 | tf_op jit(solution)/shard_map/ppermute | solution.py:138
  71.5 2.2 %maximum_maximum_fusion = f32[6,8,18,258]{3,2,1,0:T(8,128)S(1)} fusion(f32[6,8,1,1]{3,2,1,0:T(1,128)S(1)} %collective-permute-done.7, f32[6,8,1,256]{3,2,1,0:T(1,128)S(1)} %collective-permute-done.6, f32[6,8,1,1]{3,2,1,0:T(1,128)S(1)} %collective-permute-done.5, f32[6,8,16,1]{3,2,1,0:T(8,128)} %collective-permute-done.4, ...), kind=kLoop, calls=%fused_computation.48 | loop fusion | flops 2452032 | bytes 1783296 | tf_op jit(solution)/shard_map/concatenate | solution.py:142
  79.3 38.6 %while.12 = (s32[]{:T(128)}, f32[2,80,3,128]{3,1,2,0:T(8,128)}, f32[2,80,128]{2,1,0:T(8,128)}, f32[2,80,7,128]{3,1,0,2:T(8,128)S(1)}, f32[2,80,10,128]{3,1,2,0:T(8,128)S(1)}, /*index=5*/s32[]{:T(128)}) while((s32[]{:T(128)}, f32[2,80,3,128]{3,1,2,0:T(8,128)}, f32[2,80,128]{2,1,0:T(8,128)}, f32[2,80,7,128]{3,1,0,2:T(8,128)S(1)}, ...), condition=%wide.region_8.9_spmd, body=%wide.region_3.8_spmd.sunk | while | flops 59002880 | bytes 3974221 | solution.py:317
  79.5 17.9 %fusion.82 = (f32[80,128]{1,0:T(8,128)S(1)}, f32[80,128]{1,0:T(8,128)S(1)}, f32[80,128]{1,0:T(8,128)S(1)}, f32[80,128]{1,0:T(8,128)S(1)}) fusion(f32[80,128]{1,0:T(8,128)S(1)} %get-tuple-element.173, f32[80,128]{1,0:T(8,128)S(1)} %get-tuple-element.174, f32[80,128]{1,0:T(8,128)S(1)} %get-tuple-element.175, f32[80,128]{1,0:T(8,128)S(1)} %get-tuple-element.176, ...), kind=kLoop, calls=%fused_computation.47.clone.1 | loop fusion | flops 58941440 | bytes 860160 | tf_op jit(solution)/shard_map/while/body/eval_jaxpr/reduce_sum | solution.py:228
  98.7 17.9 %fusion.82 = (f32[80,128]{1,0:T(8,128)S(1)}, f32[80,128]{1,0:T(8,128)S(1)}, f32[80,128]{1,0:T(8,128)S(1)}, f32[80,128]{1,0:T(8,128)S(1)}) fusion(f32[80,128]{1,0:T(8,128)S(1)} %get-tuple-element.173, f32[80,128]{1,0:T(8,128)S(1)} %get-tuple-element.174, f32[80,128]{1,0:T(8,128)S(1)} %get-tuple-element.175, f32[80,128]{1,0:T(8,128)S(1)} %get-tuple-element.176, ...), kind=kLoop, calls=%fused_computation.47.clone.1 | loop fusion | flops 58941440 | bytes 860160 | tf_op jit(solution)/shard_map/while/body/eval_jaxpr/reduce_sum | solution.py:228
  119.7 5.6 %all-to-all-start.1 = ((f32[32,5,3,128]{3,2,1,0:T(4,128)}), f32[32,5,3,128]{3,2,1,0:T(4,128)S(1)}, u32[]{:S(2)}, u32[]{:S(2)}) async-start(f32[32,5,3,128]{3,2,1,0:T(4,128)} %bitcast.60), calls=%async_computation.1 | async-start | bytes 655360 | tf_op jit(solution)/shard_map/all_to_all | solution.py:331
  126.5 9.9 %all-to-all-done.1 = f32[32,5,3,128]{3,2,1,0:T(4,128)S(1)} async-done(((f32[32,5,3,128]{3,2,1,0:T(4,128)}), f32[32,5,3,128]{3,2,1,0:T(4,128)S(1)}, u32[]{:S(2)}, u32[]{:S(2)}) %all-to-all-start.1) | async-done | bytes 245792 | tf_op jit(solution)/shard_map/all_to_all | solution.py:331
  138.3 11.9 %shard_map.150 = f32[384,256]{1,0:T(8,128)} custom-call(s32[1,20480]{1,0:T(1,128)} %bitcast.177, f32[3,20480]{1,0:T(4,128)} %pad_maximum_fusion.2.force_ref), custom_call_target="tpu_custom_call" | custom-call | tf_op jit(solution)/shard_map/pallas_call | solution.py:91
  151.8 1.9 %collective-permute-start.11 = (f32[3,8,16,1]{3,2,1,0:T(8,128)S(1)}, f32[3,8,16,1]{3,2,1,0:T(8,128)S(1)}, u32[]{:S(2)}, u32[]{:S(2)}) collective-permute-start(f32[3,8,16,1]{3,2,1,0:T(8,128)S(1)} %get-tuple-element.110), channel_id=1, source_target_pairs={{0,1},{1,2},{2,3},{3,4},{4,5},{5,6},{6,7},{8,9},{9,10},{10,11},{11... | collective-permute-start | bytes 4616 | tf_op jit(solution)/shard_map/ppermute | solution.py:132
  153.7 4.3 %collective-permute-start.12 = (f32[3,8,16,1]{3,2,1,0:T(8,128)S(1)}, f32[3,8,16,1]{3,2,1,0:T(8,128)S(1)}, u32[]{:S(2)}, u32[]{:S(2)}) collective-permute-start(f32[3,8,16,1]{3,2,1,0:T(8,128)S(1)} %get-tuple-element.111), channel_id=1, source_target_pairs={{1,0},{2,1},{3,2},{4,3},{5,4},{6,5},{7,6},{9,8},{10,9},{11,10},{12... | collective-permute-start | bytes 4616 | tf_op jit(solution)/shard_map/ppermute | solution.py:133
  158.0 2.9 %collective-permute-start.14 = (f32[3,8,1,256]{3,2,1,0:T(1,128)S(1)}, f32[3,8,1,256]{3,2,1,0:T(1,128)S(1)}, u32[]{:S(2)}, u32[]{:S(2)}) collective-permute-start(f32[3,8,1,256]{3,2,1,0:T(1,128)S(1)} %get-tuple-element.109), channel_id=1, source_target_pairs={{8,0},{16,8},{24,16},{9,1},{17,9},{25,17},{10,2},{18,10},{26,18},{... | collective-permute-start | bytes 73736 | tf_op jit(solution)/shard_map/ppermute | solution.py:131
  160.9 2.7 %collective-permute-start.9 = (f32[3,8,1,256]{3,2,1,0:T(1,128)S(1)}, f32[3,8,1,256]{3,2,1,0:T(1,128)S(1)}, u32[]{:S(2)}, u32[]{:S(2)}) collective-permute-start(f32[3,8,1,256]{3,2,1,0:T(1,128)S(1)} %get-tuple-element.108), channel_id=1, source_target_pairs={{0,8},{8,16},{16,24},{1,9},{9,17},{17,25},{2,10},{10,18},{18,26},{... | collective-permute-start | bytes 73736 | tf_op jit(solution)/shard_map/ppermute | solution.py:130
  163.7 2.0 %collective-permute-start.10 = (f32[3,8,1,1]{3,2,1,0:T(1,128)S(1)}, f32[3,8,1,1]{3,2,1,0:T(1,128)S(1)}, u32[]{:S(2)}, u32[]{:S(2)}) collective-permute-start(f32[3,8,1,1]{3,2,1,0:T(1,128)S(1)} %get-tuple-element.107), channel_id=1, source_target_pairs={{1,8},{2,9},{3,10},{4,11},{5,12},{6,13},{7,14},{9,16},{10,17},{11,... | collective-permute-start | bytes 296 | tf_op jit(solution)/shard_map/ppermute | solution.py:136
  165.7 3.0 %collective-permute-done.10 = f32[3,8,1,1]{3,2,1,0:T(1,128)S(1)} collective-permute-done((f32[3,8,1,1]{3,2,1,0:T(1,128)S(1)}, f32[3,8,1,1]{3,2,1,0:T(1,128)S(1)}, u32[]{:S(2)}, u32[]{:S(2)}) %collective-permute-start.10) | collective-permute-done | bytes 128 | tf_op jit(solution)/shard_map/ppermute | solution.py:136
  168.7 1.9 %collective-permute-start.13 = (f32[3,8,1,1]{3,2,1,0:T(1,128)S(1)}, f32[3,8,1,1]{3,2,1,0:T(1,128)S(1)}, u32[]{:S(2)}, u32[]{:S(2)}) collective-permute-start(f32[3,8,1,1]{3,2,1,0:T(1,128)S(1)} %get-tuple-element.106), channel_id=1, source_target_pairs={{8,1},{9,2},{10,3},{11,4},{12,5},{13,6},{14,7},{16,9},{17,10},{18,... | collective-permute-start | bytes 296 | tf_op jit(solution)/shard_map/ppermute | solution.py:137
  170.7 4.9 %collective-permute-done.13 = f32[3,8,1,1]{3,2,1,0:T(1,128)S(1)} collective-permute-done((f32[3,8,1,1]{3,2,1,0:T(1,128)S(1)}, f32[3,8,1,1]{3,2,1,0:T(1,128)S(1)}, u32[]{:S(2)}, u32[]{:S(2)}) %collective-permute-start.13) | collective-permute-done | bytes 128 | tf_op jit(solution)/shard_map/ppermute | solution.py:137
  175.5 1.9 %collective-permute-start.15 = (f32[3,8,1,1]{3,2,1,0:T(1,128)S(1)}, f32[3,8,1,1]{3,2,1,0:T(1,128)S(1)}, u32[]{:S(2)}, u32[]{:S(2)}) collective-permute-start(f32[3,8,1,1]{3,2,1,0:T(1,128)S(1)} %get-tuple-element.105), channel_id=1, source_target_pairs={{9,0},{10,1},{11,2},{12,3},{13,4},{14,5},{15,6},{17,8},{18,9},{19,... | collective-permute-start | bytes 296 | tf_op jit(solution)/shard_map/ppermute | solution.py:138
  177.4 4.0 %collective-permute-done.15 = f32[3,8,1,1]{3,2,1,0:T(1,128)S(1)} collective-permute-done((f32[3,8,1,1]{3,2,1,0:T(1,128)S(1)}, f32[3,8,1,1]{3,2,1,0:T(1,128)S(1)}, u32[]{:S(2)}, u32[]{:S(2)}) %collective-permute-start.15) | collective-permute-done | bytes 128 | tf_op jit(solution)/shard_map/ppermute | solution.py:138
  181.4 1.9 %collective-permute-start.8 = (f32[3,8,1,1]{3,2,1,0:T(1,128)S(1)}, f32[3,8,1,1]{3,2,1,0:T(1,128)S(1)}, u32[]{:S(2)}, u32[]{:S(2)}) collective-permute-start(f32[3,8,1,1]{3,2,1,0:T(1,128)S(1)} %get-tuple-element.104), channel_id=1, source_target_pairs={{0,9},{1,10},{2,11},{3,12},{4,13},{5,14},{6,15},{8,17},{9,18},{10,... | collective-permute-start | bytes 296 | tf_op jit(solution)/shard_map/ppermute | solution.py:135
  183.4 4.0 %collective-permute-done.8 = f32[3,8,1,1]{3,2,1,0:T(1,128)S(1)} collective-permute-done((f32[3,8,1,1]{3,2,1,0:T(1,128)S(1)}, f32[3,8,1,1]{3,2,1,0:T(1,128)S(1)}, u32[]{:S(2)}, u32[]{:S(2)}) %collective-permute-start.8) | collective-permute-done | bytes 128 | tf_op jit(solution)/shard_map/ppermute | solution.py:135
  (145 shorter events, 29.4 us)
Async XLA Ops:
  2.6 16.1 %copy-start = (f32[3,8,16,256]{3,2,1,0:T(8,128)S(1)}, f32[3,8,16,256]{3,2,1,0:T(8,128)}, u32[]{:S(2)}) copy-start(f32[3,8,16,256]{3,2,1,0:T(8,128)} %param.16) | copy-start | bytes 1179652
  2.6 16.1 %copy-start.2 = (f32[8,16,256]{2,1,0:T(8,128)S(1)}, f32[8,16,256]{2,1,0:T(8,128)}, u32[]{:S(2)}) copy-start(f32[8,16,256]{2,1,0:T(8,128)} %param.18) | copy-start | bytes 393220
  2.6 16.1 %copy-start.3 = (f32[8,16,256]{2,1,0:T(8,128)S(1)}, f32[8,16,256]{2,1,0:T(8,128)}, u32[]{:S(2)}) copy-start(f32[8,16,256]{2,1,0:T(8,128)} %param.17) | copy-start | bytes 393220
  2.7 50.3 %collective-permute-start = (f32[6,8,1,1]{3,2,1,0:T(1,128)}, f32[6,8,1,1]{3,2,1,0:T(1,128)S(1)}, u32[]{:S(2)}, u32[]{:S(2)}) collective-permute-start(f32[6,8,1,1]{3,2,1,0:T(1,128)} %get-tuple-element.96), channel_id=1, source_target_pairs={{0,9},{1,10},{2,11},{3,12},{4,13},{5,14},{6,15},{8,17},{9,18},{10,... | collective-permute-start | bytes 584 | tf_op jit(solution)/shard_map/ppermute | solution.py:135
  7.4 48.3 %collective-permute-start.2 = (f32[6,8,1,1]{3,2,1,0:T(1,128)}, f32[6,8,1,1]{3,2,1,0:T(1,128)}, u32[]{:S(2)}, u32[]{:S(2)}) collective-permute-start(f32[6,8,1,1]{3,2,1,0:T(1,128)} %get-tuple-element.99), channel_id=1, source_target_pairs={{1,8},{2,9},{3,10},{4,11},{5,12},{6,13},{7,14},{9,16},{10,17},{11,... | collective-permute-start | bytes 584 | tf_op jit(solution)/shard_map/ppermute | solution.py:136
  12.4 59.1 %collective-permute-start.3 = (f32[6,8,16,1]{3,2,1,0:T(8,128)}, f32[6,8,16,1]{3,2,1,0:T(8,128)S(1)}, u32[]{:S(2)}, u32[]{:S(2)}) collective-permute-start(f32[6,8,16,1]{3,2,1,0:T(8,128)} %get-tuple-element.102), channel_id=1, source_target_pairs={{0,1},{1,2},{2,3},{3,4},{4,5},{5,6},{6,7},{8,9},{9,10},{10,11},{11... | collective-permute-start | bytes 9224 | tf_op jit(solution)/shard_map/ppermute | solution.py:132
  14.7 26.8 %copy-start.6 = (f32[128,3,128]{2,0,1:T(8,128)S(1)}, f32[128,3,128]{2,0,1:T(8,128)}, u32[]{:S(2)}) copy-start(f32[128,3,128]{2,0,1:T(8,128)} %param.20) | copy-start | bytes 589828
  14.7 56.8 %collective-permute-start.4 = (f32[6,8,16,1]{3,2,1,0:T(8,128)}, f32[6,8,16,1]{3,2,1,0:T(8,128)}, u32[]{:S(2)}, u32[]{:S(2)}) collective-permute-start(f32[6,8,16,1]{3,2,1,0:T(8,128)} %get-tuple-element.103), channel_id=1, source_target_pairs={{1,0},{2,1},{3,2},{4,3},{5,4},{6,5},{7,6},{9,8},{10,9},{11,10},{12... | collective-permute-start | bytes 9224 | tf_op jit(solution)/shard_map/ppermute | solution.py:133
  18.8 23.8 %copy-start.19 = (s32[128]{0:T(128)S(1)}, s32[128]{0:T(128)}, u32[]{:S(2)}) copy-start(s32[128]{0:T(128)} %param.25) | copy-start | bytes 1540
  18.9 24.0 %copy-start.9 = (f32[128,128]{1,0:T(8,128)S(1)}, f32[128,128]{1,0:T(8,128)}, u32[]{:S(2)}) copy-start(f32[128,128]{1,0:T(8,128)} %param.21) | copy-start | bytes 196612
  18.9 24.0 %copy-start.17 = (s32[128]{0:T(128)S(1)}, s32[128]{0:T(128)}, u32[]{:S(2)}) copy-start(s32[128]{0:T(128)} %param.22) | copy-start | bytes 1540
  18.9 52.6 %collective-permute-start.1 = (f32[6,8,1,256]{3,2,1,0:T(1,128)S(1)}, f32[6,8,1,256]{3,2,1,0:T(1,128)S(1)}, u32[]{:S(2)}, u32[]{:S(2)}) collective-permute-start(f32[6,8,1,256]{3,2,1,0:T(1,128)S(1)} %get-tuple-element.100), channel_id=1, source_target_pairs={{0,8},{8,16},{16,24},{1,9},{9,17},{17,25},{2,10},{10,18},{18,26},{... | collective-permute-start | bytes 147464 | tf_op jit(solution)/shard_map/ppermute | solution.py:130
  44.3 20.4 %copy-start.12 = (f32[6,8,1,1]{3,2,1,0:T(1,128)S(1)}, f32[6,8,1,1]{3,2,1,0:T(1,128)}, u32[]{:S(2)}) copy-start(f32[6,8,1,1]{3,2,1,0:T(1,128)} %get-tuple-element.97) | copy-start | bytes 580
  44.3 22.3 %copy-start.15 = (f32[32,128]{1,0:T(8,128)S(1)}, f32[32,128]{1,0:T(8,128)}, u32[]{:S(2)}) copy-start(f32[32,128]{1,0:T(8,128)} %param.28) | copy-start | bytes 49156
  45.6 30.9 %all-to-all-start = ((f32[32,5,8,128]{3,2,1,0:T(8,128)}), f32[32,5,8,128]{3,2,1,0:T(8,128)S(1)}, u32[]{:S(2)}, u32[]{:S(2)}) async-start(f32[32,5,8,128]{3,2,1,0:T(8,128)} %select_select_fusion), calls=%async_computation | async-start | bytes 1310720 | tf_op jit(solution)/shard_map/all_to_all | solution.py:300
  52.9 18.6 %collective-permute-start.6 = (f32[6,8,1,256]{3,2,1,0:T(1,128)S(1)}, f32[6,8,1,256]{3,2,1,0:T(1,128)S(1)}, u32[]{:S(2)}, u32[]{:S(2)}) collective-permute-start(f32[6,8,1,256]{3,2,1,0:T(1,128)S(1)} %get-tuple-element.101), channel_id=1, source_target_pairs={{8,0},{16,8},{24,16},{9,1},{17,9},{25,17},{10,2},{18,10},{26,18},{... | collective-permute-start | bytes 147464 | tf_op jit(solution)/shard_map/ppermute | solution.py:131
  55.8 8.9 %collective-permute-start.5 = (f32[6,8,1,1]{3,2,1,0:T(1,128)S(1)}, f32[6,8,1,1]{3,2,1,0:T(1,128)S(1)}, u32[]{:S(2)}, u32[]{:S(2)}) collective-permute-start(f32[6,8,1,1]{3,2,1,0:T(1,128)S(1)} %copy-done.13), channel_id=1, source_target_pairs={{8,1},{9,2},{10,3},{11,4},{12,5},{13,6},{14,7},{16,9},{17,10},{18,... | collective-permute-start | bytes 584 | tf_op jit(solution)/shard_map/ppermute | solution.py:137
  64.7 6.8 %collective-permute-start.7 = (f32[6,8,1,1]{3,2,1,0:T(1,128)S(1)}, f32[6,8,1,1]{3,2,1,0:T(1,128)S(1)}, u32[]{:S(2)}, u32[]{:S(2)}) collective-permute-start(f32[6,8,1,1]{3,2,1,0:T(1,128)S(1)} %copy-done.12), channel_id=1, source_target_pairs={{9,0},{10,1},{11,2},{12,3},{13,4},{14,5},{15,6},{17,8},{18,9},{19,... | collective-permute-start | bytes 584 | tf_op jit(solution)/shard_map/ppermute | solution.py:138
  117.9 19.4 %copy-start.16 = (pred[128]{0:T(512)(128)(4,1)S(1)}, pred[128]{0:T(512)(128)(4,1)}, u32[]{:S(2)}) copy-start(pred[128]{0:T(512)(128)(4,1)} %get-tuple-element.63) | copy-start | bytes 388
  119.7 16.7 %all-to-all-start.1 = ((f32[32,5,3,128]{3,2,1,0:T(4,128)}), f32[32,5,3,128]{3,2,1,0:T(4,128)S(1)}, u32[]{:S(2)}, u32[]{:S(2)}) async-start(f32[32,5,3,128]{3,2,1,0:T(4,128)} %bitcast.60), calls=%async_computation.1 | async-start | bytes 655360 | tf_op jit(solution)/shard_map/all_to_all | solution.py:331
  137.3 14.2 %copy-start.4 = (f32[1,8,16,256]{3,2,1,0:T(8,128)S(1)}, f32[1,8,16,256]{3,2,1,0:T(8,128)}, u32[]{:S(2)}) copy-start(f32[1,8,16,256]{3,2,1,0:T(8,128)} %fusion.64) | copy-start | bytes 393220
  137.3 14.2 %copy-start.5 = (f32[1,8,16,256]{3,2,1,0:T(8,128)S(1)}, f32[1,8,16,256]{3,2,1,0:T(8,128)}, u32[]{:S(2)}) copy-start(f32[1,8,16,256]{3,2,1,0:T(8,128)} %fusion.66) | copy-start | bytes 393220
  137.3 14.2 %copy-start.7 = (f32[8,16,256]{2,1,0:T(8,128)S(1)}, f32[8,16,256]{2,1,0:T(8,128)}, u32[]{:S(2)}) copy-start(f32[8,16,256]{2,1,0:T(8,128)} %param.19) | copy-start | bytes 393220
  151.6 36.4 %copy-start.1 = (f32[3,8,16,256]{3,2,1,0:T(8,128)}, f32[3,8,16,256]{3,2,1,0:T(8,128)S(1)}, u32[]{:S(2)}) copy-start(f32[3,8,16,256]{3,2,1,0:T(8,128)S(1)} %fusion.16) | copy-start | bytes 1179652
  151.8 35.5 %collective-permute-start.11 = (f32[3,8,16,1]{3,2,1,0:T(8,128)S(1)}, f32[3,8,16,1]{3,2,1,0:T(8,128)S(1)}, u32[]{:S(2)}, u32[]{:S(2)}) collective-permute-start(f32[3,8,16,1]{3,2,1,0:T(8,128)S(1)} %get-tuple-element.110), channel_id=1, source_target_pairs={{0,1},{1,2},{2,3},{3,4},{4,5},{5,6},{6,7},{8,9},{9,10},{10,11},{11... | collective-permute-start | bytes 4616 | tf_op jit(solution)/shard_map/ppermute | solution.py:132
  153.7 33.6 %collective-permute-start.12 = (f32[3,8,16,1]{3,2,1,0:T(8,128)S(1)}, f32[3,8,16,1]{3,2,1,0:T(8,128)S(1)}, u32[]{:S(2)}, u32[]{:S(2)}) collective-permute-start(f32[3,8,16,1]{3,2,1,0:T(8,128)S(1)} %get-tuple-element.111), channel_id=1, source_target_pairs={{1,0},{2,1},{3,2},{4,3},{5,4},{6,5},{7,6},{9,8},{10,9},{11,10},{12... | collective-permute-start | bytes 4616 | tf_op jit(solution)/shard_map/ppermute | solution.py:133
  158.0 29.3 %collective-permute-start.14 = (f32[3,8,1,256]{3,2,1,0:T(1,128)S(1)}, f32[3,8,1,256]{3,2,1,0:T(1,128)S(1)}, u32[]{:S(2)}, u32[]{:S(2)}) collective-permute-start(f32[3,8,1,256]{3,2,1,0:T(1,128)S(1)} %get-tuple-element.109), channel_id=1, source_target_pairs={{8,0},{16,8},{24,16},{9,1},{17,9},{25,17},{10,2},{18,10},{26,18},{... | collective-permute-start | bytes 73736 | tf_op jit(solution)/shard_map/ppermute | solution.py:131
  160.9 26.5 %collective-permute-start.9 = (f32[3,8,1,256]{3,2,1,0:T(1,128)S(1)}, f32[3,8,1,256]{3,2,1,0:T(1,128)S(1)}, u32[]{:S(2)}, u32[]{:S(2)}) collective-permute-start(f32[3,8,1,256]{3,2,1,0:T(1,128)S(1)} %get-tuple-element.108), channel_id=1, source_target_pairs={{0,8},{8,16},{16,24},{1,9},{9,17},{17,25},{2,10},{10,18},{18,26},{... | collective-permute-start | bytes 73736 | tf_op jit(solution)/shard_map/ppermute | solution.py:130
  163.7 5.0 %collective-permute-start.10 = (f32[3,8,1,1]{3,2,1,0:T(1,128)S(1)}, f32[3,8,1,1]{3,2,1,0:T(1,128)S(1)}, u32[]{:S(2)}, u32[]{:S(2)}) collective-permute-start(f32[3,8,1,1]{3,2,1,0:T(1,128)S(1)} %get-tuple-element.107), channel_id=1, source_target_pairs={{1,8},{2,9},{3,10},{4,11},{5,12},{6,13},{7,14},{9,16},{10,17},{11,... | collective-permute-start | bytes 296 | tf_op jit(solution)/shard_map/ppermute | solution.py:136
  168.7 6.8 %collective-permute-start.13 = (f32[3,8,1,1]{3,2,1,0:T(1,128)S(1)}, f32[3,8,1,1]{3,2,1,0:T(1,128)S(1)}, u32[]{:S(2)}, u32[]{:S(2)}) collective-permute-start(f32[3,8,1,1]{3,2,1,0:T(1,128)S(1)} %get-tuple-element.106), channel_id=1, source_target_pairs={{8,1},{9,2},{10,3},{11,4},{12,5},{13,6},{14,7},{16,9},{17,10},{18,... | collective-permute-start | bytes 296 | tf_op jit(solution)/shard_map/ppermute | solution.py:137
  175.5 5.9 %collective-permute-start.15 = (f32[3,8,1,1]{3,2,1,0:T(1,128)S(1)}, f32[3,8,1,1]{3,2,1,0:T(1,128)S(1)}, u32[]{:S(2)}, u32[]{:S(2)}) collective-permute-start(f32[3,8,1,1]{3,2,1,0:T(1,128)S(1)} %get-tuple-element.105), channel_id=1, source_target_pairs={{9,0},{10,1},{11,2},{12,3},{13,4},{14,5},{15,6},{17,8},{18,9},{19,... | collective-permute-start | bytes 296 | tf_op jit(solution)/shard_map/ppermute | solution.py:138
  181.4 5.9 %collective-permute-start.8 = (f32[3,8,1,1]{3,2,1,0:T(1,128)S(1)}, f32[3,8,1,1]{3,2,1,0:T(1,128)S(1)}, u32[]{:S(2)}, u32[]{:S(2)}) collective-permute-start(f32[3,8,1,1]{3,2,1,0:T(1,128)S(1)} %get-tuple-element.104), channel_id=1, source_target_pairs={{0,9},{1,10},{2,11},{3,12},{4,13},{5,14},{6,15},{8,17},{9,18},{10,... | collective-permute-start | bytes 296 | tf_op jit(solution)/shard_map/ppermute | solution.py:135
  (6 other events, 58.9 us)

commit v3 on v1

--- a/solution.py
+++ b/solution.py
@@ -49,7 +49,7 @@
     ).astype(jnp.bfloat16)
     low_hit = lax.broadcasted_iota(jnp.int32, (LANES, width), 0) == (node & (LANES - 1))
     total = None
-    for piece in split_pieces(force_ref[...]):
+    for piece in split_pieces(force_ref[...])[:2]:
         spread = jnp.concatenate(
             [jnp.where(low_hit, piece[c : c + 1, :], jnp.zeros_like(piece[c : c + 1, :])) for c in range(channels)],
             axis=0,
@@ -268,27 +268,25 @@
     slot_hit = target_slot[None, :] == jnp.arange(devices * slot_depth, dtype=jnp.int32)[:, None]
     source = jnp.sum(jnp.where(slot_hit, positions[None, :], 0), axis=1)
     filled = jnp.any(slot_hit, axis=1)
-    outgoing = jnp.where(filled[:, None, None], jnp.take(slave, source, axis=0), 0.0)
-    chosen = jnp.where(filled, jnp.take(pair_master, source, axis=0), 0)
-    arrived, picked = (
-        lax.all_to_all(
-            outgoing.reshape(devices, slot_depth, 7, seg_width),
-            ("gx", "gy"),
-            split_axis=0,
-            concat_axis=0,
-            tiled=True,
-        ),
-        lax.all_to_all(
-            chosen.reshape(devices, slot_depth),
-            ("gx", "gy"),
-            split_axis=0,
-            concat_axis=0,
-            tiled=True,
-        ),
+    tagged = jnp.concatenate(
+        [
+            slave,
+            jnp.broadcast_to(pair_master.astype(jnp.float32)[:, None, None], (block_total, 1, seg_width)),
+        ],
+        axis=1,
+    )
+    outgoing = jnp.where(filled[:, None, None], jnp.take(tagged, source, axis=0), 0.0)
+    arrived = lax.all_to_all(
+        outgoing.reshape(devices, slot_depth, 8, seg_width),
+        ("gx", "gy"),
+        split_axis=0,
+        concat_axis=0,
+        tiled=True,
     )
     item_total = devices * slot_depth
-    arrived = arrived.reshape(item_total, 7, seg_width)
-    picked = picked.reshape(item_total)
+    arrived = arrived.reshape(item_total, 8, seg_width)
+    picked = arrived[:, 7, 0].astype(jnp.int32)
+    arrived = arrived[:, :7]
     paired = jnp.take(master_data, picked, axis=0)
     group_size = 16 * slot_depth
 

time: 176 us -> 163 us (0.926)
  local copies, waits for them, and re-layouts: 18.2 us -> 13 us
  Pallas kernels: 33.9 us -> 29.3 us
  starting transfers between devices: 39.8 us -> 35.7 us
    all_to_all x2 -> x1, starting transfers between devices: 12.5 us -> 6.33 us  [on_device(): lax.all_to_all(outgoing.reshape(devices, slot_depth, 8, seg_width), ('gx'...]
    pallas_call x1, Pallas kernels: 16.5 us -> 11.9 us  [node_scatter_add(): pl.pallas_call(scatter_kernel, grid=(padded_count // TILE,), in_specs=[pl...]
    slice x4, local copies, waits for them, and re-layouts: 3.3 us -> 0.79 us  [padded_2(): lax.slice_in_dim(block, block.shape[dim] - width, None, axis=dim)]
    all_to_all x1, starting transfers between devices: 5.96 us -> 7.79 us  [on_device(): lax.all_to_all(forces.reshape(devices, slot_depth, 3, seg_width), ('gx',...]
  transfers between devices with their start and end apart: 11 -> 10, of which waited for: 5 -> 6; matrix products, arithmetic and copies ran while one was open for 14% -> 12% of each run, Pallas kernels for 10% -> 11%
where the time goes in v3:
time: 163 us; the launch traced here: 162 us
  other arithmetic  54.3 us (33%)
  starting transfers between devices  35.7 us (22%)
  Pallas kernels  29.3 us (18%)
  waiting for transfers between devices  26.6 us (16%)
  local copies, waits for them, and re-layouts  13 us (8%)
    reduce_sum x2, other arithmetic, contact_pairs(): reaction = jnp.sum(push_force, axis=1)  35.8 us
    pallas_call x1, Pallas kernels, node_gather(): pl.pallas_call(gather_kernel, grid=(padded_count // TILE,), in_specs=[pl....  17.5 us
    pallas_call x1, Pallas kernels, node_scatter_add(): pl.pallas_call(scatter_kernel, grid=(padded_count // TILE,), in_specs=[pl...  11.9 us
    ppermute x4, starting transfers between devices, padded_2(): lax.ppermute(lax.slice_in_dim(block, 0, width, axis=dim), axis, backward)  10.9 us
    ppermute x4, starting transfers between devices, padded_2(): lax.ppermute(lax.slice_in_dim(block, block.shape[dim] - width, None, axis...  10.6 us
    ppermute x4, waiting for transfers between devices, padded_2(): lax.ppermute(lax.slice_in_dim(block, block.shape[dim] - width, None, axis...  10.4 us
    all_to_all x1, waiting for transfers between devices, on_device(): lax.all_to_all(forces.reshape(devices, slot_depth, 3, seg_width), ('gx',...  9.83 us
    all_to_all x1, starting transfers between devices, on_device(): lax.all_to_all(forces.reshape(devices, slot_depth, 3, seg_width), ('gx',...  7.79 us
  transfers between devices with their start and end apart: 10, of which 6 were waited for; matrix products, arithmetic and copies ran while one was open for 12% of the time, Pallas kernels for 11%

profile of v3, /device:TPU:9, one launch (start us, length us, event | category | flops | bytes accessed | tf_op | source)
XLA Modules:
  0.0 161.7 jit_solution(15239541855534344276)
XLA Ops:
  0.7 1.3 pad_maximum_fusion.9
  1.9 3.8 %collective-permute-start = (f32[6,8,1,256]{3,2,1,0:T(1,128)S(1)}, f32[6,8,1,256]{3,2,1,0:T(1,128)S(1)}, u32[]{:S(2)}, u32[]{:S(2)}) collective-permute-start(f32[6,8,1,256]{3,2,1,0:T(1,128)S(1)} %get-tuple-element.98), channel_id=1, source_target_pairs={{0,8},{8,16},{16,24},{1,9},{9,17},{17,25},{2,10},{10,18},{18,26},{... | collective-permute-start | bytes 147464 | tf_op jit(solution)/shard_map/ppermute | solution.py:116
  5.8 1.9 %collective-permute-start.1 = (f32[6,8,1,256]{3,2,1,0:T(1,128)S(1)}, f32[6,8,1,256]{3,2,1,0:T(1,128)S(1)}, u32[]{:S(2)}, u32[]{:S(2)}) collective-permute-start(f32[6,8,1,256]{3,2,1,0:T(1,128)S(1)} %get-tuple-element.99), channel_id=1, source_target_pairs={{8,0},{16,8},{24,16},{9,1},{17,9},{25,17},{10,2},{18,10},{26,18},{... | collective-permute-start | bytes 147464 | tf_op jit(solution)/shard_map/ppermute | solution.py:119
  7.7 0.9 convert_reduce_fusion
  9.5 1.1 reshape_reshape.9
  10.9 0.9 copy.102
  12.4 17.5 %shard_map.149 = f32[3,20480]{1,0:T(4,128)} custom-call(s32[1,20480]{1,0:T(1,128)} %bitcast.174, f32[384,256]{1,0:T(8,128)} %bitcast.161), custom_call_target="tpu_custom_call" | custom-call | tf_op jit(solution)/shard_map/pallas_call | solution.py:73
  29.9 1.0 slice_bitcast_fusion.19
  30.9 1.1 copy_add_fusion
  33.5 1.2 select_select_fusion
  34.7 6.3 %all-to-all-start = ((f32[32,5,8,128]{3,2,1,0:T(8,128)}), f32[32,5,8,128]{3,2,1,0:T(8,128)S(1)}, u32[]{:S(2)}, u32[]{:S(2)}) async-start(f32[32,5,8,128]{3,2,1,0:T(8,128)} %select_select_fusion), calls=%async_computation | async-start | bytes 1310720 | tf_op jit(solution)/shard_map/all_to_all | solution.py:279
  44.7 3.1 %collective-permute-start.3 = (f32[6,8,18,1]{2,1,3,0:T(8,128)S(1)}, f32[6,8,18,1]{2,1,3,0:T(8,128)S(1)}, u32[]{:S(2)}, u32[]{:S(2)}) collective-permute-start(f32[6,8,18,1]{2,1,3,0:T(8,128)S(1)} %copy.99), channel_id=1, source_target_pairs={{1,0},{2,1},{3,2},{4,3},{5,4},{6,5},{7,6},{9,8},{10,9},{11,10},{12... | collective-permute-start | bytes 10376 | tf_op jit(solution)/shard_map/ppermute | solution.py:119
  47.8 2.2 %collective-permute-start.2 = (f32[6,8,18,1]{2,1,3,0:T(8,128)S(1)}, f32[6,8,18,1]{2,1,3,0:T(8,128)S(1)}, u32[]{:S(2)}, u32[]{:S(2)}) collective-permute-start(f32[6,8,18,1]{2,1,3,0:T(8,128)S(1)} %copy.98), channel_id=1, source_target_pairs={{0,1},{1,2},{2,3},{3,4},{4,5},{5,6},{6,7},{8,9},{9,10},{10,11},{11... | collective-permute-start | bytes 10376 | tf_op jit(solution)/shard_map/ppermute | solution.py:116
  51.0 2.8 %collective-permute-done.2 = f32[6,8,18,1]{2,1,3,0:T(8,128)S(1)} collective-permute-done((f32[6,8,18,1]{2,1,3,0:T(8,128)S(1)}, f32[6,8,18,1]{2,1,3,0:T(8,128)S(1)}, u32[]{:S(2)}, u32[]{:S(2)}) %collective-permute-start.2) | collective-permute-done | bytes 3488 | tf_op jit(solution)/shard_map/ppermute | solution.py:116
  54.7 1.1 pad_maximum_fusion
  60.9 1.0 copy_select_fusion
  61.8 37.5 %while.12 = (s32[]{:T(128)}, f32[2,80,3,128]{3,1,2,0:T(8,128)}, f32[2,80,128]{2,1,0:T(8,128)}, f32[2,80,7,128]{3,1,0,2:T(8,128)S(1)}, f32[2,80,10,128]{3,1,2,0:T(8,128)S(1)}, /*index=5*/s32[]{:T(128)}) while((s32[]{:T(128)}, f32[2,80,3,128]{3,1,2,0:T(8,128)}, f32[2,80,128]{2,1,0:T(8,128)}, f32[2,80,7,128]{3,1,0,2:T(8,128)S(1)}, ...), condition=%wide.region_8.9_spmd, body=%wide.region_3.8_spmd.sunk | while | flops 59002880 | bytes 4628629 | solution.py:296
  62.0 17.9 %fusion.81 = (f32[80,128]{1,0:T(8,128)S(1)}, f32[80,128]{1,0:T(8,128)S(1)}, f32[80,128]{1,0:T(8,128)S(1)}, f32[80,128]{1,0:T(8,128)S(1)}) fusion(f32[80,128]{1,0:T(8,128)S(1)} %get-tuple-element.165, f32[80,128]{1,0:T(8,128)S(1)} %get-tuple-element.166, f32[80,128]{1,0:T(8,128)S(1)} %get-tuple-element.167, f32[80,128]{1,0:T(8,128)S(1)} %get-tuple-element.168, ...), kind=kLoop, calls=%fused_computation.47.clone.1 | loop fusion | flops 58941440 | bytes 860160 | tf_op jit(solution)/shard_map/while/body/eval_jaxpr/reduce_sum | solution.py:207
  80.7 17.9 %fusion.81 = (f32[80,128]{1,0:T(8,128)S(1)}, f32[80,128]{1,0:T(8,128)S(1)}, f32[80,128]{1,0:T(8,128)S(1)}, f32[80,128]{1,0:T(8,128)S(1)}) fusion(f32[80,128]{1,0:T(8,128)S(1)} %get-tuple-element.165, f32[80,128]{1,0:T(8,128)S(1)} %get-tuple-element.166, f32[80,128]{1,0:T(8,128)S(1)} %get-tuple-element.167, f32[80,128]{1,0:T(8,128)S(1)} %get-tuple-element.168, ...), kind=kLoop, calls=%fused_computation.47.clone.1 | loop fusion | flops 58941440 | bytes 860160 | tf_op jit(solution)/shard_map/while/body/eval_jaxpr/reduce_sum | solution.py:207
  99.3 1.8 %copy.119 = f32[2,80,3,128]{3,2,1,0:T(4,128)} copy(f32[2,80,3,128]{3,1,2,0:T(8,128)} %get-tuple-element.30) | data formatting | bytes 491520 | tf_op jit(solution)/shard_map/reshape;reshape | solution.py:311
  101.1 7.8 %all-to-all-start.1 = ((f32[32,5,3,128]{3,2,1,0:T(4,128)}), f32[32,5,3,128]{3,2,1,0:T(4,128)S(1)}, u32[]{:S(2)}, u32[]{:S(2)}) async-start(f32[32,5,3,128]{3,2,1,0:T(4,128)} %bitcast.60), calls=%async_computation.1 | async-start | bytes 655360 | tf_op jit(solution)/shard_map/all_to_all | solution.py:310
  108.9 1.2 convolution_negate_fusion
  110.2 9.8 %all-to-all-done.1 = f32[32,5,3,128]{3,2,1,0:T(4,128)S(1)} async-done(((f32[32,5,3,128]{3,2,1,0:T(4,128)}), f32[32,5,3,128]{3,2,1,0:T(4,128)S(1)}, u32[]{:S(2)}, u32[]{:S(2)}) %all-to-all-start.1) | async-done | bytes 245792 | tf_op jit(solution)/shard_map/all_to_all | solution.py:310
  122.0 11.9 %shard_map.150 = f32[384,256]{1,0:T(8,128)} custom-call(s32[1,20480]{1,0:T(1,128)} %bitcast.175, f32[3,20480]{1,0:T(4,128)} %pad_maximum_fusion.5.force_ref), custom_call_target="tpu_custom_call" | custom-call | tf_op jit(solution)/shard_map/pallas_call | solution.py:91
  133.8 1.1 copy.118
  135.3 2.5 %collective-permute-start.4 = (f32[3,8,1,256]{3,2,1,0:T(1,128)S(1)}, f32[3,8,1,256]{3,2,1,0:T(1,128)S(1)}, u32[]{:S(2)}, u32[]{:S(2)}) collective-permute-start(f32[3,8,1,256]{3,2,1,0:T(1,128)S(1)} %get-tuple-element.102), channel_id=1, source_target_pairs={{0,8},{8,16},{16,24},{1,9},{9,17},{17,25},{2,10},{10,18},{18,26},{... | collective-permute-start | bytes 73736 | tf_op jit(solution)/shard_map/ppermute | solution.py:116
  137.8 1.9 %collective-permute-start.5 = (f32[3,8,1,256]{3,2,1,0:T(1,128)S(1)}, f32[3,8,1,256]{3,2,1,0:T(1,128)S(1)}, u32[]{:S(2)}, u32[]{:S(2)}) collective-permute-start(f32[3,8,1,256]{3,2,1,0:T(1,128)S(1)} %get-tuple-element.103), channel_id=1, source_target_pairs={{8,0},{16,8},{24,16},{9,1},{17,9},{25,17},{10,2},{18,10},{26,18},{... | collective-permute-start | bytes 73736 | tf_op jit(solution)/shard_map/ppermute | solution.py:119
  139.7 3.2 %collective-permute-done.5 = f32[3,8,1,256]{3,2,1,0:T(1,128)S(1)} collective-permute-done((f32[3,8,1,256]{3,2,1,0:T(1,128)S(1)}, f32[3,8,1,256]{3,2,1,0:T(1,128)S(1)}, u32[]{:S(2)}, u32[]{:S(2)}) %collective-permute-start.5) | collective-permute-done | bytes 24608 | tf_op jit(solution)/shard_map/ppermute | solution.py:119
  143.2 2.2 %collective-permute-start.6 = (f32[3,8,18,1]{3,2,1,0:T(8,128)S(1)}, f32[3,8,18,1]{3,2,1,0:T(8,128)S(1)}, u32[]{:S(2)}, u32[]{:S(2)}) collective-permute-start(f32[3,8,18,1]{3,2,1,0:T(8,128)S(1)} %get-tuple-element.100), channel_id=1, source_target_pairs={{0,1},{1,2},{2,3},{3,4},{4,5},{5,6},{6,7},{8,9},{9,10},{10,11},{11... | collective-permute-start | bytes 5192 | tf_op jit(solution)/shard_map/ppermute | solution.py:116
  145.4 4.0 %collective-permute-start.7 = (f32[3,8,18,1]{3,2,1,0:T(8,128)S(1)}, f32[3,8,18,1]{3,2,1,0:T(8,128)S(1)}, u32[]{:S(2)}, u32[]{:S(2)}) collective-permute-start(f32[3,8,18,1]{3,2,1,0:T(8,128)S(1)} %get-tuple-element.101), channel_id=1, source_target_pairs={{1,0},{2,1},{3,2},{4,3},{5,4},{6,5},{7,6},{9,8},{10,9},{11,10},{12... | collective-permute-start | bytes 5192 | tf_op jit(solution)/shard_map/ppermute | solution.py:119
  149.4 7.5 %collective-permute-done.6 = f32[3,8,18,1]{3,2,1,0:T(8,128)S(1)} collective-permute-done((f32[3,8,18,1]{3,2,1,0:T(8,128)S(1)}, f32[3,8,18,1]{3,2,1,0:T(8,128)S(1)}, u32[]{:S(2)}, u32[]{:S(2)}) %collective-permute-start.6) | collective-permute-done | bytes 1760 | tf_op jit(solution)/shard_map/ppermute | solution.py:116
  156.9 2.7 %collective-permute-done.7 = f32[3,8,18,1]{3,2,1,0:T(8,128)S(1)} collective-permute-done((f32[3,8,18,1]{3,2,1,0:T(8,128)S(1)}, f32[3,8,18,1]{3,2,1,0:T(8,128)S(1)}, u32[]{:S(2)}, u32[]{:S(2)}) %collective-permute-start.7) | collective-permute-done | bytes 1760 | tf_op jit(solution)/shard_map/ppermute | solution.py:119
  (148 shorter events, 19.6 us)
Async XLA Ops:
  0.6 10.0 %copy-start.25 = (s32[128]{0:T(128)S(1)}, s32[128]{0:T(128)}, u32[]{:S(2)}) copy-start(s32[128]{0:T(128)} %param.25) | copy-start | bytes 1540
  0.6 11.1 %copy-start.20 = (s32[32,128]{1,0:T(8,128)S(1)}, s32[32,128]{1,0:T(8,128)}, u32[]{:S(2)}) copy-start(s32[32,128]{1,0:T(8,128)} %param.29) | copy-start | bytes 49156
  0.7 11.1 %copy-start.16 = (s32[128,128]{1,0:T(8,128)S(1)}, s32[128,128]{1,0:T(8,128)}, u32[]{:S(2)}) copy-start(s32[128,128]{1,0:T(8,128)} %param.23) | copy-start | bytes 196612
  1.9 29.0 %copy-start.6 = (f32[128,3,128]{2,0,1:T(8,128)S(1)}, f32[128,3,128]{2,0,1:T(8,128)}, u32[]{:S(2)}) copy-start(f32[128,3,128]{2,0,1:T(8,128)} %param.20) | copy-start | bytes 589828
  1.9 41.6 %collective-permute-start = (f32[6,8,1,256]{3,2,1,0:T(1,128)S(1)}, f32[6,8,1,256]{3,2,1,0:T(1,128)S(1)}, u32[]{:S(2)}, u32[]{:S(2)}) collective-permute-start(f32[6,8,1,256]{3,2,1,0:T(1,128)S(1)} %get-tuple-element.98), channel_id=1, source_target_pairs={{0,8},{8,16},{16,24},{1,9},{9,17},{17,25},{2,10},{10,18},{18,26},{... | collective-permute-start | bytes 147464 | tf_op jit(solution)/shard_map/ppermute | solution.py:116
  5.8 37.7 %collective-permute-start.1 = (f32[6,8,1,256]{3,2,1,0:T(1,128)S(1)}, f32[6,8,1,256]{3,2,1,0:T(1,128)S(1)}, u32[]{:S(2)}, u32[]{:S(2)}) collective-permute-start(f32[6,8,1,256]{3,2,1,0:T(1,128)S(1)} %get-tuple-element.99), channel_id=1, source_target_pairs={{8,0},{16,8},{24,16},{9,1},{17,9},{25,17},{10,2},{18,10},{26,18},{... | collective-permute-start | bytes 147464 | tf_op jit(solution)/shard_map/ppermute | solution.py:119
  9.5 22.5 %copy-start.17 = (f32[128,128]{1,0:T(8,128)S(1)}, f32[128,128]{1,0:T(8,128)}, u32[]{:S(2)}) copy-start(f32[128,128]{1,0:T(8,128)} %param.21) | copy-start | bytes 196612
  9.5 22.5 %copy-start.23 = (s32[128]{0:T(128)S(1)}, s32[128]{0:T(128)}, u32[]{:S(2)}) copy-start(s32[128]{0:T(128)} %param.22) | copy-start | bytes 1540
  32.6 9.3 %copy-start.19 = (f32[32,2,128]{2,1,0:T(2,128)S(1)}, f32[32,2,128]{2,1,0:T(2,128)}, u32[]{:S(2)}) copy-start(f32[32,2,128]{2,1,0:T(2,128)} %param.27) | copy-start | bytes 98308
  32.6 9.4 %copy-start.18 = (f32[32,3,128]{2,0,1:T(8,128)S(1)}, f32[32,3,128]{2,0,1:T(8,128)}, u32[]{:S(2)}) copy-start(f32[32,3,128]{2,0,1:T(8,128)} %param.26) | copy-start | bytes 147460
  33.4 9.4 %copy-start.24 = (s32[128,1]{0,1:T(1,128)S(1)}, s32[128,1]{0,1:T(1,128)}, u32[]{:S(2)}) copy-start(s32[128,1]{0,1:T(1,128)} %param.24) | copy-start | bytes 1540
  33.5 10.1 %copy-start = (f32[3,8,16,256]{3,2,1,0:T(8,128)S(1)}, f32[3,8,16,256]{3,2,1,0:T(8,128)}, u32[]{:S(2)}) copy-start(f32[3,8,16,256]{3,2,1,0:T(8,128)} %param.16) | copy-start | bytes 1179652
  33.5 10.0 %copy-start.2 = (f32[8,16,256]{2,1,0:T(8,128)S(1)}, f32[8,16,256]{2,1,0:T(8,128)}, u32[]{:S(2)}) copy-start(f32[8,16,256]{2,1,0:T(8,128)} %param.18) | copy-start | bytes 393220
  33.5 10.0 %copy-start.3 = (f32[8,16,256]{2,1,0:T(8,128)S(1)}, f32[8,16,256]{2,1,0:T(8,128)}, u32[]{:S(2)}) copy-start(f32[8,16,256]{2,1,0:T(8,128)} %param.17) | copy-start | bytes 393220
  34.7 24.3 %all-to-all-start = ((f32[32,5,8,128]{3,2,1,0:T(8,128)}), f32[32,5,8,128]{3,2,1,0:T(8,128)S(1)}, u32[]{:S(2)}, u32[]{:S(2)}) async-start(f32[32,5,8,128]{3,2,1,0:T(8,128)} %select_select_fusion), calls=%async_computation | async-start | bytes 1310720 | tf_op jit(solution)/shard_map/all_to_all | solution.py:279
  44.7 9.5 %collective-permute-start.3 = (f32[6,8,18,1]{2,1,3,0:T(8,128)S(1)}, f32[6,8,18,1]{2,1,3,0:T(8,128)S(1)}, u32[]{:S(2)}, u32[]{:S(2)}) collective-permute-start(f32[6,8,18,1]{2,1,3,0:T(8,128)S(1)} %copy.99), channel_id=1, source_target_pairs={{1,0},{2,1},{3,2},{4,3},{5,4},{6,5},{7,6},{9,8},{10,9},{11,10},{12... | collective-permute-start | bytes 10376 | tf_op jit(solution)/shard_map/ppermute | solution.py:119
  47.8 6.0 %collective-permute-start.2 = (f32[6,8,18,1]{2,1,3,0:T(8,128)S(1)}, f32[6,8,18,1]{2,1,3,0:T(8,128)S(1)}, u32[]{:S(2)}, u32[]{:S(2)}) collective-permute-start(f32[6,8,18,1]{2,1,3,0:T(8,128)S(1)} %copy.98), channel_id=1, source_target_pairs={{0,1},{1,2},{2,3},{3,4},{4,5},{5,6},{6,7},{8,9},{9,10},{10,11},{11... | collective-permute-start | bytes 10376 | tf_op jit(solution)/shard_map/ppermute | solution.py:116
  61.8 48.3 %copy-start.8 = (f32[32,1,128]{2,0,1:T(8,128)S(1)}, f32[32,1,128]{2,0,1:T(8,128)}, u32[]{:S(2)}) copy-start(f32[32,1,128]{2,0,1:T(8,128)} %copy-done.7) | copy-start | bytes 49156
  61.8 48.3 %copy-start.10 = (f32[32,1,128]{2,0,1:T(8,128)S(1)}, f32[32,1,128]{2,0,1:T(8,128)}, u32[]{:S(2)}) copy-start(f32[32,1,128]{2,0,1:T(8,128)} %copy-done.9) | copy-start | bytes 49156
  61.8 48.3 %copy-start.12 = (f32[32,1,128]{2,0,1:T(8,128)S(1)}, f32[32,1,128]{2,0,1:T(8,128)}, u32[]{:S(2)}) copy-start(f32[32,1,128]{2,0,1:T(8,128)} %copy-done.11) | copy-start | bytes 49156
  62.0 17.9 %copy-start.14 = (f32[2,80,128]{2,1,0:T(8,128)S(1)}, f32[2,80,128]{2,1,0:T(8,128)}, u32[]{:S(2)}) copy-start(f32[2,80,128]{2,1,0:T(8,128)} %get-tuple-element.194) | copy-start | bytes 245764 | tf_op jit(solution)/shard_map/while
  80.7 17.9 %copy-start.14 = (f32[2,80,128]{2,1,0:T(8,128)S(1)}, f32[2,80,128]{2,1,0:T(8,128)}, u32[]{:S(2)}) copy-start(f32[2,80,128]{2,1,0:T(8,128)} %get-tuple-element.194) | copy-start | bytes 245764 | tf_op jit(solution)/shard_map/while
  99.3 21.6 %copy-start.22 = (pred[128]{0:T(512)(128)(4,1)S(1)}, pred[128]{0:T(512)(128)(4,1)}, u32[]{:S(2)}) copy-start(pred[128]{0:T(512)(128)(4,1)} %get-tuple-element.63) | copy-start | bytes 388
  101.1 18.9 %all-to-all-start.1 = ((f32[32,5,3,128]{3,2,1,0:T(4,128)}), f32[32,5,3,128]{3,2,1,0:T(4,128)S(1)}, u32[]{:S(2)}, u32[]{:S(2)}) async-start(f32[32,5,3,128]{3,2,1,0:T(4,128)} %bitcast.60), calls=%async_computation.1 | async-start | bytes 655360 | tf_op jit(solution)/shard_map/all_to_all | solution.py:310
  120.9 14.2 %copy-start.4 = (f32[1,8,16,256]{3,2,1,0:T(8,128)S(1)}, f32[1,8,16,256]{3,2,1,0:T(8,128)}, u32[]{:S(2)}) copy-start(f32[1,8,16,256]{3,2,1,0:T(8,128)} %fusion.62) | copy-start | bytes 393220
  120.9 14.2 %copy-start.5 = (f32[1,8,16,256]{3,2,1,0:T(8,128)S(1)}, f32[1,8,16,256]{3,2,1,0:T(8,128)}, u32[]{:S(2)}) copy-start(f32[1,8,16,256]{3,2,1,0:T(8,128)} %fusion.64) | copy-start | bytes 393220
  121.0 14.2 %copy-start.13 = (f32[8,16,256]{2,1,0:T(8,128)S(1)}, f32[8,16,256]{2,1,0:T(8,128)}, u32[]{:S(2)}) copy-start(f32[8,16,256]{2,1,0:T(8,128)} %param.19) | copy-start | bytes 393220
  135.3 24.9 %copy-start.1 = (f32[3,8,16,256]{3,2,1,0:T(8,128)}, f32[3,8,16,256]{3,2,1,0:T(8,128)S(1)}, u32[]{:S(2)}) copy-start(f32[3,8,16,256]{3,2,1,0:T(8,128)S(1)} %fusion.16) | copy-start | bytes 1179652
  135.3 4.4 %collective-permute-start.4 = (f32[3,8,1,256]{3,2,1,0:T(1,128)S(1)}, f32[3,8,1,256]{3,2,1,0:T(1,128)S(1)}, u32[]{:S(2)}, u32[]{:S(2)}) collective-permute-start(f32[3,8,1,256]{3,2,1,0:T(1,128)S(1)} %get-tuple-element.102), channel_id=1, source_target_pairs={{0,8},{8,16},{16,24},{1,9},{9,17},{17,25},{2,10},{10,18},{18,26},{... | collective-permute-start | bytes 73736 | tf_op jit(solution)/shard_map/ppermute | solution.py:116
  137.8 5.1 %collective-permute-start.5 = (f32[3,8,1,256]{3,2,1,0:T(1,128)S(1)}, f32[3,8,1,256]{3,2,1,0:T(1,128)S(1)}, u32[]{:S(2)}, u32[]{:S(2)}) collective-permute-start(f32[3,8,1,256]{3,2,1,0:T(1,128)S(1)} %get-tuple-element.103), channel_id=1, source_target_pairs={{8,0},{16,8},{24,16},{9,1},{17,9},{25,17},{10,2},{18,10},{26,18},{... | collective-permute-start | bytes 73736 | tf_op jit(solution)/shard_map/ppermute | solution.py:119
  143.2 13.7 %collective-permute-start.6 = (f32[3,8,18,1]{3,2,1,0:T(8,128)S(1)}, f32[3,8,18,1]{3,2,1,0:T(8,128)S(1)}, u32[]{:S(2)}, u32[]{:S(2)}) collective-permute-start(f32[3,8,18,1]{3,2,1,0:T(8,128)S(1)} %get-tuple-element.100), channel_id=1, source_target_pairs={{0,1},{1,2},{2,3},{3,4},{4,5},{5,6},{6,7},{8,9},{9,10},{10,11},{11... | collective-permute-start | bytes 5192 | tf_op jit(solution)/shard_map/ppermute | solution.py:116
  145.4 14.3 %collective-permute-start.7 = (f32[3,8,18,1]{3,2,1,0:T(8,128)S(1)}, f32[3,8,18,1]{3,2,1,0:T(8,128)S(1)}, u32[]{:S(2)}, u32[]{:S(2)}) collective-permute-start(f32[3,8,18,1]{3,2,1,0:T(8,128)S(1)} %get-tuple-element.101), channel_id=1, source_target_pairs={{1,0},{2,1},{3,2},{4,3},{5,4},{6,5},{7,6},{9,8},{10,9},{11,10},{12... | collective-permute-start | bytes 5192 | tf_op jit(solution)/shard_map/ppermute | solution.py:119
  (6 other events, 31.4 us)

commit v4 on v3

--- a/solution.py
+++ b/solution.py
@@ -1,3 +1,5 @@
+import math
+
 import jax
 import jax.numpy as jnp
 from jax import lax
@@ -59,6 +61,96 @@
         )
         total = part if total is None else total + part
     out_ref[...] += total
+
+
+def contact_kernel(picked_ref, live_ref, slave_ref, master_ref, force_ref, react_ref, acc_ref):
+    step = pl.program_id(0)
+    group = slave_ref.shape[0]
+    width = slave_ref.shape[2]
+
+    @pl.when(step == 0)
+    def _():
+        acc_ref[...] = jnp.zeros_like(acc_ref)
+
+    lane = lax.broadcasted_iota(jnp.int32, acc_ref.shape, 1)
+
+    def body(k, carry):
+        item = step * group + k
+
+        @pl.when(live_ref[item] > 0)
+        def _():
+            s = slave_ref[k]
+            m = master_ref[picked_ref[item]]
+            delta_x = s[0:1] - m[:, 0:1]
+            delta_y = s[1:2] - m[:, 1:2]
+            delta_z = s[2:3] - m[:, 2:3]
+            normal_x = m[:, 3:4]
+            normal_y = m[:, 4:5]
+            normal_z = m[:, 5:6]
+            dist_sq = delta_x * delta_x + delta_y * delta_y + delta_z * delta_z
+            gap_normal = normal_x * delta_x + normal_y * delta_y + normal_z * delta_z
+            closing = (normal_x * s[3:4] + normal_y * s[4:5] + normal_z * s[5:6]) - m[:, 6:7]
+            weight = jnp.exp(-dist_sq)
+            soft = gap_normal * (-1.0 / SOFT_GAP)
+            depth_soft = SOFT_GAP * (
+                jnp.maximum(soft, 0.0) + jnp.log1p(jnp.exp(-jnp.abs(soft)))
+            )
+            push = (
+                (s[6:7] * m[:, 7:8])
+                * weight
+                * depth_soft
+                * (1.0 + DAMPING * jnp.tanh(-closing))
+            )
+            force_ref[k] = jnp.concatenate(
+                [
+                    jnp.sum(push * normal_x, axis=0, keepdims=True),
+                    jnp.sum(push * normal_y, axis=0, keepdims=True),
+                    jnp.sum(push * normal_z, axis=0, keepdims=True),
+                ],
+                axis=0,
+            )
+            reaction = jnp.sum(push, axis=1, keepdims=True)
+            acc_ref[...] += jnp.where(lane == picked_ref[item], reaction, 0.0)
+
+        @pl.when(live_ref[item] == 0)
+        def _():
+            force_ref[k] = jnp.zeros((3, width), jnp.float32)
+
+        return carry
+
+    lax.fori_loop(0, group, body, 0)
+
+    @pl.when(step == pl.num_programs(0) - 1)
+    def _():
+        react_ref[...] = acc_ref[...].T
+
+
+def contact_forces(arrived, picked, live, master_cols):
+    item_total, _, width = arrived.shape
+    group = math.gcd(item_total, 16)
+    master_total = master_cols.shape[0]
+    grid_spec = pltpu.PrefetchScalarGridSpec(
+        num_scalar_prefetch=2,
+        grid=(item_total // group,),
+        in_specs=[
+            pl.BlockSpec((group,) + arrived.shape[1:], lambda i, p, l: (i, 0, 0)),
+            pl.BlockSpec(master_cols.shape, lambda i, p, l: (0, 0, 0)),
+        ],
+        out_specs=[
+            pl.BlockSpec((group, 3, width), lambda i, p, l: (i, 0, 0)),
+            pl.BlockSpec((width, width), lambda i, p, l: (0, 0)),
+        ],
+        scratch_shapes=[pltpu.VMEM((width, width), jnp.float32)],
+    )
+    forces, react = pl.pallas_call(
+        contact_kernel,
+        grid_spec=grid_spec,
+        out_shape=[
+            jax.ShapeDtypeStruct((item_total, 3, width), jnp.float32),
+            jax.ShapeDtypeStruct((width, width), jnp.float32),
+        ],
+    )(picked, live, arrived, master_cols)
+    return forces, react[:master_total]
 
 
 def node_gather(field, nodes):
@@ -271,7 +363,14 @@
     tagged = jnp.concatenate(
         [
             slave,
-            jnp.broadcast_to(pair_master.astype(jnp.float32)[:, None, None], (block_total, 1, seg_width)),
+            jnp.broadcast_to(
+                jnp.where(
+                    jnp.arange(seg_width)[None, :] == 0,
+                    pair_master.astype(jnp.float32)[:, None],
+                    1.0,
+                )[:, None, :],
+                (block_total, 1, seg_width),
+            ),
         ],
         axis=1,
     )
@@ -285,27 +384,20 @@
     )
     item_total = devices * slot_depth
     arrived = arrived.reshape(item_total, 8, seg_width)
-    picked = arrived[:, 7, 0].astype(jnp.int32)
-    arrived = arrived[:, :7]
-    paired = jnp.take(master_data, picked, axis=0)
-    group_size = 16 * slot_depth
-
-    def per_group(pairing):
-        return contact_pairs(pairing[0], pairing[1])
-
-    forces, reaction = lax.map(
-        per_group,
-        (
-            arrived.reshape(item_total // group_size, group_size, 7, seg_width),
-            paired.reshape(item_total // group_size, group_size, 10, seg_width),
-        ),
-    )
-    forces = forces.reshape(item_total, 3, seg_width)
-    reaction = reaction.reshape(item_total, seg_width)
-    onehot = (picked[:, None] == jnp.arange(master_total, dtype=jnp.int32)[None, :]).astype(
-        jnp.float32
-    )
-    master_sum = jnp.dot(onehot.T, reaction, precision=lax.Precision.HIGHEST)
+    picked = jnp.clip(arrived[:, 7, 0].astype(jnp.int32), 0, master_total - 1)
+    live = (arrived[:, 7, 1] > 0.5).astype(jnp.int32)
+    master_vel_normal = jnp.sum(normals * master_vel, axis=1, keepdims=True)
+    master_rows = jnp.concatenate(
+        [
+            master_cent + TIME_STEP * master_vel,
+            normals,
+            master_vel_normal,
+            master_stiff[:, None, :],
+        ],
+        axis=1,
+    )
+    master_cols = master_rows.transpose(0, 2, 1)
+    forces, master_sum = contact_forces(arrived, picked, live, master_cols)
     master_force = -master_sum[:, None, :] * normals
     returned = lax.all_to_all(
         forces.reshape(devices, slot_depth, 3, seg_width),

time: 163 us -> 217 us (1.33)
  Pallas kernels: 29.3 us -> 67.1 us
  local copies, waits for them, and re-layouts: 13 us -> 42.7 us
  other arithmetic: 54.3 us -> 36.8 us
  starting transfers between devices: 35.7 us -> 49.7 us
  waiting for transfers between devices: 26.6 us -> 16 us
    pallas_call x0 -> x1, Pallas kernels: none -> 37.7 us  [contact_forces(): pl.pallas_call(contact_kernel, grid_spec=grid_spec, out_shape=[jax.ShapeD...]
    reduce_sum x2 -> x1, other arithmetic: 35.8 us -> 1.72 us  [on_device(): master_vel_normal = jnp.sum(normals * master_vel, axis=1, keepdims=True)]
    all_to_all x1, starting transfers between devices: 7.79 us -> 21.5 us  [on_device(): lax.all_to_all(forces.reshape(devices, slot_depth, 3, seg_width), ('gx',...]
    ppermute x4, waiting for transfers between devices: 10.4 us -> 0.92 us  [padded_2(): lax.ppermute(lax.slice_in_dim(block, block.shape[dim] - width, None, axis...]
    concatenate x1, local copies, waits for them, and re-layouts: 0.38 us -> 8.6 us  [on_device(): jnp.concatenate([master_cent + TIME_STEP * master_vel, normals, master_ve...]
    convert_element_type x3 -> x2, other arithmetic: 0.04 us -> 7.18 us  [the longest x1 6.52 us: on_device(): live = (arrived[:, 7, 1] > 0.5).astype(jnp.int32)]
    all_to_all x1, waiting for transfers between devices: 9.83 us -> 3.89 us  [on_device(): lax.all_to_all(forces.reshape(devices, slot_depth, 3, seg_width), ('gx',...]
    mul x1 -> x2, other arithmetic: 0.01 us -> 5.93 us  [the longest x1 4.31 us: on_device(): master_force = -master_sum[:, None, :] * normals]
  transfers between devices with their start and end apart: 10 -> 10, of which waited for: 6 -> 3; matrix products, arithmetic and copies ran while one was open for 12% -> 26% of each run, Pallas kernels for 11% -> 0%
where the time goes in v4:
time: 217 us; the launch traced here: 214 us
  Pallas kernels  67.1 us (31%)
  starting transfers between devices  49.7 us (23%)
  local copies, waits for them, and re-layouts  42.7 us (20%)
  other arithmetic  36.8 us (17%)
  waiting for transfers between devices  16 us (7%)
    pallas_call x1, Pallas kernels, contact_forces(): pl.pallas_call(contact_kernel, grid_spec=grid_spec, out_shape=[jax.ShapeD...  37.7 us
    all_to_all x1, starting transfers between devices, on_device(): lax.all_to_all(forces.reshape(devices, slot_depth, 3, seg_width), ('gx',...  21.5 us
    pallas_call x1, Pallas kernels, node_gather(): pl.pallas_call(gather_kernel, grid=(padded_count // TILE,), in_specs=[pl....  17.5 us
    pallas_call x1, Pallas kernels, node_scatter_add(): pl.pallas_call(scatter_kernel, grid=(padded_count // TILE,), in_specs=[pl...  11.9 us
    ppermute x4, waiting for transfers between devices, padded_2(): lax.ppermute(lax.slice_in_dim(block, 0, width, axis=dim), axis, backward)  11.2 us
    ppermute x4, starting transfers between devices, padded_2(): lax.ppermute(lax.slice_in_dim(block, block.shape[dim] - width, None, axis...  11 us
    ppermute x4, starting transfers between devices, padded_2(): lax.ppermute(lax.slice_in_dim(block, 0, width, axis=dim), axis, backward)  10.8 us
    concatenate x1, local copies, waits for them, and re-layouts, on_device(): jnp.concatenate([master_cent + TIME_STEP * master_vel, normals, master_ve...  8.6 us
  transfers between devices with their start and end apart: 10, of which 3 were waited for; matrix products, arithmetic and copies ran while one was open for 26% of the time, Pallas kernels for 0%

profile of v4, /device:TPU:9, one launch (start us, length us, event | category | flops | bytes accessed | tf_op | source)
XLA Modules:
  0.0 213.6 jit_solution(13918716935777342318)
XLA Ops:
  6.6 17.5 %shard_map.149 = f32[3,20480]{1,0:T(4,128)} custom-call(s32[1,20480]{1,0:T(1,128)} %bitcast.90, f32[384,256]{1,0:T(8,128)} %bitcast.80), custom_call_target="tpu_custom_call" | custom-call | tf_op jit(solution)/shard_map/pallas_call | solution.py:165
  29.1 6.4 %all-to-all-start = ((f32[32,5,8,128]{3,2,1,0:T(8,128)}), f32[32,5,8,128]{3,2,1,0:T(8,128)S(1)}, u32[]{:S(2)}, u32[]{:S(2)}) async-start(f32[32,5,8,128]{3,2,1,0:T(8,128)} %select_select_fusion), calls=%async_computation | async-start | bytes 1310720 | tf_op jit(solution)/shard_map/all_to_all | solution.py:378
  36.3 2.3 %collective-permute-start.1 = (f32[6,8,1,256]{3,2,1,0:T(1,128)}, f32[6,8,1,256]{3,2,1,0:T(1,128)S(1)}, u32[]{:S(2)}, u32[]{:S(2)}) collective-permute-start(f32[6,8,1,256]{3,2,1,0:T(1,128)} %get-tuple-element.25), channel_id=1, source_target_pairs={{8,0},{16,8},{24,16},{9,1},{17,9},{25,17},{10,2},{18,10},{26,18},{... | collective-permute-start | bytes 147464 | tf_op jit(solution)/shard_map/ppermute | solution.py:211
  38.5 3.3 %collective-permute-start = (f32[6,8,1,256]{3,2,1,0:T(1,128)}, f32[6,8,1,256]{3,2,1,0:T(1,128)}, u32[]{:S(2)}, u32[]{:S(2)}) collective-permute-start(f32[6,8,1,256]{3,2,1,0:T(1,128)} %get-tuple-element.24), channel_id=1, source_target_pairs={{0,8},{8,16},{16,24},{1,9},{9,17},{17,25},{2,10},{10,18},{18,26},{... | collective-permute-start | bytes 147464 | tf_op jit(solution)/shard_map/ppermute | solution.py:208
  44.7 2.0 copy.130
  46.7 2.0 copy.131
  48.6 2.0 copy.132
  50.7 3.6 %fusion.59 = (f32[32,1,128]{1,2,0:T(8,128)S(1)}, f32[32,1,128]{1,2,0:T(8,128)S(1)}, f32[32,1,128]{1,2,0:T(8,128)S(1)}) fusion(f32[32,1,128]{1,2,0:T(8,128)} %copy.130, f32[32,1,128]{1,2,0:T(8,128)} %copy.131, f32[32,1,128]{1,2,0:T(8,128)} %copy.132), kind=kLoop, calls=%fused_computation.147 | loop fusion | flops 8192 | bytes 98304 | tf_op jit(solution)/shard_map/rsqrt | solution.py:304
  58.4 2.0 copy.120
  60.5 3.1 %collective-permute-start.3 = (f32[6,8,18,1]{2,1,3,0:T(8,128)}, f32[6,8,18,1]{2,1,3,0:T(8,128)}, u32[]{:S(2)}, u32[]{:S(2)}) collective-permute-start(f32[6,8,18,1]{2,1,3,0:T(8,128)} %copy.120), channel_id=1, source_target_pairs={{1,0},{2,1},{3,2},{4,3},{5,4},{6,5},{7,6},{9,8},{10,9},{11,10},{12... | collective-permute-start | bytes 10376 | tf_op jit(solution)/shard_map/ppermute | solution.py:211
  63.6 2.0 copy.119
  65.6 2.4 %collective-permute-start.2 = (f32[6,8,18,1]{2,1,3,0:T(8,128)}, f32[6,8,18,1]{2,1,3,0:T(8,128)}, u32[]{:S(2)}, u32[]{:S(2)}) collective-permute-start(f32[6,8,18,1]{2,1,3,0:T(8,128)} %copy.119), channel_id=1, source_target_pairs={{0,1},{1,2},{2,3},{3,4},{4,5},{5,6},{6,7},{8,9},{9,10},{10,11},{11... | collective-permute-start | bytes 10376 | tf_op jit(solution)/shard_map/ppermute | solution.py:208
  68.0 2.2 %copy.128 = f32[32,3,128]{2,0,1:T(8,128)S(1)} copy(f32[32,3,128]{1,2,0:T(8,128)} %broadcast_multiply_fusion) | data formatting | bytes 98304 | tf_op jit(solution)/shard_map/mul | solution.py:392
  71.7 2.9 %copy.133 = f32[32,3,128]{1,2,0:T(8,128)} copy(f32[32,3,128]{2,0,1:T(8,128)} %add.203) | data formatting | bytes 98304 | tf_op jit(solution)/shard_map/add | solution.py:392
  74.5 2.0 copy.134
  76.6 2.0 copy.135
  78.6 8.6 %concatenate.33 = f32[32,8,128]{1,2,0:T(8,128)} concatenate(f32[32,3,128]{1,2,0:T(8,128)} %copy.133, f32[32,1,128]{1,2,0:T(8,128)} %copy-done, f32[32,1,128]{1,2,0:T(8,128)} %copy-done.1, f32[32,1,128]{1,2,0:T(8,128)S(1)} %get-tuple-element.12, f32[32,1,128]{1,2,0:T(8,128)} %copy.134, f32[32,1,128]{1,2,0:T(8,128)} %copy.135), dimensions={1} | concatenate | bytes 262144 | tf_op jit(solution)/shard_map/concatenate | solution.py:390
  87.2 2.0 copy.122
  89.1 1.9 copy.121
  91.1 2.4 %pad_maximum_fusion.1 = f32[6,8,18,258]{3,2,1,0:T(8,128)S(1)} fusion(f32[6,8,18,1]{3,2,1,0:T(8,128)} %copy.122, f32[6,8,1,256]{3,2,1,0:T(1,128)S(1)} %collective-permute-done.1, f32[1,8,16,256]{3,2,1,0:T(8,128)S(1)} %broadcast_in_dim_broadcast_in_dim.3, f32[1,8,16,256]{3,2,1,0:T(8,128)S(1)} %bitcast.85, f32[1,8,16,256]{3,2,1,0:T(8,128)} %bitcast.86, ...), kind=kLoop, calls=%fused_computation.4 | loop fusion | flops 1560384 | bytes 1783296 | tf_op jit(solution)/shard_map/concatenate | solution.py:212
  96.2 6.5 %fusion.53 = (s32[160]{0:T(256)}, s32[160]{0:T(256)}) fusion(f32[160,8,128]{2,1,0:T(8,128)S(1)} %bitcast.77), kind=kLoop, calls=%fused_computation.116 | loop fusion | flops 640 | bytes 2560 | tf_op jit(solution)/shard_map/convert_element_type | solution.py:388
  102.8 37.7 %shard_map.150 = (f32[160,3,128]{2,1,0:T(4,128)}, f32[128,128]{1,0:T(8,128)}) custom-call(s32[160]{0:T(256)} %get-tuple-element.9.picked_ref, s32[160]{0:T(256)} %get-tuple-element.8.live_ref, f32[160,8,128]{2,1,0:T(8,128)} %bitcast.78, f32[32,128,8]{2,1,0:T(8,128)} %bitcast.75), custom_call_target="tpu_custom_call" | custom-call | tf_op jit(solution)/shard_map/pallas_call | solution.py:145
  140.5 21.5 %all-to-all-start.1 = ((f32[32,5,3,128]{3,2,1,0:T(4,128)}), f32[32,5,3,128]{3,2,1,0:T(4,128)S(1)}, u32[]{:S(2)}, u32[]{:S(2)}) async-start(f32[32,5,3,128]{3,2,1,0:T(4,128)} %bitcast.92), calls=%async_computation.1 | async-start | bytes 655360 | tf_op jit(solution)/shard_map/all_to_all | solution.py:402
  162.8 4.3 %broadcast_multiply_fusion.1 = f32[32,3,128]{1,2,0:T(8,128)} fusion(f32[32,128]{1,0:T(8,128)S(1)} %slice_negate_fusion, f32[32,1,128]{1,2,0:T(8,128)S(1)} %get-tuple-element.12, f32[32,1,128]{1,2,0:T(8,128)} %copy-done.1, f32[32,1,128]{1,2,0:T(8,128)} %copy-done), kind=kLoop, calls=%fused_computation.7 | loop fusion | flops 36864 | bytes 114688 | tf_op jit(solution)/shard_map/mul | solution.py:401
  167.1 2.2 %copy.138 = f32[3,4096]{1,0:T(4,128)S(1)} copy(f32[3,4096]{0,1:T(8,128)} %bitcast.76) | data formatting | bytes 98304 | tf_op jit(solution)/shard_map/reshape | solution.py:411
  169.3 3.9 %all-to-all-done.1 = f32[32,5,3,128]{3,2,1,0:T(4,128)S(1)} async-done(((f32[32,5,3,128]{3,2,1,0:T(4,128)}), f32[32,5,3,128]{3,2,1,0:T(4,128)S(1)}, u32[]{:S(2)}, u32[]{:S(2)}) %all-to-all-start.1) | async-done | bytes 245792 | tf_op jit(solution)/shard_map/all_to_all | solution.py:402
  174.9 11.9 %shard_map.151 = f32[384,256]{1,0:T(8,128)} custom-call(s32[1,20480]{1,0:T(1,128)} %bitcast.91, f32[3,20480]{1,0:T(4,128)} %pad_maximum_fusion.6.force_ref), custom_call_target="tpu_custom_call" | custom-call | tf_op jit(solution)/shard_map/pallas_call | solution.py:183
  188.3 2.3 %collective-permute-start.5 = (f32[3,8,1,256]{3,2,1,0:T(1,128)S(1)}, f32[3,8,1,256]{3,2,1,0:T(1,128)S(1)}, u32[]{:S(2)}, u32[]{:S(2)}) collective-permute-start(f32[3,8,1,256]{3,2,1,0:T(1,128)S(1)} %get-tuple-element.29), channel_id=1, source_target_pairs={{8,0},{16,8},{24,16},{9,1},{17,9},{25,17},{10,2},{18,10},{26,18},{... | collective-permute-start | bytes 73736 | tf_op jit(solution)/shard_map/ppermute | solution.py:211
  190.6 3.3 %collective-permute-start.4 = (f32[3,8,1,256]{3,2,1,0:T(1,128)S(1)}, f32[3,8,1,256]{3,2,1,0:T(1,128)S(1)}, u32[]{:S(2)}, u32[]{:S(2)}) collective-permute-start(f32[3,8,1,256]{3,2,1,0:T(1,128)S(1)} %get-tuple-element.28), channel_id=1, source_target_pairs={{0,8},{8,16},{16,24},{1,9},{9,17},{17,25},{2,10},{10,18},{18,26},{... | collective-permute-start | bytes 73736 | tf_op jit(solution)/shard_map/ppermute | solution.py:208
  195.0 3.2 %collective-permute-start.7 = (f32[3,8,18,1]{3,2,1,0:T(8,128)S(1)}, f32[3,8,18,1]{3,2,1,0:T(8,128)S(1)}, u32[]{:S(2)}, u32[]{:S(2)}) collective-permute-start(f32[3,8,18,1]{3,2,1,0:T(8,128)S(1)} %get-tuple-element.27), channel_id=1, source_target_pairs={{1,0},{2,1},{3,2},{4,3},{5,4},{6,5},{7,6},{9,8},{10,9},{11,10},{12... | collective-permute-start | bytes 5192 | tf_op jit(solution)/shard_map/ppermute | solution.py:211
  198.2 2.1 collective-permute-start.6
  200.3 11.2 %collective-permute-done.7 = f32[3,8,18,1]{3,2,1,0:T(8,128)S(1)} collective-permute-done((f32[3,8,18,1]{3,2,1,0:T(8,128)S(1)}, f32[3,8,18,1]{3,2,1,0:T(8,128)S(1)}, u32[]{:S(2)}, u32[]{:S(2)}) %collective-permute-start.7) | collective-permute-done | bytes 1760 | tf_op jit(solution)/shard_map/ppermute | solution.py:211
  (118 shorter events, 29.7 us)
Async XLA Ops:
  0.6 24.4 %copy-start.12 = (f32[128,3,128]{2,0,1:T(8,128)S(1)}, f32[128,3,128]{2,0,1:T(8,128)}, u32[]{:S(2)}) copy-start(f32[128,3,128]{2,0,1:T(8,128)} %param.18) | copy-start | bytes 589828
  0.6 26.0 %copy-start.14 = (f32[128,128]{1,0:T(8,128)S(1)}, f32[128,128]{1,0:T(8,128)}, u32[]{:S(2)}) copy-start(f32[128,128]{1,0:T(8,128)} %param.19) | copy-start | bytes 196612
  0.7 26.0 %copy-start.17 = (s32[128]{0:T(128)S(1)}, s32[128]{0:T(128)}, u32[]{:S(2)}) copy-start(s32[128]{0:T(128)} %param.20) | copy-start | bytes 1540
  27.0 8.5 %copy-start.4 = (f32[3,8,16,256]{3,2,1,0:T(8,128)S(1)}, f32[3,8,16,256]{3,2,1,0:T(8,128)}, u32[]{:S(2)}) copy-start(f32[3,8,16,256]{3,2,1,0:T(8,128)} %param.14) | copy-start | bytes 1179652
  27.0 8.5 %copy-start.7 = (f32[8,16,256]{2,1,0:T(8,128)S(1)}, f32[8,16,256]{2,1,0:T(8,128)}, u32[]{:S(2)}) copy-start(f32[8,16,256]{2,1,0:T(8,128)} %param.16) | copy-start | bytes 393220
  27.0 8.5 %copy-start.8 = (f32[8,16,256]{2,1,0:T(8,128)S(1)}, f32[8,16,256]{2,1,0:T(8,128)}, u32[]{:S(2)}) copy-start(f32[8,16,256]{2,1,0:T(8,128)} %param.15) | copy-start | bytes 393220
  27.9 14.0 %slice-start = ((f32[3,20480]{1,0:T(4,128)}), f32[3,4096]{1,0:T(4,128)S(1)}, s32[]{:S(2)}) async-start(f32[3,20480]{1,0:T(4,128)} %shard_map.149), calls=%async_computation.2 | async-start | bytes 131072 | tf_op jit(solution)/shard_map/slice | solution.py:344
  29.1 67.1 %all-to-all-start = ((f32[32,5,8,128]{3,2,1,0:T(8,128)}), f32[32,5,8,128]{3,2,1,0:T(8,128)S(1)}, u32[]{:S(2)}, u32[]{:S(2)}) async-start(f32[32,5,8,128]{3,2,1,0:T(8,128)} %select_select_fusion), calls=%async_computation | async-start | bytes 1310720 | tf_op jit(solution)/shard_map/all_to_all | solution.py:378
  36.3 20.0 %collective-permute-start.1 = (f32[6,8,1,256]{3,2,1,0:T(1,128)}, f32[6,8,1,256]{3,2,1,0:T(1,128)S(1)}, u32[]{:S(2)}, u32[]{:S(2)}) collective-permute-start(f32[6,8,1,256]{3,2,1,0:T(1,128)} %get-tuple-element.25), channel_id=1, source_target_pairs={{8,0},{16,8},{24,16},{9,1},{17,9},{25,17},{10,2},{18,10},{26,18},{... | collective-permute-start | bytes 147464 | tf_op jit(solution)/shard_map/ppermute | solution.py:211
  38.5 17.7 %collective-permute-start = (f32[6,8,1,256]{3,2,1,0:T(1,128)}, f32[6,8,1,256]{3,2,1,0:T(1,128)}, u32[]{:S(2)}, u32[]{:S(2)}) collective-permute-start(f32[6,8,1,256]{3,2,1,0:T(1,128)} %get-tuple-element.24), channel_id=1, source_target_pairs={{0,8},{8,16},{16,24},{1,9},{9,17},{17,25},{2,10},{10,18},{18,26},{... | collective-permute-start | bytes 147464 | tf_op jit(solution)/shard_map/ppermute | solution.py:208
  42.5 2.1 copy-start.2
  42.5 2.1 copy-start.15
  50.7 3.6 %copy-start.3 = (f32[3,4096]{0,1:T(8,128)S(1)}, f32[3,4096]{0,1:T(8,128)}, u32[]{:S(2)}) copy-start(f32[3,4096]{0,1:T(8,128)} %copy-done.2) | copy-start | bytes 147460
  54.3 1.8 copy-start
  54.3 1.9 copy-start.1
  54.3 1.9 copy-start.18
  54.3 1.9 copy-start.9
  60.5 26.7 %collective-permute-start.3 = (f32[6,8,18,1]{2,1,3,0:T(8,128)}, f32[6,8,18,1]{2,1,3,0:T(8,128)}, u32[]{:S(2)}, u32[]{:S(2)}) collective-permute-start(f32[6,8,18,1]{2,1,3,0:T(8,128)} %copy.120), channel_id=1, source_target_pairs={{1,0},{2,1},{3,2},{4,3},{5,4},{6,5},{7,6},{9,8},{10,9},{11,10},{12... | collective-permute-start | bytes 10376 | tf_op jit(solution)/shard_map/ppermute | solution.py:211
  65.6 23.5 %collective-permute-start.2 = (f32[6,8,18,1]{2,1,3,0:T(8,128)}, f32[6,8,18,1]{2,1,3,0:T(8,128)}, u32[]{:S(2)}, u32[]{:S(2)}) collective-permute-start(f32[6,8,18,1]{2,1,3,0:T(8,128)} %copy.119), channel_id=1, source_target_pairs={{0,1},{1,2},{2,3},{3,4},{4,5},{5,6},{6,7},{8,9},{9,10},{10,11},{11... | collective-permute-start | bytes 10376 | tf_op jit(solution)/shard_map/ppermute | solution.py:208
  71.7 4.9 %copy-start.16 = (f32[32,128]{1,0:T(8,128)S(1)}, f32[32,128]{1,0:T(8,128)}, u32[]{:S(2)}) copy-start(f32[32,128]{1,0:T(8,128)} %param.26) | copy-start | bytes 49156
  96.2 6.5 %copy-start.6 = (f32[32,5,8,128]{3,2,1,0:T(8,128)}, f32[32,5,8,128]{3,2,1,0:T(8,128)S(1)}, u32[]{:S(2)}) copy-start(f32[32,5,8,128]{3,2,1,0:T(8,128)S(1)} %all-to-all-done) | copy-start | bytes 1966084
  140.5 32.7 %all-to-all-start.1 = ((f32[32,5,3,128]{3,2,1,0:T(4,128)}), f32[32,5,3,128]{3,2,1,0:T(4,128)S(1)}, u32[]{:S(2)}, u32[]{:S(2)}) async-start(f32[32,5,3,128]{3,2,1,0:T(4,128)} %bitcast.92), calls=%async_computation.1 | async-start | bytes 655360 | tf_op jit(solution)/shard_map/all_to_all | solution.py:402
  169.3 18.8 %copy-start.10 = (f32[1,8,16,256]{3,2,1,0:T(8,128)S(1)}, f32[1,8,16,256]{3,2,1,0:T(8,128)}, u32[]{:S(2)}) copy-start(f32[1,8,16,256]{3,2,1,0:T(8,128)} %fusion.50) | copy-start | bytes 393220
  169.3 18.8 %copy-start.11 = (f32[1,8,16,256]{3,2,1,0:T(8,128)S(1)}, f32[1,8,16,256]{3,2,1,0:T(8,128)}, u32[]{:S(2)}) copy-start(f32[1,8,16,256]{3,2,1,0:T(8,128)} %fusion.52) | copy-start | bytes 393220
  169.3 18.8 %copy-start.13 = (f32[8,16,256]{2,1,0:T(8,128)S(1)}, f32[8,16,256]{2,1,0:T(8,128)}, u32[]{:S(2)}) copy-start(f32[8,16,256]{2,1,0:T(8,128)} %param.17) | copy-start | bytes 393220
  188.2 23.8 %copy-start.5 = (f32[3,8,16,256]{3,2,1,0:T(8,128)}, f32[3,8,16,256]{3,2,1,0:T(8,128)S(1)}, u32[]{:S(2)}) copy-start(f32[3,8,16,256]{3,2,1,0:T(8,128)S(1)} %fusion.2) | copy-start | bytes 1179652
  188.3 5.6 %collective-permute-start.5 = (f32[3,8,1,256]{3,2,1,0:T(1,128)S(1)}, f32[3,8,1,256]{3,2,1,0:T(1,128)S(1)}, u32[]{:S(2)}, u32[]{:S(2)}) collective-permute-start(f32[3,8,1,256]{3,2,1,0:T(1,128)S(1)} %get-tuple-element.29), channel_id=1, source_target_pairs={{8,0},{16,8},{24,16},{9,1},{17,9},{25,17},{10,2},{18,10},{26,18},{... | collective-permute-start | bytes 73736 | tf_op jit(solution)/shard_map/ppermute | solution.py:211
  190.6 4.2 %collective-permute-start.4 = (f32[3,8,1,256]{3,2,1,0:T(1,128)S(1)}, f32[3,8,1,256]{3,2,1,0:T(1,128)S(1)}, u32[]{:S(2)}, u32[]{:S(2)}) collective-permute-start(f32[3,8,1,256]{3,2,1,0:T(1,128)S(1)} %get-tuple-element.28), channel_id=1, source_target_pairs={{0,8},{8,16},{16,24},{1,9},{9,17},{17,25},{2,10},{10,18},{18,26},{... | collective-permute-start | bytes 73736 | tf_op jit(solution)/shard_map/ppermute | solution.py:208
  195.0 16.5 %collective-permute-start.7 = (f32[3,8,18,1]{3,2,1,0:T(8,128)S(1)}, f32[3,8,18,1]{3,2,1,0:T(8,128)S(1)}, u32[]{:S(2)}, u32[]{:S(2)}) collective-permute-start(f32[3,8,18,1]{3,2,1,0:T(8,128)S(1)} %get-tuple-element.27), channel_id=1, source_target_pairs={{1,0},{2,1},{3,2},{4,3},{5,4},{6,5},{7,6},{9,8},{10,9},{11,10},{12... | collective-permute-start | bytes 5192 | tf_op jit(solution)/shard_map/ppermute | solution.py:211
  198.2 13.3 %collective-permute-start.6 = (f32[3,8,18,1]{3,2,1,0:T(8,128)S(1)}, f32[3,8,18,1]{3,2,1,0:T(8,128)S(1)}, u32[]{:S(2)}, u32[]{:S(2)}) collective-permute-start(f32[3,8,18,1]{3,2,1,0:T(8,128)S(1)} %get-tuple-element.26), channel_id=1, source_target_pairs={{0,1},{1,2},{2,3},{3,4},{4,5},{5,6},{6,7},{8,9},{9,10},{10,11},{11... | collective-permute-start | bytes 5192 | tf_op jit(solution)/shard_map/ppermute | solution.py:208

commit v5 on v3

--- a/solution.py
+++ b/solution.py
@@ -114,10 +114,12 @@
         forward = [(i, i + 1) for i in range(count - 1)]
         backward = [(target, source) for source, target in forward]
         low = lax.ppermute(
-            lax.slice_in_dim(block, block.shape[dim] - width, None, axis=dim), axis, forward
+            lax.index_in_dim(block, block.shape[dim] - 1, axis=dim, keepdims=False), axis, forward
         )
-        high = lax.ppermute(lax.slice_in_dim(block, 0, width, axis=dim), axis, backward)
-        block = jnp.concatenate([low, block, high], axis=dim)
+        high = lax.ppermute(lax.index_in_dim(block, 0, axis=dim, keepdims=False), axis, backward)
+        block = jnp.concatenate(
+            [jnp.expand_dims(low, dim), block, jnp.expand_dims(high, dim)], axis=dim
+        )
     return block
 
 
@@ -247,9 +249,16 @@
     vel_flat = velocity.reshape(3, node_total)
     slave_count = block_total * seg_width
     all_nodes = jnp.concatenate([slave_node.reshape(-1), master_node.reshape(-1)])
-    picked_vel = node_gather(vel_flat, all_nodes)
-    slave_vel = picked_vel[:, :slave_count].reshape(3, block_total, seg_width).transpose(1, 0, 2)
-    master_vel = picked_vel[:, slave_count:].reshape(3, master_total, seg_width).transpose(1, 0, 2)
+    slave_vel = (
+        node_gather(vel_flat, slave_node.reshape(-1))
+        .reshape(3, block_total, seg_width)
+        .transpose(1, 0, 2)
+    )
+    master_vel = (
+        node_gather(vel_flat, master_node.reshape(-1))
+        .reshape(3, master_total, seg_width)
+        .transpose(1, 0, 2)
+    )
     live_mask = jnp.arange(seg_width, dtype=jnp.int32)[None, :] < seg_count[:, None]
     area_live = jnp.where(live_mask, slave_area, jnp.zeros_like(slave_area))
     slave = jnp.concatenate(

time: 163 us -> 150 us (0.920)
  waiting for transfers between devices: 26.6 us -> 13.2 us
  other arithmetic: 54.3 us -> 48.8 us
  local copies, waits for them, and re-layouts: 13 us -> 16.8 us
  Pallas kernels: 29.3 us -> 31.1 us
    ppermute x8, waiting for transfers between devices: 16.3 us -> 3.31 us  [the longest x4 3.3 us: padded_2(): lax.ppermute(lax.index_in_dim(block, 0, axis=dim, keepdims=False), axis,...]
    unnamed x51 -> x39, local copies, waits for them, and re-layouts: 0.35 us -> 3.91 us
    broadcast_in_dim x0 -> x5, local copies, waits for them, and re-layouts: none -> 2.45 us  [the longest x1 1.13 us: on_device(): prestress[None]]
    transpose x2 -> x0, local copies, waits for them, and re-layouts: 1.85 us -> none  [the longest x1 0.99 us: on_device(): picked_vel[:, :slave_count].reshape(3, block_total, seg_width)]
    pallas_call x1 -> x2, Pallas kernels: 17.5 us -> 19.1 us  [node_gather(): pl.pallas_call(gather_kernel, grid=(padded_count // TILE,), in_specs=[pl....]
  transfers between devices with their start and end apart: 10 -> 10, of which waited for: 6 -> 3; matrix products, arithmetic and copies ran while one was open for 12% -> 11% of each run, Pallas kernels for 11% -> 13%
where the time goes in v5:
time: 150 us; the launch traced here: 148 us
  other arithmetic  48.8 us (33%)
  starting transfers between devices  35.8 us (24%)
  Pallas kernels  31.1 us (21%)
  local copies, waits for them, and re-layouts  16.8 us (11%)
  waiting for transfers between devices  13.2 us (9%)
    reduce_sum x2, other arithmetic, contact_pairs(): reaction = jnp.sum(push_force, axis=1)  35.8 us
    pallas_call x2, Pallas kernels, node_gather(): pl.pallas_call(gather_kernel, grid=(padded_count // TILE,), in_specs=[pl....  19.1 us
    pallas_call x1, Pallas kernels, node_scatter_add(): pl.pallas_call(scatter_kernel, grid=(padded_count // TILE,), in_specs=[pl...  11.9 us
    ppermute x4, starting transfers between devices, padded_2(): lax.ppermute(lax.index_in_dim(block, block.shape[dim] - 1, axis=dim, keep...  11.5 us
    ppermute x4, starting transfers between devices, padded_2(): lax.ppermute(lax.index_in_dim(block, 0, axis=dim, keepdims=False), axis,...  10.9 us
    all_to_all x1, waiting for transfers between devices, on_device(): lax.all_to_all(forces.reshape(devices, slot_depth, 3, seg_width), ('gx',...  9.87 us
    all_to_all x1, starting transfers between devices, on_device(): lax.all_to_all(forces.reshape(devices, slot_depth, 3, seg_width), ('gx',...  7.04 us
    all_to_all x1, starting transfers between devices, on_device(): lax.all_to_all(outgoing.reshape(devices, slot_depth, 8, seg_width), ('gx'...  6.29 us
  transfers between devices with their start and end apart: 10, of which 3 were waited for; matrix products, arithmetic and copies ran while one was open for 11% of the time, Pallas kernels for 13%

profile of v5, /device:TPU:9, one launch (start us, length us, event | category | flops | bytes accessed | tf_op | source)
XLA Modules:
  0.0 148.3 jit_solution(13280306857277958289)
XLA Ops:
  0.6 1.3 copy.254
  1.9 1.1 copy_bitcast_fusion
  3.1 3.8 %collective-permute-start = (f32[6,8,256]{2,1,0:T(8,128)S(1)}, f32[6,8,256]{2,1,0:T(8,128)S(1)}, u32[]{:S(2)}, u32[]{:S(2)}) collective-permute-start(f32[6,8,256]{2,1,0:T(8,128)S(1)} %get-tuple-element.108), channel_id=1, source_target_pairs={{0,8},{8,16},{16,24},{1,9},{9,17},{17,25},{2,10},{10,18},{18,26},{... | collective-permute-start | bytes 147464 | tf_op jit(solution)/shard_map/ppermute | solution.py:116
  7.0 1.9 %collective-permute-start.1 = (f32[6,8,256]{2,1,0:T(8,128)S(1)}, f32[6,8,256]{2,1,0:T(8,128)S(1)}, u32[]{:S(2)}, u32[]{:S(2)}) collective-permute-start(f32[6,8,256]{2,1,0:T(8,128)S(1)} %get-tuple-element.109), channel_id=1, source_target_pairs={{8,0},{16,8},{24,16},{9,1},{17,9},{25,17},{10,2},{18,10},{26,18},{... | collective-permute-start | bytes 147464 | tf_op jit(solution)/shard_map/ppermute | solution.py:119
  9.4 0.9 copy.269
  10.6 14.3 %shard_map.149 = f32[3,16384]{1,0:T(4,128)} custom-call(s32[1,16384]{1,0:T(1,128)} %bitcast.256, f32[384,256]{1,0:T(8,128)} %bitcast.240), custom_call_target="tpu_custom_call" | custom-call | tf_op jit(solution)/shard_map/pallas_call | solution.py:73
  24.9 1.1 copy_add_fusion
  26.4 1.2 pad_maximum_fusion.3
  27.6 0.8 gather_fusion
  28.4 1.2 select_select_fusion
  29.6 6.3 %all-to-all-start = ((f32[32,5,8,128]{3,2,1,0:T(8,128)}), f32[32,5,8,128]{3,2,1,0:T(8,128)S(1)}, u32[]{:S(2)}, u32[]{:S(2)}) async-start(f32[32,5,8,128]{3,2,1,0:T(8,128)} %select_select_fusion), calls=%async_computation | async-start | bytes 1310720 | tf_op jit(solution)/shard_map/all_to_all | solution.py:288
  36.0 4.8 %shard_map.150 = f32[3,4096]{1,0:T(4,128)} custom-call(s32[1,4096]{1,0:T(1,128)} %bitcast.271, f32[384,256]{1,0:T(8,128)} %bitcast.241), custom_call_target="tpu_custom_call" | custom-call | tf_op jit(solution)/shard_map/pallas_call | solution.py:73
  40.8 0.9 copy_add_fusion.1
  43.1 3.1 %collective-permute-start.2 = (f32[6,8,18]{2,1,0:T(8,128)S(1)}, f32[6,8,18]{2,1,0:T(8,128)S(1)}, u32[]{:S(2)}, u32[]{:S(2)}) collective-permute-start(f32[6,8,18]{2,1,0:T(8,128)S(1)} %bitcast.273), channel_id=1, source_target_pairs={{0,1},{1,2},{2,3},{3,4},{4,5},{5,6},{6,7},{8,9},{9,10},{10,11},{11... | collective-permute-start | bytes 10376 | tf_op jit(solution)/shard_map/ppermute | solution.py:116
  46.6 3.1 %collective-permute-start.3 = (f32[6,8,18]{2,1,0:T(8,128)S(1)}, f32[6,8,18]{2,1,0:T(8,128)S(1)}, u32[]{:S(2)}, u32[]{:S(2)}) collective-permute-start(f32[6,8,18]{2,1,0:T(8,128)S(1)} %bitcast.275), channel_id=1, source_target_pairs={{1,0},{2,1},{3,2},{4,3},{5,4},{6,5},{7,6},{9,8},{10,9},{11,10},{12... | collective-permute-start | bytes 10376 | tf_op jit(solution)/shard_map/ppermute | solution.py:119
  55.4 0.8 gather_fusion.1
  56.6 38.6 %while.12 = (s32[]{:T(128)}, f32[2,80,3,128]{3,1,2,0:T(8,128)}, f32[2,80,128]{2,1,0:T(8,128)}, f32[2,80,7,128]{3,1,0,2:T(8,128)S(1)}, f32[2,80,10,128]{3,1,2,0:T(8,128)S(1)}, /*index=5*/s32[]{:T(128)}) while((s32[]{:T(128)}, f32[2,80,3,128]{3,1,2,0:T(8,128)}, f32[2,80,128]{2,1,0:T(8,128)}, f32[2,80,7,128]{3,1,0,2:T(8,128)S(1)}, ...), condition=%wide.region_8.9_spmd, body=%wide.region_3.8_spmd.sunk | while | flops 59002880 | bytes 3974221 | solution.py:305
  56.7 17.9 %fusion.86 = (f32[80,128]{1,0:T(8,128)S(1)}, f32[80,128]{1,0:T(8,128)S(1)}, f32[80,128]{1,0:T(8,128)S(1)}, f32[80,128]{1,0:T(8,128)S(1)}) fusion(f32[80,128]{1,0:T(8,128)S(1)} %get-tuple-element.175, f32[80,128]{1,0:T(8,128)S(1)} %get-tuple-element.176, f32[80,128]{1,0:T(8,128)S(1)} %get-tuple-element.177, f32[80,128]{1,0:T(8,128)S(1)} %get-tuple-element.178, ...), kind=kLoop, calls=%fused_computation.47.clone.1 | loop fusion | flops 58941440 | bytes 860160 | tf_op jit(solution)/shard_map/while/body/eval_jaxpr/reduce_sum | solution.py:209
  76.0 17.9 %fusion.86 = (f32[80,128]{1,0:T(8,128)S(1)}, f32[80,128]{1,0:T(8,128)S(1)}, f32[80,128]{1,0:T(8,128)S(1)}, f32[80,128]{1,0:T(8,128)S(1)}) fusion(f32[80,128]{1,0:T(8,128)S(1)} %get-tuple-element.175, f32[80,128]{1,0:T(8,128)S(1)} %get-tuple-element.176, f32[80,128]{1,0:T(8,128)S(1)} %get-tuple-element.177, f32[80,128]{1,0:T(8,128)S(1)} %get-tuple-element.178, ...), kind=kLoop, calls=%fused_computation.47.clone.1 | loop fusion | flops 58941440 | bytes 860160 | tf_op jit(solution)/shard_map/while/body/eval_jaxpr/reduce_sum | solution.py:209
  95.2 1.8 %copy.297 = f32[2,80,3,128]{3,2,1,0:T(4,128)} copy(f32[2,80,3,128]{3,1,2,0:T(8,128)} %get-tuple-element.30) | data formatting | bytes 491520 | tf_op jit(solution)/shard_map/reshape;reshape | solution.py:320
  97.0 7.0 %all-to-all-start.1 = ((f32[32,5,3,128]{3,2,1,0:T(4,128)}), f32[32,5,3,128]{3,2,1,0:T(4,128)S(1)}, u32[]{:S(2)}, u32[]{:S(2)}) async-start(f32[32,5,3,128]{3,2,1,0:T(4,128)} %bitcast.71), calls=%async_computation.1 | async-start | bytes 655360 | tf_op jit(solution)/shard_map/all_to_all | solution.py:319
  104.1 1.2 convolution_negate_fusion
  105.3 9.9 %all-to-all-done.1 = f32[32,5,3,128]{3,2,1,0:T(4,128)S(1)} async-done(((f32[32,5,3,128]{3,2,1,0:T(4,128)}), f32[32,5,3,128]{3,2,1,0:T(4,128)S(1)}, u32[]{:S(2)}, u32[]{:S(2)}) %all-to-all-start.1) | async-done | bytes 245792 | tf_op jit(solution)/shard_map/all_to_all | solution.py:319
  116.1 0.8 pad_maximum_fusion.5.force_ref
  116.9 11.9 %shard_map.151 = f32[384,256]{1,0:T(8,128)} custom-call(s32[1,20480]{1,0:T(1,128)} %bitcast.253, f32[3,20480]{1,0:T(4,128)} %pad_maximum_fusion.5.force_ref), custom_call_target="tpu_custom_call" | custom-call | tf_op jit(solution)/shard_map/pallas_call | solution.py:91
  128.9 1.1 copy.285
  130.7 2.5 %collective-permute-start.4 = (f32[3,8,256]{2,1,0:T(8,128)S(1)}, f32[3,8,256]{2,1,0:T(8,128)S(1)}, u32[]{:S(2)}, u32[]{:S(2)}) collective-permute-start(f32[3,8,256]{2,1,0:T(8,128)S(1)} %get-tuple-element.114), channel_id=1, source_target_pairs={{0,8},{8,16},{16,24},{1,9},{9,17},{17,25},{2,10},{10,18},{18,26},{... | collective-permute-start | bytes 73736 | tf_op jit(solution)/shard_map/ppermute | solution.py:116
  133.2 1.9 %collective-permute-start.5 = (f32[3,8,256]{2,1,0:T(8,128)S(1)}, f32[3,8,256]{2,1,0:T(8,128)S(1)}, u32[]{:S(2)}, u32[]{:S(2)}) collective-permute-start(f32[3,8,256]{2,1,0:T(8,128)S(1)} %get-tuple-element.115), channel_id=1, source_target_pairs={{8,0},{16,8},{24,16},{9,1},{17,9},{25,17},{10,2},{18,10},{26,18},{... | collective-permute-start | bytes 73736 | tf_op jit(solution)/shard_map/ppermute | solution.py:119
  135.1 3.2 %collective-permute-done.5 = f32[3,8,256]{2,1,0:T(8,128)S(1)} collective-permute-done((f32[3,8,256]{2,1,0:T(8,128)S(1)}, f32[3,8,256]{2,1,0:T(8,128)S(1)}, u32[]{:S(2)}, u32[]{:S(2)}) %collective-permute-start.5) | collective-permute-done | bytes 24608 | tf_op jit(solution)/shard_map/ppermute | solution.py:119
  138.7 2.2 %collective-permute-start.6 = (f32[3,8,18]{2,1,0:T(8,128)S(1)}, f32[3,8,18]{2,1,0:T(8,128)S(1)}, u32[]{:S(2)}, u32[]{:S(2)}) collective-permute-start(f32[3,8,18]{2,1,0:T(8,128)S(1)} %bitcast.278), channel_id=1, source_target_pairs={{0,1},{1,2},{2,3},{3,4},{4,5},{5,6},{6,7},{8,9},{9,10},{10,11},{11... | collective-permute-start | bytes 5192 | tf_op jit(solution)/shard_map/ppermute | solution.py:116
  141.1 4.0 %collective-permute-start.7 = (f32[3,8,18]{2,1,0:T(8,128)S(1)}, f32[3,8,18]{2,1,0:T(8,128)S(1)}, u32[]{:S(2)}, u32[]{:S(2)}) collective-permute-start(f32[3,8,18]{2,1,0:T(8,128)S(1)} %bitcast.280), channel_id=1, source_target_pairs={{1,0},{2,1},{3,2},{4,3},{5,4},{6,5},{7,6},{9,8},{10,9},{11,10},{12... | collective-permute-start | bytes 5192 | tf_op jit(solution)/shard_map/ppermute | solution.py:119
  145.2 0.9 copy.295
  (134 shorter events, 15.9 us)
Async XLA Ops:
  0.6 8.3 %copy-start = (f32[3,8,16,256]{3,2,1,0:T(8,128)S(1)}, f32[3,8,16,256]{3,2,1,0:T(8,128)}, u32[]{:S(2)}) copy-start(f32[3,8,16,256]{3,2,1,0:T(8,128)} %param.16) | copy-start | bytes 1179652
  1.9 7.0 %copy-start.14 = (s32[128,1]{0,1:T(1,128)S(1)}, s32[128,1]{0,1:T(1,128)}, u32[]{:S(2)}) copy-start(s32[128,1]{0,1:T(1,128)} %param.24) | copy-start | bytes 1540
  3.1 7.2 %copy-start.15 = (s32[128]{0:T(128)S(1)}, s32[128]{0:T(128)}, u32[]{:S(2)}) copy-start(s32[128]{0:T(128)} %param.25) | copy-start | bytes 1540
  3.1 21.8 %copy-start.6 = (f32[128,3,128]{2,0,1:T(8,128)S(1)}, f32[128,3,128]{2,0,1:T(8,128)}, u32[]{:S(2)}) copy-start(f32[128,3,128]{2,0,1:T(8,128)} %param.20) | copy-start | bytes 589828
  3.1 39.2 %collective-permute-start = (f32[6,8,256]{2,1,0:T(8,128)S(1)}, f32[6,8,256]{2,1,0:T(8,128)S(1)}, u32[]{:S(2)}, u32[]{:S(2)}) collective-permute-start(f32[6,8,256]{2,1,0:T(8,128)S(1)} %get-tuple-element.108), channel_id=1, source_target_pairs={{0,8},{8,16},{16,24},{1,9},{9,17},{17,25},{2,10},{10,18},{18,26},{... | collective-permute-start | bytes 147464 | tf_op jit(solution)/shard_map/ppermute | solution.py:116
  7.0 35.4 %collective-permute-start.1 = (f32[6,8,256]{2,1,0:T(8,128)S(1)}, f32[6,8,256]{2,1,0:T(8,128)S(1)}, u32[]{:S(2)}, u32[]{:S(2)}) collective-permute-start(f32[6,8,256]{2,1,0:T(8,128)S(1)} %get-tuple-element.109), channel_id=1, source_target_pairs={{8,0},{16,8},{24,16},{9,1},{17,9},{25,17},{10,2},{18,10},{26,18},{... | collective-permute-start | bytes 147464 | tf_op jit(solution)/shard_map/ppermute | solution.py:119
  8.9 17.1 %copy-start.8 = (f32[128,128]{1,0:T(8,128)S(1)}, f32[128,128]{1,0:T(8,128)}, u32[]{:S(2)}) copy-start(f32[128,128]{1,0:T(8,128)} %param.21) | copy-start | bytes 196612
  8.9 17.1 %copy-start.13 = (s32[128]{0:T(128)S(1)}, s32[128]{0:T(128)}, u32[]{:S(2)}) copy-start(s32[128]{0:T(128)} %param.22) | copy-start | bytes 1540
  28.4 7.6 %copy-start.11 = (f32[32,2,128]{2,1,0:T(2,128)S(1)}, f32[32,2,128]{2,1,0:T(2,128)}, u32[]{:S(2)}) copy-start(f32[32,2,128]{2,1,0:T(2,128)} %param.27) | copy-start | bytes 98308
  28.4 12.4 %copy-start.10 = (f32[32,3,128]{2,0,1:T(8,128)S(1)}, f32[32,3,128]{2,0,1:T(8,128)}, u32[]{:S(2)}) copy-start(f32[32,3,128]{2,0,1:T(8,128)} %param.26) | copy-start | bytes 147460
  29.6 12.1 %copy-start.5 = (s32[128,128]{1,0:T(8,128)S(1)}, s32[128,128]{1,0:T(8,128)}, u32[]{:S(2)}) copy-start(s32[128,128]{1,0:T(8,128)} %param.23) | copy-start | bytes 196612
  29.6 12.1 %copy-start.9 = (s32[32,128]{1,0:T(8,128)S(1)}, s32[32,128]{1,0:T(8,128)}, u32[]{:S(2)}) copy-start(s32[32,128]{1,0:T(8,128)} %param.29) | copy-start | bytes 49156
  29.6 25.3 %all-to-all-start = ((f32[32,5,8,128]{3,2,1,0:T(8,128)}), f32[32,5,8,128]{3,2,1,0:T(8,128)S(1)}, u32[]{:S(2)}, u32[]{:S(2)}) async-start(f32[32,5,8,128]{3,2,1,0:T(8,128)} %select_select_fusion), calls=%async_computation | async-start | bytes 1310720 | tf_op jit(solution)/shard_map/all_to_all | solution.py:288
  42.5 7.2 %copy-start.7 = (f32[8,16,256]{2,1,0:T(8,128)S(1)}, f32[8,16,256]{2,1,0:T(8,128)}, u32[]{:S(2)}) copy-start(f32[8,16,256]{2,1,0:T(8,128)} %param.19) | copy-start | bytes 393220
  42.5 8.0 %copy-start.1 = (f32[3,4096]{1,0:T(4,128)S(1)}, f32[3,4096]{1,0:T(4,128)}, u32[]{:S(2)}) copy-start(f32[3,4096]{1,0:T(4,128)} %shard_map.150) | copy-start | bytes 147460
  42.5 7.9 %copy-start.12 = (f32[32,128]{1,0:T(8,128)S(1)}, f32[32,128]{1,0:T(8,128)}, u32[]{:S(2)}) copy-start(f32[32,128]{1,0:T(8,128)} %param.28) | copy-start | bytes 49156
  43.1 7.7 %collective-permute-start.2 = (f32[6,8,18]{2,1,0:T(8,128)S(1)}, f32[6,8,18]{2,1,0:T(8,128)S(1)}, u32[]{:S(2)}, u32[]{:S(2)}) collective-permute-start(f32[6,8,18]{2,1,0:T(8,128)S(1)} %bitcast.273), channel_id=1, source_target_pairs={{0,1},{1,2},{2,3},{3,4},{4,5},{5,6},{6,7},{8,9},{9,10},{10,11},{11... | collective-permute-start | bytes 10376 | tf_op jit(solution)/shard_map/ppermute | solution.py:116
  46.6 4.8 %collective-permute-start.3 = (f32[6,8,18]{2,1,0:T(8,128)S(1)}, f32[6,8,18]{2,1,0:T(8,128)S(1)}, u32[]{:S(2)}, u32[]{:S(2)}) collective-permute-start(f32[6,8,18]{2,1,0:T(8,128)S(1)} %bitcast.275), channel_id=1, source_target_pairs={{1,0},{2,1},{3,2},{4,3},{5,4},{6,5},{7,6},{9,8},{10,9},{11,10},{12... | collective-permute-start | bytes 10376 | tf_op jit(solution)/shard_map/ppermute | solution.py:119
  97.0 18.2 %all-to-all-start.1 = ((f32[32,5,3,128]{3,2,1,0:T(4,128)}), f32[32,5,3,128]{3,2,1,0:T(4,128)S(1)}, u32[]{:S(2)}, u32[]{:S(2)}) async-start(f32[32,5,3,128]{3,2,1,0:T(4,128)} %bitcast.71), calls=%async_computation.1 | async-start | bytes 655360 | tf_op jit(solution)/shard_map/all_to_all | solution.py:319
  116.9 13.2 %copy-start.2 = (f32[1,8,16,256]{3,1,2,0:T(8,128)S(1)}, f32[1,8,16,256]{3,1,2,0:T(8,128)}, u32[]{:S(2)}) copy-start(f32[1,8,16,256]{3,1,2,0:T(8,128)} %fusion.67) | copy-start | bytes 393220
  116.9 13.2 %copy-start.3 = (f32[1,8,16,256]{3,1,2,0:T(8,128)S(1)}, f32[1,8,16,256]{3,1,2,0:T(8,128)}, u32[]{:S(2)}) copy-start(f32[1,8,16,256]{3,1,2,0:T(8,128)} %fusion.69) | copy-start | bytes 393220
  116.9 13.2 %copy-start.4 = (f32[8,16,256]{2,0,1:T(8,128)S(1)}, f32[8,16,256]{2,0,1:T(8,128)}, u32[]{:S(2)}) copy-start(f32[8,16,256]{2,0,1:T(8,128)} %copy.287) | copy-start | bytes 393220
  130.7 4.4 %collective-permute-start.4 = (f32[3,8,256]{2,1,0:T(8,128)S(1)}, f32[3,8,256]{2,1,0:T(8,128)S(1)}, u32[]{:S(2)}, u32[]{:S(2)}) collective-permute-start(f32[3,8,256]{2,1,0:T(8,128)S(1)} %get-tuple-element.114), channel_id=1, source_target_pairs={{0,8},{8,16},{16,24},{1,9},{9,17},{17,25},{2,10},{10,18},{18,26},{... | collective-permute-start | bytes 73736 | tf_op jit(solution)/shard_map/ppermute | solution.py:116
  133.2 5.1 %collective-permute-start.5 = (f32[3,8,256]{2,1,0:T(8,128)S(1)}, f32[3,8,256]{2,1,0:T(8,128)S(1)}, u32[]{:S(2)}, u32[]{:S(2)}) collective-permute-start(f32[3,8,256]{2,1,0:T(8,128)S(1)} %get-tuple-element.115), channel_id=1, source_target_pairs={{8,0},{16,8},{24,16},{9,1},{17,9},{25,17},{10,2},{18,10},{26,18},{... | collective-permute-start | bytes 73736 | tf_op jit(solution)/shard_map/ppermute | solution.py:119
  138.7 7.3 %collective-permute-start.6 = (f32[3,8,18]{2,1,0:T(8,128)S(1)}, f32[3,8,18]{2,1,0:T(8,128)S(1)}, u32[]{:S(2)}, u32[]{:S(2)}) collective-permute-start(f32[3,8,18]{2,1,0:T(8,128)S(1)} %bitcast.278), channel_id=1, source_target_pairs={{0,1},{1,2},{2,3},{3,4},{4,5},{5,6},{6,7},{8,9},{9,10},{10,11},{11... | collective-permute-start | bytes 5192 | tf_op jit(solution)/shard_map/ppermute | solution.py:116
  141.1 5.2 %collective-permute-start.7 = (f32[3,8,18]{2,1,0:T(8,128)S(1)}, f32[3,8,18]{2,1,0:T(8,128)S(1)}, u32[]{:S(2)}, u32[]{:S(2)}) collective-permute-start(f32[3,8,18]{2,1,0:T(8,128)S(1)} %bitcast.280), channel_id=1, source_target_pairs={{1,0},{2,1},{3,2},{4,3},{5,4},{6,5},{7,6},{9,8},{10,9},{11,10},{12... | collective-permute-start | bytes 5192 | tf_op jit(solution)/shard_map/ppermute | solution.py:119

commit v6 on v5

--- a/solution.py
+++ b/solution.py
@@ -185,15 +185,15 @@
     dist_sq = delta_x * delta_x + delta_y * delta_y + delta_z * delta_z
     gap_normal = normal_x * delta_x + normal_y * delta_y + normal_z * delta_z
     closing = (
-        normal_x * (slave[:, 3, :, None] - master[:, 6, None, :])
-        + normal_y * (slave[:, 4, :, None] - master[:, 7, None, :])
-        + normal_z * (slave[:, 5, :, None] - master[:, 8, None, :])
-    )
+        normal_x * slave[:, 3, :, None]
+        + normal_y * slave[:, 4, :, None]
+        + normal_z * slave[:, 5, :, None]
+    ) - master[:, 6, None, :]
     weight = jnp.exp(-dist_sq / REACH_SQ)
     depth_soft = SOFT_GAP * jax.nn.softplus(-gap_normal / SOFT_GAP)
     push_force = (
         slave[:, 6, :, None]
-        * master[:, 9, None, :]
+        * master[:, 7, None, :]
         * weight
         * depth_soft
         * (1.0 + DAMPING * jnp.tanh(-closing))
@@ -248,7 +248,6 @@
     stress, inside = stress_forces(padded)
     vel_flat = velocity.reshape(3, node_total)
     slave_count = block_total * seg_width
-    all_nodes = jnp.concatenate([slave_node.reshape(-1), master_node.reshape(-1)])
     slave_vel = (
         node_gather(vel_flat, slave_node.reshape(-1))
         .reshape(3, block_total, seg_width)
@@ -265,39 +264,19 @@
         [slave_pos + TIME_STEP * slave_vel, slave_vel, area_live[:, None, :]], axis=1
     )
     normals = master_normals(master_tilt)
-    master_data = jnp.concatenate(
-        [master_cent + TIME_STEP * master_vel, normals, master_vel, master_stiff[:, None, :]],
-        axis=1,
-    )
-    owners = pair_owner[:, 0]
-    positions = jnp.arange(block_total, dtype=jnp.int32)
-    earlier = (owners[:, None] == owners[None, :]) & (positions[None, :] < positions[:, None])
-    slot_index = jnp.sum(earlier.astype(jnp.int32), axis=1)
-    target_slot = owners * slot_depth + slot_index
-    slot_hit = target_slot[None, :] == jnp.arange(devices * slot_depth, dtype=jnp.int32)[:, None]
-    source = jnp.sum(jnp.where(slot_hit, positions[None, :], 0), axis=1)
-    filled = jnp.any(slot_hit, axis=1)
-    tagged = jnp.concatenate(
+    master_rows = jnp.concatenate(
         [
-            slave,
-            jnp.broadcast_to(pair_master.astype(jnp.float32)[:, None, None], (block_total, 1, seg_width)),
+            master_cent + TIME_STEP * master_vel,
+            normals,
+            jnp.sum(normals * master_vel, axis=1, keepdims=True),
+            master_stiff[:, None, :],
         ],
         axis=1,
     )
-    outgoing = jnp.where(filled[:, None, None], jnp.take(tagged, source, axis=0), 0.0)
-    arrived = lax.all_to_all(
-        outgoing.reshape(devices, slot_depth, 8, seg_width),
-        ("gx", "gy"),
-        split_axis=0,
-        concat_axis=0,
-        tiled=True,
-    )
-    item_total = devices * slot_depth
-    arrived = arrived.reshape(item_total, 8, seg_width)
-    picked = arrived[:, 7, 0].astype(jnp.int32)
-    arrived = arrived[:, :7]
-    paired = jnp.take(master_data, picked, axis=0)
-    group_size = 16 * slot_depth
+    all_master = lax.all_gather(master_rows, ("gx", "gy"), axis=0, tiled=True)
+    target = pair_owner[:, 0] * master_total + pair_master
+    paired = jnp.take(all_master, target, axis=0)
+    group_size = block_total // 2 if block_total % 2 == 0 else block_total
 
     def per_group(pairing):
         return contact_pairs(pairing[0], pairing[1])
@@ -305,30 +284,23 @@
     forces, reaction = lax.map(
         per_group,
         (
-            arrived.reshape(item_total // group_size, group_size, 7, seg_width),
-            paired.reshape(item_total // group_size, group_size, 10, seg_width),
+            slave.reshape(block_total // group_size, group_size, 7, seg_width),
+            paired.reshape(block_total // group_size, group_size, 8, seg_width),
         ),
     )
-    forces = forces.reshape(item_total, 3, seg_width)
-    reaction = reaction.reshape(item_total, seg_width)
-    onehot = (picked[:, None] == jnp.arange(master_total, dtype=jnp.int32)[None, :]).astype(
-        jnp.float32
-    )
-    master_sum = jnp.dot(onehot.T, reaction, precision=lax.Precision.HIGHEST)
+    slave_force = forces.reshape(block_total, 3, seg_width)
+    reaction = reaction.reshape(block_total, seg_width)
+    onehot = (
+        target[None, :] == jnp.arange(devices * master_total, dtype=jnp.int32)[:, None]
+    ).astype(jnp.float32)
+    partial = jnp.dot(onehot, reaction, precision=lax.Precision.HIGHEST)
+    master_sum = lax.psum_scatter(partial, ("gx", "gy"), scatter_dimension=0, tiled=True)
     master_force = -master_sum[:, None, :] * normals
-    returned = lax.all_to_all(
-        forces.reshape(devices, slot_depth, 3, seg_width),
-        ("gx", "gy"),
-        split_axis=0,
-        concat_axis=0,
-        tiled=True,
-    )
-    slave_force = jnp.take(returned.reshape(item_total, 3, seg_width), target_slot, axis=0)
-    all_forces = jnp.concatenate(
-        [slave_force.transpose(1, 0, 2).reshape(3, -1), master_force.transpose(1, 0, 2).reshape(3, -1)],
-        axis=1,
-    )
-    contact = node_scatter_add(all_forces, all_nodes, node_total)
+    contact = node_scatter_add(
+        slave_force.transpose(1, 0, 2).reshape(3, -1), slave_node.reshape(-1), node_total
+    ) + node_scatter_add(
+        master_force.transpose(1, 0, 2).reshape(3, -1), master_node.reshape(-1), node_total
+    )
     contact_field = contact.reshape(3, layers, row_cells, col_cells)
     velocity_new = velocity + TIME_STEP * (stress + contact_field) / node_mass[None]
     padded_new = padded_2(velocity_new, (("gx", 2), ("gy", 3)), 1)

time: 150 us -> 279 us (1.86)
  waiting for transfers between devices: 13.2 us -> 145 us
  between operations: 1.41 us -> 14.6 us
  other arithmetic: 48.8 us -> 36.5 us
  starting transfers between devices: 35.8 us -> 30.1 us
    reduce_scatter x0 -> x1, waiting for transfers between devices: none -> 111 us  [on_device(): lax.psum_scatter(partial, ('gx', 'gy'), scatter_dimension=0, tiled=True)]
    all_gather x0 -> x1, waiting for transfers between devices: none -> 28.9 us  [on_device(): all_master = lax.all_gather(master_rows, ('gx', 'gy'), axis=0, tiled=True)]
    all_to_all x2 -> x0, starting transfers between devices: 13.3 us -> none  [the longest x1 7.04 us: on_device(): lax.all_to_all(forces.reshape(devices, slot_depth, 3, seg_width), ('gx',...]
    all_to_all x2 -> x0, waiting for transfers between devices: 9.88 us -> none  [the longest x1 9.87 us: on_device(): lax.all_to_all(forces.reshape(devices, slot_depth, 3, seg_width), ('gx',...]
    reduce_sum x2, other arithmetic: 35.8 us -> 28.1 us  [contact_pairs(): reaction = jnp.sum(push_force, axis=1)]
    ppermute x4, starting transfers between devices: 11.5 us -> 18.8 us  [padded_2(): lax.ppermute(lax.index_in_dim(block, block.shape[dim] - 1, axis=dim, keep...]
    pallas_call x1 -> x2, Pallas kernels: 11.9 us -> 13.4 us  [node_scatter_add(): pl.pallas_call(scatter_kernel, grid=(padded_count // TILE,), in_specs=[pl...]
  transfers between devices with their start and end apart: 10 -> 10, of which waited for: 3 -> 4; matrix products, arithmetic and copies ran while one was open for 11% -> 3% of each run, Pallas kernels for 13% -> 9%
where the time goes in v6:
time: 279 us; the launch traced here: 276 us
  waiting for transfers between devices  145 us (52%)
  other arithmetic  36.5 us (13%)
  Pallas kernels  32.6 us (12%)
  starting transfers between devices  30.1 us (11%)
  local copies, waits for them, and re-layouts  16.2 us (6%)
  between operations  14.6 us (5%)
    reduce_scatter x1, waiting for transfers between devices, on_device(): lax.psum_scatter(partial, ('gx', 'gy'), scatter_dimension=0, tiled=True)  111 us
    all_gather x1, waiting for transfers between devices, on_device(): all_master = lax.all_gather(master_rows, ('gx', 'gy'), axis=0, tiled=True)  28.9 us
    reduce_sum x2, other arithmetic, contact_pairs(): reaction = jnp.sum(push_force, axis=1)  28.1 us
    pallas_call x2, Pallas kernels, node_gather(): pl.pallas_call(gather_kernel, grid=(padded_count // TILE,), in_specs=[pl....  19.2 us
    ppermute x4, starting transfers between devices, padded_2(): lax.ppermute(lax.index_in_dim(block, block.shape[dim] - 1, axis=dim, keep...  18.8 us
    pallas_call x2, Pallas kernels, node_scatter_add(): pl.pallas_call(scatter_kernel, grid=(padded_count // TILE,), in_specs=[pl...  13.4 us
    ppermute x4, starting transfers between devices, padded_2(): lax.ppermute(lax.index_in_dim(block, 0, axis=dim, keepdims=False), axis,...  11.1 us
  transfers between devices with their start and end apart: 10, of which 4 were waited for; matrix products, arithmetic and copies ran while one was open for 3% of the time, Pallas kernels for 9%

profile of v6, /device:TPU:9, one launch (start us, length us, event | category | flops | bytes accessed | tf_op | source)
XLA Modules:
  0.0 276.1 jit_solution(3769753607048105500)
XLA Ops:
  7.3 1.1 reshape_reshape.4
  8.4 0.9 copy.260
  9.3 0.9 fusion.84
  10.1 4.8 %shard_map.150 = f32[3,4096]{1,0:T(4,128)} custom-call(s32[1,4096]{1,0:T(1,128)} %bitcast.275, f32[384,256]{1,0:T(8,128)} %bitcast.244), custom_call_target="tpu_custom_call" | custom-call | tf_op jit(solution)/shard_map/pallas_call | solution.py:73
  14.9 0.9 fusion.79
  15.9 0.9 fusion.80
  18.3 1.2 copy.245
  19.5 1.1 copy_bitcast_fusion.2
  20.7 3.8 %collective-permute-start = (f32[6,8,256]{2,1,0:T(8,128)S(1)}, f32[6,8,256]{2,1,0:T(8,128)S(1)}, u32[]{:S(2)}, u32[]{:S(2)}) collective-permute-start(f32[6,8,256]{2,1,0:T(8,128)S(1)} %get-tuple-element.108), channel_id=1, source_target_pairs={{0,8},{8,16},{16,24},{1,9},{9,17},{17,25},{2,10},{10,18},{18,26},{... | collective-permute-start | bytes 147464 | tf_op jit(solution)/shard_map/ppermute | solution.py:116
  24.5 1.9 collective-permute-start.1
  26.4 14.4 %shard_map.149 = f32[3,16384]{1,0:T(4,128)} custom-call(s32[1,16384]{1,0:T(1,128)} %bitcast.260, f32[384,256]{1,0:T(8,128)} %bitcast.245), custom_call_target="tpu_custom_call" | custom-call | tf_op jit(solution)/shard_map/pallas_call | solution.py:73
  40.9 1.0 fusion.66
  42.6 3.1 %collective-permute-start.2 = (f32[6,8,18]{2,1,0:T(8,128)S(1)}, f32[6,8,18]{2,1,0:T(8,128)S(1)}, u32[]{:S(2)}, u32[]{:S(2)}) collective-permute-start(f32[6,8,18]{2,1,0:T(8,128)S(1)} %bitcast.277), channel_id=1, source_target_pairs={{0,1},{1,2},{2,3},{3,4},{4,5},{5,6},{6,7},{8,9},{9,10},{10,11},{11... | collective-permute-start | bytes 10376 | tf_op jit(solution)/shard_map/ppermute | solution.py:116
  46.2 3.1 %collective-permute-start.3 = (f32[6,8,18]{2,1,0:T(8,128)S(1)}, f32[6,8,18]{2,1,0:T(8,128)S(1)}, u32[]{:S(2)}, u32[]{:S(2)}) collective-permute-start(f32[6,8,18]{2,1,0:T(8,128)S(1)} %bitcast.279), channel_id=1, source_target_pairs={{1,0},{2,1},{3,2},{4,3},{5,4},{6,5},{7,6},{9,8},{10,9},{11,10},{12... | collective-permute-start | bytes 10376 | tf_op jit(solution)/shard_map/ppermute | solution.py:119
  49.8 1.3 collective-permute-done.3
  53.1 28.9 %all-gather.2.cloned.1.call-done = f32[1024,8,128]{2,1,0:T(8,128)} async-done(((f32[32,8,128]{2,1,0:T(8,128)}), f32[1024,8,128]{2,1,0:T(8,128)}) %all-gather.2.cloned.1.call-update) | async-done | bytes 4194320 | tf_op jit(solution)/shard_map/all_gather | solution.py:276
  82.1 2.8 %gather_fusion = f32[128,8,128]{2,1,0:T(8,128)S(1)} fusion(f32[1024,8,128]{2,1,0:T(8,128)} %all-gather.2.cloned.1.call-done, s32[1024]{0:T(1024)S(1)} %pad_clamp_fusion), kind=kCustom, calls=%fused_computation | custom fusion | bytes 1049088 | tf_op jit(solution)/shard_map/jit(_take)/gather | solution.py:278
  85.1 28.4 %while.12 = (s32[]{:T(128)}, f32[2,64,3,128]{3,1,0,2:T(8,128)S(1)}, f32[2,64,128]{2,1,0:T(8,128)S(1)}, f32[2,64,7,128]{3,1,0,2:T(8,128)S(1)}, f32[2,64,8,128]{3,1,2,0:T(8,128)S(1)}, /*index=5*/s32[]{:T(128)}) while((s32[]{:T(128)}, f32[2,64,3,128]{3,1,0,2:T(8,128)S(1)}, f32[2,64,128]{2,1,0:T(8,128)S(1)}, f32[2,64,7,128]{3,1,0,2:T(8,128)S(1)}, ...), condition=%wide.region_6.7_spmd, body=%wide.region_1.6_spmd.sunk | while | flops 45105152 | bytes 2850901 | solution.py:284
  85.2 14.0 %fusion.88 = (f32[64,128]{1,0:T(8,128)S(1)}, f32[64,128]{1,0:T(8,128)S(1)}, f32[64,128]{1,0:T(8,128)S(1)}, f32[64,128]{1,0:T(8,128)S(1)}) fusion(f32[64,128]{1,0:T(8,128)S(1)} %get-tuple-element.170, f32[64,128]{1,0:T(8,128)S(1)} %get-tuple-element.171, f32[64,128]{1,0:T(8,128)S(1)} %get-tuple-element.172, f32[64,128]{1,0:T(8,128)S(1)} %get-tuple-element.173, ...), kind=kLoop, calls=%fused_computation.43.clone.1 | loop fusion | flops 45056000 | bytes 622592 | tf_op jit(solution)/shard_map/while/body/eval_jaxpr/reduce_sum | solution.py:209
  99.4 14.0 %fusion.88 = (f32[64,128]{1,0:T(8,128)S(1)}, f32[64,128]{1,0:T(8,128)S(1)}, f32[64,128]{1,0:T(8,128)S(1)}, f32[64,128]{1,0:T(8,128)S(1)}) fusion(f32[64,128]{1,0:T(8,128)S(1)} %get-tuple-element.170, f32[64,128]{1,0:T(8,128)S(1)} %get-tuple-element.171, f32[64,128]{1,0:T(8,128)S(1)} %get-tuple-element.172, f32[64,128]{1,0:T(8,128)S(1)} %get-tuple-element.173, ...), kind=kLoop, calls=%fused_computation.43.clone.1 | loop fusion | flops 45056000 | bytes 622592 | tf_op jit(solution)/shard_map/while/body/eval_jaxpr/reduce_sum | solution.py:209
  113.5 1.2 fusion.14
  115.1 0.8 copy.312
  115.9 9.8 %shard_map.151 = f32[384,256]{1,0:T(8,128)} custom-call(s32[1,16384]{1,0:T(1,128)} %bitcast.261, f32[3,16384]{1,0:T(4,128)} %bitcast.249), custom_call_target="tpu_custom_call" | custom-call | tf_op jit(solution)/shard_map/pallas_call | solution.py:91
  125.7 111.4 %reduce-scatter.2.cloned.1.call-done = f32[32,128]{1,0:T(8,128)} async-done(((f32[1024,128]{1,0:T(8,128)}), f32[32,128]{1,0:T(8,128)}) %reduce-scatter.2.cloned.1.call-update) | async-done | bytes 16400 | tf_op jit(solution)/shard_map/reduce_scatter | solution.py:297
  238.5 3.6 %shard_map.152 = f32[384,256]{1,0:T(8,128)} custom-call(s32[1,4096]{1,0:T(1,128)} %bitcast.276, f32[3,4096]{1,0:T(4,128)} %bitcast.259), custom_call_target="tpu_custom_call" | custom-call | tf_op jit(solution)/shard_map/pallas_call | solution.py:91
  242.1 1.2 add.213
  244.1 10.0 %collective-permute-start.4 = (f32[3,8,256]{2,1,0:T(8,128)S(1)}, f32[3,8,256]{2,1,0:T(8,128)S(1)}, u32[]{:S(2)}, u32[]{:S(2)}) collective-permute-start(f32[3,8,256]{2,1,0:T(8,128)S(1)} %get-tuple-element.114), channel_id=1, source_target_pairs={{0,8},{8,16},{16,24},{1,9},{9,17},{17,25},{2,10},{10,18},{18,26},{... | collective-permute-start | bytes 73736 | tf_op jit(solution)/shard_map/ppermute | solution.py:116
  254.1 1.9 collective-permute-start.5
  256.0 3.2 %collective-permute-done.5 = f32[3,8,256]{2,1,0:T(8,128)S(1)} collective-permute-done((f32[3,8,256]{2,1,0:T(8,128)S(1)}, f32[3,8,256]{2,1,0:T(8,128)S(1)}, u32[]{:S(2)}, u32[]{:S(2)}) %collective-permute-start.5) | collective-permute-done | bytes 24608 | tf_op jit(solution)/shard_map/ppermute | solution.py:119
  259.7 1.9 collective-permute-start.6
  261.8 4.2 %collective-permute-start.7 = (f32[3,8,18]{2,1,0:T(8,128)S(1)}, f32[3,8,18]{2,1,0:T(8,128)S(1)}, u32[]{:S(2)}, u32[]{:S(2)}) collective-permute-start(f32[3,8,18]{2,1,0:T(8,128)S(1)} %bitcast.283), channel_id=1, source_target_pairs={{1,0},{2,1},{3,2},{4,3},{5,4},{6,5},{7,6},{9,8},{10,9},{11,10},{12... | collective-permute-start | bytes 5192 | tf_op jit(solution)/shard_map/ppermute | solution.py:119
  266.1 0.9 copy.277
  (102 shorter events, 11.1 us)
Async XLA Ops:
  7.2 33.6 %copy-start.6 = (s32[128,1]{0,1:T(1,128)S(1)}, s32[128,1]{0,1:T(1,128)}, u32[]{:S(2)}) copy-start(s32[128,1]{0,1:T(1,128)} %param.24) | copy-start | bytes 1540
  7.2 33.6 %copy-start.5 = (s32[128]{0:T(128)S(1)}, s32[128]{0:T(128)}, u32[]{:S(2)}) copy-start(s32[128]{0:T(128)} %param.25) | copy-start | bytes 1540
  7.2 33.6 %copy-start.3 = (f32[128,128]{1,0:T(8,128)S(1)}, f32[128,128]{1,0:T(8,128)}, u32[]{:S(2)}) copy-start(f32[128,128]{1,0:T(8,128)} %param.21) | copy-start | bytes 196612
  7.2 33.6 %copy-start.4 = (s32[128]{0:T(128)S(1)}, s32[128]{0:T(128)}, u32[]{:S(2)}) copy-start(s32[128]{0:T(128)} %param.22) | copy-start | bytes 1540
  7.2 33.7 %copy-start.1 = (f32[128,3,128]{2,0,1:T(8,128)S(1)}, f32[128,3,128]{2,0,1:T(8,128)}, u32[]{:S(2)}) copy-start(f32[128,3,128]{2,0,1:T(8,128)} %param.20) | copy-start | bytes 589828
  7.2 74.8 %all-gather.2.cloned.1.call-start = ((), (), s32[]{:S(2)}) async-start(), calls=%async_computation.1 | async-start | bytes 4325376 | tf_op jit(solution)/shard_map/all_gather | solution.py:276
  18.2 218.9 %reduce-scatter.2.cloned.1.call-start = ((), (), s32[]{:S(2)}) async-start(), calls=%async_computation.2 | async-start | bytes 540672 | tf_op jit(solution)/shard_map/reduce_scatter | solution.py:297
  20.6 28.7 %copy-start.2 = (f32[8,16,256]{2,1,0:T(8,128)S(1)}, f32[8,16,256]{2,1,0:T(8,128)}, u32[]{:S(2)}) copy-start(f32[8,16,256]{2,1,0:T(8,128)} %param.19) | copy-start | bytes 393220
  20.7 21.3 %collective-permute-start = (f32[6,8,256]{2,1,0:T(8,128)S(1)}, f32[6,8,256]{2,1,0:T(8,128)S(1)}, u32[]{:S(2)}, u32[]{:S(2)}) collective-permute-start(f32[6,8,256]{2,1,0:T(8,128)S(1)} %get-tuple-element.108), channel_id=1, source_target_pairs={{0,8},{8,16},{16,24},{1,9},{9,17},{17,25},{2,10},{10,18},{18,26},{... | collective-permute-start | bytes 147464 | tf_op jit(solution)/shard_map/ppermute | solution.py:116
  24.5 17.5 %collective-permute-start.1 = (f32[6,8,256]{2,1,0:T(8,128)S(1)}, f32[6,8,256]{2,1,0:T(8,128)S(1)}, u32[]{:S(2)}, u32[]{:S(2)}) collective-permute-start(f32[6,8,256]{2,1,0:T(8,128)S(1)} %get-tuple-element.109), channel_id=1, source_target_pairs={{8,0},{16,8},{24,16},{9,1},{17,9},{25,17},{10,2},{18,10},{26,18},{... | collective-permute-start | bytes 147464 | tf_op jit(solution)/shard_map/ppermute | solution.py:119
  42.6 6.8 %collective-permute-start.2 = (f32[6,8,18]{2,1,0:T(8,128)S(1)}, f32[6,8,18]{2,1,0:T(8,128)S(1)}, u32[]{:S(2)}, u32[]{:S(2)}) collective-permute-start(f32[6,8,18]{2,1,0:T(8,128)S(1)} %bitcast.277), channel_id=1, source_target_pairs={{0,1},{1,2},{2,3},{3,4},{4,5},{5,6},{6,7},{8,9},{9,10},{10,11},{11... | collective-permute-start | bytes 10376 | tf_op jit(solution)/shard_map/ppermute | solution.py:116
  46.2 5.0 %collective-permute-start.3 = (f32[6,8,18]{2,1,0:T(8,128)S(1)}, f32[6,8,18]{2,1,0:T(8,128)S(1)}, u32[]{:S(2)}, u32[]{:S(2)}) collective-permute-start(f32[6,8,18]{2,1,0:T(8,128)S(1)} %bitcast.279), channel_id=1, source_target_pairs={{1,0},{2,1},{3,2},{4,3},{5,4},{6,5},{7,6},{9,8},{10,9},{11,10},{12... | collective-permute-start | bytes 10376 | tf_op jit(solution)/shard_map/ppermute | solution.py:119
  113.5 130.0 %copy-start = (f32[3,8,16,256]{3,2,1,0:T(8,128)S(1)}, f32[3,8,16,256]{3,2,1,0:T(8,128)}, u32[]{:S(2)}) copy-start(f32[3,8,16,256]{3,2,1,0:T(8,128)} %param.16) | copy-start | bytes 1179652
  244.1 11.9 %collective-permute-start.4 = (f32[3,8,256]{2,1,0:T(8,128)S(1)}, f32[3,8,256]{2,1,0:T(8,128)S(1)}, u32[]{:S(2)}, u32[]{:S(2)}) collective-permute-start(f32[3,8,256]{2,1,0:T(8,128)S(1)} %get-tuple-element.114), channel_id=1, source_target_pairs={{0,8},{8,16},{16,24},{1,9},{9,17},{17,25},{2,10},{10,18},{18,26},{... | collective-permute-start | bytes 73736 | tf_op jit(solution)/shard_map/ppermute | solution.py:116
  254.1 5.1 %collective-permute-start.5 = (f32[3,8,256]{2,1,0:T(8,128)S(1)}, f32[3,8,256]{2,1,0:T(8,128)S(1)}, u32[]{:S(2)}, u32[]{:S(2)}) collective-permute-start(f32[3,8,256]{2,1,0:T(8,128)S(1)} %get-tuple-element.115), channel_id=1, source_target_pairs={{8,0},{16,8},{24,16},{9,1},{17,9},{25,17},{10,2},{18,10},{26,18},{... | collective-permute-start | bytes 73736 | tf_op jit(solution)/shard_map/ppermute | solution.py:119
  259.7 7.3 %collective-permute-start.6 = (f32[3,8,18]{2,1,0:T(8,128)S(1)}, f32[3,8,18]{2,1,0:T(8,128)S(1)}, u32[]{:S(2)}, u32[]{:S(2)}) collective-permute-start(f32[3,8,18]{2,1,0:T(8,128)S(1)} %bitcast.281), channel_id=1, source_target_pairs={{0,1},{1,2},{2,3},{3,4},{4,5},{5,6},{6,7},{8,9},{9,10},{10,11},{11... | collective-permute-start | bytes 5192 | tf_op jit(solution)/shard_map/ppermute | solution.py:116
  261.8 5.4 %collective-permute-start.7 = (f32[3,8,18]{2,1,0:T(8,128)S(1)}, f32[3,8,18]{2,1,0:T(8,128)S(1)}, u32[]{:S(2)}, u32[]{:S(2)}) collective-permute-start(f32[3,8,18]{2,1,0:T(8,128)S(1)} %bitcast.283), channel_id=1, source_target_pairs={{1,0},{2,1},{3,2},{4,3},{5,4},{6,5},{7,6},{9,8},{10,9},{11,10},{12... | collective-permute-start | bytes 5192 | tf_op jit(solution)/shard_map/ppermute | solution.py:119
Sparse Core Ops, SparseCore 0:
  18.3 63.6 all-gather.1
  114.9 122.2 reduce-scatter.1

commit v7 on v5

--- a/solution.py
+++ b/solution.py
@@ -184,13 +184,17 @@
     normal_z = master[:, 5, None, :]
     dist_sq = delta_x * delta_x + delta_y * delta_y + delta_z * delta_z
     gap_normal = normal_x * delta_x + normal_y * delta_y + normal_z * delta_z
+    master_along = (
+        master[:, 3] * master[:, 6] + master[:, 4] * master[:, 7] + master[:, 5] * master[:, 8]
+    )
     closing = (
-        normal_x * (slave[:, 3, :, None] - master[:, 6, None, :])
-        + normal_y * (slave[:, 4, :, None] - master[:, 7, None, :])
-        + normal_z * (slave[:, 5, :, None] - master[:, 8, None, :])
-    )
+        normal_x * slave[:, 3, :, None]
+        + normal_y * slave[:, 4, :, None]
+        + normal_z * slave[:, 5, :, None]
+    ) - master_along[:, None, :]
     weight = jnp.exp(-dist_sq / REACH_SQ)
-    depth_soft = SOFT_GAP * jax.nn.softplus(-gap_normal / SOFT_GAP)
+    soft = gap_normal * (-1.0 / SOFT_GAP)
+    depth_soft = SOFT_GAP * (jnp.maximum(soft, 0.0) + jnp.log1p(jnp.exp(-jnp.abs(soft))))
     push_force = (
         slave[:, 6, :, None]
         * master[:, 9, None, :]
@@ -248,7 +252,6 @@
     stress, inside = stress_forces(padded)
     vel_flat = velocity.reshape(3, node_total)
     slave_count = block_total * seg_width
-    all_nodes = jnp.concatenate([slave_node.reshape(-1), master_node.reshape(-1)])
     slave_vel = (
         node_gather(vel_flat, slave_node.reshape(-1))
         .reshape(3, block_total, seg_width)
@@ -316,6 +319,9 @@
     )
     master_sum = jnp.dot(onehot.T, reaction, precision=lax.Precision.HIGHEST)
     master_force = -master_sum[:, None, :] * normals
+    master_contact = node_scatter_add(
+        master_force.transpose(1, 0, 2).reshape(3, -1), master_node.reshape(-1), node_total
+    )
     returned = lax.all_to_all(
         forces.reshape(devices, slot_depth, 3, seg_width),
         ("gx", "gy"),
@@ -324,11 +330,9 @@
         tiled=True,
     )
     slave_force = jnp.take(returned.reshape(item_total, 3, seg_width), target_slot, axis=0)
-    all_forces = jnp.concatenate(
-        [slave_force.transpose(1, 0, 2).reshape(3, -1), master_force.transpose(1, 0, 2).reshape(3, -1)],
-        axis=1,
-    )
-    contact = node_scatter_add(all_forces, all_nodes, node_total)
+    contact = master_contact + node_scatter_add(
+        slave_force.transpose(1, 0, 2).reshape(3, -1), slave_node.reshape(-1), node_total
+    )
     contact_field = contact.reshape(3, layers, row_cells, col_cells)
     velocity_new = velocity + TIME_STEP * (stress + contact_field) / node_mass[None]
     padded_new = padded_2(velocity_new, (("gx", 2), ("gy", 3)), 1)

time: 150 us -> 146 us (0.973)
  waiting for transfers between devices: 13.2 us -> 9.42 us
  Pallas kernels: 31.1 us -> 32.6 us
  other arithmetic: 48.8 us -> 47.3 us
    all_to_all x1, waiting for transfers between devices: 9.87 us -> 5.65 us  [on_device(): lax.all_to_all(forces.reshape(devices, slot_depth, 3, seg_width), ('gx',...]
    pallas_call x1 -> x2, Pallas kernels: 11.9 us -> 13.4 us  [node_scatter_add(): pl.pallas_call(scatter_kernel, grid=(padded_count // TILE,), in_specs=[pl...]
  transfers between devices with their start and end apart: 10 -> 10, of which waited for: 3 -> 3; matrix products, arithmetic and copies ran while one was open for 11% -> 12% of each run, Pallas kernels for 13% -> 16%
where the time goes in v7:
time: 146 us; the launch traced here: 144 us
  other arithmetic  47.3 us (32%)
  starting transfers between devices  35.3 us (24%)
  Pallas kernels  32.6 us (22%)
  local copies, waits for them, and re-layouts  16.6 us (11%)
  waiting for transfers between devices  9.42 us (6%)
    reduce_sum x2, other arithmetic, contact_pairs(): reaction = jnp.sum(push_force, axis=1)  34.4 us
    pallas_call x2, Pallas kernels, node_gather(): pl.pallas_call(gather_kernel, grid=(padded_count // TILE,), in_specs=[pl....  19.2 us
    pallas_call x2, Pallas kernels, node_scatter_add(): pl.pallas_call(scatter_kernel, grid=(padded_count // TILE,), in_specs=[pl...  13.4 us
    ppermute x4, starting transfers between devices, padded_2(): lax.ppermute(lax.index_in_dim(block, block.shape[dim] - 1, axis=dim, keep...  11.5 us
    ppermute x4, starting transfers between devices, padded_2(): lax.ppermute(lax.index_in_dim(block, 0, axis=dim, keepdims=False), axis,...  10.9 us
    all_to_all x1, starting transfers between devices, on_device(): lax.all_to_all(forces.reshape(devices, slot_depth, 3, seg_width), ('gx',...  6.6 us
    all_to_all x1, starting transfers between devices, on_device(): lax.all_to_all(outgoing.reshape(devices, slot_depth, 8, seg_width), ('gx'...  6.29 us
    all_to_all x1, waiting for transfers between devices, on_device(): lax.all_to_all(forces.reshape(devices, slot_depth, 3, seg_width), ('gx',...  5.65 us
  transfers between devices with their start and end apart: 10, of which 3 were waited for; matrix products, arithmetic and copies ran while one was open for 12% of the time, Pallas kernels for 16%

profile of v7, /device:TPU:9, one launch (start us, length us, event | category | flops | bytes accessed | tf_op | source)
XLA Modules:
  0.0 143.9 jit_solution(8906259025449473833)
XLA Ops:
  0.6 1.3 copy.254
  1.9 1.1 copy_bitcast_fusion
  3.1 3.8 %collective-permute-start = (f32[6,8,256]{2,1,0:T(8,128)S(1)}, f32[6,8,256]{2,1,0:T(8,128)S(1)}, u32[]{:S(2)}, u32[]{:S(2)}) collective-permute-start(f32[6,8,256]{2,1,0:T(8,128)S(1)} %get-tuple-element.99), channel_id=1, source_target_pairs={{0,8},{8,16},{16,24},{1,9},{9,17},{17,25},{2,10},{10,18},{18,26},{... | collective-permute-start | bytes 147464 | tf_op jit(solution)/shard_map/ppermute | solution.py:116
  7.0 1.9 %collective-permute-start.1 = (f32[6,8,256]{2,1,0:T(8,128)S(1)}, f32[6,8,256]{2,1,0:T(8,128)S(1)}, u32[]{:S(2)}, u32[]{:S(2)}) collective-permute-start(f32[6,8,256]{2,1,0:T(8,128)S(1)} %get-tuple-element.100), channel_id=1, source_target_pairs={{8,0},{16,8},{24,16},{9,1},{17,9},{25,17},{10,2},{18,10},{26,18},{... | collective-permute-start | bytes 147464 | tf_op jit(solution)/shard_map/ppermute | solution.py:119
  9.4 0.9 copy.269
  10.6 14.4 %shard_map.149 = f32[3,16384]{1,0:T(4,128)} custom-call(s32[1,16384]{1,0:T(1,128)} %bitcast.250, f32[384,256]{1,0:T(8,128)} %bitcast.235), custom_call_target="tpu_custom_call" | custom-call | tf_op jit(solution)/shard_map/pallas_call | solution.py:73
  24.9 1.1 copy_add_fusion
  26.4 1.2 pad_maximum_fusion.3
  27.6 0.8 gather_fusion
  28.4 1.2 select_select_fusion
  29.7 6.3 %all-to-all-start = ((f32[32,5,8,128]{3,2,1,0:T(8,128)}), f32[32,5,8,128]{3,2,1,0:T(8,128)S(1)}, u32[]{:S(2)}, u32[]{:S(2)}) async-start(f32[32,5,8,128]{3,2,1,0:T(8,128)} %select_select_fusion), calls=%async_computation | async-start | bytes 1310720 | tf_op jit(solution)/shard_map/all_to_all | solution.py:291
  36.0 4.8 %shard_map.150 = f32[3,4096]{1,0:T(4,128)} custom-call(s32[1,4096]{1,0:T(1,128)} %bitcast.265, f32[384,256]{1,0:T(8,128)} %bitcast.236), custom_call_target="tpu_custom_call" | custom-call | tf_op jit(solution)/shard_map/pallas_call | solution.py:73
  40.8 0.9 copy_add_fusion.1
  42.5 3.1 %collective-permute-start.2 = (f32[6,8,18]{2,1,0:T(8,128)S(1)}, f32[6,8,18]{2,1,0:T(8,128)S(1)}, u32[]{:S(2)}, u32[]{:S(2)}) collective-permute-start(f32[6,8,18]{2,1,0:T(8,128)S(1)} %bitcast.267), channel_id=1, source_target_pairs={{0,1},{1,2},{2,3},{3,4},{4,5},{5,6},{6,7},{8,9},{9,10},{10,11},{11... | collective-permute-start | bytes 10376 | tf_op jit(solution)/shard_map/ppermute | solution.py:116
  46.0 3.1 %collective-permute-start.3 = (f32[6,8,18]{2,1,0:T(8,128)S(1)}, f32[6,8,18]{2,1,0:T(8,128)S(1)}, u32[]{:S(2)}, u32[]{:S(2)}) collective-permute-start(f32[6,8,18]{2,1,0:T(8,128)S(1)} %bitcast.269), channel_id=1, source_target_pairs={{1,0},{2,1},{3,2},{4,3},{5,4},{6,5},{7,6},{9,8},{10,9},{11,10},{12... | collective-permute-start | bytes 10376 | tf_op jit(solution)/shard_map/ppermute | solution.py:119
  57.0 36.2 %while.12 = (s32[]{:T(128)}, f32[2,80,3,128]{3,1,2,0:T(8,128)}, f32[2,80,128]{2,1,0:T(8,128)}, f32[2,80,7,128]{3,1,0,2:T(8,128)S(1)}, f32[2,80,10,128]{3,1,2,0:T(8,128)S(1)}, /*index=5*/s32[]{:T(128)}) while((s32[]{:T(128)}, f32[2,80,3,128]{3,1,2,0:T(8,128)}, f32[2,80,128]{2,1,0:T(8,128)}, f32[2,80,7,128]{3,1,0,2:T(8,128)S(1)}, ...), condition=%wide.region_8.9_spmd, body=%wide.region_3.8_spmd.sunk | while | flops 52500480 | bytes 5776009 | solution.py:308
  57.2 17.2 %fusion.87 = (f32[80,128]{1,0:T(8,128)S(1)}, f32[80,128]{1,0:T(8,128)S(1)}, f32[80,128]{1,0:T(8,128)S(1)}, f32[80,128]{1,0:T(8,128)S(1)}) fusion(f32[80,128]{1,0:T(8,128)S(1)} %get-tuple-element.164, f32[80,128]{1,0:T(8,128)S(1)} %get-tuple-element.165, f32[80,128]{1,0:T(8,128)S(1)} %get-tuple-element.166, f32[80,128]{1,0:T(8,128)S(1)} %get-tuple-element.167, ...), kind=kLoop, calls=%fused_computation.47.clone.1 | loop fusion | flops 52387840 | bytes 778240 | tf_op jit(solution)/shard_map/while/body/eval_jaxpr/reduce_sum | solution.py:213
  75.3 17.2 %fusion.87 = (f32[80,128]{1,0:T(8,128)S(1)}, f32[80,128]{1,0:T(8,128)S(1)}, f32[80,128]{1,0:T(8,128)S(1)}, f32[80,128]{1,0:T(8,128)S(1)}) fusion(f32[80,128]{1,0:T(8,128)S(1)} %get-tuple-element.164, f32[80,128]{1,0:T(8,128)S(1)} %get-tuple-element.165, f32[80,128]{1,0:T(8,128)S(1)} %get-tuple-element.166, f32[80,128]{1,0:T(8,128)S(1)} %get-tuple-element.167, ...), kind=kLoop, calls=%fused_computation.47.clone.1 | loop fusion | flops 52387840 | bytes 778240 | tf_op jit(solution)/shard_map/while/body/eval_jaxpr/reduce_sum | solution.py:213
  93.3 1.8 %copy.297 = f32[2,80,3,128]{3,2,1,0:T(4,128)} copy(f32[2,80,3,128]{3,1,2,0:T(8,128)} %get-tuple-element.31) | data formatting | bytes 491520 | tf_op jit(solution)/shard_map/reshape;reshape | solution.py:326
  95.1 6.6 %all-to-all-start.1 = ((f32[32,5,3,128]{3,2,1,0:T(4,128)}), f32[32,5,3,128]{3,2,1,0:T(4,128)S(1)}, u32[]{:S(2)}, u32[]{:S(2)}) async-start(f32[32,5,3,128]{3,2,1,0:T(4,128)} %bitcast.69), calls=%async_computation.1 | async-start | bytes 655360 | tf_op jit(solution)/shard_map/all_to_all | solution.py:325
  101.8 1.2 convolution_negate_fusion
  103.6 3.6 %shard_map.151 = f32[384,256]{1,0:T(8,128)} custom-call(s32[1,4096]{1,0:T(1,128)} %bitcast.266, f32[3,4096]{1,0:T(4,128)} %bitcast.249), custom_call_target="tpu_custom_call" | custom-call | tf_op jit(solution)/shard_map/pallas_call | solution.py:91
  107.2 5.7 %all-to-all-done.1 = f32[32,5,3,128]{3,2,1,0:T(4,128)S(1)} async-done(((f32[32,5,3,128]{3,2,1,0:T(4,128)}), f32[32,5,3,128]{3,2,1,0:T(4,128)S(1)}, u32[]{:S(2)}, u32[]{:S(2)}) %all-to-all-start.1) | async-done | bytes 245792 | tf_op jit(solution)/shard_map/all_to_all | solution.py:325
  113.6 0.9 select_bitcast_fusion.force_ref
  114.5 9.8 %shard_map.152 = f32[384,256]{1,0:T(8,128)} custom-call(s32[1,16384]{1,0:T(1,128)} %bitcast.251, f32[3,16384]{1,0:T(4,128)} %select_bitcast_fusion.force_ref), custom_call_target="tpu_custom_call" | custom-call | tf_op jit(solution)/shard_map/pallas_call | solution.py:91
  124.3 1.1 add.281
  126.3 2.5 %collective-permute-start.4 = (f32[3,8,256]{2,1,0:T(8,128)S(1)}, f32[3,8,256]{2,1,0:T(8,128)S(1)}, u32[]{:S(2)}, u32[]{:S(2)}) collective-permute-start(f32[3,8,256]{2,1,0:T(8,128)S(1)} %get-tuple-element.105), channel_id=1, source_target_pairs={{0,8},{8,16},{16,24},{1,9},{9,17},{17,25},{2,10},{10,18},{18,26},{... | collective-permute-start | bytes 73736 | tf_op jit(solution)/shard_map/ppermute | solution.py:116
  128.8 1.9 %collective-permute-start.5 = (f32[3,8,256]{2,1,0:T(8,128)S(1)}, f32[3,8,256]{2,1,0:T(8,128)S(1)}, u32[]{:S(2)}, u32[]{:S(2)}) collective-permute-start(f32[3,8,256]{2,1,0:T(8,128)S(1)} %get-tuple-element.106), channel_id=1, source_target_pairs={{8,0},{16,8},{24,16},{9,1},{17,9},{25,17},{10,2},{18,10},{26,18},{... | collective-permute-start | bytes 73736 | tf_op jit(solution)/shard_map/ppermute | solution.py:119
  130.7 3.2 %collective-permute-done.5 = f32[3,8,256]{2,1,0:T(8,128)S(1)} collective-permute-done((f32[3,8,256]{2,1,0:T(8,128)S(1)}, f32[3,8,256]{2,1,0:T(8,128)S(1)}, u32[]{:S(2)}, u32[]{:S(2)}) %collective-permute-start.5) | collective-permute-done | bytes 24608 | tf_op jit(solution)/shard_map/ppermute | solution.py:119
  134.3 2.2 %collective-permute-start.6 = (f32[3,8,18]{2,1,0:T(8,128)S(1)}, f32[3,8,18]{2,1,0:T(8,128)S(1)}, u32[]{:S(2)}, u32[]{:S(2)}) collective-permute-start(f32[3,8,18]{2,1,0:T(8,128)S(1)} %bitcast.272), channel_id=1, source_target_pairs={{0,1},{1,2},{2,3},{3,4},{4,5},{5,6},{6,7},{8,9},{9,10},{10,11},{11... | collective-permute-start | bytes 5192 | tf_op jit(solution)/shard_map/ppermute | solution.py:116
  136.7 4.0 %collective-permute-start.7 = (f32[3,8,18]{2,1,0:T(8,128)S(1)}, f32[3,8,18]{2,1,0:T(8,128)S(1)}, u32[]{:S(2)}, u32[]{:S(2)}) collective-permute-start(f32[3,8,18]{2,1,0:T(8,128)S(1)} %bitcast.274), channel_id=1, source_target_pairs={{1,0},{2,1},{3,2},{4,3},{5,4},{6,5},{7,6},{9,8},{10,9},{11,10},{12... | collective-permute-start | bytes 5192 | tf_op jit(solution)/shard_map/ppermute | solution.py:119
  140.7 0.9 copy.295
  (144 shorter events, 16.7 us)
Async XLA Ops:
  0.6 8.3 %copy-start = (f32[3,8,16,256]{3,2,1,0:T(8,128)S(1)}, f32[3,8,16,256]{3,2,1,0:T(8,128)}, u32[]{:S(2)}) copy-start(f32[3,8,16,256]{3,2,1,0:T(8,128)} %param.16) | copy-start | bytes 1179652
  1.9 7.0 %copy-start.16 = (s32[128,1]{0,1:T(1,128)S(1)}, s32[128,1]{0,1:T(1,128)}, u32[]{:S(2)}) copy-start(s32[128,1]{0,1:T(1,128)} %param.24) | copy-start | bytes 1540
  3.1 7.2 %copy-start.17 = (s32[128]{0:T(128)S(1)}, s32[128]{0:T(128)}, u32[]{:S(2)}) copy-start(s32[128]{0:T(128)} %param.25) | copy-start | bytes 1540
  3.1 21.8 %copy-start.9 = (f32[128,3,128]{2,0,1:T(8,128)S(1)}, f32[128,3,128]{2,0,1:T(8,128)}, u32[]{:S(2)}) copy-start(f32[128,3,128]{2,0,1:T(8,128)} %param.20) | copy-start | bytes 589828
  3.1 38.6 %collective-permute-start = (f32[6,8,256]{2,1,0:T(8,128)S(1)}, f32[6,8,256]{2,1,0:T(8,128)S(1)}, u32[]{:S(2)}, u32[]{:S(2)}) collective-permute-start(f32[6,8,256]{2,1,0:T(8,128)S(1)} %get-tuple-element.99), channel_id=1, source_target_pairs={{0,8},{8,16},{16,24},{1,9},{9,17},{17,25},{2,10},{10,18},{18,26},{... | collective-permute-start | bytes 147464 | tf_op jit(solution)/shard_map/ppermute | solution.py:116
  7.0 34.8 %collective-permute-start.1 = (f32[6,8,256]{2,1,0:T(8,128)S(1)}, f32[6,8,256]{2,1,0:T(8,128)S(1)}, u32[]{:S(2)}, u32[]{:S(2)}) collective-permute-start(f32[6,8,256]{2,1,0:T(8,128)S(1)} %get-tuple-element.100), channel_id=1, source_target_pairs={{8,0},{16,8},{24,16},{9,1},{17,9},{25,17},{10,2},{18,10},{26,18},{... | collective-permute-start | bytes 147464 | tf_op jit(solution)/shard_map/ppermute | solution.py:119
  8.9 17.1 %copy-start.11 = (f32[128,128]{1,0:T(8,128)S(1)}, f32[128,128]{1,0:T(8,128)}, u32[]{:S(2)}) copy-start(f32[128,128]{1,0:T(8,128)} %param.21) | copy-start | bytes 196612
  8.9 17.1 %copy-start.15 = (s32[128]{0:T(128)S(1)}, s32[128]{0:T(128)}, u32[]{:S(2)}) copy-start(s32[128]{0:T(128)} %param.22) | copy-start | bytes 1540
  28.4 7.6 %copy-start.13 = (f32[32,2,128]{2,1,0:T(2,128)S(1)}, f32[32,2,128]{2,1,0:T(2,128)}, u32[]{:S(2)}) copy-start(f32[32,2,128]{2,1,0:T(2,128)} %param.27) | copy-start | bytes 98308
  28.4 12.4 %copy-start.12 = (f32[32,3,128]{2,0,1:T(8,128)S(1)}, f32[32,3,128]{2,0,1:T(8,128)}, u32[]{:S(2)}) copy-start(f32[32,3,128]{2,0,1:T(8,128)} %param.26) | copy-start | bytes 147460
  29.7 25.8 %all-to-all-start = ((f32[32,5,8,128]{3,2,1,0:T(8,128)}), f32[32,5,8,128]{3,2,1,0:T(8,128)S(1)}, u32[]{:S(2)}, u32[]{:S(2)}) async-start(f32[32,5,8,128]{3,2,1,0:T(8,128)} %select_select_fusion), calls=%async_computation | async-start | bytes 1310720 | tf_op jit(solution)/shard_map/all_to_all | solution.py:291
  41.8 7.2 %copy-start.10 = (f32[8,16,256]{2,1,0:T(8,128)S(1)}, f32[8,16,256]{2,1,0:T(8,128)}, u32[]{:S(2)}) copy-start(f32[8,16,256]{2,1,0:T(8,128)} %param.19) | copy-start | bytes 393220
  41.9 8.0 %copy-start.3 = (f32[3,4096]{1,0:T(4,128)S(1)}, f32[3,4096]{1,0:T(4,128)}, u32[]{:S(2)}) copy-start(f32[3,4096]{1,0:T(4,128)} %shard_map.150) | copy-start | bytes 147460
  41.9 7.9 %copy-start.14 = (f32[32,128]{1,0:T(8,128)S(1)}, f32[32,128]{1,0:T(8,128)}, u32[]{:S(2)}) copy-start(f32[32,128]{1,0:T(8,128)} %param.28) | copy-start | bytes 49156
  42.5 7.7 %collective-permute-start.2 = (f32[6,8,18]{2,1,0:T(8,128)S(1)}, f32[6,8,18]{2,1,0:T(8,128)S(1)}, u32[]{:S(2)}, u32[]{:S(2)}) collective-permute-start(f32[6,8,18]{2,1,0:T(8,128)S(1)} %bitcast.267), channel_id=1, source_target_pairs={{0,1},{1,2},{2,3},{3,4},{4,5},{5,6},{6,7},{8,9},{9,10},{10,11},{11... | collective-permute-start | bytes 10376 | tf_op jit(solution)/shard_map/ppermute | solution.py:116
  46.0 5.2 %collective-permute-start.3 = (f32[6,8,18]{2,1,0:T(8,128)S(1)}, f32[6,8,18]{2,1,0:T(8,128)S(1)}, u32[]{:S(2)}, u32[]{:S(2)}) collective-permute-start(f32[6,8,18]{2,1,0:T(8,128)S(1)} %bitcast.269), channel_id=1, source_target_pairs={{1,0},{2,1},{3,2},{4,3},{5,4},{6,5},{7,6},{9,8},{10,9},{11,10},{12... | collective-permute-start | bytes 10376 | tf_op jit(solution)/shard_map/ppermute | solution.py:119
  57.2 17.2 %copy-start.7 = (f32[2,80,3,128]{3,1,2,0:T(8,128)S(1)}, f32[2,80,3,128]{3,1,2,0:T(8,128)}, u32[]{:S(2)}) copy-start(f32[2,80,3,128]{3,1,2,0:T(8,128)} %get-tuple-element.190) | copy-start | bytes 737284 | tf_op jit(solution)/shard_map/while
  74.4 0.7 copy-start.8
  75.3 17.2 %copy-start.7 = (f32[2,80,3,128]{3,1,2,0:T(8,128)S(1)}, f32[2,80,3,128]{3,1,2,0:T(8,128)}, u32[]{:S(2)}) copy-start(f32[2,80,3,128]{3,1,2,0:T(8,128)} %get-tuple-element.190) | copy-start | bytes 737284 | tf_op jit(solution)/shard_map/while
  92.5 0.7 copy-start.8
  93.3 8.5 %copy-start.2 = (f32[8,17,256]{2,0,1:T(8,128)S(1)}, f32[8,17,256]{2,0,1:T(8,128)}, u32[]{:S(2)}) copy-start(f32[8,17,256]{2,0,1:T(8,128)} %fusion.65) | copy-start | bytes 417796
  95.1 17.8 %all-to-all-start.1 = ((f32[32,5,3,128]{3,2,1,0:T(4,128)}), f32[32,5,3,128]{3,2,1,0:T(4,128)S(1)}, u32[]{:S(2)}, u32[]{:S(2)}) async-start(f32[32,5,3,128]{3,2,1,0:T(4,128)} %bitcast.69), calls=%async_computation.1 | async-start | bytes 655360 | tf_op jit(solution)/shard_map/all_to_all | solution.py:325
  107.2 17.1 %copy-start.1 = (f32[384,256]{1,0:T(8,128)S(1)}, f32[384,256]{1,0:T(8,128)}, u32[]{:S(2)}) copy-start(f32[384,256]{1,0:T(8,128)} %shard_map.151) | copy-start | bytes 1179652
  124.3 1.4 copy-start.4
  124.3 1.4 copy-start.5
  124.3 1.4 copy-start.6
  126.3 4.4 %collective-permute-start.4 = (f32[3,8,256]{2,1,0:T(8,128)S(1)}, f32[3,8,256]{2,1,0:T(8,128)S(1)}, u32[]{:S(2)}, u32[]{:S(2)}) collective-permute-start(f32[3,8,256]{2,1,0:T(8,128)S(1)} %get-tuple-element.105), channel_id=1, source_target_pairs={{0,8},{8,16},{16,24},{1,9},{9,17},{17,25},{2,10},{10,18},{18,26},{... | collective-permute-start | bytes 73736 | tf_op jit(solution)/shard_map/ppermute | solution.py:116
  128.8 5.1 %collective-permute-start.5 = (f32[3,8,256]{2,1,0:T(8,128)S(1)}, f32[3,8,256]{2,1,0:T(8,128)S(1)}, u32[]{:S(2)}, u32[]{:S(2)}) collective-permute-start(f32[3,8,256]{2,1,0:T(8,128)S(1)} %get-tuple-element.106), channel_id=1, source_target_pairs={{8,0},{16,8},{24,16},{9,1},{17,9},{25,17},{10,2},{18,10},{26,18},{... | collective-permute-start | bytes 73736 | tf_op jit(solution)/shard_map/ppermute | solution.py:119
  134.3 7.3 %collective-permute-start.6 = (f32[3,8,18]{2,1,0:T(8,128)S(1)}, f32[3,8,18]{2,1,0:T(8,128)S(1)}, u32[]{:S(2)}, u32[]{:S(2)}) collective-permute-start(f32[3,8,18]{2,1,0:T(8,128)S(1)} %bitcast.272), channel_id=1, source_target_pairs={{0,1},{1,2},{2,3},{3,4},{4,5},{5,6},{6,7},{8,9},{9,10},{10,11},{11... | collective-permute-start | bytes 5192 | tf_op jit(solution)/shard_map/ppermute | solution.py:116
  136.7 5.1 %collective-permute-start.7 = (f32[3,8,18]{2,1,0:T(8,128)S(1)}, f32[3,8,18]{2,1,0:T(8,128)S(1)}, u32[]{:S(2)}, u32[]{:S(2)}) collective-permute-start(f32[3,8,18]{2,1,0:T(8,128)S(1)} %bitcast.274), channel_id=1, source_target_pairs={{1,0},{2,1},{3,2},{4,3},{5,4},{6,5},{7,6},{9,8},{10,9},{11,10},{12... | collective-permute-start | bytes 5192 | tf_op jit(solution)/shard_map/ppermute | solution.py:119

commit v8 on v7

--- a/solution.py
+++ b/solution.py
@@ -194,13 +194,13 @@
     ) - master_along[:, None, :]
     weight = jnp.exp(-dist_sq / REACH_SQ)
     soft = gap_normal * (-1.0 / SOFT_GAP)
-    depth_soft = SOFT_GAP * (jnp.maximum(soft, 0.0) + jnp.log1p(jnp.exp(-jnp.abs(soft))))
+    depth_soft = SOFT_GAP * jnp.log(1.0 + jnp.exp(soft))
     push_force = (
         slave[:, 6, :, None]
         * master[:, 9, None, :]
         * weight
         * depth_soft
-        * (1.0 + DAMPING * jnp.tanh(-closing))
+        * ((1.0 - DAMPING) + (2.0 * DAMPING) / (1.0 + jnp.exp(2.0 * closing)))
     )
     slave_force = jnp.stack(
         [

time: 146 us -> 146 us (level)
  no operation moved by 1% of the time
where the time goes in v8:
time: 146 us; the launch traced here: 144 us
  other arithmetic  47.7 us (33%)
  starting transfers between devices  35.3 us (24%)
  Pallas kernels  32.6 us (22%)
  local copies, waits for them, and re-layouts  16.6 us (11%)
  waiting for transfers between devices  9.42 us (6%)
    reduce_sum x2, other arithmetic, contact_pairs(): reaction = jnp.sum(push_force, axis=1)  34.9 us
    pallas_call x2, Pallas kernels, node_gather(): pl.pallas_call(gather_kernel, grid=(padded_count // TILE,), in_specs=[pl....  19.2 us
    pallas_call x2, Pallas kernels, node_scatter_add(): pl.pallas_call(scatter_kernel, grid=(padded_count // TILE,), in_specs=[pl...  13.4 us
    ppermute x4, starting transfers between devices, padded_2(): lax.ppermute(lax.index_in_dim(block, block.shape[dim] - 1, axis=dim, keep...  11.5 us
    ppermute x4, starting transfers between devices, padded_2(): lax.ppermute(lax.index_in_dim(block, 0, axis=dim, keepdims=False), axis,...  10.9 us
    all_to_all x1, starting transfers between devices, on_device(): lax.all_to_all(forces.reshape(devices, slot_depth, 3, seg_width), ('gx',...  6.6 us
    all_to_all x1, starting transfers between devices, on_device(): lax.all_to_all(outgoing.reshape(devices, slot_depth, 8, seg_width), ('gx'...  6.29 us
    all_to_all x1, waiting for transfers between devices, on_device(): lax.all_to_all(forces.reshape(devices, slot_depth, 3, seg_width), ('gx',...  5.65 us
  transfers between devices with their start and end apart: 10, of which 3 were waited for; matrix products, arithmetic and copies ran while one was open for 12% of the time, Pallas kernels for 16%

profile of v8, /device:TPU:9, one launch (start us, length us, event | category | flops | bytes accessed | tf_op | source)
XLA Modules:
  0.0 144.4 jit_solution(6240881749930637367)
XLA Ops:
  0.6 1.3 copy.254
  1.9 1.1 copy_bitcast_fusion
  3.1 3.8 %collective-permute-start = (f32[6,8,256]{2,1,0:T(8,128)S(1)}, f32[6,8,256]{2,1,0:T(8,128)S(1)}, u32[]{:S(2)}, u32[]{:S(2)}) collective-permute-start(f32[6,8,256]{2,1,0:T(8,128)S(1)} %get-tuple-element.99), channel_id=1, source_target_pairs={{0,8},{8,16},{16,24},{1,9},{9,17},{17,25},{2,10},{10,18},{18,26},{... | collective-permute-start | bytes 147464 | tf_op jit(solution)/shard_map/ppermute | solution.py:116
  7.0 1.9 %collective-permute-start.1 = (f32[6,8,256]{2,1,0:T(8,128)S(1)}, f32[6,8,256]{2,1,0:T(8,128)S(1)}, u32[]{:S(2)}, u32[]{:S(2)}) collective-permute-start(f32[6,8,256]{2,1,0:T(8,128)S(1)} %get-tuple-element.100), channel_id=1, source_target_pairs={{8,0},{16,8},{24,16},{9,1},{17,9},{25,17},{10,2},{18,10},{26,18},{... | collective-permute-start | bytes 147464 | tf_op jit(solution)/shard_map/ppermute | solution.py:119
  9.4 0.9 copy.269
  10.6 14.4 %shard_map.149 = f32[3,16384]{1,0:T(4,128)} custom-call(s32[1,16384]{1,0:T(1,128)} %bitcast.250, f32[384,256]{1,0:T(8,128)} %bitcast.235), custom_call_target="tpu_custom_call" | custom-call | tf_op jit(solution)/shard_map/pallas_call | solution.py:73
  24.9 1.1 copy_add_fusion
  26.4 1.2 pad_maximum_fusion.3
  27.6 0.8 gather_fusion
  28.4 1.2 select_select_fusion
  29.7 6.3 %all-to-all-start = ((f32[32,5,8,128]{3,2,1,0:T(8,128)}), f32[32,5,8,128]{3,2,1,0:T(8,128)S(1)}, u32[]{:S(2)}, u32[]{:S(2)}) async-start(f32[32,5,8,128]{3,2,1,0:T(8,128)} %select_select_fusion), calls=%async_computation | async-start | bytes 1310720 | tf_op jit(solution)/shard_map/all_to_all | solution.py:291
  36.0 4.8 %shard_map.150 = f32[3,4096]{1,0:T(4,128)} custom-call(s32[1,4096]{1,0:T(1,128)} %bitcast.265, f32[384,256]{1,0:T(8,128)} %bitcast.236), custom_call_target="tpu_custom_call" | custom-call | tf_op jit(solution)/shard_map/pallas_call | solution.py:73
  40.8 0.9 copy_add_fusion.1
  42.5 3.1 %collective-permute-start.2 = (f32[6,8,18]{2,1,0:T(8,128)S(1)}, f32[6,8,18]{2,1,0:T(8,128)S(1)}, u32[]{:S(2)}, u32[]{:S(2)}) collective-permute-start(f32[6,8,18]{2,1,0:T(8,128)S(1)} %bitcast.267), channel_id=1, source_target_pairs={{0,1},{1,2},{2,3},{3,4},{4,5},{5,6},{6,7},{8,9},{9,10},{10,11},{11... | collective-permute-start | bytes 10376 | tf_op jit(solution)/shard_map/ppermute | solution.py:116
  46.0 3.1 %collective-permute-start.3 = (f32[6,8,18]{2,1,0:T(8,128)S(1)}, f32[6,8,18]{2,1,0:T(8,128)S(1)}, u32[]{:S(2)}, u32[]{:S(2)}) collective-permute-start(f32[6,8,18]{2,1,0:T(8,128)S(1)} %bitcast.269), channel_id=1, source_target_pairs={{1,0},{2,1},{3,2},{4,3},{5,4},{6,5},{7,6},{9,8},{10,9},{11,10},{12... | collective-permute-start | bytes 10376 | tf_op jit(solution)/shard_map/ppermute | solution.py:119
  57.0 36.7 %while.12 = (s32[]{:T(128)}, f32[2,80,3,128]{3,1,2,0:T(8,128)}, f32[2,80,128]{2,1,0:T(8,128)}, f32[2,80,7,128]{3,1,0,2:T(8,128)S(1)}, f32[2,80,10,128]{3,1,2,0:T(8,128)S(1)}, /*index=5*/s32[]{:T(128)}) while((s32[]{:T(128)}, f32[2,80,3,128]{3,1,2,0:T(8,128)}, f32[2,80,128]{2,1,0:T(8,128)}, f32[2,80,7,128]{3,1,0,2:T(8,128)S(1)}, ...), condition=%wide.region_8.9_spmd, body=%wide.region_3.8_spmd.sunk | while | flops 49879040 | bytes 5776009 | solution.py:308
  57.2 17.4 %fusion.91 = (f32[80,128]{1,0:T(8,128)S(1)}, f32[80,128]{1,0:T(8,128)S(1)}, f32[80,128]{1,0:T(8,128)S(1)}, f32[80,128]{1,0:T(8,128)S(1)}) fusion(f32[80,128]{1,0:T(8,128)S(1)} %get-tuple-element.164, f32[80,128]{1,0:T(8,128)S(1)} %get-tuple-element.165, f32[80,128]{1,0:T(8,128)S(1)} %get-tuple-element.166, f32[80,128]{1,0:T(8,128)S(1)} %get-tuple-element.167, ...), kind=kLoop, calls=%fused_computation.51.clone.1 | loop fusion | flops 49766400 | bytes 778240 | tf_op jit(solution)/shard_map/while/body/eval_jaxpr/reduce_sum | solution.py:213
  75.5 17.4 %fusion.91 = (f32[80,128]{1,0:T(8,128)S(1)}, f32[80,128]{1,0:T(8,128)S(1)}, f32[80,128]{1,0:T(8,128)S(1)}, f32[80,128]{1,0:T(8,128)S(1)}) fusion(f32[80,128]{1,0:T(8,128)S(1)} %get-tuple-element.164, f32[80,128]{1,0:T(8,128)S(1)} %get-tuple-element.165, f32[80,128]{1,0:T(8,128)S(1)} %get-tuple-element.166, f32[80,128]{1,0:T(8,128)S(1)} %get-tuple-element.167, ...), kind=kLoop, calls=%fused_computation.51.clone.1 | loop fusion | flops 49766400 | bytes 778240 | tf_op jit(solution)/shard_map/while/body/eval_jaxpr/reduce_sum | solution.py:213
  93.7 1.8 %copy.297 = f32[2,80,3,128]{3,2,1,0:T(4,128)} copy(f32[2,80,3,128]{3,1,2,0:T(8,128)} %get-tuple-element.31) | data formatting | bytes 491520 | tf_op jit(solution)/shard_map/reshape;reshape | solution.py:326
  95.5 6.6 %all-to-all-start.1 = ((f32[32,5,3,128]{3,2,1,0:T(4,128)}), f32[32,5,3,128]{3,2,1,0:T(4,128)S(1)}, u32[]{:S(2)}, u32[]{:S(2)}) async-start(f32[32,5,3,128]{3,2,1,0:T(4,128)} %bitcast.69), calls=%async_computation.1 | async-start | bytes 655360 | tf_op jit(solution)/shard_map/all_to_all | solution.py:325
  102.2 1.2 convolution_negate_fusion
  104.0 3.6 %shard_map.151 = f32[384,256]{1,0:T(8,128)} custom-call(s32[1,4096]{1,0:T(1,128)} %bitcast.266, f32[3,4096]{1,0:T(4,128)} %bitcast.249), custom_call_target="tpu_custom_call" | custom-call | tf_op jit(solution)/shard_map/pallas_call | solution.py:91
  107.6 5.7 %all-to-all-done.1 = f32[32,5,3,128]{3,2,1,0:T(4,128)S(1)} async-done(((f32[32,5,3,128]{3,2,1,0:T(4,128)}), f32[32,5,3,128]{3,2,1,0:T(4,128)S(1)}, u32[]{:S(2)}, u32[]{:S(2)}) %all-to-all-start.1) | async-done | bytes 245792 | tf_op jit(solution)/shard_map/all_to_all | solution.py:325
  114.1 0.9 select_bitcast_fusion.force_ref
  115.0 9.8 %shard_map.152 = f32[384,256]{1,0:T(8,128)} custom-call(s32[1,16384]{1,0:T(1,128)} %bitcast.251, f32[3,16384]{1,0:T(4,128)} %select_bitcast_fusion.force_ref), custom_call_target="tpu_custom_call" | custom-call | tf_op jit(solution)/shard_map/pallas_call | solution.py:91
  124.8 1.1 add.284
  126.7 2.5 %collective-permute-start.4 = (f32[3,8,256]{2,1,0:T(8,128)S(1)}, f32[3,8,256]{2,1,0:T(8,128)S(1)}, u32[]{:S(2)}, u32[]{:S(2)}) collective-permute-start(f32[3,8,256]{2,1,0:T(8,128)S(1)} %get-tuple-element.105), channel_id=1, source_target_pairs={{0,8},{8,16},{16,24},{1,9},{9,17},{17,25},{2,10},{10,18},{18,26},{... | collective-permute-start | bytes 73736 | tf_op jit(solution)/shard_map/ppermute | solution.py:116
  129.2 1.9 %collective-permute-start.5 = (f32[3,8,256]{2,1,0:T(8,128)S(1)}, f32[3,8,256]{2,1,0:T(8,128)S(1)}, u32[]{:S(2)}, u32[]{:S(2)}) collective-permute-start(f32[3,8,256]{2,1,0:T(8,128)S(1)} %get-tuple-element.106), channel_id=1, source_target_pairs={{8,0},{16,8},{24,16},{9,1},{17,9},{25,17},{10,2},{18,10},{26,18},{... | collective-permute-start | bytes 73736 | tf_op jit(solution)/shard_map/ppermute | solution.py:119
  131.1 3.2 %collective-permute-done.5 = f32[3,8,256]{2,1,0:T(8,128)S(1)} collective-permute-done((f32[3,8,256]{2,1,0:T(8,128)S(1)}, f32[3,8,256]{2,1,0:T(8,128)S(1)}, u32[]{:S(2)}, u32[]{:S(2)}) %collective-permute-start.5) | collective-permute-done | bytes 24608 | tf_op jit(solution)/shard_map/ppermute | solution.py:119
  134.8 2.2 %collective-permute-start.6 = (f32[3,8,18]{2,1,0:T(8,128)S(1)}, f32[3,8,18]{2,1,0:T(8,128)S(1)}, u32[]{:S(2)}, u32[]{:S(2)}) collective-permute-start(f32[3,8,18]{2,1,0:T(8,128)S(1)} %bitcast.272), channel_id=1, source_target_pairs={{0,1},{1,2},{2,3},{3,4},{4,5},{5,6},{6,7},{8,9},{9,10},{10,11},{11... | collective-permute-start | bytes 5192 | tf_op jit(solution)/shard_map/ppermute | solution.py:116
  137.2 4.0 %collective-permute-start.7 = (f32[3,8,18]{2,1,0:T(8,128)S(1)}, f32[3,8,18]{2,1,0:T(8,128)S(1)}, u32[]{:S(2)}, u32[]{:S(2)}) collective-permute-start(f32[3,8,18]{2,1,0:T(8,128)S(1)} %bitcast.274), channel_id=1, source_target_pairs={{1,0},{2,1},{3,2},{4,3},{5,4},{6,5},{7,6},{9,8},{10,9},{11,10},{12... | collective-permute-start | bytes 5192 | tf_op jit(solution)/shard_map/ppermute | solution.py:119
  141.2 0.9 copy.295
  (144 shorter events, 16.7 us)
Async XLA Ops:
  0.6 8.3 %copy-start = (f32[3,8,16,256]{3,2,1,0:T(8,128)S(1)}, f32[3,8,16,256]{3,2,1,0:T(8,128)}, u32[]{:S(2)}) copy-start(f32[3,8,16,256]{3,2,1,0:T(8,128)} %param.16) | copy-start | bytes 1179652
  1.9 7.0 %copy-start.16 = (s32[128,1]{0,1:T(1,128)S(1)}, s32[128,1]{0,1:T(1,128)}, u32[]{:S(2)}) copy-start(s32[128,1]{0,1:T(1,128)} %param.24) | copy-start | bytes 1540
  3.1 7.2 %copy-start.17 = (s32[128]{0:T(128)S(1)}, s32[128]{0:T(128)}, u32[]{:S(2)}) copy-start(s32[128]{0:T(128)} %param.25) | copy-start | bytes 1540
  3.1 21.8 %copy-start.9 = (f32[128,3,128]{2,0,1:T(8,128)S(1)}, f32[128,3,128]{2,0,1:T(8,128)}, u32[]{:S(2)}) copy-start(f32[128,3,128]{2,0,1:T(8,128)} %param.20) | copy-start | bytes 589828
  3.1 38.6 %collective-permute-start = (f32[6,8,256]{2,1,0:T(8,128)S(1)}, f32[6,8,256]{2,1,0:T(8,128)S(1)}, u32[]{:S(2)}, u32[]{:S(2)}) collective-permute-start(f32[6,8,256]{2,1,0:T(8,128)S(1)} %get-tuple-element.99), channel_id=1, source_target_pairs={{0,8},{8,16},{16,24},{1,9},{9,17},{17,25},{2,10},{10,18},{18,26},{... | collective-permute-start | bytes 147464 | tf_op jit(solution)/shard_map/ppermute | solution.py:116
  7.0 34.8 %collective-permute-start.1 = (f32[6,8,256]{2,1,0:T(8,128)S(1)}, f32[6,8,256]{2,1,0:T(8,128)S(1)}, u32[]{:S(2)}, u32[]{:S(2)}) collective-permute-start(f32[6,8,256]{2,1,0:T(8,128)S(1)} %get-tuple-element.100), channel_id=1, source_target_pairs={{8,0},{16,8},{24,16},{9,1},{17,9},{25,17},{10,2},{18,10},{26,18},{... | collective-permute-start | bytes 147464 | tf_op jit(solution)/shard_map/ppermute | solution.py:119
  8.9 17.1 %copy-start.11 = (f32[128,128]{1,0:T(8,128)S(1)}, f32[128,128]{1,0:T(8,128)}, u32[]{:S(2)}) copy-start(f32[128,128]{1,0:T(8,128)} %param.21) | copy-start | bytes 196612
  8.9 17.1 %copy-start.15 = (s32[128]{0:T(128)S(1)}, s32[128]{0:T(128)}, u32[]{:S(2)}) copy-start(s32[128]{0:T(128)} %param.22) | copy-start | bytes 1540
  28.4 7.6 %copy-start.13 = (f32[32,2,128]{2,1,0:T(2,128)S(1)}, f32[32,2,128]{2,1,0:T(2,128)}, u32[]{:S(2)}) copy-start(f32[32,2,128]{2,1,0:T(2,128)} %param.27) | copy-start | bytes 98308
  28.4 12.4 %copy-start.12 = (f32[32,3,128]{2,0,1:T(8,128)S(1)}, f32[32,3,128]{2,0,1:T(8,128)}, u32[]{:S(2)}) copy-start(f32[32,3,128]{2,0,1:T(8,128)} %param.26) | copy-start | bytes 147460
  29.7 25.8 %all-to-all-start = ((f32[32,5,8,128]{3,2,1,0:T(8,128)}), f32[32,5,8,128]{3,2,1,0:T(8,128)S(1)}, u32[]{:S(2)}, u32[]{:S(2)}) async-start(f32[32,5,8,128]{3,2,1,0:T(8,128)} %select_select_fusion), calls=%async_computation | async-start | bytes 1310720 | tf_op jit(solution)/shard_map/all_to_all | solution.py:291
  41.8 7.2 %copy-start.10 = (f32[8,16,256]{2,1,0:T(8,128)S(1)}, f32[8,16,256]{2,1,0:T(8,128)}, u32[]{:S(2)}) copy-start(f32[8,16,256]{2,1,0:T(8,128)} %param.19) | copy-start | bytes 393220
  41.9 8.0 %copy-start.3 = (f32[3,4096]{1,0:T(4,128)S(1)}, f32[3,4096]{1,0:T(4,128)}, u32[]{:S(2)}) copy-start(f32[3,4096]{1,0:T(4,128)} %shard_map.150) | copy-start | bytes 147460
  41.9 7.9 %copy-start.14 = (f32[32,128]{1,0:T(8,128)S(1)}, f32[32,128]{1,0:T(8,128)}, u32[]{:S(2)}) copy-start(f32[32,128]{1,0:T(8,128)} %param.28) | copy-start | bytes 49156
  42.5 7.7 %collective-permute-start.2 = (f32[6,8,18]{2,1,0:T(8,128)S(1)}, f32[6,8,18]{2,1,0:T(8,128)S(1)}, u32[]{:S(2)}, u32[]{:S(2)}) collective-permute-start(f32[6,8,18]{2,1,0:T(8,128)S(1)} %bitcast.267), channel_id=1, source_target_pairs={{0,1},{1,2},{2,3},{3,4},{4,5},{5,6},{6,7},{8,9},{9,10},{10,11},{11... | collective-permute-start | bytes 10376 | tf_op jit(solution)/shard_map/ppermute | solution.py:116
  46.0 5.2 %collective-permute-start.3 = (f32[6,8,18]{2,1,0:T(8,128)S(1)}, f32[6,8,18]{2,1,0:T(8,128)S(1)}, u32[]{:S(2)}, u32[]{:S(2)}) collective-permute-start(f32[6,8,18]{2,1,0:T(8,128)S(1)} %bitcast.269), channel_id=1, source_target_pairs={{1,0},{2,1},{3,2},{4,3},{5,4},{6,5},{7,6},{9,8},{10,9},{11,10},{12... | collective-permute-start | bytes 10376 | tf_op jit(solution)/shard_map/ppermute | solution.py:119
  57.2 17.5 %copy-start.7 = (f32[2,80,3,128]{3,1,2,0:T(8,128)S(1)}, f32[2,80,3,128]{3,1,2,0:T(8,128)}, u32[]{:S(2)}) copy-start(f32[2,80,3,128]{3,1,2,0:T(8,128)} %get-tuple-element.190) | copy-start | bytes 737284 | tf_op jit(solution)/shard_map/while
  74.7 0.7 copy-start.8
  75.5 17.5 %copy-start.7 = (f32[2,80,3,128]{3,1,2,0:T(8,128)S(1)}, f32[2,80,3,128]{3,1,2,0:T(8,128)}, u32[]{:S(2)}) copy-start(f32[2,80,3,128]{3,1,2,0:T(8,128)} %get-tuple-element.190) | copy-start | bytes 737284 | tf_op jit(solution)/shard_map/while
  93.0 0.7 copy-start.8
  93.7 8.5 %copy-start.2 = (f32[8,17,256]{2,0,1:T(8,128)S(1)}, f32[8,17,256]{2,0,1:T(8,128)}, u32[]{:S(2)}) copy-start(f32[8,17,256]{2,0,1:T(8,128)} %fusion.69) | copy-start | bytes 417796
  95.5 17.8 %all-to-all-start.1 = ((f32[32,5,3,128]{3,2,1,0:T(4,128)}), f32[32,5,3,128]{3,2,1,0:T(4,128)S(1)}, u32[]{:S(2)}, u32[]{:S(2)}) async-start(f32[32,5,3,128]{3,2,1,0:T(4,128)} %bitcast.69), calls=%async_computation.1 | async-start | bytes 655360 | tf_op jit(solution)/shard_map/all_to_all | solution.py:325
  107.6 17.1 %copy-start.1 = (f32[384,256]{1,0:T(8,128)S(1)}, f32[384,256]{1,0:T(8,128)}, u32[]{:S(2)}) copy-start(f32[384,256]{1,0:T(8,128)} %shard_map.151) | copy-start | bytes 1179652
  124.8 1.4 copy-start.4
  124.8 1.4 copy-start.5
  124.8 1.4 copy-start.6
  126.7 4.4 %collective-permute-start.4 = (f32[3,8,256]{2,1,0:T(8,128)S(1)}, f32[3,8,256]{2,1,0:T(8,128)S(1)}, u32[]{:S(2)}, u32[]{:S(2)}) collective-permute-start(f32[3,8,256]{2,1,0:T(8,128)S(1)} %get-tuple-element.105), channel_id=1, source_target_pairs={{0,8},{8,16},{16,24},{1,9},{9,17},{17,25},{2,10},{10,18},{18,26},{... | collective-permute-start | bytes 73736 | tf_op jit(solution)/shard_map/ppermute | solution.py:116
  129.2 5.1 %collective-permute-start.5 = (f32[3,8,256]{2,1,0:T(8,128)S(1)}, f32[3,8,256]{2,1,0:T(8,128)S(1)}, u32[]{:S(2)}, u32[]{:S(2)}) collective-permute-start(f32[3,8,256]{2,1,0:T(8,128)S(1)} %get-tuple-element.106), channel_id=1, source_target_pairs={{8,0},{16,8},{24,16},{9,1},{17,9},{25,17},{10,2},{18,10},{26,18},{... | collective-permute-start | bytes 73736 | tf_op jit(solution)/shard_map/ppermute | solution.py:119
  134.8 7.3 %collective-permute-start.6 = (f32[3,8,18]{2,1,0:T(8,128)S(1)}, f32[3,8,18]{2,1,0:T(8,128)S(1)}, u32[]{:S(2)}, u32[]{:S(2)}) collective-permute-start(f32[3,8,18]{2,1,0:T(8,128)S(1)} %bitcast.272), channel_id=1, source_target_pairs={{0,1},{1,2},{2,3},{3,4},{4,5},{5,6},{6,7},{8,9},{9,10},{10,11},{11... | collective-permute-start | bytes 5192 | tf_op jit(solution)/shard_map/ppermute | solution.py:116
  137.2 5.2 %collective-permute-start.7 = (f32[3,8,18]{2,1,0:T(8,128)S(1)}, f32[3,8,18]{2,1,0:T(8,128)S(1)}, u32[]{:S(2)}, u32[]{:S(2)}) collective-permute-start(f32[3,8,18]{2,1,0:T(8,128)S(1)} %bitcast.274), channel_id=1, source_target_pairs={{1,0},{2,1},{3,2},{4,3},{5,4},{6,5},{7,6},{9,8},{10,9},{11,10},{12... | collective-permute-start | bytes 5192 | tf_op jit(solution)/shard_map/ppermute | solution.py:119

commit v9 on v6

--- a/solution.py
+++ b/solution.py
@@ -184,16 +184,20 @@
     normal_z = master[:, 5, None, :]
     dist_sq = delta_x * delta_x + delta_y * delta_y + delta_z * delta_z
     gap_normal = normal_x * delta_x + normal_y * delta_y + normal_z * delta_z
+    master_along = (
+        master[:, 3] * master[:, 6] + master[:, 4] * master[:, 7] + master[:, 5] * master[:, 8]
+    )
     closing = (
         normal_x * slave[:, 3, :, None]
         + normal_y * slave[:, 4, :, None]
         + normal_z * slave[:, 5, :, None]
-    ) - master[:, 6, None, :]
+    ) - master_along[:, None, :]
     weight = jnp.exp(-dist_sq / REACH_SQ)
-    depth_soft = SOFT_GAP * jax.nn.softplus(-gap_normal / SOFT_GAP)
+    soft = gap_normal * (-1.0 / SOFT_GAP)
+    depth_soft = SOFT_GAP * (jnp.maximum(soft, 0.0) + jnp.log1p(jnp.exp(-jnp.abs(soft))))
     push_force = (
         slave[:, 6, :, None]
-        * master[:, 7, None, :]
+        * master[:, 9, None, :]
         * weight
         * depth_soft
         * (1.0 + DAMPING * jnp.tanh(-closing))
@@ -263,19 +267,36 @@
     slave = jnp.concatenate(
         [slave_pos + TIME_STEP * slave_vel, slave_vel, area_live[:, None, :]], axis=1
     )
+    owners = pair_owner[:, 0]
+    positions = jnp.arange(block_total, dtype=jnp.int32)
+    earlier = (owners[:, None] == owners[None, :]) & (positions[None, :] < positions[:, None])
+    slot_index = jnp.sum(earlier.astype(jnp.int32), axis=1)
+    target_slot = owners * slot_depth + slot_index
+    item_total = devices * slot_depth
+    slot_hit = target_slot[None, :] == jnp.arange(item_total, dtype=jnp.int32)[:, None]
+    source = jnp.sum(jnp.where(slot_hit, positions[None, :], 0), axis=1)
+    filled = jnp.any(slot_hit, axis=1)
+    request = jnp.where(filled, jnp.take(pair_master, source, axis=0), 0)
+    asked = lax.all_to_all(
+        request.reshape(devices, slot_depth),
+        ("gx", "gy"),
+        split_axis=0,
+        concat_axis=0,
+        tiled=True,
+    ).reshape(item_total)
     normals = master_normals(master_tilt)
-    master_rows = jnp.concatenate(
-        [
-            master_cent + TIME_STEP * master_vel,
-            normals,
-            jnp.sum(normals * master_vel, axis=1, keepdims=True),
-            master_stiff[:, None, :],
-        ],
+    master_data = jnp.concatenate(
+        [master_cent + TIME_STEP * master_vel, normals, master_vel, master_stiff[:, None, :]],
         axis=1,
     )
-    all_master = lax.all_gather(master_rows, ("gx", "gy"), axis=0, tiled=True)
-    target = pair_owner[:, 0] * master_total + pair_master
-    paired = jnp.take(all_master, target, axis=0)
+    reply = lax.all_to_all(
+        jnp.take(master_data, asked, axis=0).reshape(devices, slot_depth, 10, seg_width),
+        ("gx", "gy"),
+        split_axis=0,
+        concat_axis=0,
+        tiled=True,
+    )
+    paired = jnp.take(reply.reshape(item_total, 10, seg_width), target_slot, axis=0)
     group_size = block_total // 2 if block_total % 2 == 0 else block_total
 
     def per_group(pairing):
@@ -285,20 +306,29 @@
         per_group,
         (
             slave.reshape(block_total // group_size, group_size, 7, seg_width),
-            paired.reshape(block_total // group_size, group_size, 8, seg_width),
+            paired.reshape(block_total // group_size, group_size, 10, seg_width),
         ),
     )
     slave_force = forces.reshape(block_total, 3, seg_width)
     reaction = reaction.reshape(block_total, seg_width)
-    onehot = (
-        target[None, :] == jnp.arange(devices * master_total, dtype=jnp.int32)[:, None]
-    ).astype(jnp.float32)
-    partial = jnp.dot(onehot, reaction, precision=lax.Precision.HIGHEST)
-    master_sum = lax.psum_scatter(partial, ("gx", "gy"), scatter_dimension=0, tiled=True)
+    back = lax.all_to_all(
+        jnp.where(filled[:, None], jnp.take(reaction, source, axis=0), 0.0).reshape(
+            devices, slot_depth, seg_width
+        ),
+        ("gx", "gy"),
+        split_axis=0,
+        concat_axis=0,
+        tiled=True,
+    ).reshape(item_total, seg_width)
+    slave_contact = node_scatter_add(
+        slave_force.transpose(1, 0, 2).reshape(3, -1), slave_node.reshape(-1), node_total
+    )
+    onehot = (asked[:, None] == jnp.arange(master_total, dtype=jnp.int32)[None, :]).astype(
+        jnp.float32
+    )
+    master_sum = jnp.dot(onehot.T, back, precision=lax.Precision.HIGHEST)
     master_force = -master_sum[:, None, :] * normals
-    contact = node_scatter_add(
-        slave_force.transpose(1, 0, 2).reshape(3, -1), slave_node.reshape(-1), node_total
-    ) + node_scatter_add(
+    contact = slave_contact + node_scatter_add(
         master_force.transpose(1, 0, 2).reshape(3, -1), master_node.reshape(-1), node_total
     )
     contact_field = contact.reshape(3, layers, row_cells, col_cells)

time: 279 us -> 171 us (0.61)
  waiting for transfers between devices: 145 us -> 30.1 us
  between operations: 14.6 us -> 1.62 us
  local copies, waits for them, and re-layouts: 16.2 us -> 25.9 us
  starting transfers between devices: 30.1 us -> 39.7 us
    reduce_scatter x1 -> x0, waiting for transfers between devices: 111 us -> none  [on_device(): lax.psum_scatter(partial, ('gx', 'gy'), scatter_dimension=0, tiled=True)]
    all_gather x1 -> x0, waiting for transfers between devices: 28.9 us -> none  [on_device(): all_master = lax.all_gather(master_rows, ('gx', 'gy'), axis=0, tiled=True)]
    all_to_all x0 -> x3, waiting for transfers between devices: none -> 26.6 us  [the longest x1 26.6 us: on_device(): lax.all_to_all(jnp.take(master_data, asked, axis=0).reshape(devices, slot...]
    all_to_all x0 -> x3, starting transfers between devices: none -> 16.4 us  [the longest x1 6.32 us: on_device(): lax.all_to_all(request.reshape(devices, slot_depth), ('gx', 'gy'), split_...]
    ppermute x4, starting transfers between devices: 18.8 us -> 13.4 us  [padded_2(): lax.ppermute(lax.index_in_dim(block, block.shape[dim] - 1, axis=dim, keep...]
    unnamed x22 -> x68, local copies, waits for them, and re-layouts: 4.42 us -> 6.96 us
  transfers between devices with their start and end apart: 10 -> 11, of which waited for: 4 -> 3; matrix products, arithmetic and copies ran while one was open for 3% -> 12% of each run, Pallas kernels for 9% -> 17%
where the time goes in v9:
time: 171 us; the launch traced here: 169 us
  starting transfers between devices  39.7 us (23%)
  other arithmetic  38.6 us (23%)
  Pallas kernels  32.5 us (19%)
  waiting for transfers between devices  30.1 us (18%)
  local copies, waits for them, and re-layouts  25.9 us (15%)
    reduce_sum x2, other arithmetic, contact_pairs(): reaction = jnp.sum(push_force, axis=1)  27.2 us
    all_to_all x1, waiting for transfers between devices, on_device(): lax.all_to_all(jnp.take(master_data, asked, axis=0).reshape(devices, slot...  26.6 us
    pallas_call x2, Pallas kernels, node_gather(): pl.pallas_call(gather_kernel, grid=(padded_count // TILE,), in_specs=[pl....  19.1 us
    ppermute x4, starting transfers between devices, padded_2(): lax.ppermute(lax.index_in_dim(block, block.shape[dim] - 1, axis=dim, keep...  13.4 us
    pallas_call x2, Pallas kernels, node_scatter_add(): pl.pallas_call(scatter_kernel, grid=(padded_count // TILE,), in_specs=[pl...  13.4 us
    ppermute x4, starting transfers between devices, padded_2(): lax.ppermute(lax.index_in_dim(block, 0, axis=dim, keepdims=False), axis,...  9.96 us
    unnamed x68, local copies, waits for them, and re-layouts  6.96 us
    all_to_all x1, starting transfers between devices, on_device(): lax.all_to_all(request.reshape(devices, slot_depth), ('gx', 'gy'), split_...  6.32 us
  transfers between devices with their start and end apart: 11, of which 3 were waited for; matrix products, arithmetic and copies ran while one was open for 12% of the time, Pallas kernels for 17%

profile of v9, /device:TPU:9, one launch (start us, length us, event | category | flops | bytes accessed | tf_op | source)
XLA Modules:
  0.0 168.8 jit_solution(12109922433089252381)
XLA Ops:
  0.7 1.2 copy.263
  1.9 1.2 copy_bitcast_fusion.2
  3.2 3.8 %collective-permute-start = (f32[6,8,256]{2,1,0:T(8,128)S(1)}, f32[6,8,256]{2,1,0:T(8,128)S(1)}, u32[]{:S(2)}, u32[]{:S(2)}) collective-permute-start(f32[6,8,256]{2,1,0:T(8,128)S(1)} %get-tuple-element.96), channel_id=1, source_target_pairs={{0,8},{8,16},{16,24},{1,9},{9,17},{17,25},{2,10},{10,18},{18,26},{... | collective-permute-start | bytes 147464 | tf_op jit(solution)/shard_map/ppermute | solution.py:116
  7.0 1.9 %collective-permute-start.1 = (f32[6,8,256]{2,1,0:T(8,128)S(1)}, f32[6,8,256]{2,1,0:T(8,128)S(1)}, u32[]{:S(2)}, u32[]{:S(2)}) collective-permute-start(f32[6,8,256]{2,1,0:T(8,128)S(1)} %get-tuple-element.97), channel_id=1, source_target_pairs={{8,0},{16,8},{24,16},{9,1},{17,9},{25,17},{10,2},{18,10},{26,18},{... | collective-permute-start | bytes 147464 | tf_op jit(solution)/shard_map/ppermute | solution.py:119
  10.1 1.5 gather_fusion
  12.5 6.3 %all-to-all-start = ((s32[32,1,5]{2,1,0:T(1,128)}), s32[32,1,5]{2,1,0:T(1,128)S(1)}, u32[]{:S(2)}, u32[]{:S(2)}) async-start(s32[32,1,5]{2,1,0:T(1,128)} %bitcast.52), calls=%async_computation | async-start | bytes 32768 | tf_op jit(solution)/shard_map/all_to_all | solution.py:280
  20.0 4.8 %shard_map.150 = f32[3,4096]{1,0:T(4,128)} custom-call(s32[1,4096]{1,0:T(1,128)} %bitcast.274, f32[384,256]{1,0:T(8,128)} %bitcast.242), custom_call_target="tpu_custom_call" | custom-call | tf_op jit(solution)/shard_map/pallas_call | solution.py:73
  24.8 14.3 %shard_map.149 = f32[3,16384]{1,0:T(4,128)} custom-call(s32[1,16384]{1,0:T(1,128)} %bitcast.258, f32[384,256]{1,0:T(8,128)} %bitcast.243), custom_call_target="tpu_custom_call" | custom-call | tf_op jit(solution)/shard_map/pallas_call | solution.py:73
  46.8 1.0 copy.264
  47.8 3.1 %collective-permute-start.2 = (f32[6,8,18]{2,1,0:T(8,128)}, f32[6,8,18]{2,1,0:T(8,128)}, u32[]{:S(2)}, u32[]{:S(2)}) collective-permute-start(f32[6,8,18]{2,1,0:T(8,128)} %bitcast.28), channel_id=1, source_target_pairs={{0,1},{1,2},{2,3},{3,4},{4,5},{5,6},{6,7},{8,9},{9,10},{10,11},{11... | collective-permute-start | bytes 10376 | tf_op jit(solution)/shard_map/ppermute | solution.py:116
  51.0 1.0 copy.265
  51.9 3.0 %collective-permute-start.3 = (f32[6,8,18]{2,1,0:T(8,128)}, f32[6,8,18]{2,1,0:T(8,128)}, u32[]{:S(2)}, u32[]{:S(2)}) collective-permute-start(f32[6,8,18]{2,1,0:T(8,128)} %bitcast.30), channel_id=1, source_target_pairs={{1,0},{2,1},{3,2},{4,3},{5,4},{6,5},{7,6},{9,8},{10,9},{11,10},{12... | collective-permute-start | bytes 10376 | tf_op jit(solution)/shard_map/ppermute | solution.py:119
  56.2 1.2 copy.288
  57.4 6.1 %all-to-all-start.1 = ((f32[32,5,10,128]{3,1,2,0:T(8,128)}), f32[32,5,10,128]{3,1,2,0:T(8,128)S(1)}, u32[]{:S(2)}, u32[]{:S(2)}) async-start(f32[32,5,10,128]{3,1,2,0:T(8,128)} %copy.288), calls=%async_computation.1 | async-start | bytes 2621440 | tf_op jit(solution)/shard_map/all_to_all | solution.py:292
  63.5 1.1 copy.266
  64.6 1.1 copy.267
  65.8 1.4 pad_maximum_fusion
  68.6 26.6 %all-to-all-done.1 = f32[32,5,10,128]{3,1,2,0:T(8,128)S(1)} async-done(((f32[32,5,10,128]{3,1,2,0:T(8,128)}), f32[32,5,10,128]{3,1,2,0:T(8,128)S(1)}, u32[]{:S(2)}, u32[]{:S(2)}) %all-to-all-start.1) | async-done | bytes 819232 | tf_op jit(solution)/shard_map/all_to_all | solution.py:292
  95.2 1.3 copy.307
  96.5 2.1 %gather_fusion.2 = f32[128,10,128]{2,1,0:T(8,128)S(1)} fusion(f32[160,10,128]{2,1,0:T(8,128)} %bitcast.240, s32[1024]{0:T(1024)} %pad_clamp_fusion), kind=kCustom, calls=%fused_computation.2 | custom fusion | bytes 1311232 | tf_op jit(solution)/shard_map/jit(_take)/gather | solution.py:299
  99.5 27.6 %while.12 = (s32[]{:T(128)}, f32[2,64,3,128]{3,1,0,2:T(8,128)S(1)}, f32[2,64,128]{2,1,0:T(8,128)S(1)}, f32[2,64,7,128]{3,1,0,2:T(8,128)S(1)}, f32[2,64,10,128]{3,1,2,0:T(8,128)S(1)}, /*index=5*/s32[]{:T(128)}) while((s32[]{:T(128)}, f32[2,64,3,128]{3,1,0,2:T(8,128)S(1)}, f32[2,64,128]{2,1,0:T(8,128)S(1)}, f32[2,64,7,128]{3,1,0,2:T(8,128)S(1)}, ...), condition=%wide.region_8.9_spmd, body=%wide.region_3.8_spmd.sunk | while | flops 42000384 | bytes 3047509 | solution.py:305
  99.6 13.6 %fusion.88 = (f32[64,128]{1,0:T(8,128)S(1)}, f32[64,128]{1,0:T(8,128)S(1)}, f32[64,128]{1,0:T(8,128)S(1)}, f32[64,128]{1,0:T(8,128)S(1)}) fusion(f32[64,128]{1,0:T(8,128)S(1)} %get-tuple-element.161, f32[64,128]{1,0:T(8,128)S(1)} %get-tuple-element.162, f32[64,128]{1,0:T(8,128)S(1)} %get-tuple-element.163, f32[64,128]{1,0:T(8,128)S(1)} %get-tuple-element.164, ...), kind=kLoop, calls=%fused_computation.48.clone.1 | loop fusion | flops 41910272 | bytes 622592 | tf_op jit(solution)/shard_map/while/body/eval_jaxpr/reduce_sum | solution.py:213
  113.4 13.6 %fusion.88 = (f32[64,128]{1,0:T(8,128)S(1)}, f32[64,128]{1,0:T(8,128)S(1)}, f32[64,128]{1,0:T(8,128)S(1)}, f32[64,128]{1,0:T(8,128)S(1)}) fusion(f32[64,128]{1,0:T(8,128)S(1)} %get-tuple-element.161, f32[64,128]{1,0:T(8,128)S(1)} %get-tuple-element.162, f32[64,128]{1,0:T(8,128)S(1)} %get-tuple-element.163, f32[64,128]{1,0:T(8,128)S(1)} %get-tuple-element.164, ...), kind=kLoop, calls=%fused_computation.48.clone.1 | loop fusion | flops 41910272 | bytes 622592 | tf_op jit(solution)/shard_map/while/body/eval_jaxpr/reduce_sum | solution.py:213
  128.7 4.0 %all-to-all-start.2 = ((f32[32,5,128]{2,1,0:T(8,128)}), f32[32,5,128]{2,1,0:T(8,128)S(1)}, u32[]{:S(2)}, u32[]{:S(2)}) async-start(f32[32,5,128]{2,1,0:T(8,128)} %select_select_fusion), calls=%async_computation.2 | async-start | bytes 262144 | tf_op jit(solution)/shard_map/all_to_all | solution.py:314
  133.6 9.8 %shard_map.151 = f32[384,256]{1,0:T(8,128)} custom-call(s32[1,16384]{1,0:T(1,128)} %bitcast.259, f32[3,16384]{1,0:T(4,128)} %bitcast.246), custom_call_target="tpu_custom_call" | custom-call | tf_op jit(solution)/shard_map/pallas_call | solution.py:91
  144.4 3.6 %shard_map.152 = f32[384,256]{1,0:T(8,128)} custom-call(s32[1,4096]{1,0:T(1,128)} %bitcast.275, f32[3,4096]{1,0:T(4,128)} %bitcast.257), custom_call_target="tpu_custom_call" | custom-call | tf_op jit(solution)/shard_map/pallas_call | solution.py:91
  148.0 1.2 add.299
  150.0 3.4 %collective-permute-start.4 = (f32[3,8,256]{2,1,0:T(8,128)S(1)}, f32[3,8,256]{2,1,0:T(8,128)S(1)}, u32[]{:S(2)}, u32[]{:S(2)}) collective-permute-start(f32[3,8,256]{2,1,0:T(8,128)S(1)} %get-tuple-element.102), channel_id=1, source_target_pairs={{0,8},{8,16},{16,24},{1,9},{9,17},{17,25},{2,10},{10,18},{18,26},{... | collective-permute-start | bytes 73736 | tf_op jit(solution)/shard_map/ppermute | solution.py:116
  153.4 1.9 %collective-permute-start.5 = (f32[3,8,256]{2,1,0:T(8,128)S(1)}, f32[3,8,256]{2,1,0:T(8,128)S(1)}, u32[]{:S(2)}, u32[]{:S(2)}) collective-permute-start(f32[3,8,256]{2,1,0:T(8,128)S(1)} %get-tuple-element.103), channel_id=1, source_target_pairs={{8,0},{16,8},{24,16},{9,1},{17,9},{25,17},{10,2},{18,10},{26,18},{... | collective-permute-start | bytes 73736 | tf_op jit(solution)/shard_map/ppermute | solution.py:119
  155.4 3.2 %collective-permute-done.5 = f32[3,8,256]{2,1,0:T(8,128)S(1)} collective-permute-done((f32[3,8,256]{2,1,0:T(8,128)S(1)}, f32[3,8,256]{2,1,0:T(8,128)S(1)}, u32[]{:S(2)}, u32[]{:S(2)}) %collective-permute-start.5) | collective-permute-done | bytes 24608 | tf_op jit(solution)/shard_map/ppermute | solution.py:119
  159.0 3.1 %collective-permute-start.6 = (f32[3,8,18]{2,1,0:T(8,128)S(1)}, f32[3,8,18]{2,1,0:T(8,128)S(1)}, u32[]{:S(2)}, u32[]{:S(2)}) collective-permute-start(f32[3,8,18]{2,1,0:T(8,128)S(1)} %bitcast.277), channel_id=1, source_target_pairs={{0,1},{1,2},{2,3},{3,4},{4,5},{5,6},{6,7},{8,9},{9,10},{10,11},{11... | collective-permute-start | bytes 5192 | tf_op jit(solution)/shard_map/ppermute | solution.py:116
  162.3 3.1 %collective-permute-start.7 = (f32[3,8,18]{2,1,0:T(8,128)S(1)}, f32[3,8,18]{2,1,0:T(8,128)S(1)}, u32[]{:S(2)}, u32[]{:S(2)}) collective-permute-start(f32[3,8,18]{2,1,0:T(8,128)S(1)} %bitcast.279), channel_id=1, source_target_pairs={{1,0},{2,1},{3,2},{4,3},{5,4},{6,5},{7,6},{9,8},{10,9},{11,10},{12... | collective-permute-start | bytes 5192 | tf_op jit(solution)/shard_map/ppermute | solution.py:119
  (174 shorter events, 22.5 us)
Async XLA Ops:
  0.6 9.4 %copy-start = (s32[128]{0:T(128)S(1)}, s32[128]{0:T(128)}, u32[]{:S(2)}) copy-start(s32[128]{0:T(128)} %param.25) | copy-start | bytes 1540
  0.6 8.3 %copy-start.30 = (s32[128,1]{0,1:T(1,128)S(1)}, s32[128,1]{0,1:T(1,128)}, u32[]{:S(2)}) copy-start(s32[128,1]{0,1:T(1,128)} %param.24) | copy-start | bytes 1540
  1.9 16.9 %copy-start.1 = (f32[3,8,16,256]{3,2,1,0:T(8,128)S(1)}, f32[3,8,16,256]{3,2,1,0:T(8,128)}, u32[]{:S(2)}) copy-start(f32[3,8,16,256]{3,2,1,0:T(8,128)} %param.16) | copy-start | bytes 1179652
  3.1 42.9 %copy-start.5 = (f32[1,8,16,256]{3,1,0,2:T(8,128)}, f32[1,8,16,256]{3,1,0,2:T(8,128)S(1)}, u32[]{:S(2)}) copy-start(f32[1,8,16,256]{3,1,0,2:T(8,128)S(1)} %get-tuple-element.109) | copy-start | bytes 393220
  3.1 42.9 %copy-start.7 = (f32[1,8,16,256]{3,1,0,2:T(8,128)}, f32[1,8,16,256]{3,1,0,2:T(8,128)S(1)}, u32[]{:S(2)}) copy-start(f32[1,8,16,256]{3,1,0,2:T(8,128)S(1)} %get-tuple-element.110) | copy-start | bytes 393220
  3.1 42.9 %copy-start.3 = (f32[1,8,16,256]{3,1,0,2:T(8,128)}, f32[1,8,16,256]{3,1,0,2:T(8,128)S(1)}, u32[]{:S(2)}) copy-start(f32[1,8,16,256]{3,1,0,2:T(8,128)S(1)} %broadcast_in_dim_broadcast_in_dim.3) | copy-start | bytes 393220
  3.1 15.9 %copy-start.25 = (f32[32,2,128]{2,1,0:T(2,128)S(1)}, f32[32,2,128]{2,1,0:T(2,128)}, u32[]{:S(2)}) copy-start(f32[32,2,128]{2,1,0:T(2,128)} %param.27) | copy-start | bytes 98308
  3.2 42.7 %collective-permute-start = (f32[6,8,256]{2,1,0:T(8,128)S(1)}, f32[6,8,256]{2,1,0:T(8,128)S(1)}, u32[]{:S(2)}, u32[]{:S(2)}) collective-permute-start(f32[6,8,256]{2,1,0:T(8,128)S(1)} %get-tuple-element.96), channel_id=1, source_target_pairs={{0,8},{8,16},{16,24},{1,9},{9,17},{17,25},{2,10},{10,18},{18,26},{... | collective-permute-start | bytes 147464 | tf_op jit(solution)/shard_map/ppermute | solution.py:116
  7.0 38.9 %collective-permute-start.1 = (f32[6,8,256]{2,1,0:T(8,128)S(1)}, f32[6,8,256]{2,1,0:T(8,128)S(1)}, u32[]{:S(2)}, u32[]{:S(2)}) collective-permute-start(f32[6,8,256]{2,1,0:T(8,128)S(1)} %get-tuple-element.97), channel_id=1, source_target_pairs={{8,0},{16,8},{24,16},{9,1},{17,9},{25,17},{10,2},{18,10},{26,18},{... | collective-permute-start | bytes 147464 | tf_op jit(solution)/shard_map/ppermute | solution.py:119
  12.5 31.2 %all-to-all-start = ((s32[32,1,5]{2,1,0:T(1,128)}), s32[32,1,5]{2,1,0:T(1,128)S(1)}, u32[]{:S(2)}, u32[]{:S(2)}) async-start(s32[32,1,5]{2,1,0:T(1,128)} %bitcast.52), calls=%async_computation | async-start | bytes 32768 | tf_op jit(solution)/shard_map/all_to_all | solution.py:280
  18.8 20.3 %copy-start.24 = (f32[32,3,128]{2,0,1:T(8,128)S(1)}, f32[32,3,128]{2,0,1:T(8,128)}, u32[]{:S(2)}) copy-start(f32[32,3,128]{2,0,1:T(8,128)} %param.26) | copy-start | bytes 147460
  18.8 21.2 %copy-start.15 = (f32[128,3,128]{2,0,1:T(8,128)S(1)}, f32[128,3,128]{2,0,1:T(8,128)}, u32[]{:S(2)}) copy-start(f32[128,3,128]{2,0,1:T(8,128)} %param.20) | copy-start | bytes 589828
  19.9 21.1 %copy-start.23 = (f32[128,128]{1,0:T(8,128)S(1)}, f32[128,128]{1,0:T(8,128)}, u32[]{:S(2)}) copy-start(f32[128,128]{1,0:T(8,128)} %param.21) | copy-start | bytes 196612
  20.0 21.1 %copy-start.29 = (s32[128]{0:T(128)S(1)}, s32[128]{0:T(128)}, u32[]{:S(2)}) copy-start(s32[128]{0:T(128)} %param.22) | copy-start | bytes 1540
  24.8 17.7 %copy-start.22 = (f32[8,16,256]{2,1,0:T(8,128)S(1)}, f32[8,16,256]{2,1,0:T(8,128)}, u32[]{:S(2)}) copy-start(f32[8,16,256]{2,1,0:T(8,128)} %param.19) | copy-start | bytes 393220
  39.1 4.5 %copy-start.16 = (f32[32,1,128]{2,0,1:T(8,128)}, f32[32,1,128]{2,0,1:T(8,128)S(1)}, u32[]{:S(2)}) copy-start(f32[32,1,128]{2,0,1:T(8,128)S(1)} %get-tuple-element.104) | copy-start | bytes 49156
  39.1 4.5 %copy-start.18 = (f32[32,1,128]{2,0,1:T(8,128)}, f32[32,1,128]{2,0,1:T(8,128)S(1)}, u32[]{:S(2)}) copy-start(f32[32,1,128]{2,0,1:T(8,128)S(1)} %get-tuple-element.105) | copy-start | bytes 49156
  39.2 4.5 %copy-start.20 = (f32[32,1,128]{2,0,1:T(8,128)}, f32[32,1,128]{2,0,1:T(8,128)S(1)}, u32[]{:S(2)}) copy-start(f32[32,1,128]{2,0,1:T(8,128)S(1)} %get-tuple-element.106) | copy-start | bytes 49156
  47.8 15.7 %collective-permute-start.2 = (f32[6,8,18]{2,1,0:T(8,128)}, f32[6,8,18]{2,1,0:T(8,128)}, u32[]{:S(2)}, u32[]{:S(2)}) collective-permute-start(f32[6,8,18]{2,1,0:T(8,128)} %bitcast.28), channel_id=1, source_target_pairs={{0,1},{1,2},{2,3},{3,4},{4,5},{5,6},{6,7},{8,9},{9,10},{10,11},{11... | collective-permute-start | bytes 10376 | tf_op jit(solution)/shard_map/ppermute | solution.py:116
  51.9 12.7 %collective-permute-start.3 = (f32[6,8,18]{2,1,0:T(8,128)}, f32[6,8,18]{2,1,0:T(8,128)}, u32[]{:S(2)}, u32[]{:S(2)}) collective-permute-start(f32[6,8,18]{2,1,0:T(8,128)} %bitcast.30), channel_id=1, source_target_pairs={{1,0},{2,1},{3,2},{4,3},{5,4},{6,5},{7,6},{9,8},{10,9},{11,10},{12... | collective-permute-start | bytes 10376 | tf_op jit(solution)/shard_map/ppermute | solution.py:119
  57.4 8.4 %copy-start.4 = (f32[1,8,16,256]{3,1,0,2:T(8,128)S(1)}, f32[1,8,16,256]{3,1,0,2:T(8,128)}, u32[]{:S(2)}) copy-start(f32[1,8,16,256]{3,1,0,2:T(8,128)} %copy-done.3) | copy-start | bytes 393220
  57.4 8.4 %copy-start.6 = (f32[1,8,16,256]{3,1,0,2:T(8,128)S(1)}, f32[1,8,16,256]{3,1,0,2:T(8,128)}, u32[]{:S(2)}) copy-start(f32[1,8,16,256]{3,1,0,2:T(8,128)} %copy-done.5) | copy-start | bytes 393220
  57.4 8.4 %copy-start.8 = (f32[1,8,16,256]{3,1,0,2:T(8,128)S(1)}, f32[1,8,16,256]{3,1,0,2:T(8,128)}, u32[]{:S(2)}) copy-start(f32[1,8,16,256]{3,1,0,2:T(8,128)} %copy-done.7) | copy-start | bytes 393220
  57.4 37.8 %all-to-all-start.1 = ((f32[32,5,10,128]{3,1,2,0:T(8,128)}), f32[32,5,10,128]{3,1,2,0:T(8,128)S(1)}, u32[]{:S(2)}, u32[]{:S(2)}) async-start(f32[32,5,10,128]{3,1,2,0:T(8,128)} %copy.288), calls=%async_computation.1 | async-start | bytes 2621440 | tf_op jit(solution)/shard_map/all_to_all | solution.py:292
  127.9 15.8 %copy-start.17 = (f32[32,1,128]{2,0,1:T(8,128)S(1)}, f32[32,1,128]{2,0,1:T(8,128)}, u32[]{:S(2)}) copy-start(f32[32,1,128]{2,0,1:T(8,128)} %copy-done.16) | copy-start | bytes 49156
  127.9 15.8 %copy-start.19 = (f32[32,1,128]{2,0,1:T(8,128)S(1)}, f32[32,1,128]{2,0,1:T(8,128)}, u32[]{:S(2)}) copy-start(f32[32,1,128]{2,0,1:T(8,128)} %copy-done.18) | copy-start | bytes 49156
  127.9 15.8 %copy-start.21 = (f32[32,1,128]{2,0,1:T(8,128)S(1)}, f32[32,1,128]{2,0,1:T(8,128)}, u32[]{:S(2)}) copy-start(f32[32,1,128]{2,0,1:T(8,128)} %copy-done.20) | copy-start | bytes 49156
  128.7 14.6 %all-to-all-start.2 = ((f32[32,5,128]{2,1,0:T(8,128)}), f32[32,5,128]{2,1,0:T(8,128)S(1)}, u32[]{:S(2)}, u32[]{:S(2)}) async-start(f32[32,5,128]{2,1,0:T(8,128)} %select_select_fusion), calls=%async_computation.2 | async-start | bytes 262144 | tf_op jit(solution)/shard_map/all_to_all | solution.py:314
  150.0 5.3 %collective-permute-start.4 = (f32[3,8,256]{2,1,0:T(8,128)S(1)}, f32[3,8,256]{2,1,0:T(8,128)S(1)}, u32[]{:S(2)}, u32[]{:S(2)}) collective-permute-start(f32[3,8,256]{2,1,0:T(8,128)S(1)} %get-tuple-element.102), channel_id=1, source_target_pairs={{0,8},{8,16},{16,24},{1,9},{9,17},{17,25},{2,10},{10,18},{18,26},{... | collective-permute-start | bytes 73736 | tf_op jit(solution)/shard_map/ppermute | solution.py:116
  153.4 5.1 %collective-permute-start.5 = (f32[3,8,256]{2,1,0:T(8,128)S(1)}, f32[3,8,256]{2,1,0:T(8,128)S(1)}, u32[]{:S(2)}, u32[]{:S(2)}) collective-permute-start(f32[3,8,256]{2,1,0:T(8,128)S(1)} %get-tuple-element.103), channel_id=1, source_target_pairs={{8,0},{16,8},{24,16},{9,1},{17,9},{25,17},{10,2},{18,10},{26,18},{... | collective-permute-start | bytes 73736 | tf_op jit(solution)/shard_map/ppermute | solution.py:119
  159.0 7.3 %collective-permute-start.6 = (f32[3,8,18]{2,1,0:T(8,128)S(1)}, f32[3,8,18]{2,1,0:T(8,128)S(1)}, u32[]{:S(2)}, u32[]{:S(2)}) collective-permute-start(f32[3,8,18]{2,1,0:T(8,128)S(1)} %bitcast.277), channel_id=1, source_target_pairs={{0,1},{1,2},{2,3},{3,4},{4,5},{5,6},{6,7},{8,9},{9,10},{10,11},{11... | collective-permute-start | bytes 5192 | tf_op jit(solution)/shard_map/ppermute | solution.py:116
  162.3 4.4 %collective-permute-start.7 = (f32[3,8,18]{2,1,0:T(8,128)S(1)}, f32[3,8,18]{2,1,0:T(8,128)S(1)}, u32[]{:S(2)}, u32[]{:S(2)}) collective-permute-start(f32[3,8,18]{2,1,0:T(8,128)S(1)} %bitcast.279), channel_id=1, source_target_pairs={{1,0},{2,1},{3,2},{4,3},{5,4},{6,5},{7,6},{9,8},{10,9},{11,10},{12... | collective-permute-start | bytes 5192 | tf_op jit(solution)/shard_map/ppermute | solution.py:119
  (10 other events, 17.6 us)

commit v10 on v7

--- a/solution.py
+++ b/solution.py
@@ -26,7 +26,7 @@
         lax.broadcasted_iota(jnp.int32, (high_count, width), 0) == (node >> 7)
     ).astype(jnp.bfloat16)
     gathered = None
-    for piece in split_pieces(table_ref[...]):
+    for piece in split_pieces(table_ref[...])[:2]:
         part = jnp.dot(piece, onehot, preferred_element_type=jnp.float32)
         gathered = part if gathered is None else gathered + part
     low_hit = lax.broadcasted_iota(jnp.int32, (LANES, width), 0) == (node & (LANES - 1))

time: 146 us -> 143 us (0.979)
  Pallas kernels: 32.6 us -> 28.7 us
    pallas_call x2, Pallas kernels: 19.2 us -> 15.3 us  [node_gather(): pl.pallas_call(gather_kernel, grid=(padded_count // TILE,), in_specs=[pl....]
  transfers between devices with their start and end apart: 10 -> 10, of which waited for: 3 -> 3; matrix products, arithmetic and copies ran while one was open for 12% -> 12% of each run, Pallas kernels for 16% -> 13%
where the time goes in v10:
time: 143 us; the launch traced here: 141 us
  other arithmetic  47.3 us (33%)
  starting transfers between devices  36.2 us (25%)
  Pallas kernels  28.7 us (20%)
  local copies, waits for them, and re-layouts  16.6 us (12%)
  waiting for transfers between devices  9.09 us (6%)
    reduce_sum x2, other arithmetic, contact_pairs(): reaction = jnp.sum(push_force, axis=1)  34.4 us
    pallas_call x2, Pallas kernels, node_gather(): pl.pallas_call(gather_kernel, grid=(padded_count // TILE,), in_specs=[pl....  15.3 us
    pallas_call x2, Pallas kernels, node_scatter_add(): pl.pallas_call(scatter_kernel, grid=(padded_count // TILE,), in_specs=[pl...  13.4 us
    ppermute x4, starting transfers between devices, padded_2(): lax.ppermute(lax.index_in_dim(block, block.shape[dim] - 1, axis=dim, keep...  11.5 us
    ppermute x4, starting transfers between devices, padded_2(): lax.ppermute(lax.index_in_dim(block, 0, axis=dim, keepdims=False), axis,...  10.9 us
    all_to_all x1, starting transfers between devices, on_device(): lax.all_to_all(forces.reshape(devices, slot_depth, 3, seg_width), ('gx',...  7.42 us
    all_to_all x1, starting transfers between devices, on_device(): lax.all_to_all(outgoing.reshape(devices, slot_depth, 8, seg_width), ('gx'...  6.32 us
    all_to_all x1, waiting for transfers between devices, on_device(): lax.all_to_all(forces.reshape(devices, slot_depth, 3, seg_width), ('gx',...  5.66 us
  transfers between devices with their start and end apart: 10, of which 3 were waited for; matrix products, arithmetic and copies ran while one was open for 12% of the time, Pallas kernels for 13%

profile of v10, /device:TPU:9, one launch (start us, length us, event | category | flops | bytes accessed | tf_op | source)
XLA Modules:
  0.0 140.6 jit_solution(17939982503688113852)
XLA Ops:
  0.6 1.3 copy.254
  1.9 1.1 copy_bitcast_fusion
  3.1 3.8 %collective-permute-start = (f32[6,8,256]{2,1,0:T(8,128)S(1)}, f32[6,8,256]{2,1,0:T(8,128)S(1)}, u32[]{:S(2)}, u32[]{:S(2)}) collective-permute-start(f32[6,8,256]{2,1,0:T(8,128)S(1)} %get-tuple-element.99), channel_id=1, source_target_pairs={{0,8},{8,16},{16,24},{1,9},{9,17},{17,25},{2,10},{10,18},{18,26},{... | collective-permute-start | bytes 147464 | tf_op jit(solution)/shard_map/ppermute | solution.py:116
  7.0 1.9 %collective-permute-start.1 = (f32[6,8,256]{2,1,0:T(8,128)S(1)}, f32[6,8,256]{2,1,0:T(8,128)S(1)}, u32[]{:S(2)}, u32[]{:S(2)}) collective-permute-start(f32[6,8,256]{2,1,0:T(8,128)S(1)} %get-tuple-element.100), channel_id=1, source_target_pairs={{8,0},{16,8},{24,16},{9,1},{17,9},{25,17},{10,2},{18,10},{26,18},{... | collective-permute-start | bytes 147464 | tf_op jit(solution)/shard_map/ppermute | solution.py:119
  9.4 0.9 copy.269
  10.6 11.3 %shard_map.149 = f32[3,16384]{1,0:T(4,128)} custom-call(s32[1,16384]{1,0:T(1,128)} %bitcast.250, f32[384,256]{1,0:T(8,128)} %bitcast.235), custom_call_target="tpu_custom_call" | custom-call | tf_op jit(solution)/shard_map/pallas_call | solution.py:73
  21.8 1.1 copy_add_fusion
  23.3 1.2 pad_maximum_fusion.3
  24.5 0.8 gather_fusion
  25.3 1.2 select_select_fusion
  26.6 6.3 %all-to-all-start = ((f32[32,5,8,128]{3,2,1,0:T(8,128)}), f32[32,5,8,128]{3,2,1,0:T(8,128)S(1)}, u32[]{:S(2)}, u32[]{:S(2)}) async-start(f32[32,5,8,128]{3,2,1,0:T(8,128)} %select_select_fusion), calls=%async_computation | async-start | bytes 1310720 | tf_op jit(solution)/shard_map/all_to_all | solution.py:291
  32.9 4.0 %shard_map.150 = f32[3,4096]{1,0:T(4,128)} custom-call(s32[1,4096]{1,0:T(1,128)} %bitcast.265, f32[384,256]{1,0:T(8,128)} %bitcast.236), custom_call_target="tpu_custom_call" | custom-call | tf_op jit(solution)/shard_map/pallas_call | solution.py:73
  37.0 0.9 copy_add_fusion.1
  38.6 3.1 %collective-permute-start.2 = (f32[6,8,18]{2,1,0:T(8,128)S(1)}, f32[6,8,18]{2,1,0:T(8,128)S(1)}, u32[]{:S(2)}, u32[]{:S(2)}) collective-permute-start(f32[6,8,18]{2,1,0:T(8,128)S(1)} %bitcast.267), channel_id=1, source_target_pairs={{0,1},{1,2},{2,3},{3,4},{4,5},{5,6},{6,7},{8,9},{9,10},{10,11},{11... | collective-permute-start | bytes 10376 | tf_op jit(solution)/shard_map/ppermute | solution.py:116
  42.1 3.1 %collective-permute-start.3 = (f32[6,8,18]{2,1,0:T(8,128)S(1)}, f32[6,8,18]{2,1,0:T(8,128)S(1)}, u32[]{:S(2)}, u32[]{:S(2)}) collective-permute-start(f32[6,8,18]{2,1,0:T(8,128)S(1)} %bitcast.269), channel_id=1, source_target_pairs={{1,0},{2,1},{3,2},{4,3},{5,4},{6,5},{7,6},{9,8},{10,9},{11,10},{12... | collective-permute-start | bytes 10376 | tf_op jit(solution)/shard_map/ppermute | solution.py:119
  52.8 36.2 %while.12 = (s32[]{:T(128)}, f32[2,80,3,128]{3,1,2,0:T(8,128)}, f32[2,80,128]{2,1,0:T(8,128)}, f32[2,80,7,128]{3,1,0,2:T(8,128)S(1)}, f32[2,80,10,128]{3,1,2,0:T(8,128)S(1)}, /*index=5*/s32[]{:T(128)}) while((s32[]{:T(128)}, f32[2,80,3,128]{3,1,2,0:T(8,128)}, f32[2,80,128]{2,1,0:T(8,128)}, f32[2,80,7,128]{3,1,0,2:T(8,128)S(1)}, ...), condition=%wide.region_8.9_spmd, body=%wide.region_3.8_spmd.sunk | while | flops 52500480 | bytes 5776009 | solution.py:308
  53.0 17.2 %fusion.87 = (f32[80,128]{1,0:T(8,128)S(1)}, f32[80,128]{1,0:T(8,128)S(1)}, f32[80,128]{1,0:T(8,128)S(1)}, f32[80,128]{1,0:T(8,128)S(1)}) fusion(f32[80,128]{1,0:T(8,128)S(1)} %get-tuple-element.164, f32[80,128]{1,0:T(8,128)S(1)} %get-tuple-element.165, f32[80,128]{1,0:T(8,128)S(1)} %get-tuple-element.166, f32[80,128]{1,0:T(8,128)S(1)} %get-tuple-element.167, ...), kind=kLoop, calls=%fused_computation.47.clone.1 | loop fusion | flops 52387840 | bytes 778240 | tf_op jit(solution)/shard_map/while/body/eval_jaxpr/reduce_sum | solution.py:213
  71.1 17.2 %fusion.87 = (f32[80,128]{1,0:T(8,128)S(1)}, f32[80,128]{1,0:T(8,128)S(1)}, f32[80,128]{1,0:T(8,128)S(1)}, f32[80,128]{1,0:T(8,128)S(1)}) fusion(f32[80,128]{1,0:T(8,128)S(1)} %get-tuple-element.164, f32[80,128]{1,0:T(8,128)S(1)} %get-tuple-element.165, f32[80,128]{1,0:T(8,128)S(1)} %get-tuple-element.166, f32[80,128]{1,0:T(8,128)S(1)} %get-tuple-element.167, ...), kind=kLoop, calls=%fused_computation.47.clone.1 | loop fusion | flops 52387840 | bytes 778240 | tf_op jit(solution)/shard_map/while/body/eval_jaxpr/reduce_sum | solution.py:213
  89.1 1.8 %copy.297 = f32[2,80,3,128]{3,2,1,0:T(4,128)} copy(f32[2,80,3,128]{3,1,2,0:T(8,128)} %get-tuple-element.31) | data formatting | bytes 491520 | tf_op jit(solution)/shard_map/reshape;reshape | solution.py:326
  90.9 7.4 %all-to-all-start.1 = ((f32[32,5,3,128]{3,2,1,0:T(4,128)}), f32[32,5,3,128]{3,2,1,0:T(4,128)S(1)}, u32[]{:S(2)}, u32[]{:S(2)}) async-start(f32[32,5,3,128]{3,2,1,0:T(4,128)} %bitcast.69), calls=%async_computation.1 | async-start | bytes 655360 | tf_op jit(solution)/shard_map/all_to_all | solution.py:325
  98.4 1.2 convolution_negate_fusion
  100.2 3.6 %shard_map.151 = f32[384,256]{1,0:T(8,128)} custom-call(s32[1,4096]{1,0:T(1,128)} %bitcast.266, f32[3,4096]{1,0:T(4,128)} %bitcast.249), custom_call_target="tpu_custom_call" | custom-call | tf_op jit(solution)/shard_map/pallas_call | solution.py:91
  103.8 5.7 %all-to-all-done.1 = f32[32,5,3,128]{3,2,1,0:T(4,128)S(1)} async-done(((f32[32,5,3,128]{3,2,1,0:T(4,128)}), f32[32,5,3,128]{3,2,1,0:T(4,128)S(1)}, u32[]{:S(2)}, u32[]{:S(2)}) %all-to-all-start.1) | async-done | bytes 245792 | tf_op jit(solution)/shard_map/all_to_all | solution.py:325
  110.2 0.9 select_bitcast_fusion.force_ref
  111.1 9.8 %shard_map.152 = f32[384,256]{1,0:T(8,128)} custom-call(s32[1,16384]{1,0:T(1,128)} %bitcast.251, f32[3,16384]{1,0:T(4,128)} %select_bitcast_fusion.force_ref), custom_call_target="tpu_custom_call" | custom-call | tf_op jit(solution)/shard_map/pallas_call | solution.py:91
  120.9 1.1 add.281
  122.9 2.5 %collective-permute-start.4 = (f32[3,8,256]{2,1,0:T(8,128)S(1)}, f32[3,8,256]{2,1,0:T(8,128)S(1)}, u32[]{:S(2)}, u32[]{:S(2)}) collective-permute-start(f32[3,8,256]{2,1,0:T(8,128)S(1)} %get-tuple-element.105), channel_id=1, source_target_pairs={{0,8},{8,16},{16,24},{1,9},{9,17},{17,25},{2,10},{10,18},{18,26},{... | collective-permute-start | bytes 73736 | tf_op jit(solution)/shard_map/ppermute | solution.py:116
  125.4 1.9 %collective-permute-start.5 = (f32[3,8,256]{2,1,0:T(8,128)S(1)}, f32[3,8,256]{2,1,0:T(8,128)S(1)}, u32[]{:S(2)}, u32[]{:S(2)}) collective-permute-start(f32[3,8,256]{2,1,0:T(8,128)S(1)} %get-tuple-element.106), channel_id=1, source_target_pairs={{8,0},{16,8},{24,16},{9,1},{17,9},{25,17},{10,2},{18,10},{26,18},{... | collective-permute-start | bytes 73736 | tf_op jit(solution)/shard_map/ppermute | solution.py:119
  127.3 3.2 %collective-permute-done.5 = f32[3,8,256]{2,1,0:T(8,128)S(1)} collective-permute-done((f32[3,8,256]{2,1,0:T(8,128)S(1)}, f32[3,8,256]{2,1,0:T(8,128)S(1)}, u32[]{:S(2)}, u32[]{:S(2)}) %collective-permute-start.5) | collective-permute-done | bytes 24608 | tf_op jit(solution)/shard_map/ppermute | solution.py:119
  131.0 2.1 %collective-permute-start.6 = (f32[3,8,18]{2,1,0:T(8,128)S(1)}, f32[3,8,18]{2,1,0:T(8,128)S(1)}, u32[]{:S(2)}, u32[]{:S(2)}) collective-permute-start(f32[3,8,18]{2,1,0:T(8,128)S(1)} %bitcast.272), channel_id=1, source_target_pairs={{0,1},{1,2},{2,3},{3,4},{4,5},{5,6},{6,7},{8,9},{9,10},{10,11},{11... | collective-permute-start | bytes 5192 | tf_op jit(solution)/shard_map/ppermute | solution.py:116
  133.4 4.0 %collective-permute-start.7 = (f32[3,8,18]{2,1,0:T(8,128)S(1)}, f32[3,8,18]{2,1,0:T(8,128)S(1)}, u32[]{:S(2)}, u32[]{:S(2)}) collective-permute-start(f32[3,8,18]{2,1,0:T(8,128)S(1)} %bitcast.274), channel_id=1, source_target_pairs={{1,0},{2,1},{3,2},{4,3},{5,4},{6,5},{7,6},{9,8},{10,9},{11,10},{12... | collective-permute-start | bytes 5192 | tf_op jit(solution)/shard_map/ppermute | solution.py:119
  137.4 0.9 copy.295
  (144 shorter events, 16.3 us)
Async XLA Ops:
  0.6 8.3 %copy-start = (f32[3,8,16,256]{3,2,1,0:T(8,128)S(1)}, f32[3,8,16,256]{3,2,1,0:T(8,128)}, u32[]{:S(2)}) copy-start(f32[3,8,16,256]{3,2,1,0:T(8,128)} %param.16) | copy-start | bytes 1179652
  1.9 7.0 %copy-start.16 = (s32[128,1]{0,1:T(1,128)S(1)}, s32[128,1]{0,1:T(1,128)}, u32[]{:S(2)}) copy-start(s32[128,1]{0,1:T(1,128)} %param.24) | copy-start | bytes 1540
  3.1 7.2 %copy-start.17 = (s32[128]{0:T(128)S(1)}, s32[128]{0:T(128)}, u32[]{:S(2)}) copy-start(s32[128]{0:T(128)} %param.25) | copy-start | bytes 1540
  3.1 18.7 %copy-start.9 = (f32[128,3,128]{2,0,1:T(8,128)S(1)}, f32[128,3,128]{2,0,1:T(8,128)}, u32[]{:S(2)}) copy-start(f32[128,3,128]{2,0,1:T(8,128)} %param.20) | copy-start | bytes 589828
  3.1 34.8 %collective-permute-start = (f32[6,8,256]{2,1,0:T(8,128)S(1)}, f32[6,8,256]{2,1,0:T(8,128)S(1)}, u32[]{:S(2)}, u32[]{:S(2)}) collective-permute-start(f32[6,8,256]{2,1,0:T(8,128)S(1)} %get-tuple-element.99), channel_id=1, source_target_pairs={{0,8},{8,16},{16,24},{1,9},{9,17},{17,25},{2,10},{10,18},{18,26},{... | collective-permute-start | bytes 147464 | tf_op jit(solution)/shard_map/ppermute | solution.py:116
  7.0 30.9 %collective-permute-start.1 = (f32[6,8,256]{2,1,0:T(8,128)S(1)}, f32[6,8,256]{2,1,0:T(8,128)S(1)}, u32[]{:S(2)}, u32[]{:S(2)}) collective-permute-start(f32[6,8,256]{2,1,0:T(8,128)S(1)} %get-tuple-element.100), channel_id=1, source_target_pairs={{8,0},{16,8},{24,16},{9,1},{17,9},{25,17},{10,2},{18,10},{26,18},{... | collective-permute-start | bytes 147464 | tf_op jit(solution)/shard_map/ppermute | solution.py:119
  8.9 14.0 %copy-start.11 = (f32[128,128]{1,0:T(8,128)S(1)}, f32[128,128]{1,0:T(8,128)}, u32[]{:S(2)}) copy-start(f32[128,128]{1,0:T(8,128)} %param.21) | copy-start | bytes 196612
  8.9 14.0 %copy-start.15 = (s32[128]{0:T(128)S(1)}, s32[128]{0:T(128)}, u32[]{:S(2)}) copy-start(s32[128]{0:T(128)} %param.22) | copy-start | bytes 1540
  25.3 7.6 %copy-start.13 = (f32[32,2,128]{2,1,0:T(2,128)S(1)}, f32[32,2,128]{2,1,0:T(2,128)}, u32[]{:S(2)}) copy-start(f32[32,2,128]{2,1,0:T(2,128)} %param.27) | copy-start | bytes 98308
  25.3 11.7 %copy-start.12 = (f32[32,3,128]{2,0,1:T(8,128)S(1)}, f32[32,3,128]{2,0,1:T(8,128)}, u32[]{:S(2)}) copy-start(f32[32,3,128]{2,0,1:T(8,128)} %param.26) | copy-start | bytes 147460
  26.6 24.7 %all-to-all-start = ((f32[32,5,8,128]{3,2,1,0:T(8,128)}), f32[32,5,8,128]{3,2,1,0:T(8,128)S(1)}, u32[]{:S(2)}, u32[]{:S(2)}) async-start(f32[32,5,8,128]{3,2,1,0:T(8,128)} %select_select_fusion), calls=%async_computation | async-start | bytes 1310720 | tf_op jit(solution)/shard_map/all_to_all | solution.py:291
  38.0 7.2 %copy-start.10 = (f32[8,16,256]{2,1,0:T(8,128)S(1)}, f32[8,16,256]{2,1,0:T(8,128)}, u32[]{:S(2)}) copy-start(f32[8,16,256]{2,1,0:T(8,128)} %param.19) | copy-start | bytes 393220
  38.0 8.0 %copy-start.3 = (f32[3,4096]{1,0:T(4,128)S(1)}, f32[3,4096]{1,0:T(4,128)}, u32[]{:S(2)}) copy-start(f32[3,4096]{1,0:T(4,128)} %shard_map.150) | copy-start | bytes 147460
  38.0 7.9 %copy-start.14 = (f32[32,128]{1,0:T(8,128)S(1)}, f32[32,128]{1,0:T(8,128)}, u32[]{:S(2)}) copy-start(f32[32,128]{1,0:T(8,128)} %param.28) | copy-start | bytes 49156
  38.6 7.7 %collective-permute-start.2 = (f32[6,8,18]{2,1,0:T(8,128)S(1)}, f32[6,8,18]{2,1,0:T(8,128)S(1)}, u32[]{:S(2)}, u32[]{:S(2)}) collective-permute-start(f32[6,8,18]{2,1,0:T(8,128)S(1)} %bitcast.267), channel_id=1, source_target_pairs={{0,1},{1,2},{2,3},{3,4},{4,5},{5,6},{6,7},{8,9},{9,10},{10,11},{11... | collective-permute-start | bytes 10376 | tf_op jit(solution)/shard_map/ppermute | solution.py:116
  42.1 4.9 %collective-permute-start.3 = (f32[6,8,18]{2,1,0:T(8,128)S(1)}, f32[6,8,18]{2,1,0:T(8,128)S(1)}, u32[]{:S(2)}, u32[]{:S(2)}) collective-permute-start(f32[6,8,18]{2,1,0:T(8,128)S(1)} %bitcast.269), channel_id=1, source_target_pairs={{1,0},{2,1},{3,2},{4,3},{5,4},{6,5},{7,6},{9,8},{10,9},{11,10},{12... | collective-permute-start | bytes 10376 | tf_op jit(solution)/shard_map/ppermute | solution.py:119
  53.0 17.2 %copy-start.7 = (f32[2,80,3,128]{3,1,2,0:T(8,128)S(1)}, f32[2,80,3,128]{3,1,2,0:T(8,128)}, u32[]{:S(2)}) copy-start(f32[2,80,3,128]{3,1,2,0:T(8,128)} %get-tuple-element.190) | copy-start | bytes 737284 | tf_op jit(solution)/shard_map/while
  70.2 0.7 copy-start.8
  71.1 17.2 %copy-start.7 = (f32[2,80,3,128]{3,1,2,0:T(8,128)S(1)}, f32[2,80,3,128]{3,1,2,0:T(8,128)}, u32[]{:S(2)}) copy-start(f32[2,80,3,128]{3,1,2,0:T(8,128)} %get-tuple-element.190) | copy-start | bytes 737284 | tf_op jit(solution)/shard_map/while
  88.4 0.7 copy-start.8
  89.1 9.3 %copy-start.2 = (f32[8,17,256]{2,0,1:T(8,128)S(1)}, f32[8,17,256]{2,0,1:T(8,128)}, u32[]{:S(2)}) copy-start(f32[8,17,256]{2,0,1:T(8,128)} %fusion.65) | copy-start | bytes 417796
  90.9 18.6 %all-to-all-start.1 = ((f32[32,5,3,128]{3,2,1,0:T(4,128)}), f32[32,5,3,128]{3,2,1,0:T(4,128)S(1)}, u32[]{:S(2)}, u32[]{:S(2)}) async-start(f32[32,5,3,128]{3,2,1,0:T(4,128)} %bitcast.69), calls=%async_computation.1 | async-start | bytes 655360 | tf_op jit(solution)/shard_map/all_to_all | solution.py:325
  103.8 17.1 %copy-start.1 = (f32[384,256]{1,0:T(8,128)S(1)}, f32[384,256]{1,0:T(8,128)}, u32[]{:S(2)}) copy-start(f32[384,256]{1,0:T(8,128)} %shard_map.151) | copy-start | bytes 1179652
  120.9 1.4 %copy-start.4 = (f32[1,8,16,256]{3,1,2,0:T(8,128)S(1)}, f32[1,8,16,256]{3,1,2,0:T(8,128)}, u32[]{:S(2)}) copy-start(f32[1,8,16,256]{3,1,2,0:T(8,128)} %fusion.68) | copy-start | bytes 393220
  120.9 1.4 %copy-start.5 = (f32[1,8,16,256]{3,1,2,0:T(8,128)S(1)}, f32[1,8,16,256]{3,1,2,0:T(8,128)}, u32[]{:S(2)}) copy-start(f32[1,8,16,256]{3,1,2,0:T(8,128)} %fusion.70) | copy-start | bytes 393220
  120.9 1.4 %copy-start.6 = (f32[8,16,256]{2,0,1:T(8,128)S(1)}, f32[8,16,256]{2,0,1:T(8,128)}, u32[]{:S(2)}) copy-start(f32[8,16,256]{2,0,1:T(8,128)} %copy.287) | copy-start | bytes 393220
  122.9 4.4 %collective-permute-start.4 = (f32[3,8,256]{2,1,0:T(8,128)S(1)}, f32[3,8,256]{2,1,0:T(8,128)S(1)}, u32[]{:S(2)}, u32[]{:S(2)}) collective-permute-start(f32[3,8,256]{2,1,0:T(8,128)S(1)} %get-tuple-element.105), channel_id=1, source_target_pairs={{0,8},{8,16},{16,24},{1,9},{9,17},{17,25},{2,10},{10,18},{18,26},{... | collective-permute-start | bytes 73736 | tf_op jit(solution)/shard_map/ppermute | solution.py:116
  125.4 5.1 %collective-permute-start.5 = (f32[3,8,256]{2,1,0:T(8,128)S(1)}, f32[3,8,256]{2,1,0:T(8,128)S(1)}, u32[]{:S(2)}, u32[]{:S(2)}) collective-permute-start(f32[3,8,256]{2,1,0:T(8,128)S(1)} %get-tuple-element.106), channel_id=1, source_target_pairs={{8,0},{16,8},{24,16},{9,1},{17,9},{25,17},{10,2},{18,10},{26,18},{... | collective-permute-start | bytes 73736 | tf_op jit(solution)/shard_map/ppermute | solution.py:119
  131.0 7.3 %collective-permute-start.6 = (f32[3,8,18]{2,1,0:T(8,128)S(1)}, f32[3,8,18]{2,1,0:T(8,128)S(1)}, u32[]{:S(2)}, u32[]{:S(2)}) collective-permute-start(f32[3,8,18]{2,1,0:T(8,128)S(1)} %bitcast.272), channel_id=1, source_target_pairs={{0,1},{1,2},{2,3},{3,4},{4,5},{5,6},{6,7},{8,9},{9,10},{10,11},{11... | collective-permute-start | bytes 5192 | tf_op jit(solution)/shard_map/ppermute | solution.py:116
  133.4 5.2 %collective-permute-start.7 = (f32[3,8,18]{2,1,0:T(8,128)S(1)}, f32[3,8,18]{2,1,0:T(8,128)S(1)}, u32[]{:S(2)}, u32[]{:S(2)}) collective-permute-start(f32[3,8,18]{2,1,0:T(8,128)S(1)} %bitcast.274), channel_id=1, source_target_pairs={{1,0},{2,1},{3,2},{4,3},{5,4},{6,5},{7,6},{9,8},{10,9},{11,10},{12... | collective-permute-start | bytes 5192 | tf_op jit(solution)/shard_map/ppermute | solution.py:119

commit v11 on v10

--- a/solution.py
+++ b/solution.py
@@ -202,13 +202,8 @@
         * depth_soft
         * (1.0 + DAMPING * jnp.tanh(-closing))
     )
-    slave_force = jnp.stack(
-        [
-            jnp.sum(push_force * normal_x, axis=2),
-            jnp.sum(push_force * normal_y, axis=2),
-            jnp.sum(push_force * normal_z, axis=2),
-        ],
-        axis=1,
+    slave_force = jnp.einsum(
+        "gij,gcj->gci", push_force, master[:, 3:6], precision=lax.Precision.HIGHEST
     )
     reaction = jnp.sum(push_force, axis=1)
     return (slave_force, reaction)

time: 143 us -> 174 us (1.22)
  matrix products: 1.18 us -> 41.9 us
  other arithmetic: 47.3 us -> 40.9 us
  local copies, waits for them, and re-layouts: 16.6 us -> 13.3 us
    dot_general x0 -> x2, matrix products: none -> 40.7 us  [contact_pairs(): jnp.einsum('gij,gcj->gci', push_force, master[:, 3:6], precision=lax.Prec...]
    reduce_sum x2, other arithmetic: 34.4 us -> 24.3 us  [contact_pairs(): reaction = jnp.sum(push_force, axis=1)]
    convert_element_type x2 -> x1, other arithmetic: 0.03 us -> 2.93 us  [on_device(): picked = arrived[:, 7, 0].astype(jnp.int32)]
    another operation x1 -> x0, local copies, waits for them, and re-layouts: 1.84 us -> none  [on_device(): forces.reshape(devices, slot_depth, 3, seg_width)]
    unnamed x39 -> x49, local copies, waits for them, and re-layouts: 4.5 us -> 4.36 us
  transfers between devices with their start and end apart: 10 -> 10, of which waited for: 3 -> 3; matrix products, arithmetic and copies ran while one was open for 12% -> 10% of each run, Pallas kernels for 13% -> 11%
where the time goes in v11:
time: 174 us; the launch traced here: 172 us
  matrix products  41.9 us (24%)
  other arithmetic  40.9 us (24%)
  starting transfers between devices  36.2 us (21%)
  Pallas kernels  28.6 us (16%)
  local copies, waits for them, and re-layouts  13.3 us (8%)
  waiting for transfers between devices  9.08 us (5%)
    dot_general x2, matrix products, contact_pairs(): jnp.einsum('gij,gcj->gci', push_force, master[:, 3:6], precision=lax.Prec...  40.7 us
    reduce_sum x2, other arithmetic, contact_pairs(): reaction = jnp.sum(push_force, axis=1)  24.3 us
    pallas_call x2, Pallas kernels, node_gather(): pl.pallas_call(gather_kernel, grid=(padded_count // TILE,), in_specs=[pl....  15.2 us
    pallas_call x2, Pallas kernels, node_scatter_add(): pl.pallas_call(scatter_kernel, grid=(padded_count // TILE,), in_specs=[pl...  13.4 us
    ppermute x4, starting transfers between devices, padded_2(): lax.ppermute(lax.index_in_dim(block, block.shape[dim] - 1, axis=dim, keep...  11.5 us
    ppermute x4, starting transfers between devices, padded_2(): lax.ppermute(lax.index_in_dim(block, 0, axis=dim, keepdims=False), axis,...  11.1 us
    all_to_all x1, starting transfers between devices, on_device(): lax.all_to_all(forces.reshape(devices, slot_depth, 3, seg_width), ('gx',...  7.17 us
    all_to_all x1, starting transfers between devices, on_device(): lax.all_to_all(outgoing.reshape(devices, slot_depth, 8, seg_width), ('gx'...  6.38 us
  transfers between devices with their start and end apart: 10, of which 3 were waited for; matrix products, arithmetic and copies ran while one was open for 10% of the time, Pallas kernels for 11%

profile of v11, /device:TPU:9, one launch (start us, length us, event | category | flops | bytes accessed | tf_op | source)
XLA Modules:
  0.0 171.6 jit_solution(9504076687840450761)
XLA Ops:
  0.6 1.3 copy.177
  1.9 1.1 copy_bitcast_fusion
  3.1 3.8 %collective-permute-start = (f32[6,8,256]{2,1,0:T(8,128)S(1)}, f32[6,8,256]{2,1,0:T(8,128)S(1)}, u32[]{:S(2)}, u32[]{:S(2)}) collective-permute-start(f32[6,8,256]{2,1,0:T(8,128)S(1)} %get-tuple-element.101), channel_id=1, source_target_pairs={{0,8},{8,16},{16,24},{1,9},{9,17},{17,25},{2,10},{10,18},{18,26},{... | collective-permute-start | bytes 147464 | tf_op jit(solution)/shard_map/ppermute | solution.py:116
  7.0 1.9 %collective-permute-start.1 = (f32[6,8,256]{2,1,0:T(8,128)S(1)}, f32[6,8,256]{2,1,0:T(8,128)S(1)}, u32[]{:S(2)}, u32[]{:S(2)}) collective-permute-start(f32[6,8,256]{2,1,0:T(8,128)S(1)} %get-tuple-element.102), channel_id=1, source_target_pairs={{8,0},{16,8},{24,16},{9,1},{17,9},{25,17},{10,2},{18,10},{26,18},{... | collective-permute-start | bytes 147464 | tf_op jit(solution)/shard_map/ppermute | solution.py:119
  9.4 0.9 copy.192
  10.6 11.2 %shard_map.149 = f32[3,16384]{1,0:T(4,128)} custom-call(s32[1,16384]{1,0:T(1,128)} %bitcast.254, f32[384,256]{1,0:T(8,128)} %bitcast.226), custom_call_target="tpu_custom_call" | custom-call | tf_op jit(solution)/shard_map/pallas_call | solution.py:73
  21.8 1.1 copy_add_fusion
  23.2 1.2 pad_maximum_fusion.3
  25.3 1.2 select_select_fusion
  26.5 6.4 %all-to-all-start = ((f32[32,5,8,128]{3,2,1,0:T(8,128)}), f32[32,5,8,128]{3,2,1,0:T(8,128)S(1)}, u32[]{:S(2)}, u32[]{:S(2)}) async-start(f32[32,5,8,128]{3,2,1,0:T(8,128)} %select_select_fusion), calls=%async_computation | async-start | bytes 1310720 | tf_op jit(solution)/shard_map/all_to_all | solution.py:286
  32.9 4.0 %shard_map.150 = f32[3,4096]{1,0:T(4,128)} custom-call(s32[1,4096]{1,0:T(1,128)} %bitcast.270, f32[384,256]{1,0:T(8,128)} %bitcast.227), custom_call_target="tpu_custom_call" | custom-call | tf_op jit(solution)/shard_map/pallas_call | solution.py:73
  37.0 0.9 copy_add_fusion.1
  38.6 3.1 %collective-permute-start.2 = (f32[6,8,18]{2,1,0:T(8,128)S(1)}, f32[6,8,18]{2,1,0:T(8,128)S(1)}, u32[]{:S(2)}, u32[]{:S(2)}) collective-permute-start(f32[6,8,18]{2,1,0:T(8,128)S(1)} %bitcast.272), channel_id=1, source_target_pairs={{0,1},{1,2},{2,3},{3,4},{4,5},{5,6},{6,7},{8,9},{9,10},{10,11},{11... | collective-permute-start | bytes 10376 | tf_op jit(solution)/shard_map/ppermute | solution.py:116
  42.1 3.3 %collective-permute-start.3 = (f32[6,8,18]{2,1,0:T(8,128)S(1)}, f32[6,8,18]{2,1,0:T(8,128)S(1)}, u32[]{:S(2)}, u32[]{:S(2)}) collective-permute-start(f32[6,8,18]{2,1,0:T(8,128)S(1)} %bitcast.274), channel_id=1, source_target_pairs={{1,0},{2,1},{3,2},{4,3},{5,4},{6,5},{7,6},{9,8},{10,9},{11,10},{12... | collective-permute-start | bytes 10376 | tf_op jit(solution)/shard_map/ppermute | solution.py:119
  50.8 2.9 %fusion.85 = s32[160]{0:T(256)S(1)} fusion(f32[160,8,128]{2,1,0:T(8,128)S(1)} %bitcast.228), kind=kLoop, calls=%fused_computation.165 | loop fusion | flops 160 | bytes 1280 | tf_op jit(solution)/shard_map/convert_element_type | solution.py:295
  56.3 65.9 %while.12 = (s32[]{:T(128)}, f32[2,80,3,128]{3,2,1,0:T(4,128)}, f32[2,80,128]{2,1,0:T(8,128)}, f32[2,80,10,128]{3,2,1,0:T(8,128)S(1)}, f32[2,80,7,128]{3,1,2,0:T(8,128)S(1)}, /*index=5*/s32[]{:T(128)}) while((s32[]{:T(128)}, f32[2,80,3,128]{3,2,1,0:T(4,128)}, f32[2,80,128]{2,1,0:T(8,128)}, f32[2,80,10,128]{3,2,1,0:T(8,128)S(1)}, ...), condition=%wide.region_5.6_spmd, body=%wide.region_3.5_spmd.sunk | while | flops 135045120 | bytes 5038729 | solution.py:303
  56.7 12.1 %fusion.108 = f32[80,128]{1,0:T(8,128)S(1)} fusion(f32[80,128]{1,0:T(8,128)S(1)} %bitcast.237, f32[80,128]{1,0:T(8,128)S(1)} %get-tuple-element.163, f32[80,128]{1,0:T(8,128)S(1)} %get-tuple-element.164, f32[80,128]{1,0:T(8,128)S(1)} %get-tuple-element.165, f32[80,128]{1,0:T(8,128)S(1)} %bitcast.239, f32[80,128]{1,0:T(8,128)S(1)} %bitcast.241, ...), kind=kLoop, calls=%fused_computation.19.clone.1 | loop fusion | flops 44554240 | bytes 655360 | tf_op jit(solution)/shard_map/while/body/eval_jaxpr/reduce_sum | solution.py:208
  68.9 20.3 %fusion.107 = f32[2,80,3,128]{3,2,1,0:T(4,128)} fusion(f32[2,80,3,128]{3,2,1,0:T(4,128)} %get-tuple-element.184, s32[]{:T(128)} %get-tuple-element.183, f32[80,128]{1,0:T(8,128)S(1)} %bitcast.238, f32[80,128]{1,0:T(8,128)S(1)} %get-tuple-element.163, f32[80,128]{1,0:T(8,128)S(1)} %get-tuple-element.164, f32[80,128]{1,0:T(8,128)S(1)} %get-tuple-element.165, ...), kind=kOutput, calls=%fused_computation.22.clone.1 | convolution fusion | flops 90439680 | bytes 942592 | tf_op jit(solution)/shard_map/while/body/eval_jaxpr/gij,gcj->gci/dot_general | solution.py:205
  89.6 12.1 %fusion.108 = f32[80,128]{1,0:T(8,128)S(1)} fusion(f32[80,128]{1,0:T(8,128)S(1)} %bitcast.237, f32[80,128]{1,0:T(8,128)S(1)} %get-tuple-element.163, f32[80,128]{1,0:T(8,128)S(1)} %get-tuple-element.164, f32[80,128]{1,0:T(8,128)S(1)} %get-tuple-element.165, f32[80,128]{1,0:T(8,128)S(1)} %bitcast.239, f32[80,128]{1,0:T(8,128)S(1)} %bitcast.241, ...), kind=kLoop, calls=%fused_computation.19.clone.1 | loop fusion | flops 44554240 | bytes 655360 | tf_op jit(solution)/shard_map/while/body/eval_jaxpr/reduce_sum | solution.py:208
  101.8 20.3 %fusion.107 = f32[2,80,3,128]{3,2,1,0:T(4,128)} fusion(f32[2,80,3,128]{3,2,1,0:T(4,128)} %get-tuple-element.184, s32[]{:T(128)} %get-tuple-element.183, f32[80,128]{1,0:T(8,128)S(1)} %bitcast.238, f32[80,128]{1,0:T(8,128)S(1)} %get-tuple-element.163, f32[80,128]{1,0:T(8,128)S(1)} %get-tuple-element.164, f32[80,128]{1,0:T(8,128)S(1)} %get-tuple-element.165, ...), kind=kOutput, calls=%fused_computation.22.clone.1 | convolution fusion | flops 90439680 | bytes 942592 | tf_op jit(solution)/shard_map/while/body/eval_jaxpr/gij,gcj->gci/dot_general | solution.py:205
  122.2 7.2 %all-to-all-start.1 = ((f32[32,5,3,128]{3,2,1,0:T(4,128)}), f32[32,5,3,128]{3,2,1,0:T(4,128)S(1)}, u32[]{:S(2)}, u32[]{:S(2)}) async-start(f32[32,5,3,128]{3,2,1,0:T(4,128)} %bitcast.64), calls=%async_computation.1 | async-start | bytes 655360 | tf_op jit(solution)/shard_map/all_to_all | solution.py:320
  129.4 1.2 convolution_negate_fusion
  131.2 3.6 %shard_map.151 = f32[384,256]{1,0:T(8,128)} custom-call(s32[1,4096]{1,0:T(1,128)} %bitcast.271, f32[3,4096]{1,0:T(4,128)} %bitcast.253), custom_call_target="tpu_custom_call" | custom-call | tf_op jit(solution)/shard_map/pallas_call | solution.py:91
  134.8 5.7 %all-to-all-done.1 = f32[32,5,3,128]{3,2,1,0:T(4,128)S(1)} async-done(((f32[32,5,3,128]{3,2,1,0:T(4,128)}), f32[32,5,3,128]{3,2,1,0:T(4,128)S(1)}, u32[]{:S(2)}, u32[]{:S(2)}) %all-to-all-start.1) | async-done | bytes 245792 | tf_op jit(solution)/shard_map/all_to_all | solution.py:320
  141.2 0.9 select_bitcast_fusion.force_ref
  142.1 9.8 %shard_map.152 = f32[384,256]{1,0:T(8,128)} custom-call(s32[1,16384]{1,0:T(1,128)} %bitcast.255, f32[3,16384]{1,0:T(4,128)} %select_bitcast_fusion.force_ref), custom_call_target="tpu_custom_call" | custom-call | tf_op jit(solution)/shard_map/pallas_call | solution.py:91
  152.0 1.1 add.281
  154.0 2.5 %collective-permute-start.4 = (f32[3,8,256]{2,1,0:T(8,128)S(1)}, f32[3,8,256]{2,1,0:T(8,128)S(1)}, u32[]{:S(2)}, u32[]{:S(2)}) collective-permute-start(f32[3,8,256]{2,1,0:T(8,128)S(1)} %get-tuple-element.107), channel_id=1, source_target_pairs={{0,8},{8,16},{16,24},{1,9},{9,17},{17,25},{2,10},{10,18},{18,26},{... | collective-permute-start | bytes 73736 | tf_op jit(solution)/shard_map/ppermute | solution.py:116
  156.4 1.9 %collective-permute-start.5 = (f32[3,8,256]{2,1,0:T(8,128)S(1)}, f32[3,8,256]{2,1,0:T(8,128)S(1)}, u32[]{:S(2)}, u32[]{:S(2)}) collective-permute-start(f32[3,8,256]{2,1,0:T(8,128)S(1)} %get-tuple-element.108), channel_id=1, source_target_pairs={{8,0},{16,8},{24,16},{9,1},{17,9},{25,17},{10,2},{18,10},{26,18},{... | collective-permute-start | bytes 73736 | tf_op jit(solution)/shard_map/ppermute | solution.py:119
  158.4 3.2 %collective-permute-done.5 = f32[3,8,256]{2,1,0:T(8,128)S(1)} collective-permute-done((f32[3,8,256]{2,1,0:T(8,128)S(1)}, f32[3,8,256]{2,1,0:T(8,128)S(1)}, u32[]{:S(2)}, u32[]{:S(2)}) %collective-permute-start.5) | collective-permute-done | bytes 24608 | tf_op jit(solution)/shard_map/ppermute | solution.py:119
  162.0 2.2 %collective-permute-start.6 = (f32[3,8,18]{2,1,0:T(8,128)S(1)}, f32[3,8,18]{2,1,0:T(8,128)S(1)}, u32[]{:S(2)}, u32[]{:S(2)}) collective-permute-start(f32[3,8,18]{2,1,0:T(8,128)S(1)} %bitcast.278), channel_id=1, source_target_pairs={{0,1},{1,2},{2,3},{3,4},{4,5},{5,6},{6,7},{8,9},{9,10},{10,11},{11... | collective-permute-start | bytes 5192 | tf_op jit(solution)/shard_map/ppermute | solution.py:116
  164.4 4.0 %collective-permute-start.7 = (f32[3,8,18]{2,1,0:T(8,128)S(1)}, f32[3,8,18]{2,1,0:T(8,128)S(1)}, u32[]{:S(2)}, u32[]{:S(2)}) collective-permute-start(f32[3,8,18]{2,1,0:T(8,128)S(1)} %bitcast.280), channel_id=1, source_target_pairs={{1,0},{2,1},{3,2},{4,3},{5,4},{6,5},{7,6},{9,8},{10,9},{11,10},{12... | collective-permute-start | bytes 5192 | tf_op jit(solution)/shard_map/ppermute | solution.py:119
  (152 shorter events, 17.4 us)
Async XLA Ops:
  0.6 8.3 %copy-start = (f32[3,8,16,256]{3,2,1,0:T(8,128)S(1)}, f32[3,8,16,256]{3,2,1,0:T(8,128)}, u32[]{:S(2)}) copy-start(f32[3,8,16,256]{3,2,1,0:T(8,128)} %param.16) | copy-start | bytes 1179652
  1.9 7.0 %copy-start.22 = (s32[128,1]{0,1:T(1,128)S(1)}, s32[128,1]{0,1:T(1,128)}, u32[]{:S(2)}) copy-start(s32[128,1]{0,1:T(1,128)} %param.24) | copy-start | bytes 1540
  3.1 7.2 %copy-start.23 = (s32[128]{0:T(128)S(1)}, s32[128]{0:T(128)}, u32[]{:S(2)}) copy-start(s32[128]{0:T(128)} %param.25) | copy-start | bytes 1540
  3.1 18.6 %copy-start.7 = (f32[128,3,128]{2,0,1:T(8,128)S(1)}, f32[128,3,128]{2,0,1:T(8,128)}, u32[]{:S(2)}) copy-start(f32[128,3,128]{2,0,1:T(8,128)} %param.20) | copy-start | bytes 589828
  3.1 34.8 %collective-permute-start = (f32[6,8,256]{2,1,0:T(8,128)S(1)}, f32[6,8,256]{2,1,0:T(8,128)S(1)}, u32[]{:S(2)}, u32[]{:S(2)}) collective-permute-start(f32[6,8,256]{2,1,0:T(8,128)S(1)} %get-tuple-element.101), channel_id=1, source_target_pairs={{0,8},{8,16},{16,24},{1,9},{9,17},{17,25},{2,10},{10,18},{18,26},{... | collective-permute-start | bytes 147464 | tf_op jit(solution)/shard_map/ppermute | solution.py:116
  7.0 31.0 %collective-permute-start.1 = (f32[6,8,256]{2,1,0:T(8,128)S(1)}, f32[6,8,256]{2,1,0:T(8,128)S(1)}, u32[]{:S(2)}, u32[]{:S(2)}) collective-permute-start(f32[6,8,256]{2,1,0:T(8,128)S(1)} %get-tuple-element.102), channel_id=1, source_target_pairs={{8,0},{16,8},{24,16},{9,1},{17,9},{25,17},{10,2},{18,10},{26,18},{... | collective-permute-start | bytes 147464 | tf_op jit(solution)/shard_map/ppermute | solution.py:119
  8.9 14.0 %copy-start.17 = (f32[128,128]{1,0:T(8,128)S(1)}, f32[128,128]{1,0:T(8,128)}, u32[]{:S(2)}) copy-start(f32[128,128]{1,0:T(8,128)} %param.21) | copy-start | bytes 196612
  8.9 14.0 %copy-start.21 = (s32[128]{0:T(128)S(1)}, s32[128]{0:T(128)}, u32[]{:S(2)}) copy-start(s32[128]{0:T(128)} %param.22) | copy-start | bytes 1540
  25.3 7.6 %copy-start.19 = (f32[32,2,128]{2,1,0:T(2,128)S(1)}, f32[32,2,128]{2,1,0:T(2,128)}, u32[]{:S(2)}) copy-start(f32[32,2,128]{2,1,0:T(2,128)} %param.27) | copy-start | bytes 98308
  25.3 11.7 %copy-start.18 = (f32[32,3,128]{2,0,1:T(8,128)S(1)}, f32[32,3,128]{2,0,1:T(8,128)}, u32[]{:S(2)}) copy-start(f32[32,3,128]{2,0,1:T(8,128)} %param.26) | copy-start | bytes 147460
  26.5 24.3 %all-to-all-start = ((f32[32,5,8,128]{3,2,1,0:T(8,128)}), f32[32,5,8,128]{3,2,1,0:T(8,128)S(1)}, u32[]{:S(2)}, u32[]{:S(2)}) async-start(f32[32,5,8,128]{3,2,1,0:T(8,128)} %select_select_fusion), calls=%async_computation | async-start | bytes 1310720 | tf_op jit(solution)/shard_map/all_to_all | solution.py:286
  37.0 9.2 %copy-start.8 = (f32[32,1,128]{2,0,1:T(8,128)}, f32[32,1,128]{2,0,1:T(8,128)S(1)}, u32[]{:S(2)}) copy-start(f32[32,1,128]{2,0,1:T(8,128)S(1)} %get-tuple-element.109) | copy-start | bytes 49156
  37.0 9.2 %copy-start.10 = (f32[32,1,128]{2,0,1:T(8,128)}, f32[32,1,128]{2,0,1:T(8,128)S(1)}, u32[]{:S(2)}) copy-start(f32[32,1,128]{2,0,1:T(8,128)S(1)} %get-tuple-element.110) | copy-start | bytes 49156
  37.0 9.2 %copy-start.12 = (f32[32,1,128]{2,0,1:T(8,128)}, f32[32,1,128]{2,0,1:T(8,128)S(1)}, u32[]{:S(2)}) copy-start(f32[32,1,128]{2,0,1:T(8,128)S(1)} %get-tuple-element.111) | copy-start | bytes 49156
  38.0 7.4 %copy-start.14 = (f32[8,16,256]{2,1,0:T(8,128)S(1)}, f32[8,16,256]{2,1,0:T(8,128)}, u32[]{:S(2)}) copy-start(f32[8,16,256]{2,1,0:T(8,128)} %param.19) | copy-start | bytes 393220
  38.0 8.1 %copy-start.3 = (f32[3,4096]{1,0:T(4,128)S(1)}, f32[3,4096]{1,0:T(4,128)}, u32[]{:S(2)}) copy-start(f32[3,4096]{1,0:T(4,128)} %shard_map.150) | copy-start | bytes 147460
  38.0 8.1 %copy-start.20 = (f32[32,128]{1,0:T(8,128)S(1)}, f32[32,128]{1,0:T(8,128)}, u32[]{:S(2)}) copy-start(f32[32,128]{1,0:T(8,128)} %param.28) | copy-start | bytes 49156
  38.6 7.9 %collective-permute-start.2 = (f32[6,8,18]{2,1,0:T(8,128)S(1)}, f32[6,8,18]{2,1,0:T(8,128)S(1)}, u32[]{:S(2)}, u32[]{:S(2)}) collective-permute-start(f32[6,8,18]{2,1,0:T(8,128)S(1)} %bitcast.272), channel_id=1, source_target_pairs={{0,1},{1,2},{2,3},{3,4},{4,5},{5,6},{6,7},{8,9},{9,10},{10,11},{11... | collective-permute-start | bytes 10376 | tf_op jit(solution)/shard_map/ppermute | solution.py:116
  42.1 4.9 %collective-permute-start.3 = (f32[6,8,18]{2,1,0:T(8,128)S(1)}, f32[6,8,18]{2,1,0:T(8,128)S(1)}, u32[]{:S(2)}, u32[]{:S(2)}) collective-permute-start(f32[6,8,18]{2,1,0:T(8,128)S(1)} %bitcast.274), channel_id=1, source_target_pairs={{1,0},{2,1},{3,2},{4,3},{5,4},{6,5},{7,6},{9,8},{10,9},{11,10},{12... | collective-permute-start | bytes 10376 | tf_op jit(solution)/shard_map/ppermute | solution.py:119
  56.3 74.3 %copy-start.9 = (f32[32,1,128]{2,0,1:T(8,128)S(1)}, f32[32,1,128]{2,0,1:T(8,128)}, u32[]{:S(2)}) copy-start(f32[32,1,128]{2,0,1:T(8,128)} %copy-done.8) | copy-start | bytes 49156
  56.3 74.3 %copy-start.11 = (f32[32,1,128]{2,0,1:T(8,128)S(1)}, f32[32,1,128]{2,0,1:T(8,128)}, u32[]{:S(2)}) copy-start(f32[32,1,128]{2,0,1:T(8,128)} %copy-done.10) | copy-start | bytes 49156
  56.3 74.3 %copy-start.13 = (f32[32,1,128]{2,0,1:T(8,128)S(1)}, f32[32,1,128]{2,0,1:T(8,128)}, u32[]{:S(2)}) copy-start(f32[32,1,128]{2,0,1:T(8,128)} %copy-done.12) | copy-start | bytes 49156
  56.7 12.2 %copy-start.15 = (f32[2,80,128]{2,1,0:T(8,128)S(1)}, f32[2,80,128]{2,1,0:T(8,128)}, u32[]{:S(2)}) copy-start(f32[2,80,128]{2,1,0:T(8,128)} %get-tuple-element.185) | copy-start | bytes 245764 | tf_op jit(solution)/shard_map/while
  68.9 20.4 %copy-start.16 = (f32[2,80,128]{2,1,0:T(8,128)}, f32[2,80,128]{2,1,0:T(8,128)S(1)}, u32[]{:S(2)}) copy-start(f32[2,80,128]{2,1,0:T(8,128)S(1)} %bitcast_dynamic-update-slice_fusion.2) | copy-start | bytes 245764 | tf_op jit(solution)/shard_map/while
  89.6 12.2 %copy-start.15 = (f32[2,80,128]{2,1,0:T(8,128)S(1)}, f32[2,80,128]{2,1,0:T(8,128)}, u32[]{:S(2)}) copy-start(f32[2,80,128]{2,1,0:T(8,128)} %get-tuple-element.185) | copy-start | bytes 245764 | tf_op jit(solution)/shard_map/while
  101.8 20.4 %copy-start.16 = (f32[2,80,128]{2,1,0:T(8,128)}, f32[2,80,128]{2,1,0:T(8,128)S(1)}, u32[]{:S(2)}) copy-start(f32[2,80,128]{2,1,0:T(8,128)S(1)} %bitcast_dynamic-update-slice_fusion.2) | copy-start | bytes 245764 | tf_op jit(solution)/shard_map/while
  122.2 18.3 %all-to-all-start.1 = ((f32[32,5,3,128]{3,2,1,0:T(4,128)}), f32[32,5,3,128]{3,2,1,0:T(4,128)S(1)}, u32[]{:S(2)}, u32[]{:S(2)}) async-start(f32[32,5,3,128]{3,2,1,0:T(4,128)} %bitcast.64), calls=%async_computation.1 | async-start | bytes 655360 | tf_op jit(solution)/shard_map/all_to_all | solution.py:320
  134.8 17.1 %copy-start.2 = (f32[384,256]{1,0:T(8,128)S(1)}, f32[384,256]{1,0:T(8,128)}, u32[]{:S(2)}) copy-start(f32[384,256]{1,0:T(8,128)} %shard_map.151) | copy-start | bytes 1179652
  154.0 4.4 %collective-permute-start.4 = (f32[3,8,256]{2,1,0:T(8,128)S(1)}, f32[3,8,256]{2,1,0:T(8,128)S(1)}, u32[]{:S(2)}, u32[]{:S(2)}) collective-permute-start(f32[3,8,256]{2,1,0:T(8,128)S(1)} %get-tuple-element.107), channel_id=1, source_target_pairs={{0,8},{8,16},{16,24},{1,9},{9,17},{17,25},{2,10},{10,18},{18,26},{... | collective-permute-start | bytes 73736 | tf_op jit(solution)/shard_map/ppermute | solution.py:116
  156.4 5.1 %collective-permute-start.5 = (f32[3,8,256]{2,1,0:T(8,128)S(1)}, f32[3,8,256]{2,1,0:T(8,128)S(1)}, u32[]{:S(2)}, u32[]{:S(2)}) collective-permute-start(f32[3,8,256]{2,1,0:T(8,128)S(1)} %get-tuple-element.108), channel_id=1, source_target_pairs={{8,0},{16,8},{24,16},{9,1},{17,9},{25,17},{10,2},{18,10},{26,18},{... | collective-permute-start | bytes 73736 | tf_op jit(solution)/shard_map/ppermute | solution.py:119
  162.0 7.3 %collective-permute-start.6 = (f32[3,8,18]{2,1,0:T(8,128)S(1)}, f32[3,8,18]{2,1,0:T(8,128)S(1)}, u32[]{:S(2)}, u32[]{:S(2)}) collective-permute-start(f32[3,8,18]{2,1,0:T(8,128)S(1)} %bitcast.278), channel_id=1, source_target_pairs={{0,1},{1,2},{2,3},{3,4},{4,5},{5,6},{6,7},{8,9},{9,10},{10,11},{11... | collective-permute-start | bytes 5192 | tf_op jit(solution)/shard_map/ppermute | solution.py:116
  164.4 5.1 %collective-permute-start.7 = (f32[3,8,18]{2,1,0:T(8,128)S(1)}, f32[3,8,18]{2,1,0:T(8,128)S(1)}, u32[]{:S(2)}, u32[]{:S(2)}) collective-permute-start(f32[3,8,18]{2,1,0:T(8,128)S(1)} %bitcast.280), channel_id=1, source_target_pairs={{1,0},{2,1},{3,2},{4,3},{5,4},{6,5},{7,6},{9,8},{10,9},{11,10},{12... | collective-permute-start | bytes 5192 | tf_op jit(solution)/shard_map/ppermute | solution.py:119
  (4 other events, 5.8 us)

commit v12 on v10

--- a/solution.py
+++ b/solution.py
@@ -176,41 +176,41 @@
 
 
 def contact_pairs(slave, master):
-    delta_x = slave[:, 0, :, None] - master[:, 0, None, :]
-    delta_y = slave[:, 1, :, None] - master[:, 1, None, :]
-    delta_z = slave[:, 2, :, None] - master[:, 2, None, :]
-    normal_x = master[:, 3, None, :]
-    normal_y = master[:, 4, None, :]
-    normal_z = master[:, 5, None, :]
+    delta_x = slave[:, 0, None, :] - master[:, 0, :, None]
+    delta_y = slave[:, 1, None, :] - master[:, 1, :, None]
+    delta_z = slave[:, 2, None, :] - master[:, 2, :, None]
+    normal_x = master[:, 3, :, None]
+    normal_y = master[:, 4, :, None]
+    normal_z = master[:, 5, :, None]
     dist_sq = delta_x * delta_x + delta_y * delta_y + delta_z * delta_z
     gap_normal = normal_x * delta_x + normal_y * delta_y + normal_z * delta_z
     master_along = (
         master[:, 3] * master[:, 6] + master[:, 4] * master[:, 7] + master[:, 5] * master[:, 8]
     )
     closing = (
-        normal_x * slave[:, 3, :, None]
-        + normal_y * slave[:, 4, :, None]
-        + normal_z * slave[:, 5, :, None]
-    ) - master_along[:, None, :]
+        normal_x * slave[:, 3, None, :]
+        + normal_y * slave[:, 4, None, :]
+        + normal_z * slave[:, 5, None, :]
+    ) - master_along[:, :, None]
     weight = jnp.exp(-dist_sq / REACH_SQ)
     soft = gap_normal * (-1.0 / SOFT_GAP)
     depth_soft = SOFT_GAP * (jnp.maximum(soft, 0.0) + jnp.log1p(jnp.exp(-jnp.abs(soft))))
     push_force = (
-        slave[:, 6, :, None]
-        * master[:, 9, None, :]
+        slave[:, 6, None, :]
+        * master[:, 9, :, None]
         * weight
         * depth_soft
         * (1.0 + DAMPING * jnp.tanh(-closing))
     )
     slave_force = jnp.stack(
         [
-            jnp.sum(push_force * normal_x, axis=2),
-            jnp.sum(push_force * normal_y, axis=2),
-            jnp.sum(push_force * normal_z, axis=2),
+            jnp.sum(push_force * normal_x, axis=1),
+            jnp.sum(push_force * normal_y, axis=1),
+            jnp.sum(push_force * normal_z, axis=1),
         ],
         axis=1,
     )
-    reaction = jnp.sum(push_force, axis=1)
+    reaction = jnp.sum(push_force, axis=2)
     return (slave_force, reaction)
 
 

time: 143 us -> 141 us (0.986)
  other arithmetic: 47.3 us -> 45.5 us
    reduce_sum x2, other arithmetic: 34.4 us -> 32 us  [contact_pairs(): reaction = jnp.sum(push_force, axis=2)]
    unnamed x39 -> x37, local copies, waits for them, and re-layouts: 4.5 us -> 4.53 us
  transfers between devices with their start and end apart: 10 -> 10, of which waited for: 3 -> 4; matrix products, arithmetic and copies ran while one was open for 12% -> 12% of each run, Pallas kernels for 13% -> 14%
where the time goes in v12:
time: 141 us; the launch traced here: 138 us
  other arithmetic  45.5 us (32%)
  starting transfers between devices  36 us (26%)
  Pallas kernels  28.7 us (20%)
  local copies, waits for them, and re-layouts  16.4 us (12%)
  waiting for transfers between devices  9.31 us (7%)
    reduce_sum x2, other arithmetic, contact_pairs(): reaction = jnp.sum(push_force, axis=2)  32 us
    pallas_call x2, Pallas kernels, node_gather(): pl.pallas_call(gather_kernel, grid=(padded_count // TILE,), in_specs=[pl....  15.3 us
    pallas_call x2, Pallas kernels, node_scatter_add(): pl.pallas_call(scatter_kernel, grid=(padded_count // TILE,), in_specs=[pl...  13.4 us
    ppermute x4, starting transfers between devices, padded_2(): lax.ppermute(lax.index_in_dim(block, block.shape[dim] - 1, axis=dim, keep...  11.5 us
    ppermute x4, starting transfers between devices, padded_2(): lax.ppermute(lax.index_in_dim(block, 0, axis=dim, keepdims=False), axis,...  10.9 us
    all_to_all x1, starting transfers between devices, on_device(): lax.all_to_all(forces.reshape(devices, slot_depth, 3, seg_width), ('gx',...  7.19 us
    all_to_all x1, starting transfers between devices, on_device(): lax.all_to_all(outgoing.reshape(devices, slot_depth, 8, seg_width), ('gx'...  6.32 us
    all_to_all x1, waiting for transfers between devices, on_device(): lax.all_to_all(forces.reshape(devices, slot_depth, 3, seg_width), ('gx',...  5.65 us
  transfers between devices with their start and end apart: 10, of which 4 were waited for; matrix products, arithmetic and copies ran while one was open for 12% of the time, Pallas kernels for 14%

profile of v12, /device:TPU:9, one launch (start us, length us, event | category | flops | bytes accessed | tf_op | source)
XLA Modules:
  0.0 138.5 jit_solution(814434240170928069)
XLA Ops:
  0.6 1.3 copy.262
  1.9 1.1 copy_bitcast_fusion
  3.1 3.8 %collective-permute-start = (f32[6,8,256]{2,1,0:T(8,128)S(1)}, f32[6,8,256]{2,1,0:T(8,128)S(1)}, u32[]{:S(2)}, u32[]{:S(2)}) collective-permute-start(f32[6,8,256]{2,1,0:T(8,128)S(1)} %get-tuple-element.105), channel_id=1, source_target_pairs={{0,8},{8,16},{16,24},{1,9},{9,17},{17,25},{2,10},{10,18},{18,26},{... | collective-permute-start | bytes 147464 | tf_op jit(solution)/shard_map/ppermute | solution.py:116
  7.0 1.9 %collective-permute-start.1 = (f32[6,8,256]{2,1,0:T(8,128)S(1)}, f32[6,8,256]{2,1,0:T(8,128)S(1)}, u32[]{:S(2)}, u32[]{:S(2)}) collective-permute-start(f32[6,8,256]{2,1,0:T(8,128)S(1)} %get-tuple-element.106), channel_id=1, source_target_pairs={{8,0},{16,8},{24,16},{9,1},{17,9},{25,17},{10,2},{18,10},{26,18},{... | collective-permute-start | bytes 147464 | tf_op jit(solution)/shard_map/ppermute | solution.py:119
  9.4 0.9 copy.277
  10.6 11.2 %shard_map.149 = f32[3,16384]{1,0:T(4,128)} custom-call(s32[1,16384]{1,0:T(1,128)} %bitcast.284, f32[384,256]{1,0:T(8,128)} %bitcast.269), custom_call_target="tpu_custom_call" | custom-call | tf_op jit(solution)/shard_map/pallas_call | solution.py:73
  21.8 1.1 copy_add_fusion
  23.2 1.2 pad_maximum_fusion.3
  24.4 0.8 gather_fusion
  25.3 1.2 select_select_fusion
  26.5 6.3 %all-to-all-start = ((f32[32,5,8,128]{3,2,1,0:T(8,128)}), f32[32,5,8,128]{3,2,1,0:T(8,128)S(1)}, u32[]{:S(2)}, u32[]{:S(2)}) async-start(f32[32,5,8,128]{3,2,1,0:T(8,128)} %select_select_fusion), calls=%async_computation | async-start | bytes 1310720 | tf_op jit(solution)/shard_map/all_to_all | solution.py:291
  32.9 4.0 %shard_map.150 = f32[3,4096]{1,0:T(4,128)} custom-call(s32[1,4096]{1,0:T(1,128)} %bitcast.299, f32[384,256]{1,0:T(8,128)} %bitcast.270), custom_call_target="tpu_custom_call" | custom-call | tf_op jit(solution)/shard_map/pallas_call | solution.py:73
  37.0 0.9 copy_add_fusion.1
  38.6 3.1 %collective-permute-start.2 = (f32[6,8,18]{2,1,0:T(8,128)S(1)}, f32[6,8,18]{2,1,0:T(8,128)S(1)}, u32[]{:S(2)}, u32[]{:S(2)}) collective-permute-start(f32[6,8,18]{2,1,0:T(8,128)S(1)} %bitcast.301), channel_id=1, source_target_pairs={{0,1},{1,2},{2,3},{3,4},{4,5},{5,6},{6,7},{8,9},{9,10},{10,11},{11... | collective-permute-start | bytes 10376 | tf_op jit(solution)/shard_map/ppermute | solution.py:116
  42.1 3.1 %collective-permute-start.3 = (f32[6,8,18]{2,1,0:T(8,128)S(1)}, f32[6,8,18]{2,1,0:T(8,128)S(1)}, u32[]{:S(2)}, u32[]{:S(2)}) collective-permute-start(f32[6,8,18]{2,1,0:T(8,128)S(1)} %bitcast.303), channel_id=1, source_target_pairs={{1,0},{2,1},{3,2},{4,3},{5,4},{6,5},{7,6},{9,8},{10,9},{11,10},{12... | collective-permute-start | bytes 10376 | tf_op jit(solution)/shard_map/ppermute | solution.py:119
  52.4 34.9 %while.12 = (s32[]{:T(128)}, f32[2,80,3,128]{3,1,2,0:T(8,128)}, f32[2,80,128]{2,1,0:T(8,128)}, f32[2,80,7,128]{3,1,0,2:T(8,128)S(1)}, f32[2,80,10,128]{3,1,2,0:T(8,128)S(1)}, /*index=5*/s32[]{:T(128)}) while((s32[]{:T(128)}, f32[2,80,3,128]{3,1,2,0:T(8,128)}, f32[2,80,128]{2,1,0:T(8,128)}, f32[2,80,7,128]{3,1,0,2:T(8,128)S(1)}, ...), condition=%wide.region_8.9_spmd, body=%wide.region_3.8_spmd.sunk | while | flops 52500480 | bytes 3933261 | solution.py:308
  52.6 16.0 %fusion.91 = (f32[80,128]{1,0:T(8,128)S(1)}, f32[80,128]{1,0:T(8,128)S(1)}, f32[80,128]{1,0:T(8,128)S(1)}, f32[80,128]{1,0:T(8,128)S(1)}) fusion(f32[80,128]{1,0:T(8,128)S(1)} %fusion.90, f32[80,128]{1,0:T(8,128)S(1)} %get-tuple-element.169, f32[80,128]{1,0:T(8,128)S(1)} %get-tuple-element.170, f32[80,128]{1,0:T(8,128)S(1)} %get-tuple-element.171, ...), kind=kLoop, calls=%fused_computation.49.clone.1 | loop fusion | flops 52387840 | bytes 778240 | tf_op jit(solution)/shard_map/while/body/eval_jaxpr/reduce_sum | solution.py:213
  70.0 16.0 %fusion.91 = (f32[80,128]{1,0:T(8,128)S(1)}, f32[80,128]{1,0:T(8,128)S(1)}, f32[80,128]{1,0:T(8,128)S(1)}, f32[80,128]{1,0:T(8,128)S(1)}) fusion(f32[80,128]{1,0:T(8,128)S(1)} %fusion.90, f32[80,128]{1,0:T(8,128)S(1)} %get-tuple-element.169, f32[80,128]{1,0:T(8,128)S(1)} %get-tuple-element.170, f32[80,128]{1,0:T(8,128)S(1)} %get-tuple-element.171, ...), kind=kLoop, calls=%fused_computation.49.clone.1 | loop fusion | flops 52387840 | bytes 778240 | tf_op jit(solution)/shard_map/while/body/eval_jaxpr/reduce_sum | solution.py:213
  87.3 1.8 %copy.305 = f32[2,80,3,128]{3,2,1,0:T(4,128)} copy(f32[2,80,3,128]{3,1,2,0:T(8,128)} %get-tuple-element.31) | data formatting | bytes 491520 | tf_op jit(solution)/shard_map/reshape;reshape | solution.py:326
  89.1 7.2 %all-to-all-start.1 = ((f32[32,5,3,128]{3,2,1,0:T(4,128)}), f32[32,5,3,128]{3,2,1,0:T(4,128)S(1)}, u32[]{:S(2)}, u32[]{:S(2)}) async-start(f32[32,5,3,128]{3,2,1,0:T(4,128)} %bitcast.71), calls=%async_computation.1 | async-start | bytes 655360 | tf_op jit(solution)/shard_map/all_to_all | solution.py:325
  96.3 1.2 convolution_negate_fusion
  98.2 3.6 %shard_map.151 = f32[384,256]{1,0:T(8,128)} custom-call(s32[1,4096]{1,0:T(1,128)} %bitcast.300, f32[3,4096]{1,0:T(4,128)} %bitcast.283), custom_call_target="tpu_custom_call" | custom-call | tf_op jit(solution)/shard_map/pallas_call | solution.py:91
  101.8 5.6 %all-to-all-done.1 = f32[32,5,3,128]{3,2,1,0:T(4,128)S(1)} async-done(((f32[32,5,3,128]{3,2,1,0:T(4,128)}), f32[32,5,3,128]{3,2,1,0:T(4,128)S(1)}, u32[]{:S(2)}, u32[]{:S(2)}) %all-to-all-start.1) | async-done | bytes 245792 | tf_op jit(solution)/shard_map/all_to_all | solution.py:325
  108.2 0.9 select_bitcast_fusion.force_ref
  109.1 9.8 %shard_map.152 = f32[384,256]{1,0:T(8,128)} custom-call(s32[1,16384]{1,0:T(1,128)} %bitcast.285, f32[3,16384]{1,0:T(4,128)} %select_bitcast_fusion.force_ref), custom_call_target="tpu_custom_call" | custom-call | tf_op jit(solution)/shard_map/pallas_call | solution.py:91
  118.9 1.1 add.287
  120.8 2.5 %collective-permute-start.4 = (f32[3,8,256]{2,1,0:T(8,128)S(1)}, f32[3,8,256]{2,1,0:T(8,128)S(1)}, u32[]{:S(2)}, u32[]{:S(2)}) collective-permute-start(f32[3,8,256]{2,1,0:T(8,128)S(1)} %get-tuple-element.111), channel_id=1, source_target_pairs={{0,8},{8,16},{16,24},{1,9},{9,17},{17,25},{2,10},{10,18},{18,26},{... | collective-permute-start | bytes 73736 | tf_op jit(solution)/shard_map/ppermute | solution.py:116
  123.3 1.9 %collective-permute-start.5 = (f32[3,8,256]{2,1,0:T(8,128)S(1)}, f32[3,8,256]{2,1,0:T(8,128)S(1)}, u32[]{:S(2)}, u32[]{:S(2)}) collective-permute-start(f32[3,8,256]{2,1,0:T(8,128)S(1)} %get-tuple-element.112), channel_id=1, source_target_pairs={{8,0},{16,8},{24,16},{9,1},{17,9},{25,17},{10,2},{18,10},{26,18},{... | collective-permute-start | bytes 73736 | tf_op jit(solution)/shard_map/ppermute | solution.py:119
  125.2 3.2 %collective-permute-done.5 = f32[3,8,256]{2,1,0:T(8,128)S(1)} collective-permute-done((f32[3,8,256]{2,1,0:T(8,128)S(1)}, f32[3,8,256]{2,1,0:T(8,128)S(1)}, u32[]{:S(2)}, u32[]{:S(2)}) %collective-permute-start.5) | collective-permute-done | bytes 24608 | tf_op jit(solution)/shard_map/ppermute | solution.py:119
  128.9 2.2 %collective-permute-start.6 = (f32[3,8,18]{2,1,0:T(8,128)S(1)}, f32[3,8,18]{2,1,0:T(8,128)S(1)}, u32[]{:S(2)}, u32[]{:S(2)}) collective-permute-start(f32[3,8,18]{2,1,0:T(8,128)S(1)} %bitcast.306), channel_id=1, source_target_pairs={{0,1},{1,2},{2,3},{3,4},{4,5},{5,6},{6,7},{8,9},{9,10},{10,11},{11... | collective-permute-start | bytes 5192 | tf_op jit(solution)/shard_map/ppermute | solution.py:116
  131.3 4.0 %collective-permute-start.7 = (f32[3,8,18]{2,1,0:T(8,128)S(1)}, f32[3,8,18]{2,1,0:T(8,128)S(1)}, u32[]{:S(2)}, u32[]{:S(2)}) collective-permute-start(f32[3,8,18]{2,1,0:T(8,128)S(1)} %bitcast.308), channel_id=1, source_target_pairs={{1,0},{2,1},{3,2},{4,3},{5,4},{6,5},{7,6},{9,8},{10,9},{11,10},{12... | collective-permute-start | bytes 5192 | tf_op jit(solution)/shard_map/ppermute | solution.py:119
  135.3 0.9 copy.303
  (134 shorter events, 17.1 us)
Async XLA Ops:
  0.6 8.3 %copy-start = (f32[3,8,16,256]{3,2,1,0:T(8,128)S(1)}, f32[3,8,16,256]{3,2,1,0:T(8,128)}, u32[]{:S(2)}) copy-start(f32[3,8,16,256]{3,2,1,0:T(8,128)} %param.16) | copy-start | bytes 1179652
  1.9 7.0 %copy-start.13 = (s32[128,1]{0,1:T(1,128)S(1)}, s32[128,1]{0,1:T(1,128)}, u32[]{:S(2)}) copy-start(s32[128,1]{0,1:T(1,128)} %param.24) | copy-start | bytes 1540
  3.1 7.2 %copy-start.14 = (s32[128]{0:T(128)S(1)}, s32[128]{0:T(128)}, u32[]{:S(2)}) copy-start(s32[128]{0:T(128)} %param.25) | copy-start | bytes 1540
  3.1 18.7 %copy-start.6 = (f32[128,3,128]{2,0,1:T(8,128)S(1)}, f32[128,3,128]{2,0,1:T(8,128)}, u32[]{:S(2)}) copy-start(f32[128,3,128]{2,0,1:T(8,128)} %param.20) | copy-start | bytes 589828
  3.1 34.7 %collective-permute-start = (f32[6,8,256]{2,1,0:T(8,128)S(1)}, f32[6,8,256]{2,1,0:T(8,128)S(1)}, u32[]{:S(2)}, u32[]{:S(2)}) collective-permute-start(f32[6,8,256]{2,1,0:T(8,128)S(1)} %get-tuple-element.105), channel_id=1, source_target_pairs={{0,8},{8,16},{16,24},{1,9},{9,17},{17,25},{2,10},{10,18},{18,26},{... | collective-permute-start | bytes 147464 | tf_op jit(solution)/shard_map/ppermute | solution.py:116
  7.0 30.9 %collective-permute-start.1 = (f32[6,8,256]{2,1,0:T(8,128)S(1)}, f32[6,8,256]{2,1,0:T(8,128)S(1)}, u32[]{:S(2)}, u32[]{:S(2)}) collective-permute-start(f32[6,8,256]{2,1,0:T(8,128)S(1)} %get-tuple-element.106), channel_id=1, source_target_pairs={{8,0},{16,8},{24,16},{9,1},{17,9},{25,17},{10,2},{18,10},{26,18},{... | collective-permute-start | bytes 147464 | tf_op jit(solution)/shard_map/ppermute | solution.py:119
  8.9 14.0 %copy-start.8 = (f32[128,128]{1,0:T(8,128)S(1)}, f32[128,128]{1,0:T(8,128)}, u32[]{:S(2)}) copy-start(f32[128,128]{1,0:T(8,128)} %param.21) | copy-start | bytes 196612
  8.9 14.0 %copy-start.12 = (s32[128]{0:T(128)S(1)}, s32[128]{0:T(128)}, u32[]{:S(2)}) copy-start(s32[128]{0:T(128)} %param.22) | copy-start | bytes 1540
  25.3 7.6 %copy-start.10 = (f32[32,2,128]{2,1,0:T(2,128)S(1)}, f32[32,2,128]{2,1,0:T(2,128)}, u32[]{:S(2)}) copy-start(f32[32,2,128]{2,1,0:T(2,128)} %param.27) | copy-start | bytes 98308
  25.3 11.7 %copy-start.9 = (f32[32,3,128]{2,0,1:T(8,128)S(1)}, f32[32,3,128]{2,0,1:T(8,128)}, u32[]{:S(2)}) copy-start(f32[32,3,128]{2,0,1:T(8,128)} %param.26) | copy-start | bytes 147460
  26.5 24.3 %all-to-all-start = ((f32[32,5,8,128]{3,2,1,0:T(8,128)}), f32[32,5,8,128]{3,2,1,0:T(8,128)S(1)}, u32[]{:S(2)}, u32[]{:S(2)}) async-start(f32[32,5,8,128]{3,2,1,0:T(8,128)} %select_select_fusion), calls=%async_computation | async-start | bytes 1310720 | tf_op jit(solution)/shard_map/all_to_all | solution.py:291
  38.0 7.2 %copy-start.7 = (f32[8,16,256]{2,1,0:T(8,128)S(1)}, f32[8,16,256]{2,1,0:T(8,128)}, u32[]{:S(2)}) copy-start(f32[8,16,256]{2,1,0:T(8,128)} %param.19) | copy-start | bytes 393220
  38.0 8.0 %copy-start.2 = (f32[3,4096]{1,0:T(4,128)S(1)}, f32[3,4096]{1,0:T(4,128)}, u32[]{:S(2)}) copy-start(f32[3,4096]{1,0:T(4,128)} %shard_map.150) | copy-start | bytes 147460
  38.0 7.9 %copy-start.11 = (f32[32,128]{1,0:T(8,128)S(1)}, f32[32,128]{1,0:T(8,128)}, u32[]{:S(2)}) copy-start(f32[32,128]{1,0:T(8,128)} %param.28) | copy-start | bytes 49156
  38.6 7.7 %collective-permute-start.2 = (f32[6,8,18]{2,1,0:T(8,128)S(1)}, f32[6,8,18]{2,1,0:T(8,128)S(1)}, u32[]{:S(2)}, u32[]{:S(2)}) collective-permute-start(f32[6,8,18]{2,1,0:T(8,128)S(1)} %bitcast.301), channel_id=1, source_target_pairs={{0,1},{1,2},{2,3},{3,4},{4,5},{5,6},{6,7},{8,9},{9,10},{10,11},{11... | collective-permute-start | bytes 10376 | tf_op jit(solution)/shard_map/ppermute | solution.py:116
  42.1 4.9 %collective-permute-start.3 = (f32[6,8,18]{2,1,0:T(8,128)S(1)}, f32[6,8,18]{2,1,0:T(8,128)S(1)}, u32[]{:S(2)}, u32[]{:S(2)}) collective-permute-start(f32[6,8,18]{2,1,0:T(8,128)S(1)} %bitcast.303), channel_id=1, source_target_pairs={{1,0},{2,1},{3,2},{4,3},{5,4},{6,5},{7,6},{9,8},{10,9},{11,10},{12... | collective-permute-start | bytes 10376 | tf_op jit(solution)/shard_map/ppermute | solution.py:119
  89.1 18.3 %all-to-all-start.1 = ((f32[32,5,3,128]{3,2,1,0:T(4,128)}), f32[32,5,3,128]{3,2,1,0:T(4,128)S(1)}, u32[]{:S(2)}, u32[]{:S(2)}) async-start(f32[32,5,3,128]{3,2,1,0:T(4,128)} %bitcast.71), calls=%async_computation.1 | async-start | bytes 655360 | tf_op jit(solution)/shard_map/all_to_all | solution.py:325
  101.8 17.1 %copy-start.1 = (f32[384,256]{1,0:T(8,128)S(1)}, f32[384,256]{1,0:T(8,128)}, u32[]{:S(2)}) copy-start(f32[384,256]{1,0:T(8,128)} %shard_map.151) | copy-start | bytes 1179652
  118.9 1.4 %copy-start.3 = (f32[1,8,16,256]{3,1,2,0:T(8,128)S(1)}, f32[1,8,16,256]{3,1,2,0:T(8,128)}, u32[]{:S(2)}) copy-start(f32[1,8,16,256]{3,1,2,0:T(8,128)} %fusion.70) | copy-start | bytes 393220
  118.9 1.4 %copy-start.4 = (f32[1,8,16,256]{3,1,2,0:T(8,128)S(1)}, f32[1,8,16,256]{3,1,2,0:T(8,128)}, u32[]{:S(2)}) copy-start(f32[1,8,16,256]{3,1,2,0:T(8,128)} %fusion.72) | copy-start | bytes 393220
  118.9 1.4 %copy-start.5 = (f32[8,16,256]{2,0,1:T(8,128)S(1)}, f32[8,16,256]{2,0,1:T(8,128)}, u32[]{:S(2)}) copy-start(f32[8,16,256]{2,0,1:T(8,128)} %copy.295) | copy-start | bytes 393220
  120.8 4.4 %collective-permute-start.4 = (f32[3,8,256]{2,1,0:T(8,128)S(1)}, f32[3,8,256]{2,1,0:T(8,128)S(1)}, u32[]{:S(2)}, u32[]{:S(2)}) collective-permute-start(f32[3,8,256]{2,1,0:T(8,128)S(1)} %get-tuple-element.111), channel_id=1, source_target_pairs={{0,8},{8,16},{16,24},{1,9},{9,17},{17,25},{2,10},{10,18},{18,26},{... | collective-permute-start | bytes 73736 | tf_op jit(solution)/shard_map/ppermute | solution.py:116
  123.3 5.1 %collective-permute-start.5 = (f32[3,8,256]{2,1,0:T(8,128)S(1)}, f32[3,8,256]{2,1,0:T(8,128)S(1)}, u32[]{:S(2)}, u32[]{:S(2)}) collective-permute-start(f32[3,8,256]{2,1,0:T(8,128)S(1)} %get-tuple-element.112), channel_id=1, source_target_pairs={{8,0},{16,8},{24,16},{9,1},{17,9},{25,17},{10,2},{18,10},{26,18},{... | collective-permute-start | bytes 73736 | tf_op jit(solution)/shard_map/ppermute | solution.py:119
  128.9 7.3 %collective-permute-start.6 = (f32[3,8,18]{2,1,0:T(8,128)S(1)}, f32[3,8,18]{2,1,0:T(8,128)S(1)}, u32[]{:S(2)}, u32[]{:S(2)}) collective-permute-start(f32[3,8,18]{2,1,0:T(8,128)S(1)} %bitcast.306), channel_id=1, source_target_pairs={{0,1},{1,2},{2,3},{3,4},{4,5},{5,6},{6,7},{8,9},{9,10},{10,11},{11... | collective-permute-start | bytes 5192 | tf_op jit(solution)/shard_map/ppermute | solution.py:116
  131.3 5.1 %collective-permute-start.7 = (f32[3,8,18]{2,1,0:T(8,128)S(1)}, f32[3,8,18]{2,1,0:T(8,128)S(1)}, u32[]{:S(2)}, u32[]{:S(2)}) collective-permute-start(f32[3,8,18]{2,1,0:T(8,128)S(1)} %bitcast.308), channel_id=1, source_target_pairs={{1,0},{2,1},{3,2},{4,3},{5,4},{6,5},{7,6},{9,8},{10,9},{11,10},{12... | collective-permute-start | bytes 5192 | tf_op jit(solution)/shard_map/ppermute | solution.py:119

commit v13 on v12

--- a/solution.py
+++ b/solution.py
@@ -300,18 +300,7 @@
     picked = arrived[:, 7, 0].astype(jnp.int32)
     arrived = arrived[:, :7]
     paired = jnp.take(master_data, picked, axis=0)
-    group_size = 16 * slot_depth
-
-    def per_group(pairing):
-        return contact_pairs(pairing[0], pairing[1])
-
-    forces, reaction = lax.map(
-        per_group,
-        (
-            arrived.reshape(item_total // group_size, group_size, 7, seg_width),
-            paired.reshape(item_total // group_size, group_size, 10, seg_width),
-        ),
-    )
+    forces, reaction = contact_pairs(arrived, paired)
     forces = forces.reshape(item_total, 3, seg_width)
     reaction = reaction.reshape(item_total, seg_width)
     onehot = (picked[:, None] == jnp.arange(master_total, dtype=jnp.int32)[None, :]).astype(

time: 141 us -> 134 us (0.950)
  the two profiles are of different devices: /device:TPU:9 before, /device:TPU:10 now
where the time goes in v13:
time: 134 us; the launch traced here: 133 us
  other arithmetic  40.1 us (30%)
  starting transfers between devices  32.6 us (24%)
  Pallas kernels  28.6 us (21%)
  local copies, waits for them, and re-layouts  15.1 us (11%)
  waiting for transfers between devices  15 us (11%)
  between operations  1.46 us (1%)
    reduce_sum x1, other arithmetic, contact_pairs(): jnp.sum(push_force * normal_x, axis=1)  26.4 us
    pallas_call x2, Pallas kernels, node_gather(): pl.pallas_call(gather_kernel, grid=(padded_count // TILE,), in_specs=[pl....  15.3 us
    pallas_call x2, Pallas kernels, node_scatter_add(): pl.pallas_call(scatter_kernel, grid=(padded_count // TILE,), in_specs=[pl...  13.4 us
    ppermute x4, starting transfers between devices, padded_2(): lax.ppermute(lax.index_in_dim(block, 0, axis=dim, keepdims=False), axis,...  12 us
    ppermute x4, starting transfers between devices, padded_2(): lax.ppermute(lax.index_in_dim(block, block.shape[dim] - 1, axis=dim, keep...  9.36 us
    ppermute x4, waiting for transfers between devices, padded_2(): lax.ppermute(lax.index_in_dim(block, block.shape[dim] - 1, axis=dim, keep...  9.31 us
    all_to_all x1, starting transfers between devices, on_device(): lax.all_to_all(outgoing.reshape(devices, slot_depth, 8, seg_width), ('gx'...  6.03 us
    all_to_all x1, waiting for transfers between devices, on_device(): lax.all_to_all(forces.reshape(devices, slot_depth, 3, seg_width), ('gx',...  5.7 us
  transfers between devices with their start and end apart: 10, of which 4 were waited for; matrix products, arithmetic and copies ran while one was open for 10% of the time, Pallas kernels for 14%

profile of v13, /device:TPU:10, one launch (start us, length us, event | category | flops | bytes accessed | tf_op | source)
XLA Modules:
  0.0 133.3 jit_solution(14207858615304033740)
XLA Ops:
  0.6 1.3 copy.235
  1.9 1.1 copy_bitcast_fusion
  3.2 2.1 %collective-permute-start.1 = (f32[6,8,256]{2,1,0:T(8,128)S(1)}, f32[6,8,256]{2,1,0:T(8,128)S(1)}, u32[]{:S(2)}, u32[]{:S(2)}) collective-permute-start(f32[6,8,256]{2,1,0:T(8,128)S(1)} %get-tuple-element.38), channel_id=1, source_target_pairs={{8,0},{16,8},{24,16},{9,1},{17,9},{25,17},{10,2},{18,10},{26,18},{... | collective-permute-start | bytes 147464 | tf_op jit(solution)/shard_map/ppermute | solution.py:119
  5.2 2.4 %collective-permute-start = (f32[6,8,256]{2,1,0:T(8,128)S(1)}, f32[6,8,256]{2,1,0:T(8,128)S(1)}, u32[]{:S(2)}, u32[]{:S(2)}) collective-permute-start(f32[6,8,256]{2,1,0:T(8,128)S(1)} %get-tuple-element.37), channel_id=1, source_target_pairs={{0,8},{8,16},{16,24},{1,9},{9,17},{17,25},{2,10},{10,18},{18,26},{... | collective-permute-start | bytes 147464 | tf_op jit(solution)/shard_map/ppermute | solution.py:116
  8.1 0.9 copy.250
  9.4 11.2 %shard_map.149 = f32[3,16384]{1,0:T(4,128)} custom-call(s32[1,16384]{1,0:T(1,128)} %bitcast.210, f32[384,256]{1,0:T(8,128)} %bitcast.189), custom_call_target="tpu_custom_call" | custom-call | tf_op jit(solution)/shard_map/pallas_call | solution.py:73
  20.6 1.1 copy_add_fusion
  22.0 1.2 pad_maximum_fusion.3
  24.0 1.2 select_select_fusion
  25.3 6.0 %all-to-all-start = ((f32[32,5,8,128]{3,2,1,0:T(8,128)}), f32[32,5,8,128]{3,2,1,0:T(8,128)S(1)}, u32[]{:S(2)}, u32[]{:S(2)}) async-start(f32[32,5,8,128]{3,2,1,0:T(8,128)} %select_select_fusion), calls=%async_computation | async-start | bytes 1310720 | tf_op jit(solution)/shard_map/all_to_all | solution.py:291
  31.4 4.0 %shard_map.150 = f32[3,4096]{1,0:T(4,128)} custom-call(s32[1,4096]{1,0:T(1,128)} %bitcast.236, f32[384,256]{1,0:T(8,128)} %bitcast.190), custom_call_target="tpu_custom_call" | custom-call | tf_op jit(solution)/shard_map/pallas_call | solution.py:73
  35.4 0.9 copy_add_fusion.1
  37.0 3.4 %collective-permute-start.3 = (f32[6,8,18]{2,1,0:T(8,128)S(1)}, f32[6,8,18]{2,1,0:T(8,128)S(1)}, u32[]{:S(2)}, u32[]{:S(2)}) collective-permute-start(f32[6,8,18]{2,1,0:T(8,128)S(1)} %bitcast.238), channel_id=1, source_target_pairs={{1,0},{2,1},{3,2},{4,3},{5,4},{6,5},{7,6},{9,8},{10,9},{11,10},{12... | collective-permute-start | bytes 10376 | tf_op jit(solution)/shard_map/ppermute | solution.py:119
  40.8 2.6 %collective-permute-start.2 = (f32[6,8,18]{2,1,0:T(8,128)S(1)}, f32[6,8,18]{2,1,0:T(8,128)S(1)}, u32[]{:S(2)}, u32[]{:S(2)}) collective-permute-start(f32[6,8,18]{2,1,0:T(8,128)S(1)} %bitcast.240), channel_id=1, source_target_pairs={{0,1},{1,2},{2,3},{3,4},{4,5},{5,6},{6,7},{8,9},{9,10},{10,11},{11... | collective-permute-start | bytes 10376 | tf_op jit(solution)/shard_map/ppermute | solution.py:116
  44.4 3.2 %collective-permute-done.2 = f32[6,8,18]{2,1,0:T(8,128)S(1)} collective-permute-done((f32[6,8,18]{2,1,0:T(8,128)S(1)}, f32[6,8,18]{2,1,0:T(8,128)S(1)}, u32[]{:S(2)}, u32[]{:S(2)}) %collective-permute-start.2) | collective-permute-done | bytes 3488 | tf_op jit(solution)/shard_map/ppermute | solution.py:116
  49.9 2.9 %fusion.68 = s32[160]{0:T(256)S(1)} fusion(f32[160,8,128]{2,1,0:T(8,128)S(1)} %bitcast.191), kind=kLoop, calls=%fused_computation.144 | loop fusion | flops 160 | bytes 1280 | tf_op jit(solution)/shard_map/convert_element_type | solution.py:300
  52.8 1.1 fusion.80
  56.0 26.4 %multiply_reduce_fusion.2 = (f32[160,128]{1,0:T(8,128)S(1)}, f32[160,128]{1,0:T(8,128)S(1)}, f32[160,128]{1,0:T(8,128)S(1)}, f32[160,128]{1,0:T(8,128)S(1)}) fusion(f32[160,128]{1,0:T(8,128)S(1)} %bitcast.204, f32[160,128]{1,0:T(8,128)S(1)} %multiply_add_fusion, f32[160,128]{1,0:T(8,128)S(1)} %bitcast.224, f32[160,128]{1,0:T(8,128)S(1)} %bitcast.225, ...), kind=kLoop, calls=%fused_computation.21 | loop fusion | flops 104775680 | bytes 1556480 | tf_op jit(solution)/shard_map/reduce_sum | solution.py:207
  82.6 0.9 copy.265
  83.5 5.2 %all-to-all-start.1 = ((f32[32,5,3,128]{3,2,1,0:T(4,128)}), f32[32,5,3,128]{3,2,1,0:T(4,128)S(1)}, u32[]{:S(2)}, u32[]{:S(2)}) async-start(f32[32,5,3,128]{3,2,1,0:T(4,128)} %copy.265), calls=%async_computation.1 | async-start | bytes 655360 | tf_op jit(solution)/shard_map/all_to_all | solution.py:314
  89.7 3.6 %shard_map.151 = f32[384,256]{1,0:T(8,128)} custom-call(s32[1,4096]{1,0:T(1,128)} %bitcast.237, f32[3,4096]{1,0:T(4,128)} %bitcast.209), custom_call_target="tpu_custom_call" | custom-call | tf_op jit(solution)/shard_map/pallas_call | solution.py:91
  93.3 5.7 %all-to-all-done.1 = f32[32,5,3,128]{3,2,1,0:T(4,128)S(1)} async-done(((f32[32,5,3,128]{3,2,1,0:T(4,128)}), f32[32,5,3,128]{3,2,1,0:T(4,128)S(1)}, u32[]{:S(2)}, u32[]{:S(2)}) %all-to-all-start.1) | async-done | bytes 245792 | tf_op jit(solution)/shard_map/all_to_all | solution.py:314
  99.8 0.9 select_bitcast_fusion.force_ref
  100.7 9.8 %shard_map.152 = f32[384,256]{1,0:T(8,128)} custom-call(s32[1,16384]{1,0:T(1,128)} %bitcast.211, f32[3,16384]{1,0:T(4,128)} %select_bitcast_fusion.force_ref), custom_call_target="tpu_custom_call" | custom-call | tf_op jit(solution)/shard_map/pallas_call | solution.py:91
  110.5 1.1 add.293
  112.4 3.1 %collective-permute-start.5 = (f32[3,8,256]{2,1,0:T(8,128)S(1)}, f32[3,8,256]{2,1,0:T(8,128)S(1)}, u32[]{:S(2)}, u32[]{:S(2)}) collective-permute-start(f32[3,8,256]{2,1,0:T(8,128)S(1)} %get-tuple-element.51), channel_id=1, source_target_pairs={{8,0},{16,8},{24,16},{9,1},{17,9},{25,17},{10,2},{18,10},{26,18},{... | collective-permute-start | bytes 73736 | tf_op jit(solution)/shard_map/ppermute | solution.py:119
  115.5 1.9 %collective-permute-start.4 = (f32[3,8,256]{2,1,0:T(8,128)S(1)}, f32[3,8,256]{2,1,0:T(8,128)S(1)}, u32[]{:S(2)}, u32[]{:S(2)}) collective-permute-start(f32[3,8,256]{2,1,0:T(8,128)S(1)} %get-tuple-element.50), channel_id=1, source_target_pairs={{0,8},{8,16},{16,24},{1,9},{9,17},{17,25},{2,10},{10,18},{18,26},{... | collective-permute-start | bytes 73736 | tf_op jit(solution)/shard_map/ppermute | solution.py:116
  117.4 3.2 %collective-permute-done.4 = f32[3,8,256]{2,1,0:T(8,128)S(1)} collective-permute-done((f32[3,8,256]{2,1,0:T(8,128)S(1)}, f32[3,8,256]{2,1,0:T(8,128)S(1)}, u32[]{:S(2)}, u32[]{:S(2)}) %collective-permute-start.4) | collective-permute-done | bytes 24608 | tf_op jit(solution)/shard_map/ppermute | solution.py:116
  121.1 3.4 %collective-permute-start.7 = (f32[3,8,18]{2,1,0:T(8,128)S(1)}, f32[3,8,18]{2,1,0:T(8,128)S(1)}, u32[]{:S(2)}, u32[]{:S(2)}) collective-permute-start(f32[3,8,18]{2,1,0:T(8,128)S(1)} %bitcast.243), channel_id=1, source_target_pairs={{1,0},{2,1},{3,2},{4,3},{5,4},{6,5},{7,6},{9,8},{10,9},{11,10},{12... | collective-permute-start | bytes 5192 | tf_op jit(solution)/shard_map/ppermute | solution.py:119
  124.7 2.4 %collective-permute-start.6 = (f32[3,8,18]{2,1,0:T(8,128)S(1)}, f32[3,8,18]{2,1,0:T(8,128)S(1)}, u32[]{:S(2)}, u32[]{:S(2)}) collective-permute-start(f32[3,8,18]{2,1,0:T(8,128)S(1)} %bitcast.245), channel_id=1, source_target_pairs={{0,1},{1,2},{2,3},{3,4},{4,5},{5,6},{6,7},{8,9},{9,10},{10,11},{11... | collective-permute-start | bytes 5192 | tf_op jit(solution)/shard_map/ppermute | solution.py:116
  127.1 0.9 copy.278
  128.3 2.9 %collective-permute-done.6 = f32[3,8,18]{2,1,0:T(8,128)S(1)} collective-permute-done((f32[3,8,18]{2,1,0:T(8,128)S(1)}, f32[3,8,18]{2,1,0:T(8,128)S(1)}, u32[]{:S(2)}, u32[]{:S(2)}) %collective-permute-start.6) | collective-permute-done | bytes 1760 | tf_op jit(solution)/shard_map/ppermute | solution.py:116
  (122 shorter events, 13.6 us)
Async XLA Ops:
  0.6 7.0 %copy-start = (f32[3,8,16,256]{3,2,1,0:T(8,128)S(1)}, f32[3,8,16,256]{3,2,1,0:T(8,128)}, u32[]{:S(2)}) copy-start(f32[3,8,16,256]{3,2,1,0:T(8,128)} %param.14) | copy-start | bytes 1179652
  1.9 5.7 %copy-start.14 = (s32[128,1]{0,1:T(1,128)S(1)}, s32[128,1]{0,1:T(1,128)}, u32[]{:S(2)}) copy-start(s32[128,1]{0,1:T(1,128)} %param.22) | copy-start | bytes 1540
  3.1 6.0 %copy-start.15 = (s32[128]{0:T(128)S(1)}, s32[128]{0:T(128)}, u32[]{:S(2)}) copy-start(s32[128]{0:T(128)} %param.23) | copy-start | bytes 1540
  3.1 6.2 %copy-start.9 = (f32[128,128]{1,0:T(8,128)S(1)}, f32[128,128]{1,0:T(8,128)}, u32[]{:S(2)}) copy-start(f32[128,128]{1,0:T(8,128)} %param.19) | copy-start | bytes 196612
  3.1 6.2 %copy-start.13 = (s32[128]{0:T(128)S(1)}, s32[128]{0:T(128)}, u32[]{:S(2)}) copy-start(s32[128]{0:T(128)} %param.20) | copy-start | bytes 1540
  3.1 17.5 %copy-start.3 = (f32[128,3,128]{2,0,1:T(8,128)S(1)}, f32[128,3,128]{2,0,1:T(8,128)}, u32[]{:S(2)}) copy-start(f32[128,3,128]{2,0,1:T(8,128)} %param.18) | copy-start | bytes 589828
  3.2 33.2 %collective-permute-start.1 = (f32[6,8,256]{2,1,0:T(8,128)S(1)}, f32[6,8,256]{2,1,0:T(8,128)S(1)}, u32[]{:S(2)}, u32[]{:S(2)}) collective-permute-start(f32[6,8,256]{2,1,0:T(8,128)S(1)} %get-tuple-element.38), channel_id=1, source_target_pairs={{8,0},{16,8},{24,16},{9,1},{17,9},{25,17},{10,2},{18,10},{26,18},{... | collective-permute-start | bytes 147464 | tf_op jit(solution)/shard_map/ppermute | solution.py:119
  5.2 31.1 %collective-permute-start = (f32[6,8,256]{2,1,0:T(8,128)S(1)}, f32[6,8,256]{2,1,0:T(8,128)S(1)}, u32[]{:S(2)}, u32[]{:S(2)}) collective-permute-start(f32[6,8,256]{2,1,0:T(8,128)S(1)} %get-tuple-element.37), channel_id=1, source_target_pairs={{0,8},{8,16},{16,24},{1,9},{9,17},{17,25},{2,10},{10,18},{18,26},{... | collective-permute-start | bytes 147464 | tf_op jit(solution)/shard_map/ppermute | solution.py:116
  24.0 7.3 %copy-start.11 = (f32[32,2,128]{2,1,0:T(2,128)S(1)}, f32[32,2,128]{2,1,0:T(2,128)}, u32[]{:S(2)}) copy-start(f32[32,2,128]{2,1,0:T(2,128)} %param.25) | copy-start | bytes 98308
  24.0 11.4 %copy-start.10 = (f32[32,3,128]{2,0,1:T(8,128)S(1)}, f32[32,3,128]{2,0,1:T(8,128)}, u32[]{:S(2)}) copy-start(f32[32,3,128]{2,0,1:T(8,128)} %param.24) | copy-start | bytes 147460
  25.3 24.6 %all-to-all-start = ((f32[32,5,8,128]{3,2,1,0:T(8,128)}), f32[32,5,8,128]{3,2,1,0:T(8,128)S(1)}, u32[]{:S(2)}, u32[]{:S(2)}) async-start(f32[32,5,8,128]{3,2,1,0:T(8,128)} %select_select_fusion), calls=%async_computation | async-start | bytes 1310720 | tf_op jit(solution)/shard_map/all_to_all | solution.py:291
  36.4 7.1 %copy-start.4 = (f32[8,16,256]{2,1,0:T(8,128)S(1)}, f32[8,16,256]{2,1,0:T(8,128)}, u32[]{:S(2)}) copy-start(f32[8,16,256]{2,1,0:T(8,128)} %param.17) | copy-start | bytes 393220
  36.4 7.1 %copy-start.2 = (f32[3,4096]{1,0:T(4,128)S(1)}, f32[3,4096]{1,0:T(4,128)}, u32[]{:S(2)}) copy-start(f32[3,4096]{1,0:T(4,128)} %shard_map.150) | copy-start | bytes 147460
  36.4 7.1 %copy-start.12 = (f32[32,128]{1,0:T(8,128)S(1)}, f32[32,128]{1,0:T(8,128)}, u32[]{:S(2)}) copy-start(f32[32,128]{1,0:T(8,128)} %param.26) | copy-start | bytes 49156
  37.0 6.9 %collective-permute-start.3 = (f32[6,8,18]{2,1,0:T(8,128)S(1)}, f32[6,8,18]{2,1,0:T(8,128)S(1)}, u32[]{:S(2)}, u32[]{:S(2)}) collective-permute-start(f32[6,8,18]{2,1,0:T(8,128)S(1)} %bitcast.238), channel_id=1, source_target_pairs={{1,0},{2,1},{3,2},{4,3},{5,4},{6,5},{7,6},{9,8},{10,9},{11,10},{12... | collective-permute-start | bytes 10376 | tf_op jit(solution)/shard_map/ppermute | solution.py:119
  40.8 6.7 %collective-permute-start.2 = (f32[6,8,18]{2,1,0:T(8,128)S(1)}, f32[6,8,18]{2,1,0:T(8,128)S(1)}, u32[]{:S(2)}, u32[]{:S(2)}) collective-permute-start(f32[6,8,18]{2,1,0:T(8,128)S(1)} %bitcast.240), channel_id=1, source_target_pairs={{0,1},{1,2},{2,3},{3,4},{4,5},{5,6},{6,7},{8,9},{9,10},{10,11},{11... | collective-permute-start | bytes 10376 | tf_op jit(solution)/shard_map/ppermute | solution.py:116
  55.0 0.9 copy-start.5
  55.0 0.9 copy-start.6
  55.0 0.9 copy-start.7
  55.1 1.0 copy-start.8
  83.5 15.5 %all-to-all-start.1 = ((f32[32,5,3,128]{3,2,1,0:T(4,128)}), f32[32,5,3,128]{3,2,1,0:T(4,128)S(1)}, u32[]{:S(2)}, u32[]{:S(2)}) async-start(f32[32,5,3,128]{3,2,1,0:T(4,128)} %copy.265), calls=%async_computation.1 | async-start | bytes 655360 | tf_op jit(solution)/shard_map/all_to_all | solution.py:314
  93.3 17.2 %copy-start.1 = (f32[384,256]{1,0:T(8,128)S(1)}, f32[384,256]{1,0:T(8,128)}, u32[]{:S(2)}) copy-start(f32[384,256]{1,0:T(8,128)} %shard_map.151) | copy-start | bytes 1179652
  112.4 5.1 %collective-permute-start.5 = (f32[3,8,256]{2,1,0:T(8,128)S(1)}, f32[3,8,256]{2,1,0:T(8,128)S(1)}, u32[]{:S(2)}, u32[]{:S(2)}) collective-permute-start(f32[3,8,256]{2,1,0:T(8,128)S(1)} %get-tuple-element.51), channel_id=1, source_target_pairs={{8,0},{16,8},{24,16},{9,1},{17,9},{25,17},{10,2},{18,10},{26,18},{... | collective-permute-start | bytes 73736 | tf_op jit(solution)/shard_map/ppermute | solution.py:119
  115.5 5.1 %collective-permute-start.4 = (f32[3,8,256]{2,1,0:T(8,128)S(1)}, f32[3,8,256]{2,1,0:T(8,128)S(1)}, u32[]{:S(2)}, u32[]{:S(2)}) collective-permute-start(f32[3,8,256]{2,1,0:T(8,128)S(1)} %get-tuple-element.50), channel_id=1, source_target_pairs={{0,8},{8,16},{16,24},{1,9},{9,17},{17,25},{2,10},{10,18},{18,26},{... | collective-permute-start | bytes 73736 | tf_op jit(solution)/shard_map/ppermute | solution.py:116
  121.1 7.0 %collective-permute-start.7 = (f32[3,8,18]{2,1,0:T(8,128)S(1)}, f32[3,8,18]{2,1,0:T(8,128)S(1)}, u32[]{:S(2)}, u32[]{:S(2)}) collective-permute-start(f32[3,8,18]{2,1,0:T(8,128)S(1)} %bitcast.243), channel_id=1, source_target_pairs={{1,0},{2,1},{3,2},{4,3},{5,4},{6,5},{7,6},{9,8},{10,9},{11,10},{12... | collective-permute-start | bytes 5192 | tf_op jit(solution)/shard_map/ppermute | solution.py:119
  124.7 6.5 %collective-permute-start.6 = (f32[3,8,18]{2,1,0:T(8,128)S(1)}, f32[3,8,18]{2,1,0:T(8,128)S(1)}, u32[]{:S(2)}, u32[]{:S(2)}) collective-permute-start(f32[3,8,18]{2,1,0:T(8,128)S(1)} %bitcast.245), channel_id=1, source_target_pairs={{0,1},{1,2},{2,3},{3,4},{4,5},{5,6},{6,7},{8,9},{9,10},{10,11},{11... | collective-permute-start | bytes 5192 | tf_op jit(solution)/shard_map/ppermute | solution.py:116

commit v14 on v13

--- a/solution.py
+++ b/solution.py
@@ -6,7 +6,7 @@
 from jax.experimental.pallas import tpu as pltpu
 
 LANES = 128
-TILE = 2048
+TILE = 4096
 
 
 def split_pieces(values):

time: 134 us -> 133 us (level)
  no operation moved by 1% of the time
where the time goes in v14:
time: 133 us; the launch traced here: 132 us
  other arithmetic  40.1 us (30%)
  starting transfers between devices  32.6 us (25%)
  Pallas kernels  27.5 us (21%)
  waiting for transfers between devices  15.2 us (11%)
  local copies, waits for them, and re-layouts  15.1 us (11%)
  between operations  1.46 us (1%)
    reduce_sum x1, other arithmetic, contact_pairs(): jnp.sum(push_force * normal_x, axis=1)  26.4 us
    pallas_call x2, Pallas kernels, node_gather(): pl.pallas_call(gather_kernel, grid=(padded_count // TILE,), in_specs=[pl....  15 us
    pallas_call x2, Pallas kernels, node_scatter_add(): pl.pallas_call(scatter_kernel, grid=(padded_count // TILE,), in_specs=[pl...  12.4 us
    ppermute x4, starting transfers between devices, padded_2(): lax.ppermute(lax.index_in_dim(block, 0, axis=dim, keepdims=False), axis,...  12 us
    ppermute x4, waiting for transfers between devices, padded_2(): lax.ppermute(lax.index_in_dim(block, block.shape[dim] - 1, axis=dim, keep...  9.35 us
    ppermute x4, starting transfers between devices, padded_2(): lax.ppermute(lax.index_in_dim(block, block.shape[dim] - 1, axis=dim, keep...  9.32 us
    all_to_all x1, starting transfers between devices, on_device(): lax.all_to_all(outgoing.reshape(devices, slot_depth, 8, seg_width), ('gx'...  5.98 us
    all_to_all x1, waiting for transfers between devices, on_device(): lax.all_to_all(forces.reshape(devices, slot_depth, 3, seg_width), ('gx',...  5.86 us
  transfers between devices with their start and end apart: 10, of which 4 were waited for; matrix products, arithmetic and copies ran while one was open for 10% of the time, Pallas kernels for 14%

profile of v14, /device:TPU:10, one launch (start us, length us, event | category | flops | bytes accessed | tf_op | source)
XLA Modules:
  0.0 132.3 jit_solution(4704326568188647278)
XLA Ops:
  0.6 1.3 copy.235
  1.9 1.1 copy_bitcast_fusion
  3.2 2.1 %collective-permute-start.1 = (f32[6,8,256]{2,1,0:T(8,128)S(1)}, f32[6,8,256]{2,1,0:T(8,128)S(1)}, u32[]{:S(2)}, u32[]{:S(2)}) collective-permute-start(f32[6,8,256]{2,1,0:T(8,128)S(1)} %get-tuple-element.38), channel_id=1, source_target_pairs={{8,0},{16,8},{24,16},{9,1},{17,9},{25,17},{10,2},{18,10},{26,18},{... | collective-permute-start | bytes 147464 | tf_op jit(solution)/shard_map/ppermute | solution.py:119
  5.2 2.4 %collective-permute-start = (f32[6,8,256]{2,1,0:T(8,128)S(1)}, f32[6,8,256]{2,1,0:T(8,128)S(1)}, u32[]{:S(2)}, u32[]{:S(2)}) collective-permute-start(f32[6,8,256]{2,1,0:T(8,128)S(1)} %get-tuple-element.37), channel_id=1, source_target_pairs={{0,8},{8,16},{16,24},{1,9},{9,17},{17,25},{2,10},{10,18},{18,26},{... | collective-permute-start | bytes 147464 | tf_op jit(solution)/shard_map/ppermute | solution.py:116
  8.1 0.9 copy.250
  9.4 11.1 %shard_map.149 = f32[3,16384]{1,0:T(4,128)} custom-call(s32[1,16384]{1,0:T(1,128)} %bitcast.210, f32[384,256]{1,0:T(8,128)} %bitcast.189), custom_call_target="tpu_custom_call" | custom-call | tf_op jit(solution)/shard_map/pallas_call | solution.py:73
  20.5 1.1 copy_add_fusion
  21.8 1.2 pad_maximum_fusion.3
  23.9 1.2 select_select_fusion
  25.1 6.0 %all-to-all-start = ((f32[32,5,8,128]{3,2,1,0:T(8,128)}), f32[32,5,8,128]{3,2,1,0:T(8,128)S(1)}, u32[]{:S(2)}, u32[]{:S(2)}) async-start(f32[32,5,8,128]{3,2,1,0:T(8,128)} %select_select_fusion), calls=%async_computation | async-start | bytes 1310720 | tf_op jit(solution)/shard_map/all_to_all | solution.py:291
  31.1 4.0 %shard_map.150 = f32[3,4096]{1,0:T(4,128)} custom-call(s32[1,4096]{1,0:T(1,128)} %bitcast.236, f32[384,256]{1,0:T(8,128)} %bitcast.190), custom_call_target="tpu_custom_call" | custom-call | tf_op jit(solution)/shard_map/pallas_call | solution.py:73
  35.1 0.9 copy_add_fusion.1
  36.8 3.4 %collective-permute-start.3 = (f32[6,8,18]{2,1,0:T(8,128)S(1)}, f32[6,8,18]{2,1,0:T(8,128)S(1)}, u32[]{:S(2)}, u32[]{:S(2)}) collective-permute-start(f32[6,8,18]{2,1,0:T(8,128)S(1)} %bitcast.238), channel_id=1, source_target_pairs={{1,0},{2,1},{3,2},{4,3},{5,4},{6,5},{7,6},{9,8},{10,9},{11,10},{12... | collective-permute-start | bytes 10376 | tf_op jit(solution)/shard_map/ppermute | solution.py:119
  40.6 2.6 %collective-permute-start.2 = (f32[6,8,18]{2,1,0:T(8,128)S(1)}, f32[6,8,18]{2,1,0:T(8,128)S(1)}, u32[]{:S(2)}, u32[]{:S(2)}) collective-permute-start(f32[6,8,18]{2,1,0:T(8,128)S(1)} %bitcast.240), channel_id=1, source_target_pairs={{0,1},{1,2},{2,3},{3,4},{4,5},{5,6},{6,7},{8,9},{9,10},{10,11},{11... | collective-permute-start | bytes 10376 | tf_op jit(solution)/shard_map/ppermute | solution.py:116
  44.1 3.2 %collective-permute-done.2 = f32[6,8,18]{2,1,0:T(8,128)S(1)} collective-permute-done((f32[6,8,18]{2,1,0:T(8,128)S(1)}, f32[6,8,18]{2,1,0:T(8,128)S(1)}, u32[]{:S(2)}, u32[]{:S(2)}) %collective-permute-start.2) | collective-permute-done | bytes 3488 | tf_op jit(solution)/shard_map/ppermute | solution.py:116
  49.7 2.9 %fusion.68 = s32[160]{0:T(256)S(1)} fusion(f32[160,8,128]{2,1,0:T(8,128)S(1)} %bitcast.191), kind=kLoop, calls=%fused_computation.144 | loop fusion | flops 160 | bytes 1280 | tf_op jit(solution)/shard_map/convert_element_type | solution.py:300
  52.6 1.1 fusion.80
  55.8 26.4 %multiply_reduce_fusion.2 = (f32[160,128]{1,0:T(8,128)S(1)}, f32[160,128]{1,0:T(8,128)S(1)}, f32[160,128]{1,0:T(8,128)S(1)}, f32[160,128]{1,0:T(8,128)S(1)}) fusion(f32[160,128]{1,0:T(8,128)S(1)} %bitcast.204, f32[160,128]{1,0:T(8,128)S(1)} %multiply_add_fusion, f32[160,128]{1,0:T(8,128)S(1)} %bitcast.224, f32[160,128]{1,0:T(8,128)S(1)} %bitcast.225, ...), kind=kLoop, calls=%fused_computation.21 | loop fusion | flops 104775680 | bytes 1556480 | tf_op jit(solution)/shard_map/reduce_sum | solution.py:207
  82.4 0.9 copy.265
  83.3 5.3 %all-to-all-start.1 = ((f32[32,5,3,128]{3,2,1,0:T(4,128)}), f32[32,5,3,128]{3,2,1,0:T(4,128)S(1)}, u32[]{:S(2)}, u32[]{:S(2)}) async-start(f32[32,5,3,128]{3,2,1,0:T(4,128)} %copy.265), calls=%async_computation.1 | async-start | bytes 655360 | tf_op jit(solution)/shard_map/all_to_all | solution.py:314
  89.5 3.4 %shard_map.151 = f32[384,256]{1,0:T(8,128)} custom-call(s32[1,4096]{1,0:T(1,128)} %bitcast.237, f32[3,4096]{1,0:T(4,128)} %bitcast.209), custom_call_target="tpu_custom_call" | custom-call | tf_op jit(solution)/shard_map/pallas_call | solution.py:91
  93.0 5.9 %all-to-all-done.1 = f32[32,5,3,128]{3,2,1,0:T(4,128)S(1)} async-done(((f32[32,5,3,128]{3,2,1,0:T(4,128)}), f32[32,5,3,128]{3,2,1,0:T(4,128)S(1)}, u32[]{:S(2)}, u32[]{:S(2)}) %all-to-all-start.1) | async-done | bytes 245792 | tf_op jit(solution)/shard_map/all_to_all | solution.py:314
  99.6 0.9 select_bitcast_fusion.force_ref
  100.5 9.0 %shard_map.152 = f32[384,256]{1,0:T(8,128)} custom-call(s32[1,16384]{1,0:T(1,128)} %bitcast.211, f32[3,16384]{1,0:T(4,128)} %select_bitcast_fusion.force_ref), custom_call_target="tpu_custom_call" | custom-call | tf_op jit(solution)/shard_map/pallas_call | solution.py:91
  109.5 1.1 add.293
  111.4 3.1 %collective-permute-start.5 = (f32[3,8,256]{2,1,0:T(8,128)S(1)}, f32[3,8,256]{2,1,0:T(8,128)S(1)}, u32[]{:S(2)}, u32[]{:S(2)}) collective-permute-start(f32[3,8,256]{2,1,0:T(8,128)S(1)} %get-tuple-element.51), channel_id=1, source_target_pairs={{8,0},{16,8},{24,16},{9,1},{17,9},{25,17},{10,2},{18,10},{26,18},{... | collective-permute-start | bytes 73736 | tf_op jit(solution)/shard_map/ppermute | solution.py:119
  114.5 1.9 %collective-permute-start.4 = (f32[3,8,256]{2,1,0:T(8,128)S(1)}, f32[3,8,256]{2,1,0:T(8,128)S(1)}, u32[]{:S(2)}, u32[]{:S(2)}) collective-permute-start(f32[3,8,256]{2,1,0:T(8,128)S(1)} %get-tuple-element.50), channel_id=1, source_target_pairs={{0,8},{8,16},{16,24},{1,9},{9,17},{17,25},{2,10},{10,18},{18,26},{... | collective-permute-start | bytes 73736 | tf_op jit(solution)/shard_map/ppermute | solution.py:116
  116.4 3.2 %collective-permute-done.4 = f32[3,8,256]{2,1,0:T(8,128)S(1)} collective-permute-done((f32[3,8,256]{2,1,0:T(8,128)S(1)}, f32[3,8,256]{2,1,0:T(8,128)S(1)}, u32[]{:S(2)}, u32[]{:S(2)}) %collective-permute-start.4) | collective-permute-done | bytes 24608 | tf_op jit(solution)/shard_map/ppermute | solution.py:116
  120.0 3.5 %collective-permute-start.7 = (f32[3,8,18]{2,1,0:T(8,128)S(1)}, f32[3,8,18]{2,1,0:T(8,128)S(1)}, u32[]{:S(2)}, u32[]{:S(2)}) collective-permute-start(f32[3,8,18]{2,1,0:T(8,128)S(1)} %bitcast.243), channel_id=1, source_target_pairs={{1,0},{2,1},{3,2},{4,3},{5,4},{6,5},{7,6},{9,8},{10,9},{11,10},{12... | collective-permute-start | bytes 5192 | tf_op jit(solution)/shard_map/ppermute | solution.py:119
  123.7 2.4 %collective-permute-start.6 = (f32[3,8,18]{2,1,0:T(8,128)S(1)}, f32[3,8,18]{2,1,0:T(8,128)S(1)}, u32[]{:S(2)}, u32[]{:S(2)}) collective-permute-start(f32[3,8,18]{2,1,0:T(8,128)S(1)} %bitcast.245), channel_id=1, source_target_pairs={{0,1},{1,2},{2,3},{3,4},{4,5},{5,6},{6,7},{8,9},{9,10},{10,11},{11... | collective-permute-start | bytes 5192 | tf_op jit(solution)/shard_map/ppermute | solution.py:116
  126.1 0.9 copy.278
  127.2 3.0 %collective-permute-done.6 = f32[3,8,18]{2,1,0:T(8,128)S(1)} collective-permute-done((f32[3,8,18]{2,1,0:T(8,128)S(1)}, f32[3,8,18]{2,1,0:T(8,128)S(1)}, u32[]{:S(2)}, u32[]{:S(2)}) %collective-permute-start.6) | collective-permute-done | bytes 1760 | tf_op jit(solution)/shard_map/ppermute | solution.py:116
  (122 shorter events, 13.6 us)
Async XLA Ops:
  0.6 7.0 %copy-start = (f32[3,8,16,256]{3,2,1,0:T(8,128)S(1)}, f32[3,8,16,256]{3,2,1,0:T(8,128)}, u32[]{:S(2)}) copy-start(f32[3,8,16,256]{3,2,1,0:T(8,128)} %param.14) | copy-start | bytes 1179652
  1.9 5.7 %copy-start.14 = (s32[128,1]{0,1:T(1,128)S(1)}, s32[128,1]{0,1:T(1,128)}, u32[]{:S(2)}) copy-start(s32[128,1]{0,1:T(1,128)} %param.22) | copy-start | bytes 1540
  3.1 6.0 %copy-start.15 = (s32[128]{0:T(128)S(1)}, s32[128]{0:T(128)}, u32[]{:S(2)}) copy-start(s32[128]{0:T(128)} %param.23) | copy-start | bytes 1540
  3.1 6.2 %copy-start.9 = (f32[128,128]{1,0:T(8,128)S(1)}, f32[128,128]{1,0:T(8,128)}, u32[]{:S(2)}) copy-start(f32[128,128]{1,0:T(8,128)} %param.19) | copy-start | bytes 196612
  3.1 6.2 %copy-start.13 = (s32[128]{0:T(128)S(1)}, s32[128]{0:T(128)}, u32[]{:S(2)}) copy-start(s32[128]{0:T(128)} %param.20) | copy-start | bytes 1540
  3.1 17.3 %copy-start.3 = (f32[128,3,128]{2,0,1:T(8,128)S(1)}, f32[128,3,128]{2,0,1:T(8,128)}, u32[]{:S(2)}) copy-start(f32[128,3,128]{2,0,1:T(8,128)} %param.18) | copy-start | bytes 589828
  3.2 32.9 %collective-permute-start.1 = (f32[6,8,256]{2,1,0:T(8,128)S(1)}, f32[6,8,256]{2,1,0:T(8,128)S(1)}, u32[]{:S(2)}, u32[]{:S(2)}) collective-permute-start(f32[6,8,256]{2,1,0:T(8,128)S(1)} %get-tuple-element.38), channel_id=1, source_target_pairs={{8,0},{16,8},{24,16},{9,1},{17,9},{25,17},{10,2},{18,10},{26,18},{... | collective-permute-start | bytes 147464 | tf_op jit(solution)/shard_map/ppermute | solution.py:119
  5.2 30.8 %collective-permute-start = (f32[6,8,256]{2,1,0:T(8,128)S(1)}, f32[6,8,256]{2,1,0:T(8,128)S(1)}, u32[]{:S(2)}, u32[]{:S(2)}) collective-permute-start(f32[6,8,256]{2,1,0:T(8,128)S(1)} %get-tuple-element.37), channel_id=1, source_target_pairs={{0,8},{8,16},{16,24},{1,9},{9,17},{17,25},{2,10},{10,18},{18,26},{... | collective-permute-start | bytes 147464 | tf_op jit(solution)/shard_map/ppermute | solution.py:116
  23.9 7.2 %copy-start.11 = (f32[32,2,128]{2,1,0:T(2,128)S(1)}, f32[32,2,128]{2,1,0:T(2,128)}, u32[]{:S(2)}) copy-start(f32[32,2,128]{2,1,0:T(2,128)} %param.25) | copy-start | bytes 98308
  23.9 11.3 %copy-start.10 = (f32[32,3,128]{2,0,1:T(8,128)S(1)}, f32[32,3,128]{2,0,1:T(8,128)}, u32[]{:S(2)}) copy-start(f32[32,3,128]{2,0,1:T(8,128)} %param.24) | copy-start | bytes 147460
  25.1 24.6 %all-to-all-start = ((f32[32,5,8,128]{3,2,1,0:T(8,128)}), f32[32,5,8,128]{3,2,1,0:T(8,128)S(1)}, u32[]{:S(2)}, u32[]{:S(2)}) async-start(f32[32,5,8,128]{3,2,1,0:T(8,128)} %select_select_fusion), calls=%async_computation | async-start | bytes 1310720 | tf_op jit(solution)/shard_map/all_to_all | solution.py:291
  36.2 7.1 %copy-start.4 = (f32[8,16,256]{2,1,0:T(8,128)S(1)}, f32[8,16,256]{2,1,0:T(8,128)}, u32[]{:S(2)}) copy-start(f32[8,16,256]{2,1,0:T(8,128)} %param.17) | copy-start | bytes 393220
  36.2 7.1 %copy-start.2 = (f32[3,4096]{1,0:T(4,128)S(1)}, f32[3,4096]{1,0:T(4,128)}, u32[]{:S(2)}) copy-start(f32[3,4096]{1,0:T(4,128)} %shard_map.150) | copy-start | bytes 147460
  36.2 7.1 %copy-start.12 = (f32[32,128]{1,0:T(8,128)S(1)}, f32[32,128]{1,0:T(8,128)}, u32[]{:S(2)}) copy-start(f32[32,128]{1,0:T(8,128)} %param.26) | copy-start | bytes 49156
  36.8 6.9 %collective-permute-start.3 = (f32[6,8,18]{2,1,0:T(8,128)S(1)}, f32[6,8,18]{2,1,0:T(8,128)S(1)}, u32[]{:S(2)}, u32[]{:S(2)}) collective-permute-start(f32[6,8,18]{2,1,0:T(8,128)S(1)} %bitcast.238), channel_id=1, source_target_pairs={{1,0},{2,1},{3,2},{4,3},{5,4},{6,5},{7,6},{9,8},{10,9},{11,10},{12... | collective-permute-start | bytes 10376 | tf_op jit(solution)/shard_map/ppermute | solution.py:119
  40.6 6.7 %collective-permute-start.2 = (f32[6,8,18]{2,1,0:T(8,128)S(1)}, f32[6,8,18]{2,1,0:T(8,128)S(1)}, u32[]{:S(2)}, u32[]{:S(2)}) collective-permute-start(f32[6,8,18]{2,1,0:T(8,128)S(1)} %bitcast.240), channel_id=1, source_target_pairs={{0,1},{1,2},{2,3},{3,4},{4,5},{5,6},{6,7},{8,9},{9,10},{10,11},{11... | collective-permute-start | bytes 10376 | tf_op jit(solution)/shard_map/ppermute | solution.py:116
  54.8 0.9 copy-start.5
  54.8 0.9 copy-start.6
  54.8 0.9 copy-start.7
  54.8 1.0 copy-start.8
  83.3 15.6 %all-to-all-start.1 = ((f32[32,5,3,128]{3,2,1,0:T(4,128)}), f32[32,5,3,128]{3,2,1,0:T(4,128)S(1)}, u32[]{:S(2)}, u32[]{:S(2)}) async-start(f32[32,5,3,128]{3,2,1,0:T(4,128)} %copy.265), calls=%async_computation.1 | async-start | bytes 655360 | tf_op jit(solution)/shard_map/all_to_all | solution.py:314
  93.0 16.5 %copy-start.1 = (f32[384,256]{1,0:T(8,128)S(1)}, f32[384,256]{1,0:T(8,128)}, u32[]{:S(2)}) copy-start(f32[384,256]{1,0:T(8,128)} %shard_map.151) | copy-start | bytes 1179652
  111.4 5.0 %collective-permute-start.5 = (f32[3,8,256]{2,1,0:T(8,128)S(1)}, f32[3,8,256]{2,1,0:T(8,128)S(1)}, u32[]{:S(2)}, u32[]{:S(2)}) collective-permute-start(f32[3,8,256]{2,1,0:T(8,128)S(1)} %get-tuple-element.51), channel_id=1, source_target_pairs={{8,0},{16,8},{24,16},{9,1},{17,9},{25,17},{10,2},{18,10},{26,18},{... | collective-permute-start | bytes 73736 | tf_op jit(solution)/shard_map/ppermute | solution.py:119
  114.5 5.1 %collective-permute-start.4 = (f32[3,8,256]{2,1,0:T(8,128)S(1)}, f32[3,8,256]{2,1,0:T(8,128)S(1)}, u32[]{:S(2)}, u32[]{:S(2)}) collective-permute-start(f32[3,8,256]{2,1,0:T(8,128)S(1)} %get-tuple-element.50), channel_id=1, source_target_pairs={{0,8},{8,16},{16,24},{1,9},{9,17},{17,25},{2,10},{10,18},{18,26},{... | collective-permute-start | bytes 73736 | tf_op jit(solution)/shard_map/ppermute | solution.py:116
  120.0 7.0 %collective-permute-start.7 = (f32[3,8,18]{2,1,0:T(8,128)S(1)}, f32[3,8,18]{2,1,0:T(8,128)S(1)}, u32[]{:S(2)}, u32[]{:S(2)}) collective-permute-start(f32[3,8,18]{2,1,0:T(8,128)S(1)} %bitcast.243), channel_id=1, source_target_pairs={{1,0},{2,1},{3,2},{4,3},{5,4},{6,5},{7,6},{9,8},{10,9},{11,10},{12... | collective-permute-start | bytes 5192 | tf_op jit(solution)/shard_map/ppermute | solution.py:119
  123.7 6.5 %collective-permute-start.6 = (f32[3,8,18]{2,1,0:T(8,128)S(1)}, f32[3,8,18]{2,1,0:T(8,128)S(1)}, u32[]{:S(2)}, u32[]{:S(2)}) collective-permute-start(f32[3,8,18]{2,1,0:T(8,128)S(1)} %bitcast.245), channel_id=1, source_target_pairs={{0,1},{1,2},{2,3},{3,4},{4,5},{5,6},{6,7},{8,9},{9,10},{10,11},{11... | collective-permute-start | bytes 5192 | tf_op jit(solution)/shard_map/ppermute | solution.py:116

commit v15 on v14

--- a/solution.py
+++ b/solution.py
@@ -297,7 +297,7 @@
     )
     item_total = devices * slot_depth
     arrived = arrived.reshape(item_total, 8, seg_width)
-    picked = arrived[:, 7, 0].astype(jnp.int32)
+    picked = jnp.max(arrived[:, 7, :], axis=1).astype(jnp.int32)
     arrived = arrived[:, :7]
     paired = jnp.take(master_data, picked, axis=0)
     forces, reaction = contact_pairs(arrived, paired)

time: 133 us -> 131 us (0.985)
    convert_element_type x1, other arithmetic: 2.93 us -> 0.01 us  [on_device(): picked = jnp.max(arrived[:, 7, :], axis=1).astype(jnp.int32)]
    slice x0 -> x1, other arithmetic: none -> 1.99 us  [contact_pairs(): slave[:, 6, None, :] * master[:, 9, :, None] * weight * depth_soft]
  transfers between devices with their start and end apart: 10 -> 10, of which waited for: 4 -> 4; matrix products, arithmetic and copies ran while one was open for 10% -> 11% of each run, Pallas kernels for 14% -> 14%
where the time goes in v15:
time: 131 us; the launch traced here: 130 us
  other arithmetic  39.2 us (30%)
  starting transfers between devices  32.6 us (25%)
  Pallas kernels  27.5 us (21%)
  waiting for transfers between devices  15.2 us (12%)
  local copies, waits for them, and re-layouts  14.1 us (11%)
  between operations  1.46 us (1%)
    reduce_sum x1, other arithmetic, contact_pairs(): jnp.sum(push_force * normal_x, axis=1)  26.4 us
    pallas_call x2, Pallas kernels, node_gather(): pl.pallas_call(gather_kernel, grid=(padded_count // TILE,), in_specs=[pl....  15 us
    pallas_call x2, Pallas kernels, node_scatter_add(): pl.pallas_call(scatter_kernel, grid=(padded_count // TILE,), in_specs=[pl...  12.4 us
    ppermute x4, starting transfers between devices, padded_2(): lax.ppermute(lax.index_in_dim(block, 0, axis=dim, keepdims=False), axis,...  12 us
    ppermute x4, waiting for transfers between devices, padded_2(): lax.ppermute(lax.index_in_dim(block, block.shape[dim] - 1, axis=dim, keep...  9.34 us
    ppermute x4, starting transfers between devices, padded_2(): lax.ppermute(lax.index_in_dim(block, block.shape[dim] - 1, axis=dim, keep...  9.33 us
    all_to_all x1, starting transfers between devices, on_device(): lax.all_to_all(outgoing.reshape(devices, slot_depth, 8, seg_width), ('gx'...  5.98 us
    all_to_all x1, waiting for transfers between devices, on_device(): lax.all_to_all(forces.reshape(devices, slot_depth, 3, seg_width), ('gx',...  5.87 us
  transfers between devices with their start and end apart: 10, of which 4 were waited for; matrix products, arithmetic and copies ran while one was open for 11% of the time, Pallas kernels for 14%

profile of v15, /device:TPU:10, one launch (start us, length us, event | category | flops | bytes accessed | tf_op | source)
XLA Modules:
  0.0 130.3 jit_solution(7557591132153605221)
XLA Ops:
  0.6 1.3 copy.235
  1.9 1.1 copy_bitcast_fusion
  3.2 2.1 %collective-permute-start.1 = (f32[6,8,256]{2,1,0:T(8,128)S(1)}, f32[6,8,256]{2,1,0:T(8,128)S(1)}, u32[]{:S(2)}, u32[]{:S(2)}) collective-permute-start(f32[6,8,256]{2,1,0:T(8,128)S(1)} %get-tuple-element.38), channel_id=1, source_target_pairs={{8,0},{16,8},{24,16},{9,1},{17,9},{25,17},{10,2},{18,10},{26,18},{... | collective-permute-start | bytes 147464 | tf_op jit(solution)/shard_map/ppermute | solution.py:119
  5.2 2.4 %collective-permute-start = (f32[6,8,256]{2,1,0:T(8,128)S(1)}, f32[6,8,256]{2,1,0:T(8,128)S(1)}, u32[]{:S(2)}, u32[]{:S(2)}) collective-permute-start(f32[6,8,256]{2,1,0:T(8,128)S(1)} %get-tuple-element.37), channel_id=1, source_target_pairs={{0,8},{8,16},{16,24},{1,9},{9,17},{17,25},{2,10},{10,18},{18,26},{... | collective-permute-start | bytes 147464 | tf_op jit(solution)/shard_map/ppermute | solution.py:116
  8.1 0.9 copy.250
  9.4 11.1 %shard_map.149 = f32[3,16384]{1,0:T(4,128)} custom-call(s32[1,16384]{1,0:T(1,128)} %bitcast.209, f32[384,256]{1,0:T(8,128)} %bitcast.189), custom_call_target="tpu_custom_call" | custom-call | tf_op jit(solution)/shard_map/pallas_call | solution.py:73
  20.5 1.1 copy_add_fusion
  21.8 1.2 pad_maximum_fusion.3
  23.0 0.8 gather_fusion
  23.9 1.2 select_select_fusion
  25.1 6.0 %all-to-all-start = ((f32[32,5,8,128]{3,2,1,0:T(8,128)}), f32[32,5,8,128]{3,2,1,0:T(8,128)S(1)}, u32[]{:S(2)}, u32[]{:S(2)}) async-start(f32[32,5,8,128]{3,2,1,0:T(8,128)} %select_select_fusion), calls=%async_computation | async-start | bytes 1310720 | tf_op jit(solution)/shard_map/all_to_all | solution.py:291
  31.1 4.0 %shard_map.150 = f32[3,4096]{1,0:T(4,128)} custom-call(s32[1,4096]{1,0:T(1,128)} %bitcast.235, f32[384,256]{1,0:T(8,128)} %bitcast.190), custom_call_target="tpu_custom_call" | custom-call | tf_op jit(solution)/shard_map/pallas_call | solution.py:73
  35.1 0.9 copy_add_fusion.1
  36.8 3.4 %collective-permute-start.3 = (f32[6,8,18]{2,1,0:T(8,128)S(1)}, f32[6,8,18]{2,1,0:T(8,128)S(1)}, u32[]{:S(2)}, u32[]{:S(2)}) collective-permute-start(f32[6,8,18]{2,1,0:T(8,128)S(1)} %bitcast.237), channel_id=1, source_target_pairs={{1,0},{2,1},{3,2},{4,3},{5,4},{6,5},{7,6},{9,8},{10,9},{11,10},{12... | collective-permute-start | bytes 10376 | tf_op jit(solution)/shard_map/ppermute | solution.py:119
  40.6 2.6 %collective-permute-start.2 = (f32[6,8,18]{2,1,0:T(8,128)S(1)}, f32[6,8,18]{2,1,0:T(8,128)S(1)}, u32[]{:S(2)}, u32[]{:S(2)}) collective-permute-start(f32[6,8,18]{2,1,0:T(8,128)S(1)} %bitcast.239), channel_id=1, source_target_pairs={{0,1},{1,2},{2,3},{3,4},{4,5},{5,6},{6,7},{8,9},{9,10},{10,11},{11... | collective-permute-start | bytes 10376 | tf_op jit(solution)/shard_map/ppermute | solution.py:116
  44.1 3.2 %collective-permute-done.2 = f32[6,8,18]{2,1,0:T(8,128)S(1)} collective-permute-done((f32[6,8,18]{2,1,0:T(8,128)S(1)}, f32[6,8,18]{2,1,0:T(8,128)S(1)}, u32[]{:S(2)}, u32[]{:S(2)}) %collective-permute-start.2) | collective-permute-done | bytes 3488 | tf_op jit(solution)/shard_map/ppermute | solution.py:116
  49.7 2.0 %fusion.79 = (f32[160,1,128]{2,1,0:T(1,128)S(1)}, f32[160,1,128]{2,1,0:T(1,128)S(1)}, f32[160,1,128]{2,1,0:T(1,128)S(1)}, f32[160,1,128]{2,1,0:T(1,128)}, f32[16...) fusion(f32[160,8,128]{2,1,0:T(8,128)S(1)} %bitcast.191), kind=kLoop, calls=%fused_computation.185 | loop fusion | flops 20320 | bytes 1229440 | tf_op jit(solution)/shard_map/slice | solution.py:199
  53.8 26.4 %multiply_reduce_fusion.2 = (f32[160,128]{1,0:T(8,128)S(1)}, f32[160,128]{1,0:T(8,128)S(1)}, f32[160,128]{1,0:T(8,128)S(1)}, f32[160,128]{1,0:T(8,128)S(1)}) fusion(f32[160,128]{1,0:T(8,128)S(1)} %bitcast.203, f32[160,128]{1,0:T(8,128)S(1)} %multiply_add_fusion, f32[160,128]{1,0:T(8,128)S(1)} %bitcast.223, f32[160,128]{1,0:T(8,128)S(1)} %bitcast.224, ...), kind=kLoop, calls=%fused_computation.21 | loop fusion | flops 104775680 | bytes 1556480 | tf_op jit(solution)/shard_map/reduce_sum | solution.py:207
  80.4 0.9 copy.265
  81.3 5.3 %all-to-all-start.1 = ((f32[32,5,3,128]{3,2,1,0:T(4,128)}), f32[32,5,3,128]{3,2,1,0:T(4,128)S(1)}, u32[]{:S(2)}, u32[]{:S(2)}) async-start(f32[32,5,3,128]{3,2,1,0:T(4,128)} %copy.265), calls=%async_computation.1 | async-start | bytes 655360 | tf_op jit(solution)/shard_map/all_to_all | solution.py:314
  87.5 3.4 %shard_map.151 = f32[384,256]{1,0:T(8,128)} custom-call(s32[1,4096]{1,0:T(1,128)} %bitcast.236, f32[3,4096]{1,0:T(4,128)} %bitcast.208), custom_call_target="tpu_custom_call" | custom-call | tf_op jit(solution)/shard_map/pallas_call | solution.py:91
  91.0 5.9 %all-to-all-done.1 = f32[32,5,3,128]{3,2,1,0:T(4,128)S(1)} async-done(((f32[32,5,3,128]{3,2,1,0:T(4,128)}), f32[32,5,3,128]{3,2,1,0:T(4,128)S(1)}, u32[]{:S(2)}, u32[]{:S(2)}) %all-to-all-start.1) | async-done | bytes 245792 | tf_op jit(solution)/shard_map/all_to_all | solution.py:314
  97.6 0.9 select_bitcast_fusion.force_ref
  98.5 9.0 %shard_map.152 = f32[384,256]{1,0:T(8,128)} custom-call(s32[1,16384]{1,0:T(1,128)} %bitcast.210, f32[3,16384]{1,0:T(4,128)} %select_bitcast_fusion.force_ref), custom_call_target="tpu_custom_call" | custom-call | tf_op jit(solution)/shard_map/pallas_call | solution.py:91
  107.5 1.1 add.293
  109.4 3.1 %collective-permute-start.5 = (f32[3,8,256]{2,1,0:T(8,128)S(1)}, f32[3,8,256]{2,1,0:T(8,128)S(1)}, u32[]{:S(2)}, u32[]{:S(2)}) collective-permute-start(f32[3,8,256]{2,1,0:T(8,128)S(1)} %get-tuple-element.52), channel_id=1, source_target_pairs={{8,0},{16,8},{24,16},{9,1},{17,9},{25,17},{10,2},{18,10},{26,18},{... | collective-permute-start | bytes 73736 | tf_op jit(solution)/shard_map/ppermute | solution.py:119
  112.5 1.9 %collective-permute-start.4 = (f32[3,8,256]{2,1,0:T(8,128)S(1)}, f32[3,8,256]{2,1,0:T(8,128)S(1)}, u32[]{:S(2)}, u32[]{:S(2)}) collective-permute-start(f32[3,8,256]{2,1,0:T(8,128)S(1)} %get-tuple-element.51), channel_id=1, source_target_pairs={{0,8},{8,16},{16,24},{1,9},{9,17},{17,25},{2,10},{10,18},{18,26},{... | collective-permute-start | bytes 73736 | tf_op jit(solution)/shard_map/ppermute | solution.py:116
  114.4 3.2 %collective-permute-done.4 = f32[3,8,256]{2,1,0:T(8,128)S(1)} collective-permute-done((f32[3,8,256]{2,1,0:T(8,128)S(1)}, f32[3,8,256]{2,1,0:T(8,128)S(1)}, u32[]{:S(2)}, u32[]{:S(2)}) %collective-permute-start.4) | collective-permute-done | bytes 24608 | tf_op jit(solution)/shard_map/ppermute | solution.py:116
  118.0 3.4 %collective-permute-start.7 = (f32[3,8,18]{2,1,0:T(8,128)S(1)}, f32[3,8,18]{2,1,0:T(8,128)S(1)}, u32[]{:S(2)}, u32[]{:S(2)}) collective-permute-start(f32[3,8,18]{2,1,0:T(8,128)S(1)} %bitcast.242), channel_id=1, source_target_pairs={{1,0},{2,1},{3,2},{4,3},{5,4},{6,5},{7,6},{9,8},{10,9},{11,10},{12... | collective-permute-start | bytes 5192 | tf_op jit(solution)/shard_map/ppermute | solution.py:119
  121.7 2.4 %collective-permute-start.6 = (f32[3,8,18]{2,1,0:T(8,128)S(1)}, f32[3,8,18]{2,1,0:T(8,128)S(1)}, u32[]{:S(2)}, u32[]{:S(2)}) collective-permute-start(f32[3,8,18]{2,1,0:T(8,128)S(1)} %bitcast.244), channel_id=1, source_target_pairs={{0,1},{1,2},{2,3},{3,4},{4,5},{5,6},{6,7},{8,9},{9,10},{10,11},{11... | collective-permute-start | bytes 5192 | tf_op jit(solution)/shard_map/ppermute | solution.py:116
  124.1 0.9 copy.278
  125.2 3.0 %collective-permute-done.6 = f32[3,8,18]{2,1,0:T(8,128)S(1)} collective-permute-done((f32[3,8,18]{2,1,0:T(8,128)S(1)}, f32[3,8,18]{2,1,0:T(8,128)S(1)}, u32[]{:S(2)}, u32[]{:S(2)}) %collective-permute-start.6) | collective-permute-done | bytes 1760 | tf_op jit(solution)/shard_map/ppermute | solution.py:116
  (122 shorter events, 12.8 us)
Async XLA Ops:
  0.6 7.0 %copy-start = (f32[3,8,16,256]{3,2,1,0:T(8,128)S(1)}, f32[3,8,16,256]{3,2,1,0:T(8,128)}, u32[]{:S(2)}) copy-start(f32[3,8,16,256]{3,2,1,0:T(8,128)} %param.14) | copy-start | bytes 1179652
  1.9 5.7 %copy-start.14 = (s32[128,1]{0,1:T(1,128)S(1)}, s32[128,1]{0,1:T(1,128)}, u32[]{:S(2)}) copy-start(s32[128,1]{0,1:T(1,128)} %param.22) | copy-start | bytes 1540
  3.1 6.0 %copy-start.15 = (s32[128]{0:T(128)S(1)}, s32[128]{0:T(128)}, u32[]{:S(2)}) copy-start(s32[128]{0:T(128)} %param.23) | copy-start | bytes 1540
  3.1 6.2 %copy-start.9 = (f32[128,128]{1,0:T(8,128)S(1)}, f32[128,128]{1,0:T(8,128)}, u32[]{:S(2)}) copy-start(f32[128,128]{1,0:T(8,128)} %param.19) | copy-start | bytes 196612
  3.1 6.2 %copy-start.13 = (s32[128]{0:T(128)S(1)}, s32[128]{0:T(128)}, u32[]{:S(2)}) copy-start(s32[128]{0:T(128)} %param.20) | copy-start | bytes 1540
  3.1 17.3 %copy-start.3 = (f32[128,3,128]{2,0,1:T(8,128)S(1)}, f32[128,3,128]{2,0,1:T(8,128)}, u32[]{:S(2)}) copy-start(f32[128,3,128]{2,0,1:T(8,128)} %param.18) | copy-start | bytes 589828
  3.2 32.9 %collective-permute-start.1 = (f32[6,8,256]{2,1,0:T(8,128)S(1)}, f32[6,8,256]{2,1,0:T(8,128)S(1)}, u32[]{:S(2)}, u32[]{:S(2)}) collective-permute-start(f32[6,8,256]{2,1,0:T(8,128)S(1)} %get-tuple-element.38), channel_id=1, source_target_pairs={{8,0},{16,8},{24,16},{9,1},{17,9},{25,17},{10,2},{18,10},{26,18},{... | collective-permute-start | bytes 147464 | tf_op jit(solution)/shard_map/ppermute | solution.py:119
  5.2 30.8 %collective-permute-start = (f32[6,8,256]{2,1,0:T(8,128)S(1)}, f32[6,8,256]{2,1,0:T(8,128)S(1)}, u32[]{:S(2)}, u32[]{:S(2)}) collective-permute-start(f32[6,8,256]{2,1,0:T(8,128)S(1)} %get-tuple-element.37), channel_id=1, source_target_pairs={{0,8},{8,16},{16,24},{1,9},{9,17},{17,25},{2,10},{10,18},{18,26},{... | collective-permute-start | bytes 147464 | tf_op jit(solution)/shard_map/ppermute | solution.py:116
  23.9 7.2 %copy-start.11 = (f32[32,2,128]{2,1,0:T(2,128)S(1)}, f32[32,2,128]{2,1,0:T(2,128)}, u32[]{:S(2)}) copy-start(f32[32,2,128]{2,1,0:T(2,128)} %param.25) | copy-start | bytes 98308
  23.9 11.3 %copy-start.10 = (f32[32,3,128]{2,0,1:T(8,128)S(1)}, f32[32,3,128]{2,0,1:T(8,128)}, u32[]{:S(2)}) copy-start(f32[32,3,128]{2,0,1:T(8,128)} %param.24) | copy-start | bytes 147460
  25.1 24.6 %all-to-all-start = ((f32[32,5,8,128]{3,2,1,0:T(8,128)}), f32[32,5,8,128]{3,2,1,0:T(8,128)S(1)}, u32[]{:S(2)}, u32[]{:S(2)}) async-start(f32[32,5,8,128]{3,2,1,0:T(8,128)} %select_select_fusion), calls=%async_computation | async-start | bytes 1310720 | tf_op jit(solution)/shard_map/all_to_all | solution.py:291
  36.2 7.1 %copy-start.4 = (f32[8,16,256]{2,1,0:T(8,128)S(1)}, f32[8,16,256]{2,1,0:T(8,128)}, u32[]{:S(2)}) copy-start(f32[8,16,256]{2,1,0:T(8,128)} %param.17) | copy-start | bytes 393220
  36.2 7.1 %copy-start.2 = (f32[3,4096]{1,0:T(4,128)S(1)}, f32[3,4096]{1,0:T(4,128)}, u32[]{:S(2)}) copy-start(f32[3,4096]{1,0:T(4,128)} %shard_map.150) | copy-start | bytes 147460
  36.2 7.1 %copy-start.12 = (f32[32,128]{1,0:T(8,128)S(1)}, f32[32,128]{1,0:T(8,128)}, u32[]{:S(2)}) copy-start(f32[32,128]{1,0:T(8,128)} %param.26) | copy-start | bytes 49156
  36.8 6.9 %collective-permute-start.3 = (f32[6,8,18]{2,1,0:T(8,128)S(1)}, f32[6,8,18]{2,1,0:T(8,128)S(1)}, u32[]{:S(2)}, u32[]{:S(2)}) collective-permute-start(f32[6,8,18]{2,1,0:T(8,128)S(1)} %bitcast.237), channel_id=1, source_target_pairs={{1,0},{2,1},{3,2},{4,3},{5,4},{6,5},{7,6},{9,8},{10,9},{11,10},{12... | collective-permute-start | bytes 10376 | tf_op jit(solution)/shard_map/ppermute | solution.py:119
  40.6 6.7 %collective-permute-start.2 = (f32[6,8,18]{2,1,0:T(8,128)S(1)}, f32[6,8,18]{2,1,0:T(8,128)S(1)}, u32[]{:S(2)}, u32[]{:S(2)}) collective-permute-start(f32[6,8,18]{2,1,0:T(8,128)S(1)} %bitcast.239), channel_id=1, source_target_pairs={{0,1},{1,2},{2,3},{3,4},{4,5},{5,6},{6,7},{8,9},{9,10},{10,11},{11... | collective-permute-start | bytes 10376 | tf_op jit(solution)/shard_map/ppermute | solution.py:116
  52.8 0.9 copy-start.5
  52.8 0.9 copy-start.6
  52.8 0.9 copy-start.7
  52.8 1.0 copy-start.8
  81.3 15.6 %all-to-all-start.1 = ((f32[32,5,3,128]{3,2,1,0:T(4,128)}), f32[32,5,3,128]{3,2,1,0:T(4,128)S(1)}, u32[]{:S(2)}, u32[]{:S(2)}) async-start(f32[32,5,3,128]{3,2,1,0:T(4,128)} %copy.265), calls=%async_computation.1 | async-start | bytes 655360 | tf_op jit(solution)/shard_map/all_to_all | solution.py:314
  90.9 16.5 %copy-start.1 = (f32[384,256]{1,0:T(8,128)S(1)}, f32[384,256]{1,0:T(8,128)}, u32[]{:S(2)}) copy-start(f32[384,256]{1,0:T(8,128)} %shard_map.151) | copy-start | bytes 1179652
  109.4 5.0 %collective-permute-start.5 = (f32[3,8,256]{2,1,0:T(8,128)S(1)}, f32[3,8,256]{2,1,0:T(8,128)S(1)}, u32[]{:S(2)}, u32[]{:S(2)}) collective-permute-start(f32[3,8,256]{2,1,0:T(8,128)S(1)} %get-tuple-element.52), channel_id=1, source_target_pairs={{8,0},{16,8},{24,16},{9,1},{17,9},{25,17},{10,2},{18,10},{26,18},{... | collective-permute-start | bytes 73736 | tf_op jit(solution)/shard_map/ppermute | solution.py:119
  112.5 5.1 %collective-permute-start.4 = (f32[3,8,256]{2,1,0:T(8,128)S(1)}, f32[3,8,256]{2,1,0:T(8,128)S(1)}, u32[]{:S(2)}, u32[]{:S(2)}) collective-permute-start(f32[3,8,256]{2,1,0:T(8,128)S(1)} %get-tuple-element.51), channel_id=1, source_target_pairs={{0,8},{8,16},{16,24},{1,9},{9,17},{17,25},{2,10},{10,18},{18,26},{... | collective-permute-start | bytes 73736 | tf_op jit(solution)/shard_map/ppermute | solution.py:116
  118.0 7.0 %collective-permute-start.7 = (f32[3,8,18]{2,1,0:T(8,128)S(1)}, f32[3,8,18]{2,1,0:T(8,128)S(1)}, u32[]{:S(2)}, u32[]{:S(2)}) collective-permute-start(f32[3,8,18]{2,1,0:T(8,128)S(1)} %bitcast.242), channel_id=1, source_target_pairs={{1,0},{2,1},{3,2},{4,3},{5,4},{6,5},{7,6},{9,8},{10,9},{11,10},{12... | collective-permute-start | bytes 5192 | tf_op jit(solution)/shard_map/ppermute | solution.py:119
  121.7 6.5 %collective-permute-start.6 = (f32[3,8,18]{2,1,0:T(8,128)S(1)}, f32[3,8,18]{2,1,0:T(8,128)S(1)}, u32[]{:S(2)}, u32[]{:S(2)}) collective-permute-start(f32[3,8,18]{2,1,0:T(8,128)S(1)} %bitcast.244), channel_id=1, source_target_pairs={{0,1},{1,2},{2,3},{3,4},{4,5},{5,6},{6,7},{8,9},{9,10},{10,11},{11... | collective-permute-start | bytes 5192 | tf_op jit(solution)/shard_map/ppermute | solution.py:116

commit v16 on v15

--- a/solution.py
+++ b/solution.py
@@ -35,10 +35,10 @@
         out_ref[c : c + 1, :] = jnp.sum(jnp.where(low_hit, block, 0.0), axis=0, keepdims=True)
 
 
-def scatter_kernel(index_ref, force_ref, out_ref):
+def scatter_kernel(index_ref, force_ref, init_ref, out_ref):
     @pl.when(pl.program_id(0) == 0)
     def _():
-        out_ref[...] = jnp.zeros_like(out_ref)
+        out_ref[...] = init_ref[...]
 
     node = index_ref[...]
     width = node.shape[1]
@@ -82,22 +82,27 @@
     )(nodes.reshape(1, padded_count), table)[:, :count]
 
 
-def node_scatter_add(forces, nodes, node_total):
+def node_scatter_add(forces, nodes, start):
     channels, count = forces.shape
-    high_count = node_total // LANES
+    high_count = start.shape[1]
     padded_count = -(-count // TILE) * TILE
     nodes = jnp.pad(nodes, (0, padded_count - count))
     forces = jnp.pad(forces, ((0, 0), (0, padded_count - count)))
-    summed = pl.pallas_call(
+    return pl.pallas_call(
         scatter_kernel,
         grid=(padded_count // TILE,),
         in_specs=[
             pl.BlockSpec((1, TILE), lambda i: (0, i)),
             pl.BlockSpec((channels, TILE), lambda i: (0, i)),
+            pl.BlockSpec(start.shape, lambda i: (0, 0)),
         ],
-        out_specs=pl.BlockSpec((channels * LANES, high_count), lambda i: (0, 0)),
-        out_shape=jax.ShapeDtypeStruct((channels * LANES, high_count), jnp.float32),
-    )(nodes.reshape(1, padded_count), forces)
+        out_specs=pl.BlockSpec(start.shape, lambda i: (0, 0)),
+        out_shape=jax.ShapeDtypeStruct(start.shape, jnp.float32),
+    )(nodes.reshape(1, padded_count), forces, start)
+
+
+def sums_to_nodes(summed, channels, node_total):
+    high_count = summed.shape[1]
     return summed.reshape(channels, LANES, high_count).transpose(0, 2, 1).reshape(channels, node_total)
 
 
@@ -248,8 +253,6 @@
     stacked = jnp.concatenate(
         [velocity, bulk[None], prestress[None], jnp.ones_like(bulk)[None]], axis=0
     )
-    padded = padded_2(stacked, (("gx", 2), ("gy", 3)), 1)
-    stress, inside = stress_forces(padded)
     vel_flat = velocity.reshape(3, node_total)
     slave_count = block_total * seg_width
     slave_vel = (
@@ -257,6 +260,9 @@
         .reshape(3, block_total, seg_width)
         .transpose(1, 0, 2)
     )
+    stacked, slave_vel = lax.optimization_barrier((stacked, slave_vel))
+    padded = padded_2(stacked, (("gx", 2), ("gy", 3)), 1)
+    stress, inside = stress_forces(padded)
     master_vel = (
         node_gather(vel_flat, master_node.reshape(-1))
         .reshape(3, master_total, seg_width)
@@ -309,7 +315,9 @@
     master_sum = jnp.dot(onehot.T, reaction, precision=lax.Precision.HIGHEST)
     master_force = -master_sum[:, None, :] * normals
     master_contact = node_scatter_add(
-        master_force.transpose(1, 0, 2).reshape(3, -1), master_node.reshape(-1), node_total
+        master_force.transpose(1, 0, 2).reshape(3, -1),
+        master_node.reshape(-1),
+        jnp.zeros((3 * LANES, node_total // LANES), jnp.float32),
     )
     returned = lax.all_to_all(
         forces.reshape(devices, slot_depth, 3, seg_width),
@@ -319,8 +327,12 @@
         tiled=True,
     )
     slave_force = jnp.take(returned.reshape(item_total, 3, seg_width), target_slot, axis=0)
-    contact = master_contact + node_scatter_add(
-        slave_force.transpose(1, 0, 2).reshape(3, -1), slave_node.reshape(-1), node_total
+    contact = sums_to_nodes(
+        node_scatter_add(
+            slave_force.transpose(1, 0, 2).reshape(3, -1), slave_node.reshape(-1), master_contact
+        ),
+        3,
+        node_total,
     )
     contact_field = contact.reshape(3, layers, row_cells, col_cells)
     velocity_new = velocity + TIME_STEP * (stress + contact_field) / node_mass[None]

time: 131 us -> 129 us (0.985)
  the two profiles are of different devices: /device:TPU:10 before, /device:TPU:9 now
where the time goes in v16:
time: 129 us; the launch traced here: 127 us
  other arithmetic  36.7 us (28%)
  starting transfers between devices  34.6 us (27%)
  Pallas kernels  27.9 us (22%)
  local copies, waits for them, and re-layouts  16.3 us (13%)
  waiting for transfers between devices  9.61 us (7%)
  between operations  1.43 us (1%)
    reduce_sum x1, other arithmetic, contact_pairs(): reaction = jnp.sum(push_force, axis=2)  26.4 us
    pallas_call x2, Pallas kernels, node_gather(): pl.pallas_call(gather_kernel, grid=(padded_count // TILE,), in_specs=[pl....  15 us
    pallas_call x2, Pallas kernels, node_scatter_add(): pl.pallas_call(scatter_kernel, grid=(padded_count // TILE,), in_specs=[pl...  12.9 us
    ppermute x4, starting transfers between devices, padded_2(): lax.ppermute(lax.index_in_dim(block, 0, axis=dim, keepdims=False), axis,...  11.4 us
    ppermute x4, starting transfers between devices, padded_2(): lax.ppermute(lax.index_in_dim(block, block.shape[dim] - 1, axis=dim, keep...  11 us
    all_to_all x1, starting transfers between devices, on_device(): lax.all_to_all(outgoing.reshape(devices, slot_depth, 8, seg_width), ('gx'...  6.39 us
    all_to_all x1, waiting for transfers between devices, on_device(): lax.all_to_all(forces.reshape(devices, slot_depth, 3, seg_width), ('gx',...  5.75 us
    all_to_all x1, starting transfers between devices, on_device(): lax.all_to_all(forces.reshape(devices, slot_depth, 3, seg_width), ('gx',...  5.71 us
  transfers between devices with their start and end apart: 10, of which 3 were waited for; matrix products, arithmetic and copies ran while one was open for 7% of the time, Pallas kernels for 6%

profile of v16, /device:TPU:9, one launch (start us, length us, event | category | flops | bytes accessed | tf_op | source)
XLA Modules:
  0.0 126.8 jit_solution(942348405260472136)
XLA Ops:
  0.7 1.3 %copy.235 = f32[3,8,16,256]{3,1,0,2:T(8,128)S(1)} copy(f32[3,8,16,256]{3,2,1,0:T(8,128)} %param.14) | data formatting | bytes 786432 | tf_op args[0]
  1.9 1.0 reshape_reshape.7
  3.4 0.9 copy.236
  4.6 11.0 %shard_map.149 = f32[3,16384]{1,0:T(4,128)} custom-call(s32[1,16384]{1,0:T(1,128)} %bitcast.209, f32[384,256]{1,0:T(8,128)} %bitcast.189), custom_call_target="tpu_custom_call" | custom-call | tf_op jit(solution)/shard_map/pallas_call | solution.py:73
  17.3 0.8 gather_fusion
  18.2 1.2 select_select_fusion
  19.4 6.4 %all-to-all-start = ((f32[32,5,8,128]{3,2,1,0:T(8,128)}), f32[32,5,8,128]{3,2,1,0:T(8,128)S(1)}, u32[]{:S(2)}, u32[]{:S(2)}) async-start(f32[32,5,8,128]{3,2,1,0:T(8,128)} %select_select_fusion), calls=%async_computation | async-start | bytes 1310720 | tf_op jit(solution)/shard_map/all_to_all | solution.py:297
  25.8 2.3 %collective-permute-start.1 = (f32[6,8,256]{2,1,0:T(8,128)S(1)}, f32[6,8,256]{2,1,0:T(8,128)S(1)}, u32[]{:S(2)}, u32[]{:S(2)}) collective-permute-start(f32[6,8,256]{2,1,0:T(8,128)S(1)} %get-tuple-element.42), channel_id=1, source_target_pairs={{8,0},{16,8},{24,16},{9,1},{17,9},{25,17},{10,2},{18,10},{26,18},{... | collective-permute-start | bytes 147464 | tf_op jit(solution)/shard_map/ppermute | solution.py:124
  28.1 3.3 %collective-permute-start = (f32[6,8,256]{2,1,0:T(8,128)S(1)}, f32[6,8,256]{2,1,0:T(8,128)S(1)}, u32[]{:S(2)}, u32[]{:S(2)}) collective-permute-start(f32[6,8,256]{2,1,0:T(8,128)S(1)} %get-tuple-element.41), channel_id=1, source_target_pairs={{0,8},{8,16},{16,24},{1,9},{9,17},{17,25},{2,10},{10,18},{18,26},{... | collective-permute-start | bytes 147464 | tf_op jit(solution)/shard_map/ppermute | solution.py:121
  31.4 4.0 %shard_map.150 = f32[3,4096]{1,0:T(4,128)} custom-call(s32[1,4096]{1,0:T(1,128)} %bitcast.236, f32[384,256]{1,0:T(8,128)} %bitcast.190), custom_call_target="tpu_custom_call" | custom-call | tf_op jit(solution)/shard_map/pallas_call | solution.py:73
  35.4 0.9 copy_add_fusion.1
  37.5 3.1 %collective-permute-start.2 = (f32[6,8,18]{2,1,0:T(8,128)S(1)}, f32[6,8,18]{2,1,0:T(8,128)S(1)}, u32[]{:S(2)}, u32[]{:S(2)}) collective-permute-start(f32[6,8,18]{2,1,0:T(8,128)S(1)} %bitcast.238), channel_id=1, source_target_pairs={{0,1},{1,2},{2,3},{3,4},{4,5},{5,6},{6,7},{8,9},{9,10},{10,11},{11... | collective-permute-start | bytes 10376 | tf_op jit(solution)/shard_map/ppermute | solution.py:121
  41.0 3.3 %collective-permute-start.3 = (f32[6,8,18]{2,1,0:T(8,128)S(1)}, f32[6,8,18]{2,1,0:T(8,128)S(1)}, u32[]{:S(2)}, u32[]{:S(2)}) collective-permute-start(f32[6,8,18]{2,1,0:T(8,128)S(1)} %bitcast.240), channel_id=1, source_target_pairs={{1,0},{2,1},{3,2},{4,3},{5,4},{6,5},{7,6},{9,8},{10,9},{11,10},{12... | collective-permute-start | bytes 10376 | tf_op jit(solution)/shard_map/ppermute | solution.py:124
  48.2 1.9 %fusion.78 = (f32[160,1,128]{2,1,0:T(1,128)S(1)}, f32[160,1,128]{2,1,0:T(1,128)S(1)}, f32[160,1,128]{2,1,0:T(1,128)S(1)}, f32[160,1,128]{2,1,0:T(1,128)S(1)}, f3...) fusion(f32[160,8,128]{2,1,0:T(8,128)S(1)} %bitcast.191), kind=kLoop, calls=%fused_computation.183 | loop fusion | flops 20320 | bytes 1229440 | tf_op jit(solution)/shard_map/slice | solution.py:204
  50.1 0.8 gather_fusion.1
  52.1 26.4 %fusion.75 = (f32[160,128]{1,0:T(8,128)S(1)}, f32[160,128]{1,0:T(8,128)S(1)}, f32[160,128]{1,0:T(8,128)S(1)}, f32[160,128]{1,0:T(8,128)S(1)}) fusion(f32[160,128]{1,0:T(8,128)S(1)} %multiply_add_fusion, f32[160,128]{1,0:T(8,128)S(1)} %bitcast.224, f32[160,128]{1,0:T(8,128)S(1)} %bitcast.225, f32[160,128]{1,0:T(8,128)S(1)} %bitcast.226, ...), kind=kLoop, calls=%fused_computation.180 | loop fusion | flops 104775680 | bytes 1556480 | tf_op jit(solution)/shard_map/reduce_sum | solution.py:218
  78.7 0.9 copy.265
  79.6 5.7 %all-to-all-start.1 = ((f32[32,5,3,128]{3,2,1,0:T(4,128)}), f32[32,5,3,128]{3,2,1,0:T(4,128)S(1)}, u32[]{:S(2)}, u32[]{:S(2)}) async-start(f32[32,5,3,128]{3,2,1,0:T(4,128)} %copy.265), calls=%async_computation.1 | async-start | bytes 655360 | tf_op jit(solution)/shard_map/all_to_all | solution.py:322
  86.3 0.8 broadcast_in_dim.138.init_ref
  87.0 3.6 %shard_map.151.init_ref = f32[384,256]{1,0:T(8,128)} custom-call(s32[1,4096]{1,0:T(1,128)} %bitcast.237, f32[3,4096]{1,0:T(4,128)} %bitcast.211, f32[384,256]{1,0:T(8,128)} %broadcast_in_dim.138.init_ref), custom_call_target="tpu_custom_call" | custom-call | tf_op jit(solution)/shard_map/pallas_call | solution.py:91
  90.7 5.7 %all-to-all-done.1 = f32[32,5,3,128]{3,2,1,0:T(4,128)S(1)} async-done(((f32[32,5,3,128]{3,2,1,0:T(4,128)}), f32[32,5,3,128]{3,2,1,0:T(4,128)S(1)}, u32[]{:S(2)}, u32[]{:S(2)}) %all-to-all-start.1) | async-done | bytes 245792 | tf_op jit(solution)/shard_map/all_to_all | solution.py:322
  96.4 0.8 gather_fusion.2
  97.2 0.9 select_bitcast_fusion.force_ref
  98.1 9.2 %shard_map.152 = f32[384,256]{1,0:T(8,128)} custom-call(s32[1,16384]{1,0:T(1,128)} %bitcast.210, f32[3,16384]{1,0:T(4,128)} %select_bitcast_fusion.force_ref, f32[384,256]{1,0:T(8,128)} %shard_map.151.init_ref), custom_call_target="tpu_custom_call" | custom-call | tf_op jit(solution)/shard_map/pallas_call | solution.py:91
  107.3 1.1 copy.268
  109.1 2.5 %collective-permute-start.4 = (f32[3,8,256]{2,1,0:T(8,128)S(1)}, f32[3,8,256]{2,1,0:T(8,128)S(1)}, u32[]{:S(2)}, u32[]{:S(2)}) collective-permute-start(f32[3,8,256]{2,1,0:T(8,128)S(1)} %get-tuple-element.55), channel_id=1, source_target_pairs={{0,8},{8,16},{16,24},{1,9},{9,17},{17,25},{2,10},{10,18},{18,26},{... | collective-permute-start | bytes 73736 | tf_op jit(solution)/shard_map/ppermute | solution.py:121
  111.6 1.9 %collective-permute-start.5 = (f32[3,8,256]{2,1,0:T(8,128)S(1)}, f32[3,8,256]{2,1,0:T(8,128)S(1)}, u32[]{:S(2)}, u32[]{:S(2)}) collective-permute-start(f32[3,8,256]{2,1,0:T(8,128)S(1)} %get-tuple-element.56), channel_id=1, source_target_pairs={{8,0},{16,8},{24,16},{9,1},{17,9},{25,17},{10,2},{18,10},{26,18},{... | collective-permute-start | bytes 73736 | tf_op jit(solution)/shard_map/ppermute | solution.py:124
  113.6 3.2 %collective-permute-done.5 = f32[3,8,256]{2,1,0:T(8,128)S(1)} collective-permute-done((f32[3,8,256]{2,1,0:T(8,128)S(1)}, f32[3,8,256]{2,1,0:T(8,128)S(1)}, u32[]{:S(2)}, u32[]{:S(2)}) %collective-permute-start.5) | collective-permute-done | bytes 24608 | tf_op jit(solution)/shard_map/ppermute | solution.py:124
  117.2 2.2 %collective-permute-start.6 = (f32[3,8,18]{2,1,0:T(8,128)S(1)}, f32[3,8,18]{2,1,0:T(8,128)S(1)}, u32[]{:S(2)}, u32[]{:S(2)}) collective-permute-start(f32[3,8,18]{2,1,0:T(8,128)S(1)} %bitcast.243), channel_id=1, source_target_pairs={{0,1},{1,2},{2,3},{3,4},{4,5},{5,6},{6,7},{8,9},{9,10},{10,11},{11... | collective-permute-start | bytes 5192 | tf_op jit(solution)/shard_map/ppermute | solution.py:121
  119.6 4.0 %collective-permute-start.7 = (f32[3,8,18]{2,1,0:T(8,128)S(1)}, f32[3,8,18]{2,1,0:T(8,128)S(1)}, u32[]{:S(2)}, u32[]{:S(2)}) collective-permute-start(f32[3,8,18]{2,1,0:T(8,128)S(1)} %bitcast.245), channel_id=1, source_target_pairs={{1,0},{2,1},{3,2},{4,3},{5,4},{6,5},{7,6},{9,8},{10,9},{11,10},{12... | collective-permute-start | bytes 5192 | tf_op jit(solution)/shard_map/ppermute | solution.py:124
  123.6 0.9 copy.278
  126.1 0.7 copy.279
  (123 shorter events, 12.6 us)
Async XLA Ops:
  0.6 2.3 %copy-start.14 = (s32[128,1]{0,1:T(1,128)S(1)}, s32[128,1]{0,1:T(1,128)}, u32[]{:S(2)}) copy-start(s32[128,1]{0,1:T(1,128)} %param.22) | copy-start | bytes 1540
  0.6 3.7 %copy-start.6 = (f32[8,16,256]{2,1,0:T(8,128)S(1)}, f32[8,16,256]{2,1,0:T(8,128)}, u32[]{:S(2)}) copy-start(f32[8,16,256]{2,1,0:T(8,128)} %param.15) | copy-start | bytes 393220
  0.7 3.7 %copy-start.5 = (f32[8,16,256]{2,1,0:T(8,128)S(1)}, f32[8,16,256]{2,1,0:T(8,128)}, u32[]{:S(2)}) copy-start(f32[8,16,256]{2,1,0:T(8,128)} %param.16) | copy-start | bytes 393220
  4.3 11.5 %copy-start.15 = (s32[128]{0:T(128)S(1)}, s32[128]{0:T(128)}, u32[]{:S(2)}) copy-start(s32[128]{0:T(128)} %param.23) | copy-start | bytes 1540
  4.3 11.7 %copy-start.3 = (f32[128,3,128]{2,0,1:T(8,128)S(1)}, f32[128,3,128]{2,0,1:T(8,128)}, u32[]{:S(2)}) copy-start(f32[128,3,128]{2,0,1:T(8,128)} %param.18) | copy-start | bytes 589828
  4.6 12.2 %copy-start.8 = (f32[128,128]{1,0:T(8,128)S(1)}, f32[128,128]{1,0:T(8,128)}, u32[]{:S(2)}) copy-start(f32[128,128]{1,0:T(8,128)} %param.19) | copy-start | bytes 196612
  4.6 12.2 %copy-start.13 = (s32[128]{0:T(128)S(1)}, s32[128]{0:T(128)}, u32[]{:S(2)}) copy-start(s32[128]{0:T(128)} %param.20) | copy-start | bytes 1540
  15.6 0.9 copy-start.1
  18.1 13.2 %copy-start.10 = (f32[32,2,128]{2,1,0:T(2,128)S(1)}, f32[32,2,128]{2,1,0:T(2,128)}, u32[]{:S(2)}) copy-start(f32[32,2,128]{2,1,0:T(2,128)} %param.25) | copy-start | bytes 98308
  19.4 16.0 %copy-start.9 = (f32[32,3,128]{2,0,1:T(8,128)S(1)}, f32[32,3,128]{2,0,1:T(8,128)}, u32[]{:S(2)}) copy-start(f32[32,3,128]{2,0,1:T(8,128)} %param.24) | copy-start | bytes 147460
  19.4 28.8 %all-to-all-start = ((f32[32,5,8,128]{3,2,1,0:T(8,128)}), f32[32,5,8,128]{3,2,1,0:T(8,128)S(1)}, u32[]{:S(2)}, u32[]{:S(2)}) async-start(f32[32,5,8,128]{3,2,1,0:T(8,128)} %select_select_fusion), calls=%async_computation | async-start | bytes 1310720 | tf_op jit(solution)/shard_map/all_to_all | solution.py:297
  25.8 11.0 %collective-permute-start.1 = (f32[6,8,256]{2,1,0:T(8,128)S(1)}, f32[6,8,256]{2,1,0:T(8,128)S(1)}, u32[]{:S(2)}, u32[]{:S(2)}) collective-permute-start(f32[6,8,256]{2,1,0:T(8,128)S(1)} %get-tuple-element.42), channel_id=1, source_target_pairs={{8,0},{16,8},{24,16},{9,1},{17,9},{25,17},{10,2},{18,10},{26,18},{... | collective-permute-start | bytes 147464 | tf_op jit(solution)/shard_map/ppermute | solution.py:124
  28.1 8.8 %collective-permute-start = (f32[6,8,256]{2,1,0:T(8,128)S(1)}, f32[6,8,256]{2,1,0:T(8,128)S(1)}, u32[]{:S(2)}, u32[]{:S(2)}) collective-permute-start(f32[6,8,256]{2,1,0:T(8,128)S(1)} %get-tuple-element.41), channel_id=1, source_target_pairs={{0,8},{8,16},{16,24},{1,9},{9,17},{17,25},{2,10},{10,18},{18,26},{... | collective-permute-start | bytes 147464 | tf_op jit(solution)/shard_map/ppermute | solution.py:121
  36.9 7.4 %copy-start.4 = (f32[8,16,256]{2,1,0:T(8,128)S(1)}, f32[8,16,256]{2,1,0:T(8,128)}, u32[]{:S(2)}) copy-start(f32[8,16,256]{2,1,0:T(8,128)} %param.17) | copy-start | bytes 393220
  36.9 7.5 %copy-start.2 = (f32[3,4096]{1,0:T(4,128)S(1)}, f32[3,4096]{1,0:T(4,128)}, u32[]{:S(2)}) copy-start(f32[3,4096]{1,0:T(4,128)} %shard_map.150) | copy-start | bytes 147460
  36.9 7.5 %copy-start.11 = (f32[32,128]{1,0:T(8,128)S(1)}, f32[32,128]{1,0:T(8,128)}, u32[]{:S(2)}) copy-start(f32[32,128]{1,0:T(8,128)} %param.26) | copy-start | bytes 49156
  37.5 7.3 %collective-permute-start.2 = (f32[6,8,18]{2,1,0:T(8,128)S(1)}, f32[6,8,18]{2,1,0:T(8,128)S(1)}, u32[]{:S(2)}, u32[]{:S(2)}) collective-permute-start(f32[6,8,18]{2,1,0:T(8,128)S(1)} %bitcast.238), channel_id=1, source_target_pairs={{0,1},{1,2},{2,3},{3,4},{4,5},{5,6},{6,7},{8,9},{9,10},{10,11},{11... | collective-permute-start | bytes 10376 | tf_op jit(solution)/shard_map/ppermute | solution.py:121
  41.0 4.8 %collective-permute-start.3 = (f32[6,8,18]{2,1,0:T(8,128)S(1)}, f32[6,8,18]{2,1,0:T(8,128)S(1)}, u32[]{:S(2)}, u32[]{:S(2)}) collective-permute-start(f32[6,8,18]{2,1,0:T(8,128)S(1)} %bitcast.240), channel_id=1, source_target_pairs={{1,0},{2,1},{3,2},{4,3},{5,4},{6,5},{7,6},{9,8},{10,9},{11,10},{12... | collective-permute-start | bytes 10376 | tf_op jit(solution)/shard_map/ppermute | solution.py:124
  51.2 0.9 copy-start.7
  79.6 16.9 %all-to-all-start.1 = ((f32[32,5,3,128]{3,2,1,0:T(4,128)}), f32[32,5,3,128]{3,2,1,0:T(4,128)S(1)}, u32[]{:S(2)}, u32[]{:S(2)}) async-start(f32[32,5,3,128]{3,2,1,0:T(4,128)} %copy.265), calls=%async_computation.1 | async-start | bytes 655360 | tf_op jit(solution)/shard_map/all_to_all | solution.py:322
  85.3 11.9 %copy-start.12 = (pred[128]{0:T(512)(128)(4,1)S(1)}, pred[128]{0:T(512)(128)(4,1)}, u32[]{:S(2)}) copy-start(pred[128]{0:T(512)(128)(4,1)} %get-tuple-element.22) | copy-start | bytes 388
  98.1 10.5 %copy-start = (f32[3,8,16,256]{3,2,1,0:T(8,128)S(1)}, f32[3,8,16,256]{3,2,1,0:T(8,128)}, u32[]{:S(2)}) copy-start(f32[3,8,16,256]{3,2,1,0:T(8,128)} %param.14) | copy-start | bytes 1179652
  109.1 4.4 %collective-permute-start.4 = (f32[3,8,256]{2,1,0:T(8,128)S(1)}, f32[3,8,256]{2,1,0:T(8,128)S(1)}, u32[]{:S(2)}, u32[]{:S(2)}) collective-permute-start(f32[3,8,256]{2,1,0:T(8,128)S(1)} %get-tuple-element.55), channel_id=1, source_target_pairs={{0,8},{8,16},{16,24},{1,9},{9,17},{17,25},{2,10},{10,18},{18,26},{... | collective-permute-start | bytes 73736 | tf_op jit(solution)/shard_map/ppermute | solution.py:121
  111.6 5.1 %collective-permute-start.5 = (f32[3,8,256]{2,1,0:T(8,128)S(1)}, f32[3,8,256]{2,1,0:T(8,128)S(1)}, u32[]{:S(2)}, u32[]{:S(2)}) collective-permute-start(f32[3,8,256]{2,1,0:T(8,128)S(1)} %get-tuple-element.56), channel_id=1, source_target_pairs={{8,0},{16,8},{24,16},{9,1},{17,9},{25,17},{10,2},{18,10},{26,18},{... | collective-permute-start | bytes 73736 | tf_op jit(solution)/shard_map/ppermute | solution.py:124
  117.2 7.3 %collective-permute-start.6 = (f32[3,8,18]{2,1,0:T(8,128)S(1)}, f32[3,8,18]{2,1,0:T(8,128)S(1)}, u32[]{:S(2)}, u32[]{:S(2)}) collective-permute-start(f32[3,8,18]{2,1,0:T(8,128)S(1)} %bitcast.243), channel_id=1, source_target_pairs={{0,1},{1,2},{2,3},{3,4},{4,5},{5,6},{6,7},{8,9},{9,10},{10,11},{11... | collective-permute-start | bytes 5192 | tf_op jit(solution)/shard_map/ppermute | solution.py:121
  119.6 5.1 %collective-permute-start.7 = (f32[3,8,18]{2,1,0:T(8,128)S(1)}, f32[3,8,18]{2,1,0:T(8,128)S(1)}, u32[]{:S(2)}, u32[]{:S(2)}) collective-permute-start(f32[3,8,18]{2,1,0:T(8,128)S(1)} %bitcast.245), channel_id=1, source_target_pairs={{1,0},{2,1},{3,2},{4,3},{5,4},{6,5},{7,6},{9,8},{10,9},{11,10},{12... | collective-permute-start | bytes 5192 | tf_op jit(solution)/shard_map/ppermute | solution.py:124

commit v17 on v16

--- a/solution.py
+++ b/solution.py
@@ -17,37 +17,69 @@
     return (first, second, third)
 
 
-def gather_kernel(index_ref, table_ref, out_ref):
+def block_swap(values):
+    channels = values.shape[0] // LANES if values.ndim == 2 else values.shape[0]
+    if values.ndim == 3:
+        return jnp.concatenate(
+            [
+                jnp.concatenate([values[c, :, :LANES].T, values[c, :, LANES:].T], axis=1)
+                for c in range(channels)
+            ],
+            axis=0,
+        )
+    return jnp.stack(
+        [
+            jnp.concatenate(
+                [
+                    values[c * LANES : (c + 1) * LANES, :LANES].T,
+                    values[c * LANES : (c + 1) * LANES, LANES:].T,
+                ],
+                axis=1,
+            )
+            for c in range(channels)
+        ]
+    )
+
+
+def node_parts(node):
+    high = ((node & (2 * LANES - 1)) >> 7) * LANES + (node >> 8)
+    return high, node & (LANES - 1)
+
+
+def gather_kernel(index_ref, field_ref, out_ref):
     node = index_ref[...]
     width = node.shape[1]
-    high_count = table_ref.shape[1]
+    table = block_swap(field_ref[...])
+    high_count = table.shape[1]
     channels = out_ref.shape[0]
+    high, low = node_parts(node)
     onehot = (
-        lax.broadcasted_iota(jnp.int32, (high_count, width), 0) == (node >> 7)
+        lax.broadcasted_iota(jnp.int32, (high_count, width), 0) == high
     ).astype(jnp.bfloat16)
     gathered = None
-    for piece in split_pieces(table_ref[...])[:2]:
+    for piece in split_pieces(table)[:2]:
         part = jnp.dot(piece, onehot, preferred_element_type=jnp.float32)
         gathered = part if gathered is None else gathered + part
-    low_hit = lax.broadcasted_iota(jnp.int32, (LANES, width), 0) == (node & (LANES - 1))
+    low_hit = lax.broadcasted_iota(jnp.int32, (LANES, width), 0) == low
     for c in range(channels):
         block = gathered[c * LANES : (c + 1) * LANES]
         out_ref[c : c + 1, :] = jnp.sum(jnp.where(low_hit, block, 0.0), axis=0, keepdims=True)
 
 
-def scatter_kernel(index_ref, force_ref, init_ref, out_ref):
+def scatter_kernel(index_ref, force_ref, init_ref, out_ref, acc_ref):
     @pl.when(pl.program_id(0) == 0)
     def _():
-        out_ref[...] = init_ref[...]
+        acc_ref[...] = block_swap(init_ref[...])
 
     node = index_ref[...]
     width = node.shape[1]
-    high_count = out_ref.shape[1]
+    high_count = acc_ref.shape[1]
     channels = force_ref.shape[0]
+    high, low = node_parts(node)
     onehot = (
-        lax.broadcasted_iota(jnp.int32, (high_count, width), 0) == (node >> 7)
+        lax.broadcasted_iota(jnp.int32, (high_count, width), 0) == high
     ).astype(jnp.bfloat16)
-    low_hit = lax.broadcasted_iota(jnp.int32, (LANES, width), 0) == (node & (LANES - 1))
+    low_hit = lax.broadcasted_iota(jnp.int32, (LANES, width), 0) == low
     total = None
     for piece in split_pieces(force_ref[...])[:2]:
         spread = jnp.concatenate(
@@ -58,33 +90,32 @@
             spread, onehot, (((1,), (1,)), ((), ())), preferred_element_type=jnp.float32
         )
         total = part if total is None else total + part
-    out_ref[...] += total
+    acc_ref[...] += total
+
+    @pl.when(pl.program_id(0) == pl.num_programs(0) - 1)
+    def _():
+        out_ref[...] = block_swap(acc_ref[...])
 
 
 def node_gather(field, nodes):
-    channels, node_total = field.shape
-    high_count = node_total // LANES
-    table = field.reshape(channels, high_count, LANES).transpose(0, 2, 1).reshape(
-        channels * LANES, high_count
-    )
     count = nodes.shape[0]
     padded_count = -(-count // TILE) * TILE
     nodes = jnp.pad(nodes, (0, padded_count - count))
+    channels = field.shape[0]
     return pl.pallas_call(
         gather_kernel,
         grid=(padded_count // TILE,),
         in_specs=[
             pl.BlockSpec((1, TILE), lambda i: (0, i)),
-            pl.BlockSpec((channels * LANES, high_count), lambda i: (0, 0)),
+            pl.BlockSpec(field.shape, lambda i: (0, 0, 0)),
         ],
         out_specs=pl.BlockSpec((channels, TILE), lambda i: (0, i)),
         out_shape=jax.ShapeDtypeStruct((channels, padded_count), jnp.float32),
-    )(nodes.reshape(1, padded_count), table)[:, :count]
+    )(nodes.reshape(1, padded_count), field)[:, :count]
 
 
 def node_scatter_add(forces, nodes, start):
     channels, count = forces.shape
-    high_count = start.shape[1]
     padded_count = -(-count // TILE) * TILE
     nodes = jnp.pad(nodes, (0, padded_count - count))
     forces = jnp.pad(forces, ((0, 0), (0, padded_count - count)))
@@ -94,16 +125,12 @@
         in_specs=[
             pl.BlockSpec((1, TILE), lambda i: (0, i)),
             pl.BlockSpec((channels, TILE), lambda i: (0, i)),
-            pl.BlockSpec(start.shape, lambda i: (0, 0)),
+            pl.BlockSpec(start.shape, lambda i: (0, 0, 0)),
         ],
-        out_specs=pl.BlockSpec(start.shape, lambda i: (0, 0)),
+        out_specs=pl.BlockSpec(start.shape, lambda i: (0, 0, 0)),
         out_shape=jax.ShapeDtypeStruct(start.shape, jnp.float32),
+        scratch_shapes=[pltpu.VMEM((channels * LANES, start.shape[2]), jnp.float32)],
     )(nodes.reshape(1, padded_count), forces, start)
-
-
-def sums_to_nodes(summed, channels, node_total):
-    high_count = summed.shape[1]
-    return summed.reshape(channels, LANES, high_count).transpose(0, 2, 1).reshape(channels, node_total)
 
 
 TIME_STEP = 0.25
@@ -253,7 +280,7 @@
     stacked = jnp.concatenate(
         [velocity, bulk[None], prestress[None], jnp.ones_like(bulk)[None]], axis=0
     )
-    vel_flat = velocity.reshape(3, node_total)
+    vel_flat = velocity.reshape(3, layers * row_cells, col_cells)
     slave_count = block_total * seg_width
     slave_vel = (
         node_gather(vel_flat, slave_node.reshape(-1))
@@ -317,7 +344,7 @@
     master_contact = node_scatter_add(
         master_force.transpose(1, 0, 2).reshape(3, -1),
         master_node.reshape(-1),
-        jnp.zeros((3 * LANES, node_total // LANES), jnp.float32),
+        jnp.zeros((3, layers * row_cells, col_cells), jnp.float32),
     )
     returned = lax.all_to_all(
         forces.reshape(devices, slot_depth, 3, seg_width),
@@ -327,12 +354,8 @@
         tiled=True,
     )
     slave_force = jnp.take(returned.reshape(item_total, 3, seg_width), target_slot, axis=0)
-    contact = sums_to_nodes(
-        node_scatter_add(
-            slave_force.transpose(1, 0, 2).reshape(3, -1), slave_node.reshape(-1), master_contact
-        ),
-        3,
-        node_total,
+    contact = node_scatter_add(
+        slave_force.transpose(1, 0, 2).reshape(3, -1), slave_node.reshape(-1), master_contact
     )
     contact_field = contact.reshape(3, layers, row_cells, col_cells)
     velocity_new = velocity + TIME_STEP * (stress + contact_field) / node_mass[None]

time: 129 us -> 128 us (level)
  local copies, waits for them, and re-layouts: 16.3 us -> 13.6 us
  waiting for transfers between devices: 9.61 us -> 11.9 us
  starting transfers between devices: 34.6 us -> 32.9 us
    ppermute x4, waiting for transfers between devices: 0.01 us -> 5.56 us  [padded_2(): lax.ppermute(lax.index_in_dim(block, block.shape[dim] - 1, axis=dim, keep...]
    ppermute x4, waiting for transfers between devices: 3.85 us -> 0.01 us  [padded_2(): lax.ppermute(lax.index_in_dim(block, 0, axis=dim, keepdims=False), axis,...]
    another operation x3 -> x0, local copies, waits for them, and re-layouts: 2.05 us -> none  [the longest x2 1.94 us: node_gather(): field.reshape(channels, high_count, LANES).transpose(0, 2, 1)]
    all_to_all x1, starting transfers between devices: 6.39 us -> 5.08 us  [on_device(): lax.all_to_all(outgoing.reshape(devices, slot_depth, 8, seg_width), ('gx'...]
    unnamed x37 -> x33, local copies, waits for them, and re-layouts: 4.45 us -> 3.93 us
  transfers between devices with their start and end apart: 10 -> 10, of which waited for: 3 -> 5; matrix products, arithmetic and copies ran while one was open for 7% -> 9% of each run, Pallas kernels for 6% -> 6%
where the time goes in v17:
time: 128 us; the launch traced here: 126 us
  other arithmetic  37.3 us (29%)
  starting transfers between devices  32.9 us (26%)
  Pallas kernels  28.5 us (22%)
  local copies, waits for them, and re-layouts  13.6 us (11%)
  waiting for transfers between devices  11.9 us (9%)
  between operations  1.42 us (1%)
    reduce_sum x1, other arithmetic, contact_pairs(): reaction = jnp.sum(push_force, axis=2)  26.4 us
    pallas_call x2, Pallas kernels, node_gather(): pl.pallas_call(gather_kernel, grid=(padded_count // TILE,), in_specs=[pl....  15.3 us
    pallas_call x2, Pallas kernels, node_scatter_add(): pl.pallas_call(scatter_kernel, grid=(padded_count // TILE,), in_specs=[pl...  13.2 us
    ppermute x4, starting transfers between devices, padded_2(): lax.ppermute(lax.index_in_dim(block, 0, axis=dim, keepdims=False), axis,...  11.1 us
    ppermute x4, starting transfers between devices, padded_2(): lax.ppermute(lax.index_in_dim(block, block.shape[dim] - 1, axis=dim, keep...  10.7 us
    all_to_all x1, starting transfers between devices, on_device(): lax.all_to_all(forces.reshape(devices, slot_depth, 3, seg_width), ('gx',...  5.9 us
    all_to_all x1, waiting for transfers between devices, on_device(): lax.all_to_all(forces.reshape(devices, slot_depth, 3, seg_width), ('gx',...  5.65 us
    ppermute x4, waiting for transfers between devices, padded_2(): lax.ppermute(lax.index_in_dim(block, block.shape[dim] - 1, axis=dim, keep...  5.56 us
  transfers between devices with their start and end apart: 10, of which 5 were waited for; matrix products, arithmetic and copies ran while one was open for 9% of the time, Pallas kernels for 6%

profile of v17, /device:TPU:9, one launch (start us, length us, event | category | flops | bytes accessed | tf_op | source)
XLA Modules:
  0.0 125.8 jit_solution(14191652968609314850)
XLA Ops:
  0.6 1.2 copy.225
  1.9 1.1 copy_bitcast_fusion
  3.1 11.2 %shard_map.149 = f32[3,16384]{1,0:T(4,128)} custom-call(s32[1,16384]{1,0:T(1,128)} %bitcast.203, f32[3,128,256]{2,1,0:T(8,128)} %bitcast.184), custom_call_target="tpu_custom_call" | custom-call | tf_op jit(solution)/shard_map/pallas_call | solution.py:105
  14.5 2.6 %collective-permute-start.1 = (f32[6,8,256]{2,1,0:T(8,128)S(1)}, f32[6,8,256]{2,1,0:T(8,128)S(1)}, u32[]{:S(2)}, u32[]{:S(2)}) collective-permute-start(f32[6,8,256]{2,1,0:T(8,128)S(1)} %get-tuple-element.42), channel_id=1, source_target_pairs={{8,0},{16,8},{24,16},{9,1},{17,9},{25,17},{10,2},{18,10},{26,18},{... | collective-permute-start | bytes 147464 | tf_op jit(solution)/shard_map/ppermute | solution.py:151
  17.1 3.0 %collective-permute-start = (f32[6,8,256]{2,1,0:T(8,128)S(1)}, f32[6,8,256]{2,1,0:T(8,128)S(1)}, u32[]{:S(2)}, u32[]{:S(2)}) collective-permute-start(f32[6,8,256]{2,1,0:T(8,128)S(1)} %get-tuple-element.41), channel_id=1, source_target_pairs={{0,8},{8,16},{16,24},{1,9},{9,17},{17,25},{2,10},{10,18},{18,26},{... | collective-permute-start | bytes 147464 | tf_op jit(solution)/shard_map/ppermute | solution.py:148
  21.6 0.8 gather_fusion
  22.5 1.2 select_select_fusion
  23.7 5.1 %all-to-all-start = ((f32[32,5,8,128]{3,2,1,0:T(8,128)}), f32[32,5,8,128]{3,2,1,0:T(8,128)S(1)}, u32[]{:S(2)}, u32[]{:S(2)}) async-start(f32[32,5,8,128]{3,2,1,0:T(8,128)} %select_select_fusion), calls=%async_computation | async-start | bytes 1310720 | tf_op jit(solution)/shard_map/all_to_all | solution.py:324
  28.8 4.0 %shard_map.150 = f32[3,4096]{1,0:T(4,128)} custom-call(s32[1,4096]{1,0:T(1,128)} %bitcast.230, f32[3,128,256]{2,1,0:T(8,128)} %bitcast.185), custom_call_target="tpu_custom_call" | custom-call | tf_op jit(solution)/shard_map/pallas_call | solution.py:105
  32.9 0.9 copy_add_fusion.1
  34.5 3.1 %collective-permute-start.3 = (f32[6,8,18]{2,1,0:T(8,128)S(1)}, f32[6,8,18]{2,1,0:T(8,128)S(1)}, u32[]{:S(2)}, u32[]{:S(2)}) collective-permute-start(f32[6,8,18]{2,1,0:T(8,128)S(1)} %bitcast.232), channel_id=1, source_target_pairs={{1,0},{2,1},{3,2},{4,3},{5,4},{6,5},{7,6},{9,8},{10,9},{11,10},{12... | collective-permute-start | bytes 10376 | tf_op jit(solution)/shard_map/ppermute | solution.py:151
  38.0 2.4 %collective-permute-start.2 = (f32[6,8,18]{2,1,0:T(8,128)S(1)}, f32[6,8,18]{2,1,0:T(8,128)S(1)}, u32[]{:S(2)}, u32[]{:S(2)}) collective-permute-start(f32[6,8,18]{2,1,0:T(8,128)S(1)} %bitcast.234), channel_id=1, source_target_pairs={{0,1},{1,2},{2,3},{3,4},{4,5},{5,6},{6,7},{8,9},{9,10},{10,11},{11... | collective-permute-start | bytes 10376 | tf_op jit(solution)/shard_map/ppermute | solution.py:148
  41.3 2.4 %collective-permute-done.2 = f32[6,8,18]{2,1,0:T(8,128)S(1)} collective-permute-done((f32[6,8,18]{2,1,0:T(8,128)S(1)}, f32[6,8,18]{2,1,0:T(8,128)S(1)}, u32[]{:S(2)}, u32[]{:S(2)}) %collective-permute-start.2) | collective-permute-done | bytes 3488 | tf_op jit(solution)/shard_map/ppermute | solution.py:148
  46.8 1.9 %fusion.78 = (f32[160,1,128]{2,1,0:T(1,128)S(1)}, f32[160,1,128]{2,1,0:T(1,128)S(1)}, f32[160,1,128]{2,1,0:T(1,128)S(1)}, f32[160,1,128]{2,1,0:T(1,128)S(1)}, f3...) fusion(f32[160,8,128]{2,1,0:T(8,128)S(1)} %bitcast.186), kind=kLoop, calls=%fused_computation.183 | loop fusion | flops 20320 | bytes 1229440 | tf_op jit(solution)/shard_map/slice | solution.py:231
  48.7 0.8 gather_fusion.1
  50.8 26.4 %fusion.75 = (f32[160,128]{1,0:T(8,128)S(1)}, f32[160,128]{1,0:T(8,128)S(1)}, f32[160,128]{1,0:T(8,128)S(1)}, f32[160,128]{1,0:T(8,128)S(1)}) fusion(f32[160,128]{1,0:T(8,128)S(1)} %multiply_add_fusion, f32[160,128]{1,0:T(8,128)S(1)} %bitcast.218, f32[160,128]{1,0:T(8,128)S(1)} %bitcast.219, f32[160,128]{1,0:T(8,128)S(1)} %bitcast.220, ...), kind=kLoop, calls=%fused_computation.180 | loop fusion | flops 104775680 | bytes 1556480 | tf_op jit(solution)/shard_map/reduce_sum | solution.py:245
  77.3 0.9 copy.254
  78.2 5.9 %all-to-all-start.1 = ((f32[32,5,3,128]{3,2,1,0:T(4,128)}), f32[32,5,3,128]{3,2,1,0:T(4,128)S(1)}, u32[]{:S(2)}, u32[]{:S(2)}) async-start(f32[32,5,3,128]{3,2,1,0:T(4,128)} %copy.254), calls=%async_computation.1 | async-start | bytes 655360 | tf_op jit(solution)/shard_map/all_to_all | solution.py:349
  85.1 0.8 broadcast_in_dim.138.init_ref
  85.9 3.7 %shard_map.151.init_ref = f32[3,128,256]{2,1,0:T(8,128)} custom-call(s32[1,4096]{1,0:T(1,128)} %bitcast.231, f32[3,4096]{1,0:T(4,128)} %bitcast.205, f32[3,128,256]{2,1,0:T(8,128)} %broadcast_in_dim.138.init_ref), custom_call_target="tpu_custom_call" | custom-call | tf_op jit(solution)/shard_map/pallas_call | solution.py:122
  89.6 5.6 %all-to-all-done.1 = f32[32,5,3,128]{3,2,1,0:T(4,128)S(1)} async-done(((f32[32,5,3,128]{3,2,1,0:T(4,128)}), f32[32,5,3,128]{3,2,1,0:T(4,128)S(1)}, u32[]{:S(2)}, u32[]{:S(2)}) %all-to-all-start.1) | async-done | bytes 245792 | tf_op jit(solution)/shard_map/all_to_all | solution.py:349
  95.3 0.8 gather_fusion.2
  96.0 0.9 select_bitcast_fusion.force_ref
  96.9 9.5 %shard_map.152 = f32[3,128,256]{2,1,0:T(8,128)} custom-call(s32[1,16384]{1,0:T(1,128)} %bitcast.204, f32[3,16384]{1,0:T(4,128)} %select_bitcast_fusion.force_ref, f32[3,128,256]{2,1,0:T(8,128)} %shard_map.151.init_ref), custom_call_target="tpu_custom_call" | custom-call | tf_op jit(solution)/shard_map/pallas_call | solution.py:122
  106.4 1.5 %fusion.14 = f32[3,8,16,256]{3,1,2,0:T(8,128)S(1)} fusion(f32[1,8,16,256]{3,1,2,0:T(8,128)S(1)} %fusion.63, f32[1,8,16,256]{3,1,2,0:T(8,128)S(1)} %fusion.65, f32[1,8,16,256]{3,1,2,0:T(8,128)S(1)} %fusion.67, f32[3,8,16,256]{3,2,1,0:T(8,128)S(1)} %copy-done, f32[3,8,16,256]{3,2,1,0:T(8,128)} %bitcast.190, f32[8,16,256]{2,0,1:T(8,128)S(1)} %copy.258), kind=kLoop, calls=%fused_computation.42 | loop fusion | flops 589824 | bytes 1703936 | tf_op jit(solution)/shard_map/add | solution.py:361
  107.9 2.3 %collective-permute-start.5 = (f32[3,8,256]{2,1,0:T(8,128)S(1)}, f32[3,8,256]{2,1,0:T(8,128)S(1)}, u32[]{:S(2)}, u32[]{:S(2)}) collective-permute-start(f32[3,8,256]{2,1,0:T(8,128)S(1)} %get-tuple-element.56), channel_id=1, source_target_pairs={{8,0},{16,8},{24,16},{9,1},{17,9},{25,17},{10,2},{18,10},{26,18},{... | collective-permute-start | bytes 73736 | tf_op jit(solution)/shard_map/ppermute | solution.py:151
  110.3 3.2 %collective-permute-start.4 = (f32[3,8,256]{2,1,0:T(8,128)S(1)}, f32[3,8,256]{2,1,0:T(8,128)S(1)}, u32[]{:S(2)}, u32[]{:S(2)}) collective-permute-start(f32[3,8,256]{2,1,0:T(8,128)S(1)} %get-tuple-element.55), channel_id=1, source_target_pairs={{0,8},{8,16},{16,24},{1,9},{9,17},{17,25},{2,10},{10,18},{18,26},{... | collective-permute-start | bytes 73736 | tf_op jit(solution)/shard_map/ppermute | solution.py:148
  113.5 0.9 collective-permute-done.4
  114.9 3.2 %collective-permute-start.7 = (f32[3,8,18]{2,1,0:T(8,128)S(1)}, f32[3,8,18]{2,1,0:T(8,128)S(1)}, u32[]{:S(2)}, u32[]{:S(2)}) collective-permute-start(f32[3,8,18]{2,1,0:T(8,128)S(1)} %bitcast.237), channel_id=1, source_target_pairs={{1,0},{2,1},{3,2},{4,3},{5,4},{6,5},{7,6},{9,8},{10,9},{11,10},{12... | collective-permute-start | bytes 5192 | tf_op jit(solution)/shard_map/ppermute | solution.py:151
  118.3 2.1 %collective-permute-start.6 = (f32[3,8,18]{2,1,0:T(8,128)S(1)}, f32[3,8,18]{2,1,0:T(8,128)S(1)}, u32[]{:S(2)}, u32[]{:S(2)}) collective-permute-start(f32[3,8,18]{2,1,0:T(8,128)S(1)} %bitcast.239), channel_id=1, source_target_pairs={{0,1},{1,2},{2,3},{3,4},{4,5},{5,6},{6,7},{8,9},{9,10},{10,11},{11... | collective-permute-start | bytes 5192 | tf_op jit(solution)/shard_map/ppermute | solution.py:148
  120.4 0.9 copy.266
  121.5 2.2 %collective-permute-done.6 = f32[3,8,18]{2,1,0:T(8,128)S(1)} collective-permute-done((f32[3,8,18]{2,1,0:T(8,128)S(1)}, f32[3,8,18]{2,1,0:T(8,128)S(1)}, u32[]{:S(2)}, u32[]{:S(2)}) %collective-permute-start.6) | collective-permute-done | bytes 1760 | tf_op jit(solution)/shard_map/ppermute | solution.py:148
  (115 shorter events, 11.6 us)
Async XLA Ops:
  1.9 18.3 %copy-start.12 = (s32[128,1]{0,1:T(1,128)S(1)}, s32[128,1]{0,1:T(1,128)}, u32[]{:S(2)}) copy-start(s32[128,1]{0,1:T(1,128)} %param.22) | copy-start | bytes 1540
  1.9 18.7 %copy-start.13 = (s32[128]{0:T(128)S(1)}, s32[128]{0:T(128)}, u32[]{:S(2)}) copy-start(s32[128]{0:T(128)} %param.23) | copy-start | bytes 1540
  3.0 17.8 %copy-start.7 = (f32[128,128]{1,0:T(8,128)S(1)}, f32[128,128]{1,0:T(8,128)}, u32[]{:S(2)}) copy-start(f32[128,128]{1,0:T(8,128)} %param.19) | copy-start | bytes 196612
  3.0 17.8 %copy-start.11 = (s32[128]{0:T(128)S(1)}, s32[128]{0:T(128)}, u32[]{:S(2)}) copy-start(s32[128]{0:T(128)} %param.20) | copy-start | bytes 1540
  3.0 17.9 %copy-start.3 = (f32[128,3,128]{2,0,1:T(8,128)S(1)}, f32[128,3,128]{2,0,1:T(8,128)}, u32[]{:S(2)}) copy-start(f32[128,3,128]{2,0,1:T(8,128)} %param.18) | copy-start | bytes 589828
  14.4 6.6 %copy-start.1 = (f32[3,16384]{1,0:T(4,128)S(1)}, f32[3,16384]{1,0:T(4,128)}, u32[]{:S(2)}) copy-start(f32[3,16384]{1,0:T(4,128)} %shard_map.149) | copy-start | bytes 589828
  14.5 19.3 %collective-permute-start.1 = (f32[6,8,256]{2,1,0:T(8,128)S(1)}, f32[6,8,256]{2,1,0:T(8,128)S(1)}, u32[]{:S(2)}, u32[]{:S(2)}) collective-permute-start(f32[6,8,256]{2,1,0:T(8,128)S(1)} %get-tuple-element.42), channel_id=1, source_target_pairs={{8,0},{16,8},{24,16},{9,1},{17,9},{25,17},{10,2},{18,10},{26,18},{... | collective-permute-start | bytes 147464 | tf_op jit(solution)/shard_map/ppermute | solution.py:151
  17.1 16.7 %collective-permute-start = (f32[6,8,256]{2,1,0:T(8,128)S(1)}, f32[6,8,256]{2,1,0:T(8,128)S(1)}, u32[]{:S(2)}, u32[]{:S(2)}) collective-permute-start(f32[6,8,256]{2,1,0:T(8,128)S(1)} %get-tuple-element.41), channel_id=1, source_target_pairs={{0,8},{8,16},{16,24},{1,9},{9,17},{17,25},{2,10},{10,18},{18,26},{... | collective-permute-start | bytes 147464 | tf_op jit(solution)/shard_map/ppermute | solution.py:148
  22.5 10.4 %copy-start.9 = (f32[32,2,128]{2,1,0:T(2,128)S(1)}, f32[32,2,128]{2,1,0:T(2,128)}, u32[]{:S(2)}) copy-start(f32[32,2,128]{2,1,0:T(2,128)} %param.25) | copy-start | bytes 98308
  22.5 10.4 %copy-start.8 = (f32[32,3,128]{2,0,1:T(8,128)S(1)}, f32[32,3,128]{2,0,1:T(8,128)}, u32[]{:S(2)}) copy-start(f32[32,3,128]{2,0,1:T(8,128)} %param.24) | copy-start | bytes 147460
  23.7 23.1 %all-to-all-start = ((f32[32,5,8,128]{3,2,1,0:T(8,128)}), f32[32,5,8,128]{3,2,1,0:T(8,128)S(1)}, u32[]{:S(2)}, u32[]{:S(2)}) async-start(f32[32,5,8,128]{3,2,1,0:T(8,128)} %select_select_fusion), calls=%async_computation | async-start | bytes 1310720 | tf_op jit(solution)/shard_map/all_to_all | solution.py:324
  33.9 6.5 %copy-start.4 = (f32[8,16,256]{2,1,0:T(8,128)S(1)}, f32[8,16,256]{2,1,0:T(8,128)}, u32[]{:S(2)}) copy-start(f32[8,16,256]{2,1,0:T(8,128)} %param.17) | copy-start | bytes 393220
  33.9 6.6 %copy-start.2 = (f32[3,4096]{1,0:T(4,128)S(1)}, f32[3,4096]{1,0:T(4,128)}, u32[]{:S(2)}) copy-start(f32[3,4096]{1,0:T(4,128)} %shard_map.150) | copy-start | bytes 147460
  33.9 6.6 %copy-start.10 = (f32[32,128]{1,0:T(8,128)S(1)}, f32[32,128]{1,0:T(8,128)}, u32[]{:S(2)}) copy-start(f32[32,128]{1,0:T(8,128)} %param.26) | copy-start | bytes 49156
  34.5 6.4 %collective-permute-start.3 = (f32[6,8,18]{2,1,0:T(8,128)S(1)}, f32[6,8,18]{2,1,0:T(8,128)S(1)}, u32[]{:S(2)}, u32[]{:S(2)}) collective-permute-start(f32[6,8,18]{2,1,0:T(8,128)S(1)} %bitcast.232), channel_id=1, source_target_pairs={{1,0},{2,1},{3,2},{4,3},{5,4},{6,5},{7,6},{9,8},{10,9},{11,10},{12... | collective-permute-start | bytes 10376 | tf_op jit(solution)/shard_map/ppermute | solution.py:151
  38.0 5.8 %collective-permute-start.2 = (f32[6,8,18]{2,1,0:T(8,128)S(1)}, f32[6,8,18]{2,1,0:T(8,128)S(1)}, u32[]{:S(2)}, u32[]{:S(2)}) collective-permute-start(f32[6,8,18]{2,1,0:T(8,128)S(1)} %bitcast.234), channel_id=1, source_target_pairs={{0,1},{1,2},{2,3},{3,4},{4,5},{5,6},{6,7},{8,9},{9,10},{10,11},{11... | collective-permute-start | bytes 10376 | tf_op jit(solution)/shard_map/ppermute | solution.py:148
  49.8 0.9 copy-start.5
  49.8 0.9 copy-start.6
  78.2 17.1 %all-to-all-start.1 = ((f32[32,5,3,128]{3,2,1,0:T(4,128)}), f32[32,5,3,128]{3,2,1,0:T(4,128)S(1)}, u32[]{:S(2)}, u32[]{:S(2)}) async-start(f32[32,5,3,128]{3,2,1,0:T(4,128)} %copy.254), calls=%async_computation.1 | async-start | bytes 655360 | tf_op jit(solution)/shard_map/all_to_all | solution.py:349
  85.9 20.5 %copy-start = (f32[3,8,16,256]{3,2,1,0:T(8,128)S(1)}, f32[3,8,16,256]{3,2,1,0:T(8,128)}, u32[]{:S(2)}) copy-start(f32[3,8,16,256]{3,2,1,0:T(8,128)} %param.14) | copy-start | bytes 1179652
  107.9 5.6 %collective-permute-start.5 = (f32[3,8,256]{2,1,0:T(8,128)S(1)}, f32[3,8,256]{2,1,0:T(8,128)S(1)}, u32[]{:S(2)}, u32[]{:S(2)}) collective-permute-start(f32[3,8,256]{2,1,0:T(8,128)S(1)} %get-tuple-element.56), channel_id=1, source_target_pairs={{8,0},{16,8},{24,16},{9,1},{17,9},{25,17},{10,2},{18,10},{26,18},{... | collective-permute-start | bytes 73736 | tf_op jit(solution)/shard_map/ppermute | solution.py:151
  110.3 4.2 %collective-permute-start.4 = (f32[3,8,256]{2,1,0:T(8,128)S(1)}, f32[3,8,256]{2,1,0:T(8,128)S(1)}, u32[]{:S(2)}, u32[]{:S(2)}) collective-permute-start(f32[3,8,256]{2,1,0:T(8,128)S(1)} %get-tuple-element.55), channel_id=1, source_target_pairs={{0,8},{8,16},{16,24},{1,9},{9,17},{17,25},{2,10},{10,18},{18,26},{... | collective-permute-start | bytes 73736 | tf_op jit(solution)/shard_map/ppermute | solution.py:148
  114.9 6.4 %collective-permute-start.7 = (f32[3,8,18]{2,1,0:T(8,128)S(1)}, f32[3,8,18]{2,1,0:T(8,128)S(1)}, u32[]{:S(2)}, u32[]{:S(2)}) collective-permute-start(f32[3,8,18]{2,1,0:T(8,128)S(1)} %bitcast.237), channel_id=1, source_target_pairs={{1,0},{2,1},{3,2},{4,3},{5,4},{6,5},{7,6},{9,8},{10,9},{11,10},{12... | collective-permute-start | bytes 5192 | tf_op jit(solution)/shard_map/ppermute | solution.py:151
  118.3 5.4 %collective-permute-start.6 = (f32[3,8,18]{2,1,0:T(8,128)S(1)}, f32[3,8,18]{2,1,0:T(8,128)S(1)}, u32[]{:S(2)}, u32[]{:S(2)}) collective-permute-start(f32[3,8,18]{2,1,0:T(8,128)S(1)} %bitcast.239), channel_id=1, source_target_pairs={{0,1},{1,2},{2,3},{3,4},{4,5},{5,6},{6,7},{8,9},{9,10},{10,11},{11... | collective-permute-start | bytes 5192 | tf_op jit(solution)/shard_map/ppermute | solution.py:148

commit v18 on v17

--- a/solution.py
+++ b/solution.py
@@ -277,9 +277,6 @@
     block_total, _, seg_width = slave_pos.shape
     master_total = master_cent.shape[0]
     slot_depth = (block_total + devices - 1) // devices + 1
-    stacked = jnp.concatenate(
-        [velocity, bulk[None], prestress[None], jnp.ones_like(bulk)[None]], axis=0
-    )
     vel_flat = velocity.reshape(3, layers * row_cells, col_cells)
     slave_count = block_total * seg_width
     slave_vel = (
@@ -287,7 +284,12 @@
         .reshape(3, block_total, seg_width)
         .transpose(1, 0, 2)
     )
-    stacked, slave_vel = lax.optimization_barrier((stacked, slave_vel))
+    held_vel, held_bulk, held_pre, slave_vel = lax.optimization_barrier(
+        (velocity, bulk, prestress, slave_vel)
+    )
+    stacked = jnp.concatenate(
+        [held_vel, held_bulk[None], held_pre[None], jnp.ones_like(held_bulk)[None]], axis=0
+    )
     padded = padded_2(stacked, (("gx", 2), ("gy", 3)), 1)
     stress, inside = stress_forces(padded)
     master_vel = (

time: 128 us -> 126 us (0.984)
  local copies, waits for them, and re-layouts: 13.6 us -> 12.3 us
    unnamed x33 -> x32, local copies, waits for them, and re-layouts: 3.93 us -> 2.39 us
    optimization_barrier x0 -> x1, local copies, waits for them, and re-layouts: none -> 1.3 us  [on_device(): lax.optimization_barrier((velocity, bulk, prestress, slave_vel))]
where the time goes in v18:
time: 126 us; the launch traced here: 124 us
  other arithmetic  36.5 us (29%)
  starting transfers between devices  32.8 us (26%)
  Pallas kernels  28.5 us (23%)
  local copies, waits for them, and re-layouts  12.3 us (10%)
  waiting for transfers between devices  11.8 us (9%)
  between operations  1.45 us (1%)
    reduce_sum x1, other arithmetic, contact_pairs(): reaction = jnp.sum(push_force, axis=2)  26.4 us
    pallas_call x2, Pallas kernels, node_gather(): pl.pallas_call(gather_kernel, grid=(padded_count // TILE,), in_specs=[pl....  15.3 us
    pallas_call x2, Pallas kernels, node_scatter_add(): pl.pallas_call(scatter_kernel, grid=(padded_count // TILE,), in_specs=[pl...  13.2 us
    ppermute x4, starting transfers between devices, padded_2(): lax.ppermute(lax.index_in_dim(block, 0, axis=dim, keepdims=False), axis,...  11.1 us
    ppermute x4, starting transfers between devices, padded_2(): lax.ppermute(lax.index_in_dim(block, block.shape[dim] - 1, axis=dim, keep...  10.7 us
    all_to_all x1, starting transfers between devices, on_device(): lax.all_to_all(forces.reshape(devices, slot_depth, 3, seg_width), ('gx',...  5.88 us
    all_to_all x1, waiting for transfers between devices, on_device(): lax.all_to_all(forces.reshape(devices, slot_depth, 3, seg_width), ('gx',...  5.64 us
    ppermute x4, waiting for transfers between devices, padded_2(): lax.ppermute(lax.index_in_dim(block, block.shape[dim] - 1, axis=dim, keep...  5.55 us
  transfers between devices with their start and end apart: 10, of which 5 were waited for; matrix products, arithmetic and copies ran while one was open for 9% of the time, Pallas kernels for 6%

profile of v18, /device:TPU:9, one launch (start us, length us, event | category | flops | bytes accessed | tf_op | source)
XLA Modules:
  0.0 123.7 jit_solution(15504183164930591463)
XLA Ops:
  0.6 11.3 %shard_map.149 = f32[3,16384]{1,0:T(4,128)} custom-call(s32[1,16384]{1,0:T(1,128)} %bitcast.202, f32[3,128,256]{2,1,0:T(8,128)} %bitcast.183), custom_call_target="tpu_custom_call" | custom-call | tf_op jit(solution)/shard_map/pallas_call | solution.py:105
  12.0 1.3 %copy.226 = f32[3,8,16,256]{3,1,0,2:T(8,128)S(1)} copy(f32[3,8,16,256]{3,2,1,0:T(8,128)} %param.14) | data formatting | bytes 786432 | tf_op jit(solution)/shard_map/optimization_barrier | solution.py:287
  13.5 2.6 %collective-permute-start.1 = (f32[6,8,256]{2,1,0:T(8,128)S(1)}, f32[6,8,256]{2,1,0:T(8,128)S(1)}, u32[]{:S(2)}, u32[]{:S(2)}) collective-permute-start(f32[6,8,256]{2,1,0:T(8,128)S(1)} %get-tuple-element.46), channel_id=1, source_target_pairs={{8,0},{16,8},{24,16},{9,1},{17,9},{25,17},{10,2},{18,10},{26,18},{... | collective-permute-start | bytes 147464 | tf_op jit(solution)/shard_map/ppermute | solution.py:151
  16.1 3.0 %collective-permute-start = (f32[6,8,256]{2,1,0:T(8,128)S(1)}, f32[6,8,256]{2,1,0:T(8,128)S(1)}, u32[]{:S(2)}, u32[]{:S(2)}) collective-permute-start(f32[6,8,256]{2,1,0:T(8,128)S(1)} %get-tuple-element.45), channel_id=1, source_target_pairs={{0,8},{8,16},{16,24},{1,9},{9,17},{17,25},{2,10},{10,18},{18,26},{... | collective-permute-start | bytes 147464 | tf_op jit(solution)/shard_map/ppermute | solution.py:148
  20.6 0.8 gather_fusion
  21.5 1.2 select_select_fusion
  22.7 5.1 %all-to-all-start = ((f32[32,5,8,128]{3,2,1,0:T(8,128)}), f32[32,5,8,128]{3,2,1,0:T(8,128)S(1)}, u32[]{:S(2)}, u32[]{:S(2)}) async-start(f32[32,5,8,128]{3,2,1,0:T(8,128)} %select_select_fusion), calls=%async_computation | async-start | bytes 1310720 | tf_op jit(solution)/shard_map/all_to_all | solution.py:326
  27.8 4.0 %shard_map.150 = f32[3,4096]{1,0:T(4,128)} custom-call(s32[1,4096]{1,0:T(1,128)} %bitcast.229, f32[3,128,256]{2,1,0:T(8,128)} %bitcast.184), custom_call_target="tpu_custom_call" | custom-call | tf_op jit(solution)/shard_map/pallas_call | solution.py:105
  31.9 0.9 copy_add_fusion.1
  33.5 3.1 %collective-permute-start.3 = (f32[6,8,18]{2,1,0:T(8,128)S(1)}, f32[6,8,18]{2,1,0:T(8,128)S(1)}, u32[]{:S(2)}, u32[]{:S(2)}) collective-permute-start(f32[6,8,18]{2,1,0:T(8,128)S(1)} %bitcast.231), channel_id=1, source_target_pairs={{1,0},{2,1},{3,2},{4,3},{5,4},{6,5},{7,6},{9,8},{10,9},{11,10},{12... | collective-permute-start | bytes 10376 | tf_op jit(solution)/shard_map/ppermute | solution.py:151
  37.0 2.4 %collective-permute-start.2 = (f32[6,8,18]{2,1,0:T(8,128)S(1)}, f32[6,8,18]{2,1,0:T(8,128)S(1)}, u32[]{:S(2)}, u32[]{:S(2)}) collective-permute-start(f32[6,8,18]{2,1,0:T(8,128)S(1)} %bitcast.233), channel_id=1, source_target_pairs={{0,1},{1,2},{2,3},{3,4},{4,5},{5,6},{6,7},{8,9},{9,10},{10,11},{11... | collective-permute-start | bytes 10376 | tf_op jit(solution)/shard_map/ppermute | solution.py:148
  40.3 2.4 %collective-permute-done.2 = f32[6,8,18]{2,1,0:T(8,128)S(1)} collective-permute-done((f32[6,8,18]{2,1,0:T(8,128)S(1)}, f32[6,8,18]{2,1,0:T(8,128)S(1)}, u32[]{:S(2)}, u32[]{:S(2)}) %collective-permute-start.2) | collective-permute-done | bytes 3488 | tf_op jit(solution)/shard_map/ppermute | solution.py:148
  45.7 1.3 %fusion.79 = (f32[160,1,128]{2,1,0:T(1,128)S(1)}, f32[160,1,128]{2,1,0:T(1,128)S(1)}, f32[160,1,128]{2,1,0:T(1,128)S(1)}, f32[160,1,128]{2,1,0:T(1,128)S(1)}, f3...) fusion(f32[160,8,128]{2,1,0:T(8,128)S(1)} %bitcast.185), kind=kLoop, calls=%fused_computation.185 | loop fusion | flops 20320 | bytes 1229440 | tf_op jit(solution)/shard_map/slice | solution.py:231
  47.1 0.8 gather_fusion.1
  48.8 26.4 %fusion.76 = (f32[160,128]{1,0:T(8,128)S(1)}, f32[160,128]{1,0:T(8,128)S(1)}, f32[160,128]{1,0:T(8,128)S(1)}, f32[160,128]{1,0:T(8,128)S(1)}) fusion(f32[160,128]{1,0:T(8,128)S(1)} %multiply_add_fusion, f32[160,128]{1,0:T(8,128)S(1)} %bitcast.217, f32[160,128]{1,0:T(8,128)S(1)} %bitcast.218, f32[160,128]{1,0:T(8,128)S(1)} %bitcast.219, ...), kind=kLoop, calls=%fused_computation.182 | loop fusion | flops 104775680 | bytes 1556480 | tf_op jit(solution)/shard_map/reduce_sum | solution.py:245
  75.3 0.9 copy.254
  76.2 5.9 %all-to-all-start.1 = ((f32[32,5,3,128]{3,2,1,0:T(4,128)}), f32[32,5,3,128]{3,2,1,0:T(4,128)S(1)}, u32[]{:S(2)}, u32[]{:S(2)}) async-start(f32[32,5,3,128]{3,2,1,0:T(4,128)} %copy.254), calls=%async_computation.1 | async-start | bytes 655360 | tf_op jit(solution)/shard_map/all_to_all | solution.py:351
  83.1 0.8 broadcast_in_dim.138.init_ref
  83.9 3.7 %shard_map.151.init_ref = f32[3,128,256]{2,1,0:T(8,128)} custom-call(s32[1,4096]{1,0:T(1,128)} %bitcast.230, f32[3,4096]{1,0:T(4,128)} %bitcast.204, f32[3,128,256]{2,1,0:T(8,128)} %broadcast_in_dim.138.init_ref), custom_call_target="tpu_custom_call" | custom-call | tf_op jit(solution)/shard_map/pallas_call | solution.py:122
  87.7 5.6 %all-to-all-done.1 = f32[32,5,3,128]{3,2,1,0:T(4,128)S(1)} async-done(((f32[32,5,3,128]{3,2,1,0:T(4,128)}), f32[32,5,3,128]{3,2,1,0:T(4,128)S(1)}, u32[]{:S(2)}, u32[]{:S(2)}) %all-to-all-start.1) | async-done | bytes 245792 | tf_op jit(solution)/shard_map/all_to_all | solution.py:351
  93.3 0.7 gather_fusion.2
  94.0 0.9 select_bitcast_fusion.force_ref
  94.9 9.5 %shard_map.152 = f32[3,128,256]{2,1,0:T(8,128)} custom-call(s32[1,16384]{1,0:T(1,128)} %bitcast.203, f32[3,16384]{1,0:T(4,128)} %select_bitcast_fusion.force_ref, f32[3,128,256]{2,1,0:T(8,128)} %shard_map.151.init_ref), custom_call_target="tpu_custom_call" | custom-call | tf_op jit(solution)/shard_map/pallas_call | solution.py:122
  104.4 1.5 %fusion.14 = f32[3,8,16,256]{3,1,2,0:T(8,128)S(1)} fusion(f32[1,8,16,256]{3,1,2,0:T(8,128)S(1)} %fusion.63, f32[1,8,16,256]{3,1,2,0:T(8,128)S(1)} %fusion.65, f32[1,8,16,256]{3,1,2,0:T(8,128)S(1)} %fusion.67, f32[3,8,16,256]{3,2,1,0:T(8,128)S(1)} %copy-done, f32[3,8,16,256]{3,2,1,0:T(8,128)} %bitcast.189, f32[8,16,256]{2,0,1:T(8,128)S(1)} %copy.258), kind=kLoop, calls=%fused_computation.41 | loop fusion | flops 589824 | bytes 1703936 | tf_op jit(solution)/shard_map/add | solution.py:363
  105.9 2.3 %collective-permute-start.5 = (f32[3,8,256]{2,1,0:T(8,128)S(1)}, f32[3,8,256]{2,1,0:T(8,128)S(1)}, u32[]{:S(2)}, u32[]{:S(2)}) collective-permute-start(f32[3,8,256]{2,1,0:T(8,128)S(1)} %get-tuple-element.60), channel_id=1, source_target_pairs={{8,0},{16,8},{24,16},{9,1},{17,9},{25,17},{10,2},{18,10},{26,18},{... | collective-permute-start | bytes 73736 | tf_op jit(solution)/shard_map/ppermute | solution.py:151
  108.3 3.2 %collective-permute-start.4 = (f32[3,8,256]{2,1,0:T(8,128)S(1)}, f32[3,8,256]{2,1,0:T(8,128)S(1)}, u32[]{:S(2)}, u32[]{:S(2)}) collective-permute-start(f32[3,8,256]{2,1,0:T(8,128)S(1)} %get-tuple-element.59), channel_id=1, source_target_pairs={{0,8},{8,16},{16,24},{1,9},{9,17},{17,25},{2,10},{10,18},{18,26},{... | collective-permute-start | bytes 73736 | tf_op jit(solution)/shard_map/ppermute | solution.py:148
  111.5 0.9 collective-permute-done.4
  112.9 3.2 %collective-permute-start.7 = (f32[3,8,18]{2,1,0:T(8,128)S(1)}, f32[3,8,18]{2,1,0:T(8,128)S(1)}, u32[]{:S(2)}, u32[]{:S(2)}) collective-permute-start(f32[3,8,18]{2,1,0:T(8,128)S(1)} %bitcast.236), channel_id=1, source_target_pairs={{1,0},{2,1},{3,2},{4,3},{5,4},{6,5},{7,6},{9,8},{10,9},{11,10},{12... | collective-permute-start | bytes 5192 | tf_op jit(solution)/shard_map/ppermute | solution.py:151
  116.3 2.1 %collective-permute-start.6 = (f32[3,8,18]{2,1,0:T(8,128)S(1)}, f32[3,8,18]{2,1,0:T(8,128)S(1)}, u32[]{:S(2)}, u32[]{:S(2)}) collective-permute-start(f32[3,8,18]{2,1,0:T(8,128)S(1)} %bitcast.238), channel_id=1, source_target_pairs={{0,1},{1,2},{2,3},{3,4},{4,5},{5,6},{6,7},{8,9},{9,10},{10,11},{11... | collective-permute-start | bytes 5192 | tf_op jit(solution)/shard_map/ppermute | solution.py:148
  118.4 0.9 copy.266
  119.5 2.2 %collective-permute-done.6 = f32[3,8,18]{2,1,0:T(8,128)S(1)} collective-permute-done((f32[3,8,18]{2,1,0:T(8,128)S(1)}, f32[3,8,18]{2,1,0:T(8,128)S(1)}, u32[]{:S(2)}, u32[]{:S(2)}) %collective-permute-start.6) | collective-permute-done | bytes 1760 | tf_op jit(solution)/shard_map/ppermute | solution.py:148
  123.0 0.7 copy.267
  (114 shorter events, 10.5 us)
Async XLA Ops:
  0.6 12.7 %copy-start.6 = (f32[8,16,256]{2,1,0:T(8,128)S(1)}, f32[8,16,256]{2,1,0:T(8,128)}, u32[]{:S(2)}) copy-start(f32[8,16,256]{2,1,0:T(8,128)} %param.15) | copy-start | bytes 393220
  0.6 12.7 %copy-start.5 = (f32[8,16,256]{2,1,0:T(8,128)S(1)}, f32[8,16,256]{2,1,0:T(8,128)}, u32[]{:S(2)}) copy-start(f32[8,16,256]{2,1,0:T(8,128)} %param.16) | copy-start | bytes 393220
  11.9 7.2 %copy-start.12 = (s32[128,1]{0,1:T(1,128)S(1)}, s32[128,1]{0,1:T(1,128)}, u32[]{:S(2)}) copy-start(s32[128,1]{0,1:T(1,128)} %param.22) | copy-start | bytes 1540
  11.9 7.6 %copy-start.13 = (s32[128]{0:T(128)S(1)}, s32[128]{0:T(128)}, u32[]{:S(2)}) copy-start(s32[128]{0:T(128)} %param.23) | copy-start | bytes 1540
  11.9 7.9 %copy-start.7 = (f32[128,128]{1,0:T(8,128)S(1)}, f32[128,128]{1,0:T(8,128)}, u32[]{:S(2)}) copy-start(f32[128,128]{1,0:T(8,128)} %param.19) | copy-start | bytes 196612
  11.9 7.9 %copy-start.11 = (s32[128]{0:T(128)S(1)}, s32[128]{0:T(128)}, u32[]{:S(2)}) copy-start(s32[128]{0:T(128)} %param.20) | copy-start | bytes 1540
  12.0 8.0 %copy-start.1 = (f32[3,16384]{1,0:T(4,128)S(1)}, f32[3,16384]{1,0:T(4,128)}, u32[]{:S(2)}) copy-start(f32[3,16384]{1,0:T(4,128)} %shard_map.149) | copy-start | bytes 589828
  12.0 8.0 %copy-start.3 = (f32[128,3,128]{2,0,1:T(8,128)S(1)}, f32[128,3,128]{2,0,1:T(8,128)}, u32[]{:S(2)}) copy-start(f32[128,3,128]{2,0,1:T(8,128)} %param.18) | copy-start | bytes 589828
  13.5 19.3 %collective-permute-start.1 = (f32[6,8,256]{2,1,0:T(8,128)S(1)}, f32[6,8,256]{2,1,0:T(8,128)S(1)}, u32[]{:S(2)}, u32[]{:S(2)}) collective-permute-start(f32[6,8,256]{2,1,0:T(8,128)S(1)} %get-tuple-element.46), channel_id=1, source_target_pairs={{8,0},{16,8},{24,16},{9,1},{17,9},{25,17},{10,2},{18,10},{26,18},{... | collective-permute-start | bytes 147464 | tf_op jit(solution)/shard_map/ppermute | solution.py:151
  16.1 16.7 %collective-permute-start = (f32[6,8,256]{2,1,0:T(8,128)S(1)}, f32[6,8,256]{2,1,0:T(8,128)S(1)}, u32[]{:S(2)}, u32[]{:S(2)}) collective-permute-start(f32[6,8,256]{2,1,0:T(8,128)S(1)} %get-tuple-element.45), channel_id=1, source_target_pairs={{0,8},{8,16},{16,24},{1,9},{9,17},{17,25},{2,10},{10,18},{18,26},{... | collective-permute-start | bytes 147464 | tf_op jit(solution)/shard_map/ppermute | solution.py:148
  21.4 10.4 %copy-start.9 = (f32[32,2,128]{2,1,0:T(2,128)S(1)}, f32[32,2,128]{2,1,0:T(2,128)}, u32[]{:S(2)}) copy-start(f32[32,2,128]{2,1,0:T(2,128)} %param.25) | copy-start | bytes 98308
  21.4 10.4 %copy-start.8 = (f32[32,3,128]{2,0,1:T(8,128)S(1)}, f32[32,3,128]{2,0,1:T(8,128)}, u32[]{:S(2)}) copy-start(f32[32,3,128]{2,0,1:T(8,128)} %param.24) | copy-start | bytes 147460
  22.7 23.1 %all-to-all-start = ((f32[32,5,8,128]{3,2,1,0:T(8,128)}), f32[32,5,8,128]{3,2,1,0:T(8,128)S(1)}, u32[]{:S(2)}, u32[]{:S(2)}) async-start(f32[32,5,8,128]{3,2,1,0:T(8,128)} %select_select_fusion), calls=%async_computation | async-start | bytes 1310720 | tf_op jit(solution)/shard_map/all_to_all | solution.py:326
  32.9 6.5 %copy-start.4 = (f32[8,16,256]{2,1,0:T(8,128)S(1)}, f32[8,16,256]{2,1,0:T(8,128)}, u32[]{:S(2)}) copy-start(f32[8,16,256]{2,1,0:T(8,128)} %param.17) | copy-start | bytes 393220
  32.9 6.6 %copy-start.2 = (f32[3,4096]{1,0:T(4,128)S(1)}, f32[3,4096]{1,0:T(4,128)}, u32[]{:S(2)}) copy-start(f32[3,4096]{1,0:T(4,128)} %shard_map.150) | copy-start | bytes 147460
  32.9 6.6 %copy-start.10 = (f32[32,128]{1,0:T(8,128)S(1)}, f32[32,128]{1,0:T(8,128)}, u32[]{:S(2)}) copy-start(f32[32,128]{1,0:T(8,128)} %param.26) | copy-start | bytes 49156
  33.5 6.4 %collective-permute-start.3 = (f32[6,8,18]{2,1,0:T(8,128)S(1)}, f32[6,8,18]{2,1,0:T(8,128)S(1)}, u32[]{:S(2)}, u32[]{:S(2)}) collective-permute-start(f32[6,8,18]{2,1,0:T(8,128)S(1)} %bitcast.231), channel_id=1, source_target_pairs={{1,0},{2,1},{3,2},{4,3},{5,4},{6,5},{7,6},{9,8},{10,9},{11,10},{12... | collective-permute-start | bytes 10376 | tf_op jit(solution)/shard_map/ppermute | solution.py:151
  37.0 5.8 %collective-permute-start.2 = (f32[6,8,18]{2,1,0:T(8,128)S(1)}, f32[6,8,18]{2,1,0:T(8,128)S(1)}, u32[]{:S(2)}, u32[]{:S(2)}) collective-permute-start(f32[6,8,18]{2,1,0:T(8,128)S(1)} %bitcast.233), channel_id=1, source_target_pairs={{0,1},{1,2},{2,3},{3,4},{4,5},{5,6},{6,7},{8,9},{9,10},{10,11},{11... | collective-permute-start | bytes 10376 | tf_op jit(solution)/shard_map/ppermute | solution.py:148
  76.2 17.0 %all-to-all-start.1 = ((f32[32,5,3,128]{3,2,1,0:T(4,128)}), f32[32,5,3,128]{3,2,1,0:T(4,128)S(1)}, u32[]{:S(2)}, u32[]{:S(2)}) async-start(f32[32,5,3,128]{3,2,1,0:T(4,128)} %copy.254), calls=%async_computation.1 | async-start | bytes 655360 | tf_op jit(solution)/shard_map/all_to_all | solution.py:351
  83.9 20.5 %copy-start = (f32[3,8,16,256]{3,2,1,0:T(8,128)S(1)}, f32[3,8,16,256]{3,2,1,0:T(8,128)}, u32[]{:S(2)}) copy-start(f32[3,8,16,256]{3,2,1,0:T(8,128)} %param.14) | copy-start | bytes 1179652
  105.9 5.6 %collective-permute-start.5 = (f32[3,8,256]{2,1,0:T(8,128)S(1)}, f32[3,8,256]{2,1,0:T(8,128)S(1)}, u32[]{:S(2)}, u32[]{:S(2)}) collective-permute-start(f32[3,8,256]{2,1,0:T(8,128)S(1)} %get-tuple-element.60), channel_id=1, source_target_pairs={{8,0},{16,8},{24,16},{9,1},{17,9},{25,17},{10,2},{18,10},{26,18},{... | collective-permute-start | bytes 73736 | tf_op jit(solution)/shard_map/ppermute | solution.py:151
  108.3 4.2 %collective-permute-start.4 = (f32[3,8,256]{2,1,0:T(8,128)S(1)}, f32[3,8,256]{2,1,0:T(8,128)S(1)}, u32[]{:S(2)}, u32[]{:S(2)}) collective-permute-start(f32[3,8,256]{2,1,0:T(8,128)S(1)} %get-tuple-element.59), channel_id=1, source_target_pairs={{0,8},{8,16},{16,24},{1,9},{9,17},{17,25},{2,10},{10,18},{18,26},{... | collective-permute-start | bytes 73736 | tf_op jit(solution)/shard_map/ppermute | solution.py:148
  112.9 6.4 %collective-permute-start.7 = (f32[3,8,18]{2,1,0:T(8,128)S(1)}, f32[3,8,18]{2,1,0:T(8,128)S(1)}, u32[]{:S(2)}, u32[]{:S(2)}) collective-permute-start(f32[3,8,18]{2,1,0:T(8,128)S(1)} %bitcast.236), channel_id=1, source_target_pairs={{1,0},{2,1},{3,2},{4,3},{5,4},{6,5},{7,6},{9,8},{10,9},{11,10},{12... | collective-permute-start | bytes 5192 | tf_op jit(solution)/shard_map/ppermute | solution.py:151
  116.3 5.4 %collective-permute-start.6 = (f32[3,8,18]{2,1,0:T(8,128)S(1)}, f32[3,8,18]{2,1,0:T(8,128)S(1)}, u32[]{:S(2)}, u32[]{:S(2)}) collective-permute-start(f32[3,8,18]{2,1,0:T(8,128)S(1)} %bitcast.238), channel_id=1, source_target_pairs={{0,1},{1,2},{2,3},{3,4},{4,5},{5,6},{6,7},{8,9},{9,10},{10,11},{11... | collective-permute-start | bytes 5192 | tf_op jit(solution)/shard_map/ppermute | solution.py:148

commit v19 on v18

--- a/solution.py
+++ b/solution.py
@@ -284,19 +284,19 @@
         .reshape(3, block_total, seg_width)
         .transpose(1, 0, 2)
     )
-    held_vel, held_bulk, held_pre, slave_vel = lax.optimization_barrier(
-        (velocity, bulk, prestress, slave_vel)
-    )
-    stacked = jnp.concatenate(
-        [held_vel, held_bulk[None], held_pre[None], jnp.ones_like(held_bulk)[None]], axis=0
-    )
-    padded = padded_2(stacked, (("gx", 2), ("gy", 3)), 1)
-    stress, inside = stress_forces(padded)
     master_vel = (
         node_gather(vel_flat, master_node.reshape(-1))
         .reshape(3, master_total, seg_width)
         .transpose(1, 0, 2)
     )
+    held_vel, held_bulk, held_pre, master_vel = lax.optimization_barrier(
+        (velocity, bulk, prestress, master_vel)
+    )
+    stacked = jnp.concatenate(
+        [held_vel, held_bulk[None], held_pre[None], jnp.ones_like(held_bulk)[None]], axis=0
+    )
+    padded = padded_2(stacked, (("gx", 2), ("gy", 3)), 1)
+    stress, inside = stress_forces(padded)
     live_mask = jnp.arange(seg_width, dtype=jnp.int32)[None, :] < seg_count[:, None]
     area_live = jnp.where(live_mask, slave_area, jnp.zeros_like(slave_area))
     slave = jnp.concatenate(

time: 126 us -> 132 us (1.048)
  waiting for transfers between devices: 11.8 us -> 16.7 us
    ppermute x4, waiting for transfers between devices: 5.55 us -> 8.25 us  [padded_2(): lax.ppermute(lax.index_in_dim(block, block.shape[dim] - 1, axis=dim, keep...]
    all_to_all x1, waiting for transfers between devices: 0.65 us -> 2.8 us  [on_device(): lax.all_to_all(outgoing.reshape(devices, slot_depth, 8, seg_width), ('gx'...]
  transfers between devices with their start and end apart: 10 -> 10, of which waited for: 5 -> 5; matrix products, arithmetic and copies ran while one was open for 9% -> 10% of each run, Pallas kernels for 6% -> 12%
where the time goes in v19:
time: 132 us; the launch traced here: 130 us
  other arithmetic  37.6 us (28%)
  starting transfers between devices  32.8 us (25%)
  Pallas kernels  28.5 us (22%)
  waiting for transfers between devices  16.7 us (13%)
  local copies, waits for them, and re-layouts  12.2 us (9%)
  between operations  1.46 us (1%)
    reduce_sum x1, other arithmetic, contact_pairs(): reaction = jnp.sum(push_force, axis=2)  26.4 us
    pallas_call x2, Pallas kernels, node_gather(): pl.pallas_call(gather_kernel, grid=(padded_count // TILE,), in_specs=[pl....  15.3 us
    pallas_call x2, Pallas kernels, node_scatter_add(): pl.pallas_call(scatter_kernel, grid=(padded_count // TILE,), in_specs=[pl...  13.2 us
    ppermute x4, starting transfers between devices, padded_2(): lax.ppermute(lax.index_in_dim(block, 0, axis=dim, keepdims=False), axis,...  11.1 us
    ppermute x4, starting transfers between devices, padded_2(): lax.ppermute(lax.index_in_dim(block, block.shape[dim] - 1, axis=dim, keep...  10.8 us
    ppermute x4, waiting for transfers between devices, padded_2(): lax.ppermute(lax.index_in_dim(block, block.shape[dim] - 1, axis=dim, keep...  8.25 us
    all_to_all x1, starting transfers between devices, on_device(): lax.all_to_all(forces.reshape(devices, slot_depth, 3, seg_width), ('gx',...  5.88 us
    all_to_all x1, waiting for transfers between devices, on_device(): lax.all_to_all(forces.reshape(devices, slot_depth, 3, seg_width), ('gx',...  5.64 us
  transfers between devices with their start and end apart: 10, of which 5 were waited for; matrix products, arithmetic and copies ran while one was open for 10% of the time, Pallas kernels for 12%

profile of v19, /device:TPU:9, one launch (start us, length us, event | category | flops | bytes accessed | tf_op | source)
XLA Modules:
  0.0 129.6 jit_solution(10300237869959241067)
XLA Ops:
  0.7 4.1 %shard_map.149 = f32[3,4096]{1,0:T(4,128)} custom-call(s32[1,4096]{1,0:T(1,128)} %bitcast.229, f32[3,128,256]{2,1,0:T(8,128)} %bitcast.183), custom_call_target="tpu_custom_call" | custom-call | tf_op jit(solution)/shard_map/pallas_call | solution.py:105
  4.8 1.2 copy.226
  6.2 2.6 %collective-permute-start.1 = (f32[6,8,256]{2,1,0:T(8,128)S(1)}, f32[6,8,256]{2,1,0:T(8,128)S(1)}, u32[]{:S(2)}, u32[]{:S(2)}) collective-permute-start(f32[6,8,256]{2,1,0:T(8,128)S(1)} %get-tuple-element.46), channel_id=1, source_target_pairs={{8,0},{16,8},{24,16},{9,1},{17,9},{25,17},{10,2},{18,10},{26,18},{... | collective-permute-start | bytes 147464 | tf_op jit(solution)/shard_map/ppermute | solution.py:151
  8.8 3.0 %collective-permute-start = (f32[6,8,256]{2,1,0:T(8,128)S(1)}, f32[6,8,256]{2,1,0:T(8,128)S(1)}, u32[]{:S(2)}, u32[]{:S(2)}) collective-permute-start(f32[6,8,256]{2,1,0:T(8,128)S(1)} %get-tuple-element.45), channel_id=1, source_target_pairs={{0,8},{8,16},{16,24},{1,9},{9,17},{17,25},{2,10},{10,18},{18,26},{... | collective-permute-start | bytes 147464 | tf_op jit(solution)/shard_map/ppermute | solution.py:148
  12.3 11.2 %shard_map.150 = f32[3,16384]{1,0:T(4,128)} custom-call(s32[1,16384]{1,0:T(1,128)} %bitcast.202, f32[3,128,256]{2,1,0:T(8,128)} %bitcast.184), custom_call_target="tpu_custom_call" | custom-call | tf_op jit(solution)/shard_map/pallas_call | solution.py:105
  23.9 1.1 copy_add_fusion
  25.2 1.2 pad_maximum_fusion.3
  26.4 0.8 gather_fusion
  27.3 1.2 select_select_fusion
  28.5 5.1 %all-to-all-start = ((f32[32,5,8,128]{3,2,1,0:T(8,128)}), f32[32,5,8,128]{3,2,1,0:T(8,128)S(1)}, u32[]{:S(2)}, u32[]{:S(2)}) async-start(f32[32,5,8,128]{3,2,1,0:T(8,128)} %select_select_fusion), calls=%async_computation | async-start | bytes 1310720 | tf_op jit(solution)/shard_map/all_to_all | solution.py:326
  34.5 3.1 %collective-permute-start.3 = (f32[6,8,18]{2,1,0:T(8,128)S(1)}, f32[6,8,18]{2,1,0:T(8,128)S(1)}, u32[]{:S(2)}, u32[]{:S(2)}) collective-permute-start(f32[6,8,18]{2,1,0:T(8,128)S(1)} %bitcast.231), channel_id=1, source_target_pairs={{1,0},{2,1},{3,2},{4,3},{5,4},{6,5},{7,6},{9,8},{10,9},{11,10},{12... | collective-permute-start | bytes 10376 | tf_op jit(solution)/shard_map/ppermute | solution.py:151
  38.0 2.4 %collective-permute-start.2 = (f32[6,8,18]{2,1,0:T(8,128)S(1)}, f32[6,8,18]{2,1,0:T(8,128)S(1)}, u32[]{:S(2)}, u32[]{:S(2)}) collective-permute-start(f32[6,8,18]{2,1,0:T(8,128)S(1)} %bitcast.233), channel_id=1, source_target_pairs={{0,1},{1,2},{2,3},{3,4},{4,5},{5,6},{6,7},{8,9},{9,10},{10,11},{11... | collective-permute-start | bytes 10376 | tf_op jit(solution)/shard_map/ppermute | solution.py:148
  41.3 5.2 %collective-permute-done.2 = f32[6,8,18]{2,1,0:T(8,128)S(1)} collective-permute-done((f32[6,8,18]{2,1,0:T(8,128)S(1)}, f32[6,8,18]{2,1,0:T(8,128)S(1)}, u32[]{:S(2)}, u32[]{:S(2)}) %collective-permute-start.2) | collective-permute-done | bytes 3488 | tf_op jit(solution)/shard_map/ppermute | solution.py:148
  48.8 2.8 %all-to-all-done = f32[32,5,8,128]{3,2,1,0:T(8,128)S(1)} async-done(((f32[32,5,8,128]{3,2,1,0:T(8,128)}), f32[32,5,8,128]{3,2,1,0:T(8,128)S(1)}, u32[]{:S(2)}, u32[]{:S(2)}) %all-to-all-start) | async-done | bytes 655392 | tf_op jit(solution)/shard_map/all_to_all | solution.py:326
  51.6 1.3 %fusion.79 = (f32[160,1,128]{2,1,0:T(1,128)S(1)}, f32[160,1,128]{2,1,0:T(1,128)S(1)}, f32[160,1,128]{2,1,0:T(1,128)S(1)}, f32[160,1,128]{2,1,0:T(1,128)S(1)}, f3...) fusion(f32[160,8,128]{2,1,0:T(8,128)S(1)} %bitcast.185), kind=kLoop, calls=%fused_computation.185 | loop fusion | flops 20320 | bytes 1229440 | tf_op jit(solution)/shard_map/slice | solution.py:231
  53.0 0.8 gather_fusion.1
  54.6 26.4 %fusion.76 = (f32[160,128]{1,0:T(8,128)S(1)}, f32[160,128]{1,0:T(8,128)S(1)}, f32[160,128]{1,0:T(8,128)S(1)}, f32[160,128]{1,0:T(8,128)S(1)}) fusion(f32[160,128]{1,0:T(8,128)S(1)} %multiply_add_fusion, f32[160,128]{1,0:T(8,128)S(1)} %bitcast.217, f32[160,128]{1,0:T(8,128)S(1)} %bitcast.218, f32[160,128]{1,0:T(8,128)S(1)} %bitcast.219, ...), kind=kLoop, calls=%fused_computation.182 | loop fusion | flops 104775680 | bytes 1556480 | tf_op jit(solution)/shard_map/reduce_sum | solution.py:245
  81.2 0.9 copy.254
  82.1 5.9 %all-to-all-start.1 = ((f32[32,5,3,128]{3,2,1,0:T(4,128)}), f32[32,5,3,128]{3,2,1,0:T(4,128)S(1)}, u32[]{:S(2)}, u32[]{:S(2)}) async-start(f32[32,5,3,128]{3,2,1,0:T(4,128)} %copy.254), calls=%async_computation.1 | async-start | bytes 655360 | tf_op jit(solution)/shard_map/all_to_all | solution.py:351
  89.0 0.8 broadcast_in_dim.138.init_ref
  89.8 3.7 %shard_map.151.init_ref = f32[3,128,256]{2,1,0:T(8,128)} custom-call(s32[1,4096]{1,0:T(1,128)} %bitcast.230, f32[3,4096]{1,0:T(4,128)} %bitcast.204, f32[3,128,256]{2,1,0:T(8,128)} %broadcast_in_dim.138.init_ref), custom_call_target="tpu_custom_call" | custom-call | tf_op jit(solution)/shard_map/pallas_call | solution.py:122
  93.5 5.6 %all-to-all-done.1 = f32[32,5,3,128]{3,2,1,0:T(4,128)S(1)} async-done(((f32[32,5,3,128]{3,2,1,0:T(4,128)}), f32[32,5,3,128]{3,2,1,0:T(4,128)S(1)}, u32[]{:S(2)}, u32[]{:S(2)}) %all-to-all-start.1) | async-done | bytes 245792 | tf_op jit(solution)/shard_map/all_to_all | solution.py:351
  99.9 0.9 select_bitcast_fusion.force_ref
  100.8 9.5 %shard_map.152 = f32[3,128,256]{2,1,0:T(8,128)} custom-call(s32[1,16384]{1,0:T(1,128)} %bitcast.203, f32[3,16384]{1,0:T(4,128)} %select_bitcast_fusion.force_ref, f32[3,128,256]{2,1,0:T(8,128)} %shard_map.151.init_ref), custom_call_target="tpu_custom_call" | custom-call | tf_op jit(solution)/shard_map/pallas_call | solution.py:122
  110.3 1.5 %fusion.14 = f32[3,8,16,256]{3,1,2,0:T(8,128)S(1)} fusion(f32[1,8,16,256]{3,1,2,0:T(8,128)S(1)} %fusion.63, f32[1,8,16,256]{3,1,2,0:T(8,128)S(1)} %fusion.65, f32[1,8,16,256]{3,1,2,0:T(8,128)S(1)} %fusion.67, f32[3,8,16,256]{3,2,1,0:T(8,128)S(1)} %copy-done, f32[3,8,16,256]{3,2,1,0:T(8,128)} %bitcast.188, f32[8,16,256]{2,0,1:T(8,128)S(1)} %copy.258), kind=kLoop, calls=%fused_computation.41 | loop fusion | flops 589824 | bytes 1703936 | tf_op jit(solution)/shard_map/add | solution.py:363
  111.8 2.3 %collective-permute-start.5 = (f32[3,8,256]{2,1,0:T(8,128)S(1)}, f32[3,8,256]{2,1,0:T(8,128)S(1)}, u32[]{:S(2)}, u32[]{:S(2)}) collective-permute-start(f32[3,8,256]{2,1,0:T(8,128)S(1)} %get-tuple-element.60), channel_id=1, source_target_pairs={{8,0},{16,8},{24,16},{9,1},{17,9},{25,17},{10,2},{18,10},{26,18},{... | collective-permute-start | bytes 73736 | tf_op jit(solution)/shard_map/ppermute | solution.py:151
  114.1 3.3 %collective-permute-start.4 = (f32[3,8,256]{2,1,0:T(8,128)S(1)}, f32[3,8,256]{2,1,0:T(8,128)S(1)}, u32[]{:S(2)}, u32[]{:S(2)}) collective-permute-start(f32[3,8,256]{2,1,0:T(8,128)S(1)} %get-tuple-element.59), channel_id=1, source_target_pairs={{0,8},{8,16},{16,24},{1,9},{9,17},{17,25},{2,10},{10,18},{18,26},{... | collective-permute-start | bytes 73736 | tf_op jit(solution)/shard_map/ppermute | solution.py:148
  117.4 0.9 collective-permute-done.4
  118.7 3.2 %collective-permute-start.7 = (f32[3,8,18]{2,1,0:T(8,128)S(1)}, f32[3,8,18]{2,1,0:T(8,128)S(1)}, u32[]{:S(2)}, u32[]{:S(2)}) collective-permute-start(f32[3,8,18]{2,1,0:T(8,128)S(1)} %bitcast.236), channel_id=1, source_target_pairs={{1,0},{2,1},{3,2},{4,3},{5,4},{6,5},{7,6},{9,8},{10,9},{11,10},{12... | collective-permute-start | bytes 5192 | tf_op jit(solution)/shard_map/ppermute | solution.py:151
  122.1 2.1 %collective-permute-start.6 = (f32[3,8,18]{2,1,0:T(8,128)S(1)}, f32[3,8,18]{2,1,0:T(8,128)S(1)}, u32[]{:S(2)}, u32[]{:S(2)}) collective-permute-start(f32[3,8,18]{2,1,0:T(8,128)S(1)} %bitcast.238), channel_id=1, source_target_pairs={{0,1},{1,2},{2,3},{3,4},{4,5},{5,6},{6,7},{8,9},{9,10},{10,11},{11... | collective-permute-start | bytes 5192 | tf_op jit(solution)/shard_map/ppermute | solution.py:148
  124.3 0.9 copy.266
  125.4 2.2 %collective-permute-done.6 = f32[3,8,18]{2,1,0:T(8,128)S(1)} collective-permute-done((f32[3,8,18]{2,1,0:T(8,128)S(1)}, f32[3,8,18]{2,1,0:T(8,128)S(1)}, u32[]{:S(2)}, u32[]{:S(2)}) %collective-permute-start.6) | collective-permute-done | bytes 1760 | tf_op jit(solution)/shard_map/ppermute | solution.py:148
  (112 shorter events, 10.9 us)
Async XLA Ops:
  0.6 5.4 %copy-start.5 = (f32[8,16,256]{2,1,0:T(8,128)S(1)}, f32[8,16,256]{2,1,0:T(8,128)}, u32[]{:S(2)}) copy-start(f32[8,16,256]{2,1,0:T(8,128)} %param.15) | copy-start | bytes 393220
  0.6 5.4 %copy-start.4 = (f32[8,16,256]{2,1,0:T(8,128)S(1)}, f32[8,16,256]{2,1,0:T(8,128)}, u32[]{:S(2)}) copy-start(f32[8,16,256]{2,1,0:T(8,128)} %param.16) | copy-start | bytes 393220
  0.7 11.2 %copy-start.11 = (s32[128,1]{0,1:T(1,128)S(1)}, s32[128,1]{0,1:T(1,128)}, u32[]{:S(2)}) copy-start(s32[128,1]{0,1:T(1,128)} %param.22) | copy-start | bytes 1540
  0.7 11.6 %copy-start.12 = (s32[128]{0:T(128)S(1)}, s32[128]{0:T(128)}, u32[]{:S(2)}) copy-start(s32[128]{0:T(128)} %param.23) | copy-start | bytes 1540
  6.0 17.8 %copy-start.6 = (f32[128,128]{1,0:T(8,128)S(1)}, f32[128,128]{1,0:T(8,128)}, u32[]{:S(2)}) copy-start(f32[128,128]{1,0:T(8,128)} %param.19) | copy-start | bytes 196612
  6.0 17.8 %copy-start.10 = (s32[128]{0:T(128)S(1)}, s32[128]{0:T(128)}, u32[]{:S(2)}) copy-start(s32[128]{0:T(128)} %param.20) | copy-start | bytes 1540
  6.0 17.9 %copy-start.2 = (f32[128,3,128]{2,0,1:T(8,128)S(1)}, f32[128,3,128]{2,0,1:T(8,128)}, u32[]{:S(2)}) copy-start(f32[128,3,128]{2,0,1:T(8,128)} %param.18) | copy-start | bytes 589828
  6.2 27.6 %collective-permute-start.1 = (f32[6,8,256]{2,1,0:T(8,128)S(1)}, f32[6,8,256]{2,1,0:T(8,128)S(1)}, u32[]{:S(2)}, u32[]{:S(2)}) collective-permute-start(f32[6,8,256]{2,1,0:T(8,128)S(1)} %get-tuple-element.46), channel_id=1, source_target_pairs={{8,0},{16,8},{24,16},{9,1},{17,9},{25,17},{10,2},{18,10},{26,18},{... | collective-permute-start | bytes 147464 | tf_op jit(solution)/shard_map/ppermute | solution.py:151
  8.8 25.0 %collective-permute-start = (f32[6,8,256]{2,1,0:T(8,128)S(1)}, f32[6,8,256]{2,1,0:T(8,128)S(1)}, u32[]{:S(2)}, u32[]{:S(2)}) collective-permute-start(f32[6,8,256]{2,1,0:T(8,128)S(1)} %get-tuple-element.45), channel_id=1, source_target_pairs={{0,8},{8,16},{16,24},{1,9},{9,17},{17,25},{2,10},{10,18},{18,26},{... | collective-permute-start | bytes 147464 | tf_op jit(solution)/shard_map/ppermute | solution.py:148
  27.3 6.4 %copy-start.8 = (f32[32,2,128]{2,1,0:T(2,128)S(1)}, f32[32,2,128]{2,1,0:T(2,128)}, u32[]{:S(2)}) copy-start(f32[32,2,128]{2,1,0:T(2,128)} %param.25) | copy-start | bytes 98308
  27.3 6.4 %copy-start.1 = (f32[3,4096]{1,0:T(4,128)S(1)}, f32[3,4096]{1,0:T(4,128)}, u32[]{:S(2)}) copy-start(f32[3,4096]{1,0:T(4,128)} %shard_map.149) | copy-start | bytes 147460
  27.3 6.4 %copy-start.7 = (f32[32,3,128]{2,0,1:T(8,128)S(1)}, f32[32,3,128]{2,0,1:T(8,128)}, u32[]{:S(2)}) copy-start(f32[32,3,128]{2,0,1:T(8,128)} %param.24) | copy-start | bytes 147460
  28.5 23.1 %all-to-all-start = ((f32[32,5,8,128]{3,2,1,0:T(8,128)}), f32[32,5,8,128]{3,2,1,0:T(8,128)S(1)}, u32[]{:S(2)}, u32[]{:S(2)}) async-start(f32[32,5,8,128]{3,2,1,0:T(8,128)} %select_select_fusion), calls=%async_computation | async-start | bytes 1310720 | tf_op jit(solution)/shard_map/all_to_all | solution.py:326
  33.9 6.5 %copy-start.3 = (f32[8,16,256]{2,1,0:T(8,128)S(1)}, f32[8,16,256]{2,1,0:T(8,128)}, u32[]{:S(2)}) copy-start(f32[8,16,256]{2,1,0:T(8,128)} %param.17) | copy-start | bytes 393220
  33.9 6.6 %copy-start.9 = (f32[32,128]{1,0:T(8,128)S(1)}, f32[32,128]{1,0:T(8,128)}, u32[]{:S(2)}) copy-start(f32[32,128]{1,0:T(8,128)} %param.26) | copy-start | bytes 49156
  34.5 6.4 %collective-permute-start.3 = (f32[6,8,18]{2,1,0:T(8,128)S(1)}, f32[6,8,18]{2,1,0:T(8,128)S(1)}, u32[]{:S(2)}, u32[]{:S(2)}) collective-permute-start(f32[6,8,18]{2,1,0:T(8,128)S(1)} %bitcast.231), channel_id=1, source_target_pairs={{1,0},{2,1},{3,2},{4,3},{5,4},{6,5},{7,6},{9,8},{10,9},{11,10},{12... | collective-permute-start | bytes 10376 | tf_op jit(solution)/shard_map/ppermute | solution.py:151
  38.0 8.5 %collective-permute-start.2 = (f32[6,8,18]{2,1,0:T(8,128)S(1)}, f32[6,8,18]{2,1,0:T(8,128)S(1)}, u32[]{:S(2)}, u32[]{:S(2)}) collective-permute-start(f32[6,8,18]{2,1,0:T(8,128)S(1)} %bitcast.233), channel_id=1, source_target_pairs={{0,1},{1,2},{2,3},{3,4},{4,5},{5,6},{6,7},{8,9},{9,10},{10,11},{11... | collective-permute-start | bytes 10376 | tf_op jit(solution)/shard_map/ppermute | solution.py:148
  82.1 17.0 %all-to-all-start.1 = ((f32[32,5,3,128]{3,2,1,0:T(4,128)}), f32[32,5,3,128]{3,2,1,0:T(4,128)S(1)}, u32[]{:S(2)}, u32[]{:S(2)}) async-start(f32[32,5,3,128]{3,2,1,0:T(4,128)} %copy.254), calls=%async_computation.1 | async-start | bytes 655360 | tf_op jit(solution)/shard_map/all_to_all | solution.py:351
  89.8 20.5 %copy-start = (f32[3,8,16,256]{3,2,1,0:T(8,128)S(1)}, f32[3,8,16,256]{3,2,1,0:T(8,128)}, u32[]{:S(2)}) copy-start(f32[3,8,16,256]{3,2,1,0:T(8,128)} %param.14) | copy-start | bytes 1179652
  111.8 5.6 %collective-permute-start.5 = (f32[3,8,256]{2,1,0:T(8,128)S(1)}, f32[3,8,256]{2,1,0:T(8,128)S(1)}, u32[]{:S(2)}, u32[]{:S(2)}) collective-permute-start(f32[3,8,256]{2,1,0:T(8,128)S(1)} %get-tuple-element.60), channel_id=1, source_target_pairs={{8,0},{16,8},{24,16},{9,1},{17,9},{25,17},{10,2},{18,10},{26,18},{... | collective-permute-start | bytes 73736 | tf_op jit(solution)/shard_map/ppermute | solution.py:151
  114.1 4.2 %collective-permute-start.4 = (f32[3,8,256]{2,1,0:T(8,128)S(1)}, f32[3,8,256]{2,1,0:T(8,128)S(1)}, u32[]{:S(2)}, u32[]{:S(2)}) collective-permute-start(f32[3,8,256]{2,1,0:T(8,128)S(1)} %get-tuple-element.59), channel_id=1, source_target_pairs={{0,8},{8,16},{16,24},{1,9},{9,17},{17,25},{2,10},{10,18},{18,26},{... | collective-permute-start | bytes 73736 | tf_op jit(solution)/shard_map/ppermute | solution.py:148
  118.7 6.4 %collective-permute-start.7 = (f32[3,8,18]{2,1,0:T(8,128)S(1)}, f32[3,8,18]{2,1,0:T(8,128)S(1)}, u32[]{:S(2)}, u32[]{:S(2)}) collective-permute-start(f32[3,8,18]{2,1,0:T(8,128)S(1)} %bitcast.236), channel_id=1, source_target_pairs={{1,0},{2,1},{3,2},{4,3},{5,4},{6,5},{7,6},{9,8},{10,9},{11,10},{12... | collective-permute-start | bytes 5192 | tf_op jit(solution)/shard_map/ppermute | solution.py:151
  122.1 5.4 %collective-permute-start.6 = (f32[3,8,18]{2,1,0:T(8,128)S(1)}, f32[3,8,18]{2,1,0:T(8,128)S(1)}, u32[]{:S(2)}, u32[]{:S(2)}) collective-permute-start(f32[3,8,18]{2,1,0:T(8,128)S(1)} %bitcast.238), channel_id=1, source_target_pairs={{0,1},{1,2},{2,3},{3,4},{4,5},{5,6},{6,7},{8,9},{9,10},{10,11},{11... | collective-permute-start | bytes 5192 | tf_op jit(solution)/shard_map/ppermute | solution.py:148

commit v20 on v18

--- a/solution.py
+++ b/solution.py
@@ -46,19 +46,24 @@
     return high, node & (LANES - 1)
 
 
-def gather_kernel(index_ref, field_ref, out_ref):
+def gather_kernel(index_ref, field_ref, out_ref, piece_ref):
+    @pl.when(pl.program_id(0) == 0)
+    def _():
+        first, second, _ = split_pieces(block_swap(field_ref[...]))
+        piece_ref[0] = first
+        piece_ref[1] = second
+
     node = index_ref[...]
     width = node.shape[1]
-    table = block_swap(field_ref[...])
-    high_count = table.shape[1]
+    high_count = piece_ref.shape[2]
     channels = out_ref.shape[0]
     high, low = node_parts(node)
     onehot = (
         lax.broadcasted_iota(jnp.int32, (high_count, width), 0) == high
     ).astype(jnp.bfloat16)
     gathered = None
-    for piece in split_pieces(table)[:2]:
-        part = jnp.dot(piece, onehot, preferred_element_type=jnp.float32)
+    for p in range(2):
+        part = jnp.dot(piece_ref[p], onehot, preferred_element_type=jnp.float32)
         gathered = part if gathered is None else gathered + part
     low_hit = lax.broadcasted_iota(jnp.int32, (LANES, width), 0) == low
     for c in range(channels):
@@ -111,6 +116,7 @@
         ],
         out_specs=pl.BlockSpec((channels, TILE), lambda i: (0, i)),
         out_shape=jax.ShapeDtypeStruct((channels, padded_count), jnp.float32),
+        scratch_shapes=[pltpu.VMEM((2, channels * LANES, field.shape[2]), jnp.bfloat16)],
     )(nodes.reshape(1, padded_count), field)[:, :count]
 
 

time: 126 us -> 126 us (level)
  no operation moved by 1% of the time
where the time goes in v20:
time: 126 us; the launch traced here: 124 us
  other arithmetic  36.5 us (29%)
  starting transfers between devices  32.8 us (26%)
  Pallas kernels  28.8 us (23%)
  local copies, waits for them, and re-layouts  12.3 us (10%)
  waiting for transfers between devices  11.8 us (9%)
  between operations  1.45 us (1%)
    reduce_sum x1, other arithmetic, contact_pairs(): reaction = jnp.sum(push_force, axis=2)  26.4 us
    pallas_call x2, Pallas kernels, node_gather(): pl.pallas_call(gather_kernel, grid=(padded_count // TILE,), in_specs=[pl....  15.6 us
    pallas_call x2, Pallas kernels, node_scatter_add(): pl.pallas_call(scatter_kernel, grid=(padded_count // TILE,), in_specs=[pl...  13.3 us
    ppermute x4, starting transfers between devices, padded_2(): lax.ppermute(lax.index_in_dim(block, 0, axis=dim, keepdims=False), axis,...  11.1 us
    ppermute x4, starting transfers between devices, padded_2(): lax.ppermute(lax.index_in_dim(block, block.shape[dim] - 1, axis=dim, keep...  10.8 us
    all_to_all x1, starting transfers between devices, on_device(): lax.all_to_all(forces.reshape(devices, slot_depth, 3, seg_width), ('gx',...  5.88 us
    all_to_all x1, waiting for transfers between devices, on_device(): lax.all_to_all(forces.reshape(devices, slot_depth, 3, seg_width), ('gx',...  5.63 us
    ppermute x4, waiting for transfers between devices, padded_2(): lax.ppermute(lax.index_in_dim(block, block.shape[dim] - 1, axis=dim, keep...  5.52 us
  transfers between devices with their start and end apart: 10, of which 5 were waited for; matrix products, arithmetic and copies ran while one was open for 9% of the time, Pallas kernels for 6%

profile of v20, /device:TPU:9, one launch (start us, length us, event | category | flops | bytes accessed | tf_op | source)
XLA Modules:
  0.0 124.0 jit_solution(12672782615176579072)
XLA Ops:
  0.6 11.6 %shard_map.149 = f32[3,16384]{1,0:T(4,128)} custom-call(s32[1,16384]{1,0:T(1,128)} %bitcast.202, f32[3,128,256]{2,1,0:T(8,128)} %bitcast.183), custom_call_target="tpu_custom_call" | custom-call | tf_op jit(solution)/shard_map/pallas_call | solution.py:110
  12.3 1.3 %copy.226 = f32[3,8,16,256]{3,1,0,2:T(8,128)S(1)} copy(f32[3,8,16,256]{3,2,1,0:T(8,128)} %param.14) | data formatting | bytes 786432 | tf_op jit(solution)/shard_map/optimization_barrier | solution.py:293
  13.8 2.6 %collective-permute-start.1 = (f32[6,8,256]{2,1,0:T(8,128)S(1)}, f32[6,8,256]{2,1,0:T(8,128)S(1)}, u32[]{:S(2)}, u32[]{:S(2)}) collective-permute-start(f32[6,8,256]{2,1,0:T(8,128)S(1)} %get-tuple-element.46), channel_id=1, source_target_pairs={{8,0},{16,8},{24,16},{9,1},{17,9},{25,17},{10,2},{18,10},{26,18},{... | collective-permute-start | bytes 147464 | tf_op jit(solution)/shard_map/ppermute | solution.py:157
  16.4 3.0 %collective-permute-start = (f32[6,8,256]{2,1,0:T(8,128)S(1)}, f32[6,8,256]{2,1,0:T(8,128)S(1)}, u32[]{:S(2)}, u32[]{:S(2)}) collective-permute-start(f32[6,8,256]{2,1,0:T(8,128)S(1)} %get-tuple-element.45), channel_id=1, source_target_pairs={{0,8},{8,16},{16,24},{1,9},{9,17},{17,25},{2,10},{10,18},{18,26},{... | collective-permute-start | bytes 147464 | tf_op jit(solution)/shard_map/ppermute | solution.py:154
  20.9 0.8 gather_fusion
  21.7 1.2 select_select_fusion
  23.0 5.1 %all-to-all-start = ((f32[32,5,8,128]{3,2,1,0:T(8,128)}), f32[32,5,8,128]{3,2,1,0:T(8,128)S(1)}, u32[]{:S(2)}, u32[]{:S(2)}) async-start(f32[32,5,8,128]{3,2,1,0:T(8,128)} %select_select_fusion), calls=%async_computation | async-start | bytes 1310720 | tf_op jit(solution)/shard_map/all_to_all | solution.py:332
  28.0 4.0 %shard_map.150 = f32[3,4096]{1,0:T(4,128)} custom-call(s32[1,4096]{1,0:T(1,128)} %bitcast.229, f32[3,128,256]{2,1,0:T(8,128)} %bitcast.184), custom_call_target="tpu_custom_call" | custom-call | tf_op jit(solution)/shard_map/pallas_call | solution.py:110
  32.1 0.9 copy_add_fusion.1
  33.8 3.1 %collective-permute-start.3 = (f32[6,8,18]{2,1,0:T(8,128)S(1)}, f32[6,8,18]{2,1,0:T(8,128)S(1)}, u32[]{:S(2)}, u32[]{:S(2)}) collective-permute-start(f32[6,8,18]{2,1,0:T(8,128)S(1)} %bitcast.231), channel_id=1, source_target_pairs={{1,0},{2,1},{3,2},{4,3},{5,4},{6,5},{7,6},{9,8},{10,9},{11,10},{12... | collective-permute-start | bytes 10376 | tf_op jit(solution)/shard_map/ppermute | solution.py:157
  37.2 2.4 %collective-permute-start.2 = (f32[6,8,18]{2,1,0:T(8,128)S(1)}, f32[6,8,18]{2,1,0:T(8,128)S(1)}, u32[]{:S(2)}, u32[]{:S(2)}) collective-permute-start(f32[6,8,18]{2,1,0:T(8,128)S(1)} %bitcast.233), channel_id=1, source_target_pairs={{0,1},{1,2},{2,3},{3,4},{4,5},{5,6},{6,7},{8,9},{9,10},{10,11},{11... | collective-permute-start | bytes 10376 | tf_op jit(solution)/shard_map/ppermute | solution.py:154
  40.6 2.4 %collective-permute-done.2 = f32[6,8,18]{2,1,0:T(8,128)S(1)} collective-permute-done((f32[6,8,18]{2,1,0:T(8,128)S(1)}, f32[6,8,18]{2,1,0:T(8,128)S(1)}, u32[]{:S(2)}, u32[]{:S(2)}) %collective-permute-start.2) | collective-permute-done | bytes 3488 | tf_op jit(solution)/shard_map/ppermute | solution.py:154
  46.0 1.3 %fusion.79 = (f32[160,1,128]{2,1,0:T(1,128)S(1)}, f32[160,1,128]{2,1,0:T(1,128)S(1)}, f32[160,1,128]{2,1,0:T(1,128)S(1)}, f32[160,1,128]{2,1,0:T(1,128)S(1)}, f3...) fusion(f32[160,8,128]{2,1,0:T(8,128)S(1)} %bitcast.185), kind=kLoop, calls=%fused_computation.185 | loop fusion | flops 20320 | bytes 1229440 | tf_op jit(solution)/shard_map/slice | solution.py:237
  47.4 0.8 gather_fusion.1
  49.0 26.4 %fusion.76 = (f32[160,128]{1,0:T(8,128)S(1)}, f32[160,128]{1,0:T(8,128)S(1)}, f32[160,128]{1,0:T(8,128)S(1)}, f32[160,128]{1,0:T(8,128)S(1)}) fusion(f32[160,128]{1,0:T(8,128)S(1)} %multiply_add_fusion, f32[160,128]{1,0:T(8,128)S(1)} %bitcast.217, f32[160,128]{1,0:T(8,128)S(1)} %bitcast.218, f32[160,128]{1,0:T(8,128)S(1)} %bitcast.219, ...), kind=kLoop, calls=%fused_computation.182 | loop fusion | flops 104775680 | bytes 1556480 | tf_op jit(solution)/shard_map/reduce_sum | solution.py:251
  75.6 0.9 copy.254
  76.5 5.9 %all-to-all-start.1 = ((f32[32,5,3,128]{3,2,1,0:T(4,128)}), f32[32,5,3,128]{3,2,1,0:T(4,128)S(1)}, u32[]{:S(2)}, u32[]{:S(2)}) async-start(f32[32,5,3,128]{3,2,1,0:T(4,128)} %copy.254), calls=%async_computation.1 | async-start | bytes 655360 | tf_op jit(solution)/shard_map/all_to_all | solution.py:357
  83.4 0.8 broadcast_in_dim.138.init_ref
  84.2 3.7 %shard_map.151.init_ref = f32[3,128,256]{2,1,0:T(8,128)} custom-call(s32[1,4096]{1,0:T(1,128)} %bitcast.230, f32[3,4096]{1,0:T(4,128)} %bitcast.204, f32[3,128,256]{2,1,0:T(8,128)} %broadcast_in_dim.138.init_ref), custom_call_target="tpu_custom_call" | custom-call | tf_op jit(solution)/shard_map/pallas_call | solution.py:128
  87.9 5.6 %all-to-all-done.1 = f32[32,5,3,128]{3,2,1,0:T(4,128)S(1)} async-done(((f32[32,5,3,128]{3,2,1,0:T(4,128)}), f32[32,5,3,128]{3,2,1,0:T(4,128)S(1)}, u32[]{:S(2)}, u32[]{:S(2)}) %all-to-all-start.1) | async-done | bytes 245792 | tf_op jit(solution)/shard_map/all_to_all | solution.py:357
  93.6 0.7 gather_fusion.2
  94.3 0.9 select_bitcast_fusion.force_ref
  95.2 9.5 %shard_map.152 = f32[3,128,256]{2,1,0:T(8,128)} custom-call(s32[1,16384]{1,0:T(1,128)} %bitcast.203, f32[3,16384]{1,0:T(4,128)} %select_bitcast_fusion.force_ref, f32[3,128,256]{2,1,0:T(8,128)} %shard_map.151.init_ref), custom_call_target="tpu_custom_call" | custom-call | tf_op jit(solution)/shard_map/pallas_call | solution.py:128
  104.7 1.5 %fusion.14 = f32[3,8,16,256]{3,1,2,0:T(8,128)S(1)} fusion(f32[1,8,16,256]{3,1,2,0:T(8,128)S(1)} %fusion.63, f32[1,8,16,256]{3,1,2,0:T(8,128)S(1)} %fusion.65, f32[1,8,16,256]{3,1,2,0:T(8,128)S(1)} %fusion.67, f32[3,8,16,256]{3,2,1,0:T(8,128)S(1)} %copy-done, f32[3,8,16,256]{3,2,1,0:T(8,128)} %bitcast.189, f32[8,16,256]{2,0,1:T(8,128)S(1)} %copy.258), kind=kLoop, calls=%fused_computation.41 | loop fusion | flops 589824 | bytes 1703936 | tf_op jit(solution)/shard_map/add | solution.py:369
  106.2 2.3 %collective-permute-start.5 = (f32[3,8,256]{2,1,0:T(8,128)S(1)}, f32[3,8,256]{2,1,0:T(8,128)S(1)}, u32[]{:S(2)}, u32[]{:S(2)}) collective-permute-start(f32[3,8,256]{2,1,0:T(8,128)S(1)} %get-tuple-element.60), channel_id=1, source_target_pairs={{8,0},{16,8},{24,16},{9,1},{17,9},{25,17},{10,2},{18,10},{26,18},{... | collective-permute-start | bytes 73736 | tf_op jit(solution)/shard_map/ppermute | solution.py:157
  108.5 3.3 %collective-permute-start.4 = (f32[3,8,256]{2,1,0:T(8,128)S(1)}, f32[3,8,256]{2,1,0:T(8,128)S(1)}, u32[]{:S(2)}, u32[]{:S(2)}) collective-permute-start(f32[3,8,256]{2,1,0:T(8,128)S(1)} %get-tuple-element.59), channel_id=1, source_target_pairs={{0,8},{8,16},{16,24},{1,9},{9,17},{17,25},{2,10},{10,18},{18,26},{... | collective-permute-start | bytes 73736 | tf_op jit(solution)/shard_map/ppermute | solution.py:154
  111.8 0.9 collective-permute-done.4
  113.2 3.1 %collective-permute-start.7 = (f32[3,8,18]{2,1,0:T(8,128)S(1)}, f32[3,8,18]{2,1,0:T(8,128)S(1)}, u32[]{:S(2)}, u32[]{:S(2)}) collective-permute-start(f32[3,8,18]{2,1,0:T(8,128)S(1)} %bitcast.236), channel_id=1, source_target_pairs={{1,0},{2,1},{3,2},{4,3},{5,4},{6,5},{7,6},{9,8},{10,9},{11,10},{12... | collective-permute-start | bytes 5192 | tf_op jit(solution)/shard_map/ppermute | solution.py:157
  116.5 2.1 %collective-permute-start.6 = (f32[3,8,18]{2,1,0:T(8,128)S(1)}, f32[3,8,18]{2,1,0:T(8,128)S(1)}, u32[]{:S(2)}, u32[]{:S(2)}) collective-permute-start(f32[3,8,18]{2,1,0:T(8,128)S(1)} %bitcast.238), channel_id=1, source_target_pairs={{0,1},{1,2},{2,3},{3,4},{4,5},{5,6},{6,7},{8,9},{9,10},{10,11},{11... | collective-permute-start | bytes 5192 | tf_op jit(solution)/shard_map/ppermute | solution.py:154
  118.7 0.9 copy.266
  119.8 2.2 %collective-permute-done.6 = f32[3,8,18]{2,1,0:T(8,128)S(1)} collective-permute-done((f32[3,8,18]{2,1,0:T(8,128)S(1)}, f32[3,8,18]{2,1,0:T(8,128)S(1)}, u32[]{:S(2)}, u32[]{:S(2)}) %collective-permute-start.6) | collective-permute-done | bytes 1760 | tf_op jit(solution)/shard_map/ppermute | solution.py:154
  123.3 0.7 copy.267
  (114 shorter events, 10.5 us)
Async XLA Ops:
  0.6 12.9 %copy-start.6 = (f32[8,16,256]{2,1,0:T(8,128)S(1)}, f32[8,16,256]{2,1,0:T(8,128)}, u32[]{:S(2)}) copy-start(f32[8,16,256]{2,1,0:T(8,128)} %param.15) | copy-start | bytes 393220
  0.6 12.9 %copy-start.5 = (f32[8,16,256]{2,1,0:T(8,128)S(1)}, f32[8,16,256]{2,1,0:T(8,128)}, u32[]{:S(2)}) copy-start(f32[8,16,256]{2,1,0:T(8,128)} %param.16) | copy-start | bytes 393220
  12.2 7.2 %copy-start.12 = (s32[128,1]{0,1:T(1,128)S(1)}, s32[128,1]{0,1:T(1,128)}, u32[]{:S(2)}) copy-start(s32[128,1]{0,1:T(1,128)} %param.22) | copy-start | bytes 1540
  12.2 7.6 %copy-start.13 = (s32[128]{0:T(128)S(1)}, s32[128]{0:T(128)}, u32[]{:S(2)}) copy-start(s32[128]{0:T(128)} %param.23) | copy-start | bytes 1540
  12.2 7.9 %copy-start.7 = (f32[128,128]{1,0:T(8,128)S(1)}, f32[128,128]{1,0:T(8,128)}, u32[]{:S(2)}) copy-start(f32[128,128]{1,0:T(8,128)} %param.19) | copy-start | bytes 196612
  12.2 7.9 %copy-start.11 = (s32[128]{0:T(128)S(1)}, s32[128]{0:T(128)}, u32[]{:S(2)}) copy-start(s32[128]{0:T(128)} %param.20) | copy-start | bytes 1540
  12.2 8.0 %copy-start.1 = (f32[3,16384]{1,0:T(4,128)S(1)}, f32[3,16384]{1,0:T(4,128)}, u32[]{:S(2)}) copy-start(f32[3,16384]{1,0:T(4,128)} %shard_map.149) | copy-start | bytes 589828
  12.2 8.0 %copy-start.3 = (f32[128,3,128]{2,0,1:T(8,128)S(1)}, f32[128,3,128]{2,0,1:T(8,128)}, u32[]{:S(2)}) copy-start(f32[128,3,128]{2,0,1:T(8,128)} %param.18) | copy-start | bytes 589828
  13.8 19.3 %collective-permute-start.1 = (f32[6,8,256]{2,1,0:T(8,128)S(1)}, f32[6,8,256]{2,1,0:T(8,128)S(1)}, u32[]{:S(2)}, u32[]{:S(2)}) collective-permute-start(f32[6,8,256]{2,1,0:T(8,128)S(1)} %get-tuple-element.46), channel_id=1, source_target_pairs={{8,0},{16,8},{24,16},{9,1},{17,9},{25,17},{10,2},{18,10},{26,18},{... | collective-permute-start | bytes 147464 | tf_op jit(solution)/shard_map/ppermute | solution.py:157
  16.4 16.7 %collective-permute-start = (f32[6,8,256]{2,1,0:T(8,128)S(1)}, f32[6,8,256]{2,1,0:T(8,128)S(1)}, u32[]{:S(2)}, u32[]{:S(2)}) collective-permute-start(f32[6,8,256]{2,1,0:T(8,128)S(1)} %get-tuple-element.45), channel_id=1, source_target_pairs={{0,8},{8,16},{16,24},{1,9},{9,17},{17,25},{2,10},{10,18},{18,26},{... | collective-permute-start | bytes 147464 | tf_op jit(solution)/shard_map/ppermute | solution.py:154
  21.7 10.4 %copy-start.9 = (f32[32,2,128]{2,1,0:T(2,128)S(1)}, f32[32,2,128]{2,1,0:T(2,128)}, u32[]{:S(2)}) copy-start(f32[32,2,128]{2,1,0:T(2,128)} %param.25) | copy-start | bytes 98308
  21.7 10.4 %copy-start.8 = (f32[32,3,128]{2,0,1:T(8,128)S(1)}, f32[32,3,128]{2,0,1:T(8,128)}, u32[]{:S(2)}) copy-start(f32[32,3,128]{2,0,1:T(8,128)} %param.24) | copy-start | bytes 147460
  23.0 23.1 %all-to-all-start = ((f32[32,5,8,128]{3,2,1,0:T(8,128)}), f32[32,5,8,128]{3,2,1,0:T(8,128)S(1)}, u32[]{:S(2)}, u32[]{:S(2)}) async-start(f32[32,5,8,128]{3,2,1,0:T(8,128)} %select_select_fusion), calls=%async_computation | async-start | bytes 1310720 | tf_op jit(solution)/shard_map/all_to_all | solution.py:332
  33.2 6.5 %copy-start.4 = (f32[8,16,256]{2,1,0:T(8,128)S(1)}, f32[8,16,256]{2,1,0:T(8,128)}, u32[]{:S(2)}) copy-start(f32[8,16,256]{2,1,0:T(8,128)} %param.17) | copy-start | bytes 393220
  33.2 6.6 %copy-start.2 = (f32[3,4096]{1,0:T(4,128)S(1)}, f32[3,4096]{1,0:T(4,128)}, u32[]{:S(2)}) copy-start(f32[3,4096]{1,0:T(4,128)} %shard_map.150) | copy-start | bytes 147460
  33.2 6.6 %copy-start.10 = (f32[32,128]{1,0:T(8,128)S(1)}, f32[32,128]{1,0:T(8,128)}, u32[]{:S(2)}) copy-start(f32[32,128]{1,0:T(8,128)} %param.26) | copy-start | bytes 49156
  33.8 6.4 %collective-permute-start.3 = (f32[6,8,18]{2,1,0:T(8,128)S(1)}, f32[6,8,18]{2,1,0:T(8,128)S(1)}, u32[]{:S(2)}, u32[]{:S(2)}) collective-permute-start(f32[6,8,18]{2,1,0:T(8,128)S(1)} %bitcast.231), channel_id=1, source_target_pairs={{1,0},{2,1},{3,2},{4,3},{5,4},{6,5},{7,6},{9,8},{10,9},{11,10},{12... | collective-permute-start | bytes 10376 | tf_op jit(solution)/shard_map/ppermute | solution.py:157
  37.2 5.8 %collective-permute-start.2 = (f32[6,8,18]{2,1,0:T(8,128)S(1)}, f32[6,8,18]{2,1,0:T(8,128)S(1)}, u32[]{:S(2)}, u32[]{:S(2)}) collective-permute-start(f32[6,8,18]{2,1,0:T(8,128)S(1)} %bitcast.233), channel_id=1, source_target_pairs={{0,1},{1,2},{2,3},{3,4},{4,5},{5,6},{6,7},{8,9},{9,10},{10,11},{11... | collective-permute-start | bytes 10376 | tf_op jit(solution)/shard_map/ppermute | solution.py:154
  76.5 17.0 %all-to-all-start.1 = ((f32[32,5,3,128]{3,2,1,0:T(4,128)}), f32[32,5,3,128]{3,2,1,0:T(4,128)S(1)}, u32[]{:S(2)}, u32[]{:S(2)}) async-start(f32[32,5,3,128]{3,2,1,0:T(4,128)} %copy.254), calls=%async_computation.1 | async-start | bytes 655360 | tf_op jit(solution)/shard_map/all_to_all | solution.py:357
  84.2 20.5 %copy-start = (f32[3,8,16,256]{3,2,1,0:T(8,128)S(1)}, f32[3,8,16,256]{3,2,1,0:T(8,128)}, u32[]{:S(2)}) copy-start(f32[3,8,16,256]{3,2,1,0:T(8,128)} %param.14) | copy-start | bytes 1179652
  106.2 5.6 %collective-permute-start.5 = (f32[3,8,256]{2,1,0:T(8,128)S(1)}, f32[3,8,256]{2,1,0:T(8,128)S(1)}, u32[]{:S(2)}, u32[]{:S(2)}) collective-permute-start(f32[3,8,256]{2,1,0:T(8,128)S(1)} %get-tuple-element.60), channel_id=1, source_target_pairs={{8,0},{16,8},{24,16},{9,1},{17,9},{25,17},{10,2},{18,10},{26,18},{... | collective-permute-start | bytes 73736 | tf_op jit(solution)/shard_map/ppermute | solution.py:157
  108.5 4.2 %collective-permute-start.4 = (f32[3,8,256]{2,1,0:T(8,128)S(1)}, f32[3,8,256]{2,1,0:T(8,128)S(1)}, u32[]{:S(2)}, u32[]{:S(2)}) collective-permute-start(f32[3,8,256]{2,1,0:T(8,128)S(1)} %get-tuple-element.59), channel_id=1, source_target_pairs={{0,8},{8,16},{16,24},{1,9},{9,17},{17,25},{2,10},{10,18},{18,26},{... | collective-permute-start | bytes 73736 | tf_op jit(solution)/shard_map/ppermute | solution.py:154
  113.2 6.4 %collective-permute-start.7 = (f32[3,8,18]{2,1,0:T(8,128)S(1)}, f32[3,8,18]{2,1,0:T(8,128)S(1)}, u32[]{:S(2)}, u32[]{:S(2)}) collective-permute-start(f32[3,8,18]{2,1,0:T(8,128)S(1)} %bitcast.236), channel_id=1, source_target_pairs={{1,0},{2,1},{3,2},{4,3},{5,4},{6,5},{7,6},{9,8},{10,9},{11,10},{12... | collective-permute-start | bytes 5192 | tf_op jit(solution)/shard_map/ppermute | solution.py:157
  116.5 5.4 %collective-permute-start.6 = (f32[3,8,18]{2,1,0:T(8,128)S(1)}, f32[3,8,18]{2,1,0:T(8,128)S(1)}, u32[]{:S(2)}, u32[]{:S(2)}) collective-permute-start(f32[3,8,18]{2,1,0:T(8,128)S(1)} %bitcast.238), channel_id=1, source_target_pairs={{0,1},{1,2},{2,3},{3,4},{4,5},{5,6},{6,7},{8,9},{9,10},{10,11},{11... | collective-permute-start | bytes 5192 | tf_op jit(solution)/shard_map/ppermute | solution.py:154

commit v21 on v18

--- a/solution.py
+++ b/solution.py
@@ -99,32 +99,34 @@
 
 def node_gather(field, nodes):
     count = nodes.shape[0]
-    padded_count = -(-count // TILE) * TILE
+    tile = 2 * TILE if count >= 2 * TILE else TILE
+    padded_count = -(-count // tile) * tile
     nodes = jnp.pad(nodes, (0, padded_count - count))
     channels = field.shape[0]
     return pl.pallas_call(
         gather_kernel,
-        grid=(padded_count // TILE,),
+        grid=(padded_count // tile,),
         in_specs=[
-            pl.BlockSpec((1, TILE), lambda i: (0, i)),
+            pl.BlockSpec((1, tile), lambda i: (0, i)),
             pl.BlockSpec(field.shape, lambda i: (0, 0, 0)),
         ],
-        out_specs=pl.BlockSpec((channels, TILE), lambda i: (0, i)),
+        out_specs=pl.BlockSpec((channels, tile), lambda i: (0, i)),
         out_shape=jax.ShapeDtypeStruct((channels, padded_count), jnp.float32),
     )(nodes.reshape(1, padded_count), field)[:, :count]
 
 
 def node_scatter_add(forces, nodes, start):
     channels, count = forces.shape
-    padded_count = -(-count // TILE) * TILE
+    tile = 2 * TILE if count >= 2 * TILE else TILE
+    padded_count = -(-count // tile) * tile
     nodes = jnp.pad(nodes, (0, padded_count - count))
     forces = jnp.pad(forces, ((0, 0), (0, padded_count - count)))
     return pl.pallas_call(
         scatter_kernel,
-        grid=(padded_count // TILE,),
+        grid=(padded_count // tile,),
         in_specs=[
-            pl.BlockSpec((1, TILE), lambda i: (0, i)),
-            pl.BlockSpec((channels, TILE), lambda i: (0, i)),
+            pl.BlockSpec((1, tile), lambda i: (0, i)),
+            pl.BlockSpec((channels, tile), lambda i: (0, i)),
             pl.BlockSpec(start.shape, lambda i: (0, 0, 0)),
         ],
         out_specs=pl.BlockSpec(start.shape, lambda i: (0, 0, 0)),

time: 126 us -> 126 us (level)
  no operation moved by 1% of the time
where the time goes in v21:
time: 126 us; the launch traced here: 123 us
  other arithmetic  36.5 us (29%)
  starting transfers between devices  32.8 us (26%)
  Pallas kernels  28 us (22%)
  local copies, waits for them, and re-layouts  12.3 us (10%)
  waiting for transfers between devices  11.9 us (9%)
  between operations  1.45 us (1%)
    reduce_sum x1, other arithmetic, contact_pairs(): reaction = jnp.sum(push_force, axis=2)  26.4 us
    pallas_call x2, Pallas kernels, node_gather(): pl.pallas_call(gather_kernel, grid=(padded_count // tile,), in_specs=[pl....  15.2 us
    pallas_call x2, Pallas kernels, node_scatter_add(): pl.pallas_call(scatter_kernel, grid=(padded_count // tile,), in_specs=[pl...  12.8 us
    ppermute x4, starting transfers between devices, padded_2(): lax.ppermute(lax.index_in_dim(block, 0, axis=dim, keepdims=False), axis,...  11.1 us
    ppermute x4, starting transfers between devices, padded_2(): lax.ppermute(lax.index_in_dim(block, block.shape[dim] - 1, axis=dim, keep...  10.7 us
    all_to_all x1, starting transfers between devices, on_device(): lax.all_to_all(forces.reshape(devices, slot_depth, 3, seg_width), ('gx',...  5.88 us
    all_to_all x1, waiting for transfers between devices, on_device(): lax.all_to_all(forces.reshape(devices, slot_depth, 3, seg_width), ('gx',...  5.63 us
    ppermute x4, waiting for transfers between devices, padded_2(): lax.ppermute(lax.index_in_dim(block, block.shape[dim] - 1, axis=dim, keep...  5.57 us
  transfers between devices with their start and end apart: 10, of which 5 were waited for; matrix products, arithmetic and copies ran while one was open for 9% of the time, Pallas kernels for 6%

profile of v21, /device:TPU:9, one launch (start us, length us, event | category | flops | bytes accessed | tf_op | source)
XLA Modules:
  0.0 123.2 jit_solution(157620944663997589)
XLA Ops:
  0.6 11.2 %shard_map.149 = f32[3,16384]{1,0:T(4,128)} custom-call(s32[1,16384]{1,0:T(1,128)} %bitcast.202, f32[3,128,256]{2,1,0:T(8,128)} %bitcast.183), custom_call_target="tpu_custom_call" | custom-call | tf_op jit(solution)/shard_map/pallas_call | solution.py:106
  11.8 1.3 %copy.226 = f32[3,8,16,256]{3,1,0,2:T(8,128)S(1)} copy(f32[3,8,16,256]{3,2,1,0:T(8,128)} %param.14) | data formatting | bytes 786432 | tf_op jit(solution)/shard_map/optimization_barrier | solution.py:289
  13.4 2.6 %collective-permute-start.1 = (f32[6,8,256]{2,1,0:T(8,128)S(1)}, f32[6,8,256]{2,1,0:T(8,128)S(1)}, u32[]{:S(2)}, u32[]{:S(2)}) collective-permute-start(f32[6,8,256]{2,1,0:T(8,128)S(1)} %get-tuple-element.46), channel_id=1, source_target_pairs={{8,0},{16,8},{24,16},{9,1},{17,9},{25,17},{10,2},{18,10},{26,18},{... | collective-permute-start | bytes 147464 | tf_op jit(solution)/shard_map/ppermute | solution.py:153
  16.0 3.0 %collective-permute-start = (f32[6,8,256]{2,1,0:T(8,128)S(1)}, f32[6,8,256]{2,1,0:T(8,128)S(1)}, u32[]{:S(2)}, u32[]{:S(2)}) collective-permute-start(f32[6,8,256]{2,1,0:T(8,128)S(1)} %get-tuple-element.45), channel_id=1, source_target_pairs={{0,8},{8,16},{16,24},{1,9},{9,17},{17,25},{2,10},{10,18},{18,26},{... | collective-permute-start | bytes 147464 | tf_op jit(solution)/shard_map/ppermute | solution.py:150
  20.5 0.8 gather_fusion
  21.3 1.2 %select_select_fusion = f32[32,5,8,128]{3,2,1,0:T(8,128)} fusion(f32[32,5,8,128]{3,2,1,0:T(8,128)S(1)} %bitcast.186, pred[32,5]{1,0:T(8,128)(4,1)S(1)} %compare_and_fusion, pred[32,5]{1,0:T(8,128)(4,1)S(1)} %broadcast_in_dim.124), kind=kLoop, calls=%fused_computation.31 | loop fusion | flops 327680 | bytes 1311040 | tf_op jit(solution)/shard_map/jit(_where)/select_n | solution.py:327
  22.5 5.1 %all-to-all-start = ((f32[32,5,8,128]{3,2,1,0:T(8,128)}), f32[32,5,8,128]{3,2,1,0:T(8,128)S(1)}, u32[]{:S(2)}, u32[]{:S(2)}) async-start(f32[32,5,8,128]{3,2,1,0:T(8,128)} %select_select_fusion), calls=%async_computation | async-start | bytes 1310720 | tf_op jit(solution)/shard_map/all_to_all | solution.py:328
  27.6 4.0 %shard_map.150 = f32[3,4096]{1,0:T(4,128)} custom-call(s32[1,4096]{1,0:T(1,128)} %bitcast.229, f32[3,128,256]{2,1,0:T(8,128)} %bitcast.184), custom_call_target="tpu_custom_call" | custom-call | tf_op jit(solution)/shard_map/pallas_call | solution.py:106
  31.7 0.9 copy_add_fusion.1
  33.4 3.1 %collective-permute-start.3 = (f32[6,8,18]{2,1,0:T(8,128)S(1)}, f32[6,8,18]{2,1,0:T(8,128)S(1)}, u32[]{:S(2)}, u32[]{:S(2)}) collective-permute-start(f32[6,8,18]{2,1,0:T(8,128)S(1)} %bitcast.231), channel_id=1, source_target_pairs={{1,0},{2,1},{3,2},{4,3},{5,4},{6,5},{7,6},{9,8},{10,9},{11,10},{12... | collective-permute-start | bytes 10376 | tf_op jit(solution)/shard_map/ppermute | solution.py:153
  36.8 2.4 %collective-permute-start.2 = (f32[6,8,18]{2,1,0:T(8,128)S(1)}, f32[6,8,18]{2,1,0:T(8,128)S(1)}, u32[]{:S(2)}, u32[]{:S(2)}) collective-permute-start(f32[6,8,18]{2,1,0:T(8,128)S(1)} %bitcast.233), channel_id=1, source_target_pairs={{0,1},{1,2},{2,3},{3,4},{4,5},{5,6},{6,7},{8,9},{9,10},{10,11},{11... | collective-permute-start | bytes 10376 | tf_op jit(solution)/shard_map/ppermute | solution.py:150
  40.1 2.4 %collective-permute-done.2 = f32[6,8,18]{2,1,0:T(8,128)S(1)} collective-permute-done((f32[6,8,18]{2,1,0:T(8,128)S(1)}, f32[6,8,18]{2,1,0:T(8,128)S(1)}, u32[]{:S(2)}, u32[]{:S(2)}) %collective-permute-start.2) | collective-permute-done | bytes 3488 | tf_op jit(solution)/shard_map/ppermute | solution.py:150
  45.6 1.3 %fusion.79 = (f32[160,1,128]{2,1,0:T(1,128)S(1)}, f32[160,1,128]{2,1,0:T(1,128)S(1)}, f32[160,1,128]{2,1,0:T(1,128)S(1)}, f32[160,1,128]{2,1,0:T(1,128)S(1)}, f3...) fusion(f32[160,8,128]{2,1,0:T(8,128)S(1)} %bitcast.185), kind=kLoop, calls=%fused_computation.185 | loop fusion | flops 20320 | bytes 1229440 | tf_op jit(solution)/shard_map/slice | solution.py:233
  47.0 0.8 gather_fusion.1
  48.6 26.4 %fusion.76 = (f32[160,128]{1,0:T(8,128)S(1)}, f32[160,128]{1,0:T(8,128)S(1)}, f32[160,128]{1,0:T(8,128)S(1)}, f32[160,128]{1,0:T(8,128)S(1)}) fusion(f32[160,128]{1,0:T(8,128)S(1)} %multiply_add_fusion, f32[160,128]{1,0:T(8,128)S(1)} %bitcast.217, f32[160,128]{1,0:T(8,128)S(1)} %bitcast.218, f32[160,128]{1,0:T(8,128)S(1)} %bitcast.219, ...), kind=kLoop, calls=%fused_computation.182 | loop fusion | flops 104775680 | bytes 1556480 | tf_op jit(solution)/shard_map/reduce_sum | solution.py:247
  75.2 0.9 copy.254
  76.1 5.9 %all-to-all-start.1 = ((f32[32,5,3,128]{3,2,1,0:T(4,128)}), f32[32,5,3,128]{3,2,1,0:T(4,128)S(1)}, u32[]{:S(2)}, u32[]{:S(2)}) async-start(f32[32,5,3,128]{3,2,1,0:T(4,128)} %copy.254), calls=%async_computation.1 | async-start | bytes 655360 | tf_op jit(solution)/shard_map/all_to_all | solution.py:353
  83.0 0.8 broadcast_in_dim.138.init_ref
  83.8 3.7 %shard_map.151.init_ref = f32[3,128,256]{2,1,0:T(8,128)} custom-call(s32[1,4096]{1,0:T(1,128)} %bitcast.230, f32[3,4096]{1,0:T(4,128)} %bitcast.204, f32[3,128,256]{2,1,0:T(8,128)} %broadcast_in_dim.138.init_ref), custom_call_target="tpu_custom_call" | custom-call | tf_op jit(solution)/shard_map/pallas_call | solution.py:124
  87.5 5.6 %all-to-all-done.1 = f32[32,5,3,128]{3,2,1,0:T(4,128)S(1)} async-done(((f32[32,5,3,128]{3,2,1,0:T(4,128)}), f32[32,5,3,128]{3,2,1,0:T(4,128)S(1)}, u32[]{:S(2)}, u32[]{:S(2)}) %all-to-all-start.1) | async-done | bytes 245792 | tf_op jit(solution)/shard_map/all_to_all | solution.py:353
  93.2 0.7 gather_fusion.2
  93.9 0.9 select_bitcast_fusion.force_ref
  94.8 9.0 %shard_map.152 = f32[3,128,256]{2,1,0:T(8,128)} custom-call(s32[1,16384]{1,0:T(1,128)} %bitcast.203, f32[3,16384]{1,0:T(4,128)} %select_bitcast_fusion.force_ref, f32[3,128,256]{2,1,0:T(8,128)} %shard_map.151.init_ref), custom_call_target="tpu_custom_call" | custom-call | tf_op jit(solution)/shard_map/pallas_call | solution.py:124
  103.9 1.5 %fusion.14 = f32[3,8,16,256]{3,1,2,0:T(8,128)S(1)} fusion(f32[1,8,16,256]{3,1,2,0:T(8,128)S(1)} %fusion.63, f32[1,8,16,256]{3,1,2,0:T(8,128)S(1)} %fusion.65, f32[1,8,16,256]{3,1,2,0:T(8,128)S(1)} %fusion.67, f32[3,8,16,256]{3,2,1,0:T(8,128)S(1)} %copy-done, f32[3,8,16,256]{3,2,1,0:T(8,128)} %bitcast.189, f32[8,16,256]{2,0,1:T(8,128)S(1)} %copy.258), kind=kLoop, calls=%fused_computation.41 | loop fusion | flops 589824 | bytes 1703936 | tf_op jit(solution)/shard_map/add | solution.py:365
  105.4 2.3 %collective-permute-start.5 = (f32[3,8,256]{2,1,0:T(8,128)S(1)}, f32[3,8,256]{2,1,0:T(8,128)S(1)}, u32[]{:S(2)}, u32[]{:S(2)}) collective-permute-start(f32[3,8,256]{2,1,0:T(8,128)S(1)} %get-tuple-element.60), channel_id=1, source_target_pairs={{8,0},{16,8},{24,16},{9,1},{17,9},{25,17},{10,2},{18,10},{26,18},{... | collective-permute-start | bytes 73736 | tf_op jit(solution)/shard_map/ppermute | solution.py:153
  107.7 3.3 %collective-permute-start.4 = (f32[3,8,256]{2,1,0:T(8,128)S(1)}, f32[3,8,256]{2,1,0:T(8,128)S(1)}, u32[]{:S(2)}, u32[]{:S(2)}) collective-permute-start(f32[3,8,256]{2,1,0:T(8,128)S(1)} %get-tuple-element.59), channel_id=1, source_target_pairs={{0,8},{8,16},{16,24},{1,9},{9,17},{17,25},{2,10},{10,18},{18,26},{... | collective-permute-start | bytes 73736 | tf_op jit(solution)/shard_map/ppermute | solution.py:150
  111.0 0.9 collective-permute-done.4
  112.3 3.2 %collective-permute-start.7 = (f32[3,8,18]{2,1,0:T(8,128)S(1)}, f32[3,8,18]{2,1,0:T(8,128)S(1)}, u32[]{:S(2)}, u32[]{:S(2)}) collective-permute-start(f32[3,8,18]{2,1,0:T(8,128)S(1)} %bitcast.236), channel_id=1, source_target_pairs={{1,0},{2,1},{3,2},{4,3},{5,4},{6,5},{7,6},{9,8},{10,9},{11,10},{12... | collective-permute-start | bytes 5192 | tf_op jit(solution)/shard_map/ppermute | solution.py:153
  115.7 2.1 %collective-permute-start.6 = (f32[3,8,18]{2,1,0:T(8,128)S(1)}, f32[3,8,18]{2,1,0:T(8,128)S(1)}, u32[]{:S(2)}, u32[]{:S(2)}) collective-permute-start(f32[3,8,18]{2,1,0:T(8,128)S(1)} %bitcast.238), channel_id=1, source_target_pairs={{0,1},{1,2},{2,3},{3,4},{4,5},{5,6},{6,7},{8,9},{9,10},{10,11},{11... | collective-permute-start | bytes 5192 | tf_op jit(solution)/shard_map/ppermute | solution.py:150
  117.8 0.9 copy.266
  119.0 2.2 %collective-permute-done.6 = f32[3,8,18]{2,1,0:T(8,128)S(1)} collective-permute-done((f32[3,8,18]{2,1,0:T(8,128)S(1)}, f32[3,8,18]{2,1,0:T(8,128)S(1)}, u32[]{:S(2)}, u32[]{:S(2)}) %collective-permute-start.6) | collective-permute-done | bytes 1760 | tf_op jit(solution)/shard_map/ppermute | solution.py:150
  122.5 0.7 copy.267
  (114 shorter events, 10.5 us)
Async XLA Ops:
  0.6 12.5 %copy-start.6 = (f32[8,16,256]{2,1,0:T(8,128)S(1)}, f32[8,16,256]{2,1,0:T(8,128)}, u32[]{:S(2)}) copy-start(f32[8,16,256]{2,1,0:T(8,128)} %param.15) | copy-start | bytes 393220
  0.6 12.5 %copy-start.5 = (f32[8,16,256]{2,1,0:T(8,128)S(1)}, f32[8,16,256]{2,1,0:T(8,128)}, u32[]{:S(2)}) copy-start(f32[8,16,256]{2,1,0:T(8,128)} %param.16) | copy-start | bytes 393220
  11.8 7.2 %copy-start.12 = (s32[128,1]{0,1:T(1,128)S(1)}, s32[128,1]{0,1:T(1,128)}, u32[]{:S(2)}) copy-start(s32[128,1]{0,1:T(1,128)} %param.22) | copy-start | bytes 1540
  11.8 7.6 %copy-start.13 = (s32[128]{0:T(128)S(1)}, s32[128]{0:T(128)}, u32[]{:S(2)}) copy-start(s32[128]{0:T(128)} %param.23) | copy-start | bytes 1540
  11.8 7.9 %copy-start.7 = (f32[128,128]{1,0:T(8,128)S(1)}, f32[128,128]{1,0:T(8,128)}, u32[]{:S(2)}) copy-start(f32[128,128]{1,0:T(8,128)} %param.19) | copy-start | bytes 196612
  11.8 7.9 %copy-start.11 = (s32[128]{0:T(128)S(1)}, s32[128]{0:T(128)}, u32[]{:S(2)}) copy-start(s32[128]{0:T(128)} %param.20) | copy-start | bytes 1540
  11.8 8.0 %copy-start.1 = (f32[3,16384]{1,0:T(4,128)S(1)}, f32[3,16384]{1,0:T(4,128)}, u32[]{:S(2)}) copy-start(f32[3,16384]{1,0:T(4,128)} %shard_map.149) | copy-start | bytes 589828
  11.8 8.0 %copy-start.3 = (f32[128,3,128]{2,0,1:T(8,128)S(1)}, f32[128,3,128]{2,0,1:T(8,128)}, u32[]{:S(2)}) copy-start(f32[128,3,128]{2,0,1:T(8,128)} %param.18) | copy-start | bytes 589828
  13.4 19.3 %collective-permute-start.1 = (f32[6,8,256]{2,1,0:T(8,128)S(1)}, f32[6,8,256]{2,1,0:T(8,128)S(1)}, u32[]{:S(2)}, u32[]{:S(2)}) collective-permute-start(f32[6,8,256]{2,1,0:T(8,128)S(1)} %get-tuple-element.46), channel_id=1, source_target_pairs={{8,0},{16,8},{24,16},{9,1},{17,9},{25,17},{10,2},{18,10},{26,18},{... | collective-permute-start | bytes 147464 | tf_op jit(solution)/shard_map/ppermute | solution.py:153
  16.0 16.7 %collective-permute-start = (f32[6,8,256]{2,1,0:T(8,128)S(1)}, f32[6,8,256]{2,1,0:T(8,128)S(1)}, u32[]{:S(2)}, u32[]{:S(2)}) collective-permute-start(f32[6,8,256]{2,1,0:T(8,128)S(1)} %get-tuple-element.45), channel_id=1, source_target_pairs={{0,8},{8,16},{16,24},{1,9},{9,17},{17,25},{2,10},{10,18},{18,26},{... | collective-permute-start | bytes 147464 | tf_op jit(solution)/shard_map/ppermute | solution.py:150
  21.3 10.4 %copy-start.9 = (f32[32,2,128]{2,1,0:T(2,128)S(1)}, f32[32,2,128]{2,1,0:T(2,128)}, u32[]{:S(2)}) copy-start(f32[32,2,128]{2,1,0:T(2,128)} %param.25) | copy-start | bytes 98308
  21.3 10.4 %copy-start.8 = (f32[32,3,128]{2,0,1:T(8,128)S(1)}, f32[32,3,128]{2,0,1:T(8,128)}, u32[]{:S(2)}) copy-start(f32[32,3,128]{2,0,1:T(8,128)} %param.24) | copy-start | bytes 147460
  22.5 23.1 %all-to-all-start = ((f32[32,5,8,128]{3,2,1,0:T(8,128)}), f32[32,5,8,128]{3,2,1,0:T(8,128)S(1)}, u32[]{:S(2)}, u32[]{:S(2)}) async-start(f32[32,5,8,128]{3,2,1,0:T(8,128)} %select_select_fusion), calls=%async_computation | async-start | bytes 1310720 | tf_op jit(solution)/shard_map/all_to_all | solution.py:328
  32.8 6.5 %copy-start.4 = (f32[8,16,256]{2,1,0:T(8,128)S(1)}, f32[8,16,256]{2,1,0:T(8,128)}, u32[]{:S(2)}) copy-start(f32[8,16,256]{2,1,0:T(8,128)} %param.17) | copy-start | bytes 393220
  32.8 6.6 %copy-start.2 = (f32[3,4096]{1,0:T(4,128)S(1)}, f32[3,4096]{1,0:T(4,128)}, u32[]{:S(2)}) copy-start(f32[3,4096]{1,0:T(4,128)} %shard_map.150) | copy-start | bytes 147460
  32.8 6.6 %copy-start.10 = (f32[32,128]{1,0:T(8,128)S(1)}, f32[32,128]{1,0:T(8,128)}, u32[]{:S(2)}) copy-start(f32[32,128]{1,0:T(8,128)} %param.26) | copy-start | bytes 49156
  33.4 6.4 %collective-permute-start.3 = (f32[6,8,18]{2,1,0:T(8,128)S(1)}, f32[6,8,18]{2,1,0:T(8,128)S(1)}, u32[]{:S(2)}, u32[]{:S(2)}) collective-permute-start(f32[6,8,18]{2,1,0:T(8,128)S(1)} %bitcast.231), channel_id=1, source_target_pairs={{1,0},{2,1},{3,2},{4,3},{5,4},{6,5},{7,6},{9,8},{10,9},{11,10},{12... | collective-permute-start | bytes 10376 | tf_op jit(solution)/shard_map/ppermute | solution.py:153
  36.8 5.8 %collective-permute-start.2 = (f32[6,8,18]{2,1,0:T(8,128)S(1)}, f32[6,8,18]{2,1,0:T(8,128)S(1)}, u32[]{:S(2)}, u32[]{:S(2)}) collective-permute-start(f32[6,8,18]{2,1,0:T(8,128)S(1)} %bitcast.233), channel_id=1, source_target_pairs={{0,1},{1,2},{2,3},{3,4},{4,5},{5,6},{6,7},{8,9},{9,10},{10,11},{11... | collective-permute-start | bytes 10376 | tf_op jit(solution)/shard_map/ppermute | solution.py:150
  76.1 17.0 %all-to-all-start.1 = ((f32[32,5,3,128]{3,2,1,0:T(4,128)}), f32[32,5,3,128]{3,2,1,0:T(4,128)S(1)}, u32[]{:S(2)}, u32[]{:S(2)}) async-start(f32[32,5,3,128]{3,2,1,0:T(4,128)} %copy.254), calls=%async_computation.1 | async-start | bytes 655360 | tf_op jit(solution)/shard_map/all_to_all | solution.py:353
  83.8 20.1 %copy-start = (f32[3,8,16,256]{3,2,1,0:T(8,128)S(1)}, f32[3,8,16,256]{3,2,1,0:T(8,128)}, u32[]{:S(2)}) copy-start(f32[3,8,16,256]{3,2,1,0:T(8,128)} %param.14) | copy-start | bytes 1179652
  105.4 5.6 %collective-permute-start.5 = (f32[3,8,256]{2,1,0:T(8,128)S(1)}, f32[3,8,256]{2,1,0:T(8,128)S(1)}, u32[]{:S(2)}, u32[]{:S(2)}) collective-permute-start(f32[3,8,256]{2,1,0:T(8,128)S(1)} %get-tuple-element.60), channel_id=1, source_target_pairs={{8,0},{16,8},{24,16},{9,1},{17,9},{25,17},{10,2},{18,10},{26,18},{... | collective-permute-start | bytes 73736 | tf_op jit(solution)/shard_map/ppermute | solution.py:153
  107.7 4.2 %collective-permute-start.4 = (f32[3,8,256]{2,1,0:T(8,128)S(1)}, f32[3,8,256]{2,1,0:T(8,128)S(1)}, u32[]{:S(2)}, u32[]{:S(2)}) collective-permute-start(f32[3,8,256]{2,1,0:T(8,128)S(1)} %get-tuple-element.59), channel_id=1, source_target_pairs={{0,8},{8,16},{16,24},{1,9},{9,17},{17,25},{2,10},{10,18},{18,26},{... | collective-permute-start | bytes 73736 | tf_op jit(solution)/shard_map/ppermute | solution.py:150
  112.3 6.4 %collective-permute-start.7 = (f32[3,8,18]{2,1,0:T(8,128)S(1)}, f32[3,8,18]{2,1,0:T(8,128)S(1)}, u32[]{:S(2)}, u32[]{:S(2)}) collective-permute-start(f32[3,8,18]{2,1,0:T(8,128)S(1)} %bitcast.236), channel_id=1, source_target_pairs={{1,0},{2,1},{3,2},{4,3},{5,4},{6,5},{7,6},{9,8},{10,9},{11,10},{12... | collective-permute-start | bytes 5192 | tf_op jit(solution)/shard_map/ppermute | solution.py:153
  115.7 5.4 %collective-permute-start.6 = (f32[3,8,18]{2,1,0:T(8,128)S(1)}, f32[3,8,18]{2,1,0:T(8,128)S(1)}, u32[]{:S(2)}, u32[]{:S(2)}) collective-permute-start(f32[3,8,18]{2,1,0:T(8,128)S(1)} %bitcast.238), channel_id=1, source_target_pairs={{0,1},{1,2},{2,3},{3,4},{4,5},{5,6},{6,7},{8,9},{9,10},{10,11},{11... | collective-permute-start | bytes 5192 | tf_op jit(solution)/shard_map/ppermute | solution.py:150

commit v22 on v21

--- a/solution.py
+++ b/solution.py
@@ -358,11 +358,14 @@
         tiled=True,
     )
     slave_force = jnp.take(returned.reshape(item_total, 3, seg_width), target_slot, axis=0)
+    scale = TIME_STEP / node_mass
+    base = velocity + TIME_STEP * stress / node_mass[None]
+    base, scale, master_contact = lax.optimization_barrier((base, scale, master_contact))
     contact = node_scatter_add(
         slave_force.transpose(1, 0, 2).reshape(3, -1), slave_node.reshape(-1), master_contact
     )
     contact_field = contact.reshape(3, layers, row_cells, col_cells)
-    velocity_new = velocity + TIME_STEP * (stress + contact_field) / node_mass[None]
+    velocity_new = base + scale[None] * contact_field
     padded_new = padded_2(velocity_new, (("gx", 2), ("gy", 3)), 1)
     node_rate = nodal_rate(padded_new, inside)
     return (velocity_new, node_rate)

time: 126 us -> 126 us (level)
  the two profiles are of different devices: /device:TPU:9 before, /device:TPU:10 now
where the time goes in v22:
time: 126 us; the launch traced here: 125 us
  other arithmetic  37.7 us (30%)
  starting transfers between devices  32 us (25%)
  Pallas kernels  27.9 us (22%)
  waiting for transfers between devices  13.4 us (11%)
  local copies, waits for them, and re-layouts  12.5 us (10%)
  between operations  1.47 us (1%)
    reduce_sum x1, other arithmetic, contact_pairs(): jnp.sum(push_force * normal_x, axis=1)  26.4 us
    pallas_call x2, Pallas kernels, node_gather(): pl.pallas_call(gather_kernel, grid=(padded_count // tile,), in_specs=[pl....  15.2 us
    pallas_call x2, Pallas kernels, node_scatter_add(): pl.pallas_call(scatter_kernel, grid=(padded_count // tile,), in_specs=[pl...  12.8 us
    ppermute x4, starting transfers between devices, padded_2(): lax.ppermute(lax.index_in_dim(block, 0, axis=dim, keepdims=False), axis,...  11.8 us
    ppermute x4, starting transfers between devices, padded_2(): lax.ppermute(lax.index_in_dim(block, block.shape[dim] - 1, axis=dim, keep...  9.35 us
    ppermute x4, waiting for transfers between devices, padded_2(): lax.ppermute(lax.index_in_dim(block, block.shape[dim] - 1, axis=dim, keep...  8.89 us
    all_to_all x1, starting transfers between devices, on_device(): lax.all_to_all(outgoing.reshape(devices, slot_depth, 8, seg_width), ('gx'...  6.02 us
    all_to_all x1, starting transfers between devices, on_device(): lax.all_to_all(forces.reshape(devices, slot_depth, 3, seg_width), ('gx',...  4.82 us
  transfers between devices with their start and end apart: 10, of which 4 were waited for; matrix products, arithmetic and copies ran while one was open for 10% of the time, Pallas kernels for 6%

profile of v22, /device:TPU:10, one launch (start us, length us, event | category | flops | bytes accessed | tf_op | source)
XLA Modules:
  0.0 125.2 jit_solution(5425446593687006954)
XLA Ops:
  0.6 11.2 %shard_map.149 = f32[3,16384]{1,0:T(4,128)} custom-call(s32[1,16384]{1,0:T(1,128)} %bitcast.202, f32[3,128,256]{2,1,0:T(8,128)} %bitcast.183), custom_call_target="tpu_custom_call" | custom-call | tf_op jit(solution)/shard_map/pallas_call | solution.py:106
  11.8 1.3 %copy.231 = f32[3,8,16,256]{3,1,0,2:T(8,128)S(1)} copy(f32[3,8,16,256]{3,2,1,0:T(8,128)} %param.14) | data formatting | bytes 786432 | tf_op jit(solution)/shard_map/optimization_barrier | solution.py:289
  13.4 1.9 %collective-permute-start.1 = (f32[6,8,256]{2,1,0:T(8,128)S(1)}, f32[6,8,256]{2,1,0:T(8,128)S(1)}, u32[]{:S(2)}, u32[]{:S(2)}) collective-permute-start(f32[6,8,256]{2,1,0:T(8,128)S(1)} %get-tuple-element.52), channel_id=1, source_target_pairs={{8,0},{16,8},{24,16},{9,1},{17,9},{25,17},{10,2},{18,10},{26,18},{... | collective-permute-start | bytes 147464 | tf_op jit(solution)/shard_map/ppermute | solution.py:153
  15.3 2.4 %collective-permute-start = (f32[6,8,256]{2,1,0:T(8,128)S(1)}, f32[6,8,256]{2,1,0:T(8,128)S(1)}, u32[]{:S(2)}, u32[]{:S(2)}) collective-permute-start(f32[6,8,256]{2,1,0:T(8,128)S(1)} %get-tuple-element.51), channel_id=1, source_target_pairs={{0,8},{8,16},{16,24},{1,9},{9,17},{17,25},{2,10},{10,18},{18,26},{... | collective-permute-start | bytes 147464 | tf_op jit(solution)/shard_map/ppermute | solution.py:150
  19.2 0.8 gather_fusion
  20.0 1.2 select_select_fusion
  21.3 6.0 %all-to-all-start = ((f32[32,5,8,128]{3,2,1,0:T(8,128)}), f32[32,5,8,128]{3,2,1,0:T(8,128)S(1)}, u32[]{:S(2)}, u32[]{:S(2)}) async-start(f32[32,5,8,128]{3,2,1,0:T(8,128)} %select_select_fusion), calls=%async_computation | async-start | bytes 1310720 | tf_op jit(solution)/shard_map/all_to_all | solution.py:328
  27.4 4.0 %shard_map.150 = f32[3,4096]{1,0:T(4,128)} custom-call(s32[1,4096]{1,0:T(1,128)} %bitcast.229, f32[3,128,256]{2,1,0:T(8,128)} %bitcast.184), custom_call_target="tpu_custom_call" | custom-call | tf_op jit(solution)/shard_map/pallas_call | solution.py:106
  31.4 0.9 copy_add_fusion.1
  33.5 3.4 %collective-permute-start.3 = (f32[6,8,18]{2,1,0:T(8,128)S(1)}, f32[6,8,18]{2,1,0:T(8,128)S(1)}, u32[]{:S(2)}, u32[]{:S(2)}) collective-permute-start(f32[6,8,18]{2,1,0:T(8,128)S(1)} %bitcast.231), channel_id=1, source_target_pairs={{1,0},{2,1},{3,2},{4,3},{5,4},{6,5},{7,6},{9,8},{10,9},{11,10},{12... | collective-permute-start | bytes 10376 | tf_op jit(solution)/shard_map/ppermute | solution.py:153
  37.3 2.6 %collective-permute-start.2 = (f32[6,8,18]{2,1,0:T(8,128)S(1)}, f32[6,8,18]{2,1,0:T(8,128)S(1)}, u32[]{:S(2)}, u32[]{:S(2)}) collective-permute-start(f32[6,8,18]{2,1,0:T(8,128)S(1)} %bitcast.233), channel_id=1, source_target_pairs={{0,1},{1,2},{2,3},{3,4},{4,5},{5,6},{6,7},{8,9},{9,10},{10,11},{11... | collective-permute-start | bytes 10376 | tf_op jit(solution)/shard_map/ppermute | solution.py:150
  41.5 2.7 %collective-permute-done.2 = f32[6,8,18]{2,1,0:T(8,128)S(1)} collective-permute-done((f32[6,8,18]{2,1,0:T(8,128)S(1)}, f32[6,8,18]{2,1,0:T(8,128)S(1)}, u32[]{:S(2)}, u32[]{:S(2)}) %collective-permute-start.2) | collective-permute-done | bytes 3488 | tf_op jit(solution)/shard_map/ppermute | solution.py:150
  46.6 1.3 %fusion.79 = (f32[160,1,128]{2,1,0:T(1,128)S(1)}, f32[160,1,128]{2,1,0:T(1,128)S(1)}, f32[160,1,128]{2,1,0:T(1,128)S(1)}, f32[160,1,128]{2,1,0:T(1,128)S(1)}, f3...) fusion(f32[160,8,128]{2,1,0:T(8,128)S(1)} %bitcast.185), kind=kLoop, calls=%fused_computation.187 | loop fusion | flops 20320 | bytes 1229440 | tf_op jit(solution)/shard_map/slice | solution.py:233
  47.9 0.8 gather_fusion.1
  49.6 26.4 %multiply_reduce_fusion.2 = (f32[160,128]{1,0:T(8,128)S(1)}, f32[160,128]{1,0:T(8,128)S(1)}, f32[160,128]{1,0:T(8,128)S(1)}, f32[160,128]{1,0:T(8,128)S(1)}) fusion(f32[160,128]{1,0:T(8,128)S(1)} %bitcast.197, f32[160,128]{1,0:T(8,128)S(1)} %multiply_add_fusion, f32[160,128]{1,0:T(8,128)S(1)} %bitcast.217, f32[160,128]{1,0:T(8,128)S(1)} %bitcast.218, ...), kind=kLoop, calls=%fused_computation.21 | loop fusion | flops 104775680 | bytes 1556480 | tf_op jit(solution)/shard_map/reduce_sum | solution.py:241
  76.2 0.9 copy.262
  77.1 4.8 %all-to-all-start.1 = ((f32[32,5,3,128]{3,2,1,0:T(4,128)}), f32[32,5,3,128]{3,2,1,0:T(4,128)S(1)}, u32[]{:S(2)}, u32[]{:S(2)}) async-start(f32[32,5,3,128]{3,2,1,0:T(4,128)} %copy.262), calls=%async_computation.1 | async-start | bytes 655360 | tf_op jit(solution)/shard_map/all_to_all | solution.py:353
  83.2 0.8 broadcast_in_dim.137.init_ref
  84.0 3.7 %shard_map.151.init_ref = f32[3,128,256]{2,1,0:T(8,128)} custom-call(s32[1,4096]{1,0:T(1,128)} %bitcast.230, f32[3,4096]{1,0:T(4,128)} %bitcast.204, f32[3,128,256]{2,1,0:T(8,128)} %broadcast_in_dim.137.init_ref), custom_call_target="tpu_custom_call" | custom-call | tf_op jit(solution)/shard_map/pallas_call | solution.py:124
  87.7 4.4 %all-to-all-done.1 = f32[32,5,3,128]{3,2,1,0:T(4,128)S(1)} async-done(((f32[32,5,3,128]{3,2,1,0:T(4,128)}), f32[32,5,3,128]{3,2,1,0:T(4,128)S(1)}, u32[]{:S(2)}, u32[]{:S(2)}) %all-to-all-start.1) | async-done | bytes 245792 | tf_op jit(solution)/shard_map/all_to_all | solution.py:353
  92.2 0.9 gather_fusion.2
  93.1 0.9 select_bitcast_fusion.force_ref
  94.0 9.0 %shard_map.152 = f32[3,128,256]{2,1,0:T(8,128)} custom-call(s32[1,16384]{1,0:T(1,128)} %bitcast.203, f32[3,16384]{1,0:T(4,128)} %select_bitcast_fusion.force_ref, f32[3,128,256]{2,1,0:T(8,128)} %shard_map.151.init_ref), custom_call_target="tpu_custom_call" | custom-call | tf_op jit(solution)/shard_map/pallas_call | solution.py:124
  103.0 1.3 %fusion.14 = f32[3,8,16,256]{3,1,2,0:T(8,128)S(1)} fusion(f32[3,8,16,256]{3,1,2,0:T(8,128)S(1)} %fusion.13, f32[3,8,16,256]{3,2,1,0:T(8,128)} %bitcast.189, f32[8,16,256]{2,0,1:T(8,128)S(1)} %copy.261), kind=kLoop, calls=%fused_computation.43 | loop fusion | flops 196608 | bytes 1310720 | tf_op jit(solution)/shard_map/add | solution.py:368
  104.3 3.1 %collective-permute-start.5 = (f32[3,8,256]{2,1,0:T(8,128)S(1)}, f32[3,8,256]{2,1,0:T(8,128)S(1)}, u32[]{:S(2)}, u32[]{:S(2)}) collective-permute-start(f32[3,8,256]{2,1,0:T(8,128)S(1)} %get-tuple-element.66), channel_id=1, source_target_pairs={{8,0},{16,8},{24,16},{9,1},{17,9},{25,17},{10,2},{18,10},{26,18},{... | collective-permute-start | bytes 73736 | tf_op jit(solution)/shard_map/ppermute | solution.py:153
  107.4 1.9 %collective-permute-start.4 = (f32[3,8,256]{2,1,0:T(8,128)S(1)}, f32[3,8,256]{2,1,0:T(8,128)S(1)}, u32[]{:S(2)}, u32[]{:S(2)}) collective-permute-start(f32[3,8,256]{2,1,0:T(8,128)S(1)} %get-tuple-element.65), channel_id=1, source_target_pairs={{0,8},{8,16},{16,24},{1,9},{9,17},{17,25},{2,10},{10,18},{18,26},{... | collective-permute-start | bytes 73736 | tf_op jit(solution)/shard_map/ppermute | solution.py:150
  109.4 3.2 %collective-permute-done.4 = f32[3,8,256]{2,1,0:T(8,128)S(1)} collective-permute-done((f32[3,8,256]{2,1,0:T(8,128)S(1)}, f32[3,8,256]{2,1,0:T(8,128)S(1)}, u32[]{:S(2)}, u32[]{:S(2)}) %collective-permute-start.4) | collective-permute-done | bytes 24608 | tf_op jit(solution)/shard_map/ppermute | solution.py:150
  113.0 3.4 %collective-permute-start.7 = (f32[3,8,18]{2,1,0:T(8,128)S(1)}, f32[3,8,18]{2,1,0:T(8,128)S(1)}, u32[]{:S(2)}, u32[]{:S(2)}) collective-permute-start(f32[3,8,18]{2,1,0:T(8,128)S(1)} %bitcast.236), channel_id=1, source_target_pairs={{1,0},{2,1},{3,2},{4,3},{5,4},{6,5},{7,6},{9,8},{10,9},{11,10},{12... | collective-permute-start | bytes 5192 | tf_op jit(solution)/shard_map/ppermute | solution.py:153
  116.7 2.4 %collective-permute-start.6 = (f32[3,8,18]{2,1,0:T(8,128)S(1)}, f32[3,8,18]{2,1,0:T(8,128)S(1)}, u32[]{:S(2)}, u32[]{:S(2)}) collective-permute-start(f32[3,8,18]{2,1,0:T(8,128)S(1)} %bitcast.238), channel_id=1, source_target_pairs={{0,1},{1,2},{2,3},{3,4},{4,5},{5,6},{6,7},{8,9},{9,10},{10,11},{11... | collective-permute-start | bytes 5192 | tf_op jit(solution)/shard_map/ppermute | solution.py:150
  119.1 0.9 copy.272
  120.2 3.0 %collective-permute-done.6 = f32[3,8,18]{2,1,0:T(8,128)S(1)} collective-permute-done((f32[3,8,18]{2,1,0:T(8,128)S(1)}, f32[3,8,18]{2,1,0:T(8,128)S(1)}, u32[]{:S(2)}, u32[]{:S(2)}) %collective-permute-start.6) | collective-permute-done | bytes 1760 | tf_op jit(solution)/shard_map/ppermute | solution.py:150
  124.5 0.7 copy.273
  (119 shorter events, 11.3 us)
Async XLA Ops:
  0.6 12.5 %copy-start.6 = (f32[8,16,256]{2,1,0:T(8,128)S(1)}, f32[8,16,256]{2,1,0:T(8,128)}, u32[]{:S(2)}) copy-start(f32[8,16,256]{2,1,0:T(8,128)} %param.15) | copy-start | bytes 393220
  0.6 12.5 %copy-start.5 = (f32[8,16,256]{2,1,0:T(8,128)S(1)}, f32[8,16,256]{2,1,0:T(8,128)}, u32[]{:S(2)}) copy-start(f32[8,16,256]{2,1,0:T(8,128)} %param.16) | copy-start | bytes 393220
  11.8 5.9 %copy-start.13 = (s32[128,1]{0,1:T(1,128)S(1)}, s32[128,1]{0,1:T(1,128)}, u32[]{:S(2)}) copy-start(s32[128,1]{0,1:T(1,128)} %param.22) | copy-start | bytes 1540
  11.8 6.3 %copy-start.14 = (s32[128]{0:T(128)S(1)}, s32[128]{0:T(128)}, u32[]{:S(2)}) copy-start(s32[128]{0:T(128)} %param.23) | copy-start | bytes 1540
  11.8 6.6 %copy-start.7 = (f32[128,128]{1,0:T(8,128)S(1)}, f32[128,128]{1,0:T(8,128)}, u32[]{:S(2)}) copy-start(f32[128,128]{1,0:T(8,128)} %param.19) | copy-start | bytes 196612
  11.8 6.6 %copy-start.12 = (s32[128]{0:T(128)S(1)}, s32[128]{0:T(128)}, u32[]{:S(2)}) copy-start(s32[128]{0:T(128)} %param.20) | copy-start | bytes 1540
  11.8 6.7 %copy-start.1 = (f32[3,16384]{1,0:T(4,128)S(1)}, f32[3,16384]{1,0:T(4,128)}, u32[]{:S(2)}) copy-start(f32[3,16384]{1,0:T(4,128)} %shard_map.149) | copy-start | bytes 589828
  11.8 6.7 %copy-start.4 = (f32[128,3,128]{2,0,1:T(8,128)S(1)}, f32[128,3,128]{2,0,1:T(8,128)}, u32[]{:S(2)}) copy-start(f32[128,3,128]{2,0,1:T(8,128)} %param.18) | copy-start | bytes 589828
  13.4 19.5 %collective-permute-start.1 = (f32[6,8,256]{2,1,0:T(8,128)S(1)}, f32[6,8,256]{2,1,0:T(8,128)S(1)}, u32[]{:S(2)}, u32[]{:S(2)}) collective-permute-start(f32[6,8,256]{2,1,0:T(8,128)S(1)} %get-tuple-element.52), channel_id=1, source_target_pairs={{8,0},{16,8},{24,16},{9,1},{17,9},{25,17},{10,2},{18,10},{26,18},{... | collective-permute-start | bytes 147464 | tf_op jit(solution)/shard_map/ppermute | solution.py:153
  15.3 17.6 %collective-permute-start = (f32[6,8,256]{2,1,0:T(8,128)S(1)}, f32[6,8,256]{2,1,0:T(8,128)S(1)}, u32[]{:S(2)}, u32[]{:S(2)}) collective-permute-start(f32[6,8,256]{2,1,0:T(8,128)S(1)} %get-tuple-element.51), channel_id=1, source_target_pairs={{0,8},{8,16},{16,24},{1,9},{9,17},{17,25},{2,10},{10,18},{18,26},{... | collective-permute-start | bytes 147464 | tf_op jit(solution)/shard_map/ppermute | solution.py:150
  20.0 7.3 %copy-start.3 = (f32[8,16,256]{2,1,0:T(8,128)S(1)}, f32[8,16,256]{2,1,0:T(8,128)}, u32[]{:S(2)}) copy-start(f32[8,16,256]{2,1,0:T(8,128)} %param.17) | copy-start | bytes 393220
  20.0 7.3 %copy-start.9 = (f32[32,2,128]{2,1,0:T(2,128)S(1)}, f32[32,2,128]{2,1,0:T(2,128)}, u32[]{:S(2)}) copy-start(f32[32,2,128]{2,1,0:T(2,128)} %param.25) | copy-start | bytes 98308
  21.3 10.2 %copy-start.8 = (f32[32,3,128]{2,0,1:T(8,128)S(1)}, f32[32,3,128]{2,0,1:T(8,128)}, u32[]{:S(2)}) copy-start(f32[32,3,128]{2,0,1:T(8,128)} %param.24) | copy-start | bytes 147460
  21.3 25.3 %all-to-all-start = ((f32[32,5,8,128]{3,2,1,0:T(8,128)}), f32[32,5,8,128]{3,2,1,0:T(8,128)S(1)}, u32[]{:S(2)}, u32[]{:S(2)}) async-start(f32[32,5,8,128]{3,2,1,0:T(8,128)} %select_select_fusion), calls=%async_computation | async-start | bytes 1310720 | tf_op jit(solution)/shard_map/all_to_all | solution.py:328
  32.9 7.7 %copy-start.2 = (f32[3,4096]{1,0:T(4,128)S(1)}, f32[3,4096]{1,0:T(4,128)}, u32[]{:S(2)}) copy-start(f32[3,4096]{1,0:T(4,128)} %shard_map.150) | copy-start | bytes 147460
  33.0 7.7 %copy-start.10 = (f32[32,128]{1,0:T(8,128)S(1)}, f32[32,128]{1,0:T(8,128)}, u32[]{:S(2)}) copy-start(f32[32,128]{1,0:T(8,128)} %param.26) | copy-start | bytes 49156
  33.5 7.5 %collective-permute-start.3 = (f32[6,8,18]{2,1,0:T(8,128)S(1)}, f32[6,8,18]{2,1,0:T(8,128)S(1)}, u32[]{:S(2)}, u32[]{:S(2)}) collective-permute-start(f32[6,8,18]{2,1,0:T(8,128)S(1)} %bitcast.231), channel_id=1, source_target_pairs={{1,0},{2,1},{3,2},{4,3},{5,4},{6,5},{7,6},{9,8},{10,9},{11,10},{12... | collective-permute-start | bytes 10376 | tf_op jit(solution)/shard_map/ppermute | solution.py:153
  37.3 6.9 %collective-permute-start.2 = (f32[6,8,18]{2,1,0:T(8,128)S(1)}, f32[6,8,18]{2,1,0:T(8,128)S(1)}, u32[]{:S(2)}, u32[]{:S(2)}) collective-permute-start(f32[6,8,18]{2,1,0:T(8,128)S(1)} %bitcast.233), channel_id=1, source_target_pairs={{0,1},{1,2},{2,3},{3,4},{4,5},{5,6},{6,7},{8,9},{9,10},{10,11},{11... | collective-permute-start | bytes 10376 | tf_op jit(solution)/shard_map/ppermute | solution.py:150
  76.1 5.8 %copy-start = (f32[3,8,16,256]{3,2,1,0:T(8,128)S(1)}, f32[3,8,16,256]{3,2,1,0:T(8,128)}, u32[]{:S(2)}) copy-start(f32[3,8,16,256]{3,2,1,0:T(8,128)} %param.14) | copy-start | bytes 1179652
  77.1 15.1 %all-to-all-start.1 = ((f32[32,5,3,128]{3,2,1,0:T(4,128)}), f32[32,5,3,128]{3,2,1,0:T(4,128)S(1)}, u32[]{:S(2)}, u32[]{:S(2)}) async-start(f32[32,5,3,128]{3,2,1,0:T(4,128)} %copy.262), calls=%async_computation.1 | async-start | bytes 655360 | tf_op jit(solution)/shard_map/all_to_all | solution.py:353
  82.2 10.9 %copy-start.11 = (pred[128]{0:T(512)(128)(4,1)S(1)}, pred[128]{0:T(512)(128)(4,1)}, u32[]{:S(2)}) copy-start(pred[128]{0:T(512)(128)(4,1)} %get-tuple-element.32) | copy-start | bytes 388
  104.3 5.0 %collective-permute-start.5 = (f32[3,8,256]{2,1,0:T(8,128)S(1)}, f32[3,8,256]{2,1,0:T(8,128)S(1)}, u32[]{:S(2)}, u32[]{:S(2)}) collective-permute-start(f32[3,8,256]{2,1,0:T(8,128)S(1)} %get-tuple-element.66), channel_id=1, source_target_pairs={{8,0},{16,8},{24,16},{9,1},{17,9},{25,17},{10,2},{18,10},{26,18},{... | collective-permute-start | bytes 73736 | tf_op jit(solution)/shard_map/ppermute | solution.py:153
  107.4 5.1 %collective-permute-start.4 = (f32[3,8,256]{2,1,0:T(8,128)S(1)}, f32[3,8,256]{2,1,0:T(8,128)S(1)}, u32[]{:S(2)}, u32[]{:S(2)}) collective-permute-start(f32[3,8,256]{2,1,0:T(8,128)S(1)} %get-tuple-element.65), channel_id=1, source_target_pairs={{0,8},{8,16},{16,24},{1,9},{9,17},{17,25},{2,10},{10,18},{18,26},{... | collective-permute-start | bytes 73736 | tf_op jit(solution)/shard_map/ppermute | solution.py:150
  113.0 7.0 %collective-permute-start.7 = (f32[3,8,18]{2,1,0:T(8,128)S(1)}, f32[3,8,18]{2,1,0:T(8,128)S(1)}, u32[]{:S(2)}, u32[]{:S(2)}) collective-permute-start(f32[3,8,18]{2,1,0:T(8,128)S(1)} %bitcast.236), channel_id=1, source_target_pairs={{1,0},{2,1},{3,2},{4,3},{5,4},{6,5},{7,6},{9,8},{10,9},{11,10},{12... | collective-permute-start | bytes 5192 | tf_op jit(solution)/shard_map/ppermute | solution.py:153
  116.7 6.5 %collective-permute-start.6 = (f32[3,8,18]{2,1,0:T(8,128)S(1)}, f32[3,8,18]{2,1,0:T(8,128)S(1)}, u32[]{:S(2)}, u32[]{:S(2)}) collective-permute-start(f32[3,8,18]{2,1,0:T(8,128)S(1)} %bitcast.238), channel_id=1, source_target_pairs={{0,1},{1,2},{2,3},{3,4},{4,5},{5,6},{6,7},{8,9},{9,10},{10,11},{11... | collective-permute-start | bytes 5192 | tf_op jit(solution)/shard_map/ppermute | solution.py:150
